TPU v7x, 512 devices: a whole 4x4x16 slice. The times are simulated.
512 devices in a mesh: context: 64 (over x, z), tensor: 8 (over y, core).
Axes of the slice: x: 4, y: 4, z: 16, core: 2. Of those that a mesh axis runs over, the one named last changes fastest.
Arguments:
- inputs: bfloat16 [8192, 8192], P('context', 'tensor'), may hold values from -0.8984375 to 0.8984375
- grads: bfloat16 [8192, 8192], P('context', 'tensor'), may hold values from -0.8984375 to 0.8984375
- step_size: float32 [128, 8192], P('tensor', 'context'), may hold values from 0.25 to 4
- decay_rate: float32 [128], P('tensor'), may hold values from 0 to 1, as said below
- skip_gain: float32 [128], P('tensor'), may hold values from 0.5 to 1.5
- b_rows: bfloat16 [8192, 128], P(('context', 'tensor')), may hold values from -0.59765625 to 0.59765625
- c_rows: bfloat16 [8192, 128], P(('context', 'tensor')), may hold values from -0.59765625 to 0.59765625
- doc_lengths: int32 [64], replicated, may hold values from 1 to 1536, 8192 in all
Outputs:
- grad_x: float32 [8192, 8192], P('context', 'tensor')
- grad_step: float32 [128, 8192], P('tensor', 'context')
- grad_b: float32 [8192, 128], P(('context', 'tensor'))
- grad_c: float32 [8192, 128], P(('context', 'tensor'))
Inputs may be any that keep to these rules, and one draw needn't show every extreme that they name: doc_lengths sum to 8192; the longest document has exactly 1536 tokens. `decay_rate`: decay rates are positive.
All inputs are finite; a program needn't handle non-finite values.
Results may differ from a plain program's by a relative error of at most 0.0005.
Values may be sent and summed in bfloat16 or wider, within the bound.
No kernel may reach another device: no remote copies, remote signals or barrier semaphores. Data moves between devices by JAX's collectives and lax.ppermute only.
A program may use at most 192 MiB of HBM per device.

v0:
```python
import jax
import jax.numpy as jnp
from jax import lax
from jax.sharding import PartitionSpec as P

HIGH = lax.Precision.HIGHEST


def from_behind(x, axis, by):
    peers = lax.axis_size(axis)
    pairs = [(i, i + by) for i in range(peers) if 0 <= i + by < peers]
    return lax.ppermute(x, axis, pairs)


def local(inputs, grads, step_size, decay_rate, skip_gain, b_rows, c_rows, doc_lengths):
    b_all, c_all = (
        lax.all_gather(b_rows, "tensor", axis=0, tiled=True),
        lax.all_gather(c_rows, "tensor", axis=0, tiled=True),
    )
    bmat = b_all.astype(jnp.float32)
    cmat = c_all.astype(jnp.float32)
    length = inputs.shape[0]
    heads = step_size.shape[0]
    width = inputs.shape[1] // heads
    xs_heads = inputs.astype(jnp.float32).reshape(length, heads, width).transpose(1, 0, 2)
    dy_heads = grads.astype(jnp.float32).reshape(length, heads, width).transpose(1, 0, 2)
    offset = lax.axis_index("context") * length
    ends = jnp.cumsum(doc_lengths)
    starts = ends - doc_lengths
    position = offset + jnp.arange(length, dtype=jnp.int32)
    seg = jnp.sum(
        ((starts[None, :] >= offset) & (starts[None, :] <= position[:, None])).astype(jnp.int32),
        axis=1,
    )
    logc = jnp.cumsum(-step_size * decay_rate[:, None], axis=1)
    enter = jnp.exp(logc) * (seg == 0).astype(jnp.float32)[None, :]
    leave = jnp.exp(logc[:, -1:] - logc) * (seg == seg[-1]).astype(jnp.float32)[None, :]
    total = enter[:, -1]
    moved = step_size[:, :, None] * xs_heads
    local_state = jnp.einsum("hlp,ln->hpn", leave[:, :, None] * moved, bmat, precision=HIGH)
    local_adj = jnp.einsum("hlp,ln->hpn", enter[:, :, None] * dy_heads, cmat, precision=HIGH)
    turns = 3 * lax.axis_size("context") // 16

    def turn(step, carry):
        inc_state, inc_adj = carry
        out_state = local_state + total[:, None, None] * inc_state
        out_adj = local_adj + total[:, None, None] * inc_adj
        inc_state = from_behind(out_state, "context", 1)
        inc_adj = from_behind(out_adj, "context", -1)
        return (inc_state, inc_adj)

    empty = jnp.zeros_like(local_state)
    state_in, adj_in = lax.fori_loop(0, turns, turn, (empty, empty))
    index = jnp.arange(length)
    keep = (index[:, None] >= index[None, :]) & (seg[:, None] == seg[None, :])
    scores = jnp.dot(cmat, bmat.T, precision=HIGH)

    def per_head(items):
        xh, dyh, uh, dth, lch, enh, lvh, rate, skip, s_in, g_in = items
        weights = jnp.exp(jnp.where(keep, lch[:, None] - lch[None, :], -1e30))
        mixed = weights * scores
        b_adj = jnp.dot(bmat, g_in.T, precision=HIGH)
        core = jnp.dot(mixed.T, dyh, precision=HIGH) + lvh[:, None] * b_adj
        gx = dth[:, None] * core + skip * dyh
        along = jnp.sum(xh * core, axis=1)
        pairs = jnp.dot(dyh, uh.T, precision=HIGH)
        paired = mixed * pairs
        col_total = jnp.sum(paired, axis=0)
        row_total = jnp.sum(paired, axis=1)
        inner = jnp.cumsum(col_total) - (jnp.cumsum(row_total) - row_total)
        c_state = jnp.dot(cmat, s_in.T, precision=HIGH)
        from_state = enh * jnp.dot(weights.T, jnp.sum(dyh * c_state, axis=1), precision=HIGH)
        from_adj = lvh * jnp.dot(weights, jnp.sum(uh * b_adj, axis=1), precision=HIGH)
        both = lvh * enh * jnp.sum(g_in * s_in)
        intersection_sum = inner + from_state + from_adj + both
        gdt = along * (1.0 + rate * dth) - rate * intersection_sum
        weighted = weights * pairs
        gb = jnp.dot(weighted.T, cmat, precision=HIGH) + jnp.dot(
            lvh[:, None] * uh, g_in, precision=HIGH
        )
        gc = jnp.dot(weighted, bmat, precision=HIGH) + enh[:, None] * jnp.dot(
            dyh, s_in, precision=HIGH
        )
        return (gx, gdt, gb, gc)

    gx, grad_step, gb, gc = lax.map(
        per_head,
        (
            xs_heads,
            dy_heads,
            moved,
            step_size,
            logc,
            enter,
            leave,
            decay_rate,
            skip_gain,
            state_in,
            adj_in,
        ),
    )
    grad_x = gx.transpose(1, 0, 2).reshape(length, heads * width)
    grad_b, grad_c = (
        lax.psum_scatter(jnp.sum(gb, axis=0), "tensor", scatter_dimension=0, tiled=True),
        lax.psum_scatter(jnp.sum(gc, axis=0), "tensor", scatter_dimension=0, tiled=True),
    )
    return (grad_x, grad_step, grad_b, grad_c)


def solution(mesh):
    in_specs = (
        P("context", "tensor"),
        P("context", "tensor"),
        P("tensor", "context"),
        P("tensor"),
        P("tensor"),
        P(("context", "tensor"), None),
        P(("context", "tensor"), None),
        P(),
    )
    out_specs = (
        P("context", "tensor"),
        P("tensor", "context"),
        P(("context", "tensor"), None),
        P(("context", "tensor"), None),
    )
    return jax.shard_map(local, mesh=mesh, in_specs=in_specs, out_specs=out_specs, check_vma=False)
```

profile of v0, /device:TPU:4, one launch (start us, length us, event | category | flops | bytes accessed | tf_op | source)
XLA Modules:
  0.0 571.9 jit_solution(3596716359012853880)
XLA Ops:
  7.2 13.5 %all_gather.7 = bf16[128,128]{1,0:T(8,128)(2,1)S(1)} all-gather(bf16[16,128]{1,0:T(8,128)(2,1)} %param.17), channel_id=1, replica_groups=mesh['context'=64,'tensor'=8] {'tensor'}, dimensions={0}, use_global_device_ids=true | all-gather | bytes 36864 | tf_op jit(solution)/shard_map/all_gather | solution.py:17
  20.7 12.8 %all_gather.6 = bf16[128,128]{1,0:T(8,128)(2,1)S(1)} all-gather(bf16[16,128]{1,0:T(8,128)(2,1)S(1)} %copy-done.8), channel_id=1, replica_groups=mesh['context'=64,'tensor'=8] {'tensor'}, dimensions={0}, use_global_device_ids=true | all-gather | bytes 36864 | tf_op jit(solution)/shard_map/all_gather | solution.py:18
  40.1 207.7 %while.29 = (s32[]{:T(128)}, f32[16,64,128]{2,1,0:T(8,128)S(1)}, f32[16,64,128]{2,1,0:T(8,128)S(1)}, f32[16,1]{0,1:T(1,128)S(1)}, f32[16,64,128]{2,1,0:T(8,128)S(1)}, /*index=5*/f32[16,64,128]{2,1,0:T(8,128)S(1)}, s32[]{:T(128)}) while((s32[]{:T(128)}, f32[16,64,128]{2,1,0:T(8,128)S(1)}, f32[16,64,128]{2,1,0:T(8,128)S(1)}, ...), condition=%wide.region_4.5_spmd, body=%wide.region_3.4_spmd.sunk | while | flops 524290 | bytes 7340253 | solution.py:53
  40.3 3.8 collective-permute-start
  44.1 9.5 %collective-permute-start.1 = (f32[16,64,128]{2,1,0:T(8,128)S(1)}, f32[16,64,128]{2,1,0:T(8,128)S(1)}, u32[]{:S(2)}, u32[]{:S(2)}) collective-permute-start(f32[16,64,128]{2,1,0:T(8,128)S(1)} %get-tuple-element.440), channel_id=1, source_target_pairs={{8,0},{16,8},{24,16},{32,24},{40,32},{48,40},{56,48},{64,56},{72,6... | collective-permute-start | bytes 1572872 | tf_op jit(solution)/shard_map/while/body/eval_jaxpr/ppermute | solution.py:12
  53.6 10.4 %collective-permute-done = f32[16,64,128]{2,1,0:T(8,128)S(1)} collective-permute-done((f32[16,64,128]{2,1,0:T(8,128)S(1)}, f32[16,64,128]{2,1,0:T(8,128)S(1)}, u32[]{:S(2)}, u32[]{:S(2)}) %collective-permute-start) | collective-permute-done | bytes 524320 | tf_op jit(solution)/shard_map/while/body/eval_jaxpr/ppermute | solution.py:12
  65.4 1.9 collective-permute-start
  67.3 6.5 %collective-permute-start.1 = (f32[16,64,128]{2,1,0:T(8,128)S(1)}, f32[16,64,128]{2,1,0:T(8,128)S(1)}, u32[]{:S(2)}, u32[]{:S(2)}) collective-permute-start(f32[16,64,128]{2,1,0:T(8,128)S(1)} %get-tuple-element.440), channel_id=1, source_target_pairs={{8,0},{16,8},{24,16},{32,24},{40,32},{48,40},{56,48},{64,56},{72,6... | collective-permute-start | bytes 1572872 | tf_op jit(solution)/shard_map/while/body/eval_jaxpr/ppermute | solution.py:12
  73.9 9.6 %collective-permute-done = f32[16,64,128]{2,1,0:T(8,128)S(1)} collective-permute-done((f32[16,64,128]{2,1,0:T(8,128)S(1)}, f32[16,64,128]{2,1,0:T(8,128)S(1)}, u32[]{:S(2)}, u32[]{:S(2)}) %collective-permute-start) | collective-permute-done | bytes 524320 | tf_op jit(solution)/shard_map/while/body/eval_jaxpr/ppermute | solution.py:12
  84.8 1.9 collective-permute-start
  86.8 6.5 %collective-permute-start.1 = (f32[16,64,128]{2,1,0:T(8,128)S(1)}, f32[16,64,128]{2,1,0:T(8,128)S(1)}, u32[]{:S(2)}, u32[]{:S(2)}) collective-permute-start(f32[16,64,128]{2,1,0:T(8,128)S(1)} %get-tuple-element.440), channel_id=1, source_target_pairs={{8,0},{16,8},{24,16},{32,24},{40,32},{48,40},{56,48},{64,56},{72,6... | collective-permute-start | bytes 1572872 | tf_op jit(solution)/shard_map/while/body/eval_jaxpr/ppermute | solution.py:12
  93.3 8.7 %collective-permute-done = f32[16,64,128]{2,1,0:T(8,128)S(1)} collective-permute-done((f32[16,64,128]{2,1,0:T(8,128)S(1)}, f32[16,64,128]{2,1,0:T(8,128)S(1)}, u32[]{:S(2)}, u32[]{:S(2)}) %collective-permute-start) | collective-permute-done | bytes 524320 | tf_op jit(solution)/shard_map/while/body/eval_jaxpr/ppermute | solution.py:12
  103.3 1.9 collective-permute-start
  105.3 6.5 %collective-permute-start.1 = (f32[16,64,128]{2,1,0:T(8,128)S(1)}, f32[16,64,128]{2,1,0:T(8,128)S(1)}, u32[]{:S(2)}, u32[]{:S(2)}) collective-permute-start(f32[16,64,128]{2,1,0:T(8,128)S(1)} %get-tuple-element.440), channel_id=1, source_target_pairs={{8,0},{16,8},{24,16},{32,24},{40,32},{48,40},{56,48},{64,56},{72,6... | collective-permute-start | bytes 1572872 | tf_op jit(solution)/shard_map/while/body/eval_jaxpr/ppermute | solution.py:12
  111.8 7.8 %collective-permute-done = f32[16,64,128]{2,1,0:T(8,128)S(1)} collective-permute-done((f32[16,64,128]{2,1,0:T(8,128)S(1)}, f32[16,64,128]{2,1,0:T(8,128)S(1)}, u32[]{:S(2)}, u32[]{:S(2)}) %collective-permute-start) | collective-permute-done | bytes 524320 | tf_op jit(solution)/shard_map/while/body/eval_jaxpr/ppermute | solution.py:12
  120.9 1.9 collective-permute-start
  122.9 6.5 %collective-permute-start.1 = (f32[16,64,128]{2,1,0:T(8,128)S(1)}, f32[16,64,128]{2,1,0:T(8,128)S(1)}, u32[]{:S(2)}, u32[]{:S(2)}) collective-permute-start(f32[16,64,128]{2,1,0:T(8,128)S(1)} %get-tuple-element.440), channel_id=1, source_target_pairs={{8,0},{16,8},{24,16},{32,24},{40,32},{48,40},{56,48},{64,56},{72,6... | collective-permute-start | bytes 1572872 | tf_op jit(solution)/shard_map/while/body/eval_jaxpr/ppermute | solution.py:12
  129.4 6.9 %collective-permute-done = f32[16,64,128]{2,1,0:T(8,128)S(1)} collective-permute-done((f32[16,64,128]{2,1,0:T(8,128)S(1)}, f32[16,64,128]{2,1,0:T(8,128)S(1)}, u32[]{:S(2)}, u32[]{:S(2)}) %collective-permute-start) | collective-permute-done | bytes 524320 | tf_op jit(solution)/shard_map/while/body/eval_jaxpr/ppermute | solution.py:12
  137.6 1.9 collective-permute-start
  139.5 6.5 %collective-permute-start.1 = (f32[16,64,128]{2,1,0:T(8,128)S(1)}, f32[16,64,128]{2,1,0:T(8,128)S(1)}, u32[]{:S(2)}, u32[]{:S(2)}) collective-permute-start(f32[16,64,128]{2,1,0:T(8,128)S(1)} %get-tuple-element.440), channel_id=1, source_target_pairs={{8,0},{16,8},{24,16},{32,24},{40,32},{48,40},{56,48},{64,56},{72,6... | collective-permute-start | bytes 1572872 | tf_op jit(solution)/shard_map/while/body/eval_jaxpr/ppermute | solution.py:12
  146.0 5.9 %collective-permute-done = f32[16,64,128]{2,1,0:T(8,128)S(1)} collective-permute-done((f32[16,64,128]{2,1,0:T(8,128)S(1)}, f32[16,64,128]{2,1,0:T(8,128)S(1)}, u32[]{:S(2)}, u32[]{:S(2)}) %collective-permute-start) | collective-permute-done | bytes 524320 | tf_op jit(solution)/shard_map/while/body/eval_jaxpr/ppermute | solution.py:12
  153.3 1.9 collective-permute-start
  155.3 6.5 %collective-permute-start.1 = (f32[16,64,128]{2,1,0:T(8,128)S(1)}, f32[16,64,128]{2,1,0:T(8,128)S(1)}, u32[]{:S(2)}, u32[]{:S(2)}) collective-permute-start(f32[16,64,128]{2,1,0:T(8,128)S(1)} %get-tuple-element.440), channel_id=1, source_target_pairs={{8,0},{16,8},{24,16},{32,24},{40,32},{48,40},{56,48},{64,56},{72,6... | collective-permute-start | bytes 1572872 | tf_op jit(solution)/shard_map/while/body/eval_jaxpr/ppermute | solution.py:12
  161.8 5.2 collective-permute-done
  168.6 1.9 collective-permute-start
  170.5 6.5 %collective-permute-start.1 = (f32[16,64,128]{2,1,0:T(8,128)S(1)}, f32[16,64,128]{2,1,0:T(8,128)S(1)}, u32[]{:S(2)}, u32[]{:S(2)}) collective-permute-start(f32[16,64,128]{2,1,0:T(8,128)S(1)} %get-tuple-element.440), channel_id=1, source_target_pairs={{8,0},{16,8},{24,16},{32,24},{40,32},{48,40},{56,48},{64,56},{72,6... | collective-permute-start | bytes 1572872 | tf_op jit(solution)/shard_map/while/body/eval_jaxpr/ppermute | solution.py:12
  177.1 5.2 collective-permute-done
  183.9 1.9 collective-permute-start
  185.8 6.5 %collective-permute-start.1 = (f32[16,64,128]{2,1,0:T(8,128)S(1)}, f32[16,64,128]{2,1,0:T(8,128)S(1)}, u32[]{:S(2)}, u32[]{:S(2)}) collective-permute-start(f32[16,64,128]{2,1,0:T(8,128)S(1)} %get-tuple-element.440), channel_id=1, source_target_pairs={{8,0},{16,8},{24,16},{32,24},{40,32},{48,40},{56,48},{64,56},{72,6... | collective-permute-start | bytes 1572872 | tf_op jit(solution)/shard_map/while/body/eval_jaxpr/ppermute | solution.py:12
  192.3 5.2 collective-permute-done
  199.2 1.9 collective-permute-start
  201.1 6.5 %collective-permute-start.1 = (f32[16,64,128]{2,1,0:T(8,128)S(1)}, f32[16,64,128]{2,1,0:T(8,128)S(1)}, u32[]{:S(2)}, u32[]{:S(2)}) collective-permute-start(f32[16,64,128]{2,1,0:T(8,128)S(1)} %get-tuple-element.440), channel_id=1, source_target_pairs={{8,0},{16,8},{24,16},{32,24},{40,32},{48,40},{56,48},{64,56},{72,6... | collective-permute-start | bytes 1572872 | tf_op jit(solution)/shard_map/while/body/eval_jaxpr/ppermute | solution.py:12
  207.6 5.9 %collective-permute-done = f32[16,64,128]{2,1,0:T(8,128)S(1)} collective-permute-done((f32[16,64,128]{2,1,0:T(8,128)S(1)}, f32[16,64,128]{2,1,0:T(8,128)S(1)}, u32[]{:S(2)}, u32[]{:S(2)}) %collective-permute-start) | collective-permute-done | bytes 524320 | tf_op jit(solution)/shard_map/while/body/eval_jaxpr/ppermute | solution.py:12
  213.5 1.7 collective-permute-done.1
  215.4 1.9 collective-permute-start
  217.3 6.5 %collective-permute-start.1 = (f32[16,64,128]{2,1,0:T(8,128)S(1)}, f32[16,64,128]{2,1,0:T(8,128)S(1)}, u32[]{:S(2)}, u32[]{:S(2)}) collective-permute-start(f32[16,64,128]{2,1,0:T(8,128)S(1)} %get-tuple-element.440), channel_id=1, source_target_pairs={{8,0},{16,8},{24,16},{32,24},{40,32},{48,40},{56,48},{64,56},{72,6... | collective-permute-start | bytes 1572872 | tf_op jit(solution)/shard_map/while/body/eval_jaxpr/ppermute | solution.py:12
  223.9 7.0 %collective-permute-done = f32[16,64,128]{2,1,0:T(8,128)S(1)} collective-permute-done((f32[16,64,128]{2,1,0:T(8,128)S(1)}, f32[16,64,128]{2,1,0:T(8,128)S(1)}, u32[]{:S(2)}, u32[]{:S(2)}) %collective-permute-start) | collective-permute-done | bytes 524320 | tf_op jit(solution)/shard_map/while/body/eval_jaxpr/ppermute | solution.py:12
  230.8 1.7 collective-permute-done.1
  232.7 2.2 collective-permute-start
  234.9 6.2 %collective-permute-start.1 = (f32[16,64,128]{2,1,0:T(8,128)S(1)}, f32[16,64,128]{2,1,0:T(8,128)S(1)}, u32[]{:S(2)}, u32[]{:S(2)}) collective-permute-start(f32[16,64,128]{2,1,0:T(8,128)S(1)} %get-tuple-element.440), channel_id=1, source_target_pairs={{8,0},{16,8},{24,16},{32,24},{40,32},{48,40},{56,48},{64,56},{72,6... | collective-permute-start | bytes 1572872 | tf_op jit(solution)/shard_map/while/body/eval_jaxpr/ppermute | solution.py:12
  241.2 5.2 collective-permute-done
  248.5 241.2 %while.30 = (s32[]{:T(128)}, f32[16,128,64]{1,2,0:T(8,128)}, f32[16,128]{1,0:T(8,128)S(1)}, f32[16,128,128]{2,1,0:T(8,128)}, f32[16,128,128]{2,1,0:T(8,128)}, /*...) while((s32[]{:T(128)}, f32[16,128,64]{1,2,0:T(8,128)}, ...), condition=%wide.region_14.15_spmd.clone, body=%wide.region_5.14_spmd.clone.sunk | while | flops 126829440 | bytes 1805085 | solution.py:86
  255.5 2.4 bitcast_dynamic-update-slice_fusion.2
  270.5 2.4 bitcast_dynamic-update-slice_fusion.2
  285.6 2.4 bitcast_dynamic-update-slice_fusion.2
  300.7 2.4 bitcast_dynamic-update-slice_fusion.2
  315.7 2.4 bitcast_dynamic-update-slice_fusion.2
  325.6 1.7 fusion.158
  330.8 2.4 bitcast_dynamic-update-slice_fusion.2
  345.9 2.4 bitcast_dynamic-update-slice_fusion.2
  361.0 2.4 bitcast_dynamic-update-slice_fusion.2
  370.8 1.7 fusion.158
  376.0 2.4 bitcast_dynamic-update-slice_fusion.2
  391.1 2.4 bitcast_dynamic-update-slice_fusion.2
  406.2 2.4 bitcast_dynamic-update-slice_fusion.2
  421.3 2.4 bitcast_dynamic-update-slice_fusion.2
  436.3 2.4 bitcast_dynamic-update-slice_fusion.2
  451.4 2.4 bitcast_dynamic-update-slice_fusion.2
  466.5 2.4 bitcast_dynamic-update-slice_fusion.2
  476.3 1.7 fusion.158
  481.6 2.4 bitcast_dynamic-update-slice_fusion.2
  489.7 2.0 reduce_sum.82
  493.8 30.8 %reduce-scatter.3.cloned.1.call-done = f32[16,128]{1,0:T(8,128)} async-done(((f32[128,128]{1,0:T(8,128)}), f32[16,128]{1,0:T(8,128)}) %reduce-scatter.3.cloned.1.call-update) | async-done | bytes 8208 | tf_op jit(solution)/shard_map/reduce_scatter | solution.py:104
  524.6 40.4 %reduce-scatter.5.cloned.1.call-done = f32[16,128]{1,0:T(8,128)} async-done(((f32[128,128]{1,0:T(8,128)}), f32[16,128]{1,0:T(8,128)}) %reduce-scatter.5.cloned.1.call-update) | async-done | bytes 8208 | tf_op jit(solution)/shard_map/reduce_scatter | solution.py:105
  (463 shorter events, 220.9 us)
Async XLA Ops:
  7.2 517.5 %reduce-scatter.3.cloned.1.call-start = ((), (), s32[]{:S(2)}) async-start(), calls=%async_computation.2 | async-start | bytes 73728 | tf_op jit(solution)/shard_map/reduce_scatter | solution.py:104
  7.2 13.5 %copy-start.8 = (bf16[16,128]{1,0:T(8,128)(2,1)S(1)}, bf16[16,128]{1,0:T(8,128)(2,1)}, u32[]{:S(2)}) copy-start(bf16[16,128]{1,0:T(8,128)(2,1)} %param.18) | copy-start | bytes 12292
  33.5 3.1 copy-start.5
  33.7 0.7 copy-start.9
  34.7 1.4 copy-start.7
  35.4 0.7 copy-start.10
  36.8 0.8 copy-start.2
  37.6 0.9 copy-start.6
  38.6 1.1 copy-start.1
  38.7 0.8 copy-start
  40.3 23.8 %collective-permute-start = (f32[16,64,128]{2,1,0:T(8,128)S(1)}, f32[16,64,128]{2,1,0:T(8,128)S(1)}, u32[]{:S(2)}, u32[]{:S(2)}) collective-permute-start(f32[16,64,128]{2,1,0:T(8,128)S(1)} %get-tuple-element.439), channel_id=1, source_target_pairs={{0,8},{8,16},{16,24},{24,32},{32,40},{40,48},{48,56},{56,64},{64,7... | collective-permute-start | bytes 1572872 | tf_op jit(solution)/shard_map/while/body/eval_jaxpr/ppermute | solution.py:12
  44.1 21.1 %collective-permute-start.1 = (f32[16,64,128]{2,1,0:T(8,128)S(1)}, f32[16,64,128]{2,1,0:T(8,128)S(1)}, u32[]{:S(2)}, u32[]{:S(2)}) collective-permute-start(f32[16,64,128]{2,1,0:T(8,128)S(1)} %get-tuple-element.440), channel_id=1, source_target_pairs={{8,0},{16,8},{24,16},{32,24},{40,32},{48,40},{56,48},{64,56},{72,6... | collective-permute-start | bytes 1572872 | tf_op jit(solution)/shard_map/while/body/eval_jaxpr/ppermute | solution.py:12
  65.4 18.1 %collective-permute-start = (f32[16,64,128]{2,1,0:T(8,128)S(1)}, f32[16,64,128]{2,1,0:T(8,128)S(1)}, u32[]{:S(2)}, u32[]{:S(2)}) collective-permute-start(f32[16,64,128]{2,1,0:T(8,128)S(1)} %get-tuple-element.439), channel_id=1, source_target_pairs={{0,8},{8,16},{16,24},{24,32},{32,40},{40,48},{48,56},{56,64},{64,7... | collective-permute-start | bytes 1572872 | tf_op jit(solution)/shard_map/while/body/eval_jaxpr/ppermute | solution.py:12
  67.3 17.3 %collective-permute-start.1 = (f32[16,64,128]{2,1,0:T(8,128)S(1)}, f32[16,64,128]{2,1,0:T(8,128)S(1)}, u32[]{:S(2)}, u32[]{:S(2)}) collective-permute-start(f32[16,64,128]{2,1,0:T(8,128)S(1)} %get-tuple-element.440), channel_id=1, source_target_pairs={{8,0},{16,8},{24,16},{32,24},{40,32},{48,40},{56,48},{64,56},{72,6... | collective-permute-start | bytes 1572872 | tf_op jit(solution)/shard_map/while/body/eval_jaxpr/ppermute | solution.py:12
  84.8 17.2 %collective-permute-start = (f32[16,64,128]{2,1,0:T(8,128)S(1)}, f32[16,64,128]{2,1,0:T(8,128)S(1)}, u32[]{:S(2)}, u32[]{:S(2)}) collective-permute-start(f32[16,64,128]{2,1,0:T(8,128)S(1)} %get-tuple-element.439), channel_id=1, source_target_pairs={{0,8},{8,16},{16,24},{24,32},{32,40},{40,48},{48,56},{56,64},{64,7... | collective-permute-start | bytes 1572872 | tf_op jit(solution)/shard_map/while/body/eval_jaxpr/ppermute | solution.py:12
  86.8 16.4 %collective-permute-start.1 = (f32[16,64,128]{2,1,0:T(8,128)S(1)}, f32[16,64,128]{2,1,0:T(8,128)S(1)}, u32[]{:S(2)}, u32[]{:S(2)}) collective-permute-start(f32[16,64,128]{2,1,0:T(8,128)S(1)} %get-tuple-element.440), channel_id=1, source_target_pairs={{8,0},{16,8},{24,16},{32,24},{40,32},{48,40},{56,48},{64,56},{72,6... | collective-permute-start | bytes 1572872 | tf_op jit(solution)/shard_map/while/body/eval_jaxpr/ppermute | solution.py:12
  103.3 16.2 %collective-permute-start = (f32[16,64,128]{2,1,0:T(8,128)S(1)}, f32[16,64,128]{2,1,0:T(8,128)S(1)}, u32[]{:S(2)}, u32[]{:S(2)}) collective-permute-start(f32[16,64,128]{2,1,0:T(8,128)S(1)} %get-tuple-element.439), channel_id=1, source_target_pairs={{0,8},{8,16},{16,24},{24,32},{32,40},{40,48},{48,56},{56,64},{64,7... | collective-permute-start | bytes 1572872 | tf_op jit(solution)/shard_map/while/body/eval_jaxpr/ppermute | solution.py:12
  105.3 15.5 %collective-permute-start.1 = (f32[16,64,128]{2,1,0:T(8,128)S(1)}, f32[16,64,128]{2,1,0:T(8,128)S(1)}, u32[]{:S(2)}, u32[]{:S(2)}) collective-permute-start(f32[16,64,128]{2,1,0:T(8,128)S(1)} %get-tuple-element.440), channel_id=1, source_target_pairs={{8,0},{16,8},{24,16},{32,24},{40,32},{48,40},{56,48},{64,56},{72,6... | collective-permute-start | bytes 1572872 | tf_op jit(solution)/shard_map/while/body/eval_jaxpr/ppermute | solution.py:12
  120.9 15.3 %collective-permute-start = (f32[16,64,128]{2,1,0:T(8,128)S(1)}, f32[16,64,128]{2,1,0:T(8,128)S(1)}, u32[]{:S(2)}, u32[]{:S(2)}) collective-permute-start(f32[16,64,128]{2,1,0:T(8,128)S(1)} %get-tuple-element.439), channel_id=1, source_target_pairs={{0,8},{8,16},{16,24},{24,32},{32,40},{40,48},{48,56},{56,64},{64,7... | collective-permute-start | bytes 1572872 | tf_op jit(solution)/shard_map/while/body/eval_jaxpr/ppermute | solution.py:12
  122.9 14.6 %collective-permute-start.1 = (f32[16,64,128]{2,1,0:T(8,128)S(1)}, f32[16,64,128]{2,1,0:T(8,128)S(1)}, u32[]{:S(2)}, u32[]{:S(2)}) collective-permute-start(f32[16,64,128]{2,1,0:T(8,128)S(1)} %get-tuple-element.440), channel_id=1, source_target_pairs={{8,0},{16,8},{24,16},{32,24},{40,32},{48,40},{56,48},{64,56},{72,6... | collective-permute-start | bytes 1572872 | tf_op jit(solution)/shard_map/while/body/eval_jaxpr/ppermute | solution.py:12
  137.6 14.4 %collective-permute-start = (f32[16,64,128]{2,1,0:T(8,128)S(1)}, f32[16,64,128]{2,1,0:T(8,128)S(1)}, u32[]{:S(2)}, u32[]{:S(2)}) collective-permute-start(f32[16,64,128]{2,1,0:T(8,128)S(1)} %get-tuple-element.439), channel_id=1, source_target_pairs={{0,8},{8,16},{16,24},{24,32},{32,40},{40,48},{48,56},{56,64},{64,7... | collective-permute-start | bytes 1572872 | tf_op jit(solution)/shard_map/while/body/eval_jaxpr/ppermute | solution.py:12
  139.5 13.6 %collective-permute-start.1 = (f32[16,64,128]{2,1,0:T(8,128)S(1)}, f32[16,64,128]{2,1,0:T(8,128)S(1)}, u32[]{:S(2)}, u32[]{:S(2)}) collective-permute-start(f32[16,64,128]{2,1,0:T(8,128)S(1)} %get-tuple-element.440), channel_id=1, source_target_pairs={{8,0},{16,8},{24,16},{32,24},{40,32},{48,40},{56,48},{64,56},{72,6... | collective-permute-start | bytes 1572872 | tf_op jit(solution)/shard_map/while/body/eval_jaxpr/ppermute | solution.py:12
  153.3 13.7 %collective-permute-start = (f32[16,64,128]{2,1,0:T(8,128)S(1)}, f32[16,64,128]{2,1,0:T(8,128)S(1)}, u32[]{:S(2)}, u32[]{:S(2)}) collective-permute-start(f32[16,64,128]{2,1,0:T(8,128)S(1)} %get-tuple-element.439), channel_id=1, source_target_pairs={{0,8},{8,16},{16,24},{24,32},{32,40},{40,48},{48,56},{56,64},{64,7... | collective-permute-start | bytes 1572872 | tf_op jit(solution)/shard_map/while/body/eval_jaxpr/ppermute | solution.py:12
  155.3 13.2 %collective-permute-start.1 = (f32[16,64,128]{2,1,0:T(8,128)S(1)}, f32[16,64,128]{2,1,0:T(8,128)S(1)}, u32[]{:S(2)}, u32[]{:S(2)}) collective-permute-start(f32[16,64,128]{2,1,0:T(8,128)S(1)} %get-tuple-element.440), channel_id=1, source_target_pairs={{8,0},{16,8},{24,16},{32,24},{40,32},{48,40},{56,48},{64,56},{72,6... | collective-permute-start | bytes 1572872 | tf_op jit(solution)/shard_map/while/body/eval_jaxpr/ppermute | solution.py:12
  168.6 13.7 %collective-permute-start = (f32[16,64,128]{2,1,0:T(8,128)S(1)}, f32[16,64,128]{2,1,0:T(8,128)S(1)}, u32[]{:S(2)}, u32[]{:S(2)}) collective-permute-start(f32[16,64,128]{2,1,0:T(8,128)S(1)} %get-tuple-element.439), channel_id=1, source_target_pairs={{0,8},{8,16},{16,24},{24,32},{32,40},{40,48},{48,56},{56,64},{64,7... | collective-permute-start | bytes 1572872 | tf_op jit(solution)/shard_map/while/body/eval_jaxpr/ppermute | solution.py:12
  170.5 13.2 %collective-permute-start.1 = (f32[16,64,128]{2,1,0:T(8,128)S(1)}, f32[16,64,128]{2,1,0:T(8,128)S(1)}, u32[]{:S(2)}, u32[]{:S(2)}) collective-permute-start(f32[16,64,128]{2,1,0:T(8,128)S(1)} %get-tuple-element.440), channel_id=1, source_target_pairs={{8,0},{16,8},{24,16},{32,24},{40,32},{48,40},{56,48},{64,56},{72,6... | collective-permute-start | bytes 1572872 | tf_op jit(solution)/shard_map/while/body/eval_jaxpr/ppermute | solution.py:12
  183.9 13.7 %collective-permute-start = (f32[16,64,128]{2,1,0:T(8,128)S(1)}, f32[16,64,128]{2,1,0:T(8,128)S(1)}, u32[]{:S(2)}, u32[]{:S(2)}) collective-permute-start(f32[16,64,128]{2,1,0:T(8,128)S(1)} %get-tuple-element.439), channel_id=1, source_target_pairs={{0,8},{8,16},{16,24},{24,32},{32,40},{40,48},{48,56},{56,64},{64,7... | collective-permute-start | bytes 1572872 | tf_op jit(solution)/shard_map/while/body/eval_jaxpr/ppermute | solution.py:12
  185.8 13.2 %collective-permute-start.1 = (f32[16,64,128]{2,1,0:T(8,128)S(1)}, f32[16,64,128]{2,1,0:T(8,128)S(1)}, u32[]{:S(2)}, u32[]{:S(2)}) collective-permute-start(f32[16,64,128]{2,1,0:T(8,128)S(1)} %get-tuple-element.440), channel_id=1, source_target_pairs={{8,0},{16,8},{24,16},{32,24},{40,32},{48,40},{56,48},{64,56},{72,6... | collective-permute-start | bytes 1572872 | tf_op jit(solution)/shard_map/while/body/eval_jaxpr/ppermute | solution.py:12
  199.2 14.3 %collective-permute-start = (f32[16,64,128]{2,1,0:T(8,128)S(1)}, f32[16,64,128]{2,1,0:T(8,128)S(1)}, u32[]{:S(2)}, u32[]{:S(2)}) collective-permute-start(f32[16,64,128]{2,1,0:T(8,128)S(1)} %get-tuple-element.439), channel_id=1, source_target_pairs={{0,8},{8,16},{16,24},{24,32},{32,40},{40,48},{48,56},{56,64},{64,7... | collective-permute-start | bytes 1572872 | tf_op jit(solution)/shard_map/while/body/eval_jaxpr/ppermute | solution.py:12
  201.1 14.1 %collective-permute-start.1 = (f32[16,64,128]{2,1,0:T(8,128)S(1)}, f32[16,64,128]{2,1,0:T(8,128)S(1)}, u32[]{:S(2)}, u32[]{:S(2)}) collective-permute-start(f32[16,64,128]{2,1,0:T(8,128)S(1)} %get-tuple-element.440), channel_id=1, source_target_pairs={{8,0},{16,8},{24,16},{32,24},{40,32},{48,40},{56,48},{64,56},{72,6... | collective-permute-start | bytes 1572872 | tf_op jit(solution)/shard_map/while/body/eval_jaxpr/ppermute | solution.py:12
  215.4 15.4 %collective-permute-start = (f32[16,64,128]{2,1,0:T(8,128)S(1)}, f32[16,64,128]{2,1,0:T(8,128)S(1)}, u32[]{:S(2)}, u32[]{:S(2)}) collective-permute-start(f32[16,64,128]{2,1,0:T(8,128)S(1)} %get-tuple-element.439), channel_id=1, source_target_pairs={{0,8},{8,16},{16,24},{24,32},{32,40},{40,48},{48,56},{56,64},{64,7... | collective-permute-start | bytes 1572872 | tf_op jit(solution)/shard_map/while/body/eval_jaxpr/ppermute | solution.py:12
  217.3 15.2 %collective-permute-start.1 = (f32[16,64,128]{2,1,0:T(8,128)S(1)}, f32[16,64,128]{2,1,0:T(8,128)S(1)}, u32[]{:S(2)}, u32[]{:S(2)}) collective-permute-start(f32[16,64,128]{2,1,0:T(8,128)S(1)} %get-tuple-element.440), channel_id=1, source_target_pairs={{8,0},{16,8},{24,16},{32,24},{40,32},{48,40},{56,48},{64,56},{72,6... | collective-permute-start | bytes 1572872 | tf_op jit(solution)/shard_map/while/body/eval_jaxpr/ppermute | solution.py:12
  232.7 13.7 %collective-permute-start = (f32[16,64,128]{2,1,0:T(8,128)S(1)}, f32[16,64,128]{2,1,0:T(8,128)S(1)}, u32[]{:S(2)}, u32[]{:S(2)}) collective-permute-start(f32[16,64,128]{2,1,0:T(8,128)S(1)} %get-tuple-element.439), channel_id=1, source_target_pairs={{0,8},{8,16},{16,24},{24,32},{32,40},{40,48},{48,56},{56,64},{64,7... | collective-permute-start | bytes 1572872 | tf_op jit(solution)/shard_map/while/body/eval_jaxpr/ppermute | solution.py:12
  234.9 12.9 %collective-permute-start.1 = (f32[16,64,128]{2,1,0:T(8,128)S(1)}, f32[16,64,128]{2,1,0:T(8,128)S(1)}, u32[]{:S(2)}, u32[]{:S(2)}) collective-permute-start(f32[16,64,128]{2,1,0:T(8,128)S(1)} %get-tuple-element.440), channel_id=1, source_target_pairs={{8,0},{16,8},{24,16},{32,24},{40,32},{48,40},{56,48},{64,56},{72,6... | collective-permute-start | bytes 1572872 | tf_op jit(solution)/shard_map/while/body/eval_jaxpr/ppermute | solution.py:12
  247.8 0.7 copy-start.12
  489.7 2.0 copy-start.11
  489.7 2.1 copy-start.3
  491.7 73.3 %reduce-scatter.5.cloned.1.call-start = ((), (), s32[]{:S(2)}) async-start(), calls=%async_computation.3 | async-start | bytes 73728 | tf_op jit(solution)/shard_map/reduce_scatter | solution.py:105
  491.8 1.1 copy-start.4
Sparse Core Ops, SparseCore 0:
  491.8 32.7 reduce-scatter.2
  528.2 36.7 reduce-scatter.4
where the time goes:
time: 581 us; the launch traced here: 572 us
  matrix products  182 us (31%)
  waiting for transfers between devices  171 us (29%)
  starting transfers between devices  106 us (18%)
  other arithmetic  38.8 us (7%)
  local copies, waits for them, and re-layouts  31.9 us (5%)
  blocking collectives  26.3 us (5%)
  between operations  14.3 us (2%)
    ppermute x24, starting transfers between devices, from_behind(): return lax.ppermute(x, axis, pairs)  106 us
    ppermute x24, waiting for transfers between devices, from_behind(): return lax.ppermute(x, axis, pairs)  99.5 us
    reduce_scatter x1, waiting for transfers between devices, local(): lax.psum_scatter(jnp.sum(gc, axis=0), 'tensor', scatter_dimension=0, tile...  40.4 us
    dot_general x16, matrix products, per_head(): core = jnp.dot(mixed.T, dyh, precision=HIGH) + lvh[:, None] * b_adj  37.8 us
    reduce_scatter x1, waiting for transfers between devices, local(): lax.psum_scatter(jnp.sum(gb, axis=0), 'tensor', scatter_dimension=0, tile...  30.8 us
    dot_general x16, matrix products, per_head(): jnp.dot(lvh[:, None] * uh, g_in, precision=HIGH)  26.8 us
    dot_general x16, matrix products, per_head(): jnp.dot(dyh, s_in, precision=HIGH)  26.8 us
    dot_general x16, matrix products, per_head(): jnp.dot(weights.T, jnp.sum(dyh * c_state, axis=1), precision=HIGH)  24.8 us
  transfers between devices with their start and end apart: 26, of which 26 were waited for; matrix products, arithmetic and copies ran while one was open for 0% of the time, Pallas kernels for 0%

commit v1 on v0

v1 whole, which is shorter than its diff:
```python
import jax
import jax.numpy as jnp
from jax import lax
from jax.sharding import PartitionSpec as P

HIGH = lax.Precision.HIGHEST


def from_behind(x, axis, by):
    peers = lax.axis_size(axis)
    pairs = [(i, i + by) for i in range(peers) if 0 <= i + by < peers]
    return lax.ppermute(x, axis, pairs)


def local(inputs, grads, step_size, decay_rate, skip_gain, b_rows, c_rows, doc_lengths):
    length = inputs.shape[0]
    heads = step_size.shape[0]
    width = inputs.shape[1] // heads
    rows = lax.all_gather(jnp.stack([b_rows, c_rows]), "tensor", axis=1, tiled=True)
    b_bf, c_bf = rows[0], rows[1]
    bmat = b_bf.astype(jnp.float32)
    cmat = c_bf.astype(jnp.float32)
    xs = inputs.astype(jnp.float32).reshape(length, heads, width).transpose(1, 0, 2)
    dys = grads.astype(jnp.float32).reshape(length, heads, width).transpose(1, 0, 2)
    offset = lax.axis_index("context") * length
    ends = jnp.cumsum(doc_lengths)
    starts = ends - doc_lengths
    position = offset + jnp.arange(length, dtype=jnp.int32)
    seg = jnp.sum(
        ((starts[None, :] >= offset) & (starts[None, :] <= position[:, None])).astype(jnp.int32),
        axis=1,
    )
    rate = decay_rate[:, None]
    logc = jnp.cumsum(-step_size * rate, axis=1)
    enter = jnp.exp(logc) * (seg == 0).astype(jnp.float32)[None, :]
    leave = jnp.exp(logc[:, -1:] - logc) * (seg == seg[-1]).astype(jnp.float32)[None, :]
    total = enter[:, -1][:, None, None]
    moved = step_size[:, :, None] * xs
    left_u = leave[:, :, None] * moved
    enter_dy = enter[:, :, None] * dys
    local_state = jnp.einsum("hlp,ln->hpn", left_u, bmat, precision=HIGH)
    local_adj = jnp.einsum("hlp,ln->hpn", enter_dy, cmat, precision=HIGH)

    turns = 3 * lax.axis_size("context") // 16
    inc_state = jnp.zeros_like(local_state)
    inc_adj = jnp.zeros_like(local_adj)
    for _ in range(turns):
        send_state, send_adj = lax.optimization_barrier(
            (local_state + total * inc_state, local_adj + total * inc_adj)
        )
        inc_state, inc_adj = lax.optimization_barrier(
            (from_behind(send_state, "context", 1), from_behind(send_adj, "context", -1))
        )
    s_in, g_in = inc_state, inc_adj

    index = jnp.arange(length)
    keep = (index[:, None] >= index[None, :]) & (seg[:, None] == seg[None, :])
    weights = jnp.exp(jnp.where(keep[None], logc[:, :, None] - logc[:, None, :], -1e30))
    scores = jnp.dot(c_bf, b_bf.T, preferred_element_type=jnp.float32)
    mixed = weights * scores[None]
    core_loc = jnp.einsum("hij,hip->hjp", mixed, dys, precision=HIGH)
    pairs = jnp.einsum("hip,hjp->hij", dys, moved, precision=HIGH)
    paired = mixed * pairs
    col_total = jnp.sum(paired, axis=1)
    row_total = jnp.sum(paired, axis=2)
    inner = jnp.cumsum(col_total, axis=1) - (jnp.cumsum(row_total, axis=1) - row_total)
    weighted = jnp.sum(weights * pairs, axis=0)
    gb_loc = jnp.dot(weighted.T, cmat, precision=HIGH)
    gc_loc = jnp.dot(weighted, bmat, precision=HIGH)

    b_adj = jnp.einsum("ln,hpn->hlp", bmat, g_in, precision=HIGH)
    c_state = jnp.einsum("ln,hpn->hlp", cmat, s_in, precision=HIGH)
    core = core_loc + leave[:, :, None] * b_adj
    gx = step_size[:, :, None] * core + skip_gain[:, None, None] * dys
    along = jnp.sum(xs * core, axis=2)
    from_state = enter * jnp.einsum(
        "hij,hi->hj", weights, jnp.sum(dys * c_state, axis=2), precision=HIGH
    )
    from_adj = leave * jnp.einsum(
        "hij,hj->hi", weights, jnp.sum(moved * b_adj, axis=2), precision=HIGH
    )
    both = leave * enter * jnp.sum(g_in * s_in, axis=(1, 2))[:, None]
    grad_step = along * (1.0 + rate * step_size) - rate * (inner + from_state + from_adj + both)
    gb = gb_loc + jnp.einsum("hlp,hpn->ln", left_u, g_in, precision=HIGH)
    gc = gc_loc + jnp.einsum("hlp,hpn->ln", enter_dy, s_in, precision=HIGH)

    grad_x = gx.transpose(1, 0, 2).reshape(length, heads * width)
    grad_bc = lax.psum_scatter(jnp.stack([gb, gc]), "tensor", scatter_dimension=1, tiled=True)
    return (grad_x, grad_step, grad_bc[0], grad_bc[1])


def solution(mesh):
    in_specs = (
        P("context", "tensor"),
        P("context", "tensor"),
        P("tensor", "context"),
        P("tensor"),
        P("tensor"),
        P(("context", "tensor"), None),
        P(("context", "tensor"), None),
        P(),
    )
    out_specs = (
        P("context", "tensor"),
        P("tensor", "context"),
        P(("context", "tensor"), None),
        P(("context", "tensor"), None),
    )
    return jax.shard_map(local, mesh=mesh, in_specs=in_specs, out_specs=out_specs, check_vma=False)
```

time: 581 us -> 280 us (0.48)
  the two profiles are of different devices: /device:TPU:4 before, /device:TPU:2 now
where the time goes in v1:
time: 280 us; the launch traced here: 278 us
  waiting for transfers between devices  119 us (42%)
  starting transfers between devices  106 us (38%)
  between operations  14.6 us (5%)
  blocking collectives  13.3 us (5%)
  matrix products  10.1 us (4%)
  local copies, waits for them, and re-layouts  8.7 us (3%)
  other arithmetic  6.84 us (2%)
    ppermute x24, starting transfers between devices, from_behind(): return lax.ppermute(x, axis, pairs)  106 us
    ppermute x24, waiting for transfers between devices, from_behind(): return lax.ppermute(x, axis, pairs)  93.1 us
    reduce_scatter x1, waiting for transfers between devices, local(): lax.psum_scatter(jnp.stack([gb, gc]), 'tensor', scatter_dimension=1, tile...  25.7 us
    all_gather x1, blocking collectives, local(): lax.all_gather(jnp.stack([b_rows, c_rows]), 'tensor', axis=1, tiled=True)  13.3 us
  transfers between devices with their start and end apart: 25, of which 25 were waited for; matrix products, arithmetic and copies ran while one was open for 4% of the time, Pallas kernels for 0%

profile of v1, /device:TPU:2, one launch (start us, length us, event | category | flops | bytes accessed | tf_op | source)
XLA Modules:
  0.0 278.4 jit_solution(14510431676233515382)
XLA Ops:
  8.9 0.7 compare_convert_fusion
  10.7 13.3 %all_gather.3 = bf16[2,128,128]{2,1,0:T(8,128)(2,1)S(1)} all-gather(bf16[2,16,128]{2,1,0:T(8,128)(2,1)S(1)} %pad_maximum_fusion.1), channel_id=1, replica_groups=mesh['context'=64,'tensor'=8] {'tensor'}, dimensions={1}, use_global_device_ids=true | all-gather | bytes 73728 | tf_op jit(solution)/shard_map/all_gather | solution.py:19
  23.9 1.1 copy.34
  26.3 3.8 %collective-permute-start = (f32[16,64,128]{2,1,0:T(8,128)S(1)}, f32[16,64,128]{2,1,0:T(8,128)S(1)}, u32[]{:S(2)}, u32[]{:S(2)}) collective-permute-start(f32[16,64,128]{2,1,0:T(8,128)S(1)} %get-tuple-element.52), channel_id=1, source_target_pairs={{0,8},{8,16},{16,24},{24,32},{32,40},{40,48},{48,56},{56,64},{64,7... | collective-permute-start | bytes 1572872 | tf_op jit(solution)/shard_map/ppermute | solution.py:12
  30.2 9.5 %collective-permute-start.1 = (f32[16,64,128]{2,1,0:T(8,128)S(1)}, f32[16,64,128]{2,1,0:T(8,128)S(1)}, u32[]{:S(2)}, u32[]{:S(2)}) collective-permute-start(f32[16,64,128]{2,1,0:T(8,128)S(1)} %get-tuple-element.53), channel_id=1, source_target_pairs={{8,0},{16,8},{24,16},{32,24},{40,32},{48,40},{56,48},{64,56},{72,6... | collective-permute-start | bytes 1572872 | tf_op jit(solution)/shard_map/ppermute | solution.py:12
  39.6 10.5 %collective-permute-done = f32[16,64,128]{2,1,0:T(8,128)S(1)} collective-permute-done((f32[16,64,128]{2,1,0:T(8,128)S(1)}, f32[16,64,128]{2,1,0:T(8,128)S(1)}, u32[]{:S(2)}, u32[]{:S(2)}) %collective-permute-start) | collective-permute-done | bytes 524320 | tf_op jit(solution)/shard_map/ppermute | solution.py:12
  50.1 1.2 collective-permute-done.1
  51.5 1.9 collective-permute-start.2
  53.4 6.5 %collective-permute-start.3 = (f32[16,64,128]{2,1,0:T(8,128)S(1)}, f32[16,64,128]{2,1,0:T(8,128)S(1)}, u32[]{:S(2)}, u32[]{:S(2)}) collective-permute-start(f32[16,64,128]{2,1,0:T(8,128)S(1)} %get-tuple-element.57), channel_id=1, source_target_pairs={{8,0},{16,8},{24,16},{32,24},{40,32},{48,40},{56,48},{64,56},{72,6... | collective-permute-start | bytes 1572872 | tf_op jit(solution)/shard_map/ppermute | solution.py:12
  59.9 9.7 %collective-permute-done.2 = f32[16,64,128]{2,1,0:T(8,128)S(1)} collective-permute-done((f32[16,64,128]{2,1,0:T(8,128)S(1)}, f32[16,64,128]{2,1,0:T(8,128)S(1)}, u32[]{:S(2)}, u32[]{:S(2)}) %collective-permute-start.2) | collective-permute-done | bytes 524320 | tf_op jit(solution)/shard_map/ppermute | solution.py:12
  69.6 1.2 collective-permute-done.3
  70.9 1.9 collective-permute-start.4
  72.8 6.5 %collective-permute-start.5 = (f32[16,64,128]{2,1,0:T(8,128)S(1)}, f32[16,64,128]{2,1,0:T(8,128)S(1)}, u32[]{:S(2)}, u32[]{:S(2)}) collective-permute-start(f32[16,64,128]{2,1,0:T(8,128)S(1)} %get-tuple-element.61), channel_id=1, source_target_pairs={{8,0},{16,8},{24,16},{32,24},{40,32},{48,40},{56,48},{64,56},{72,6... | collective-permute-start | bytes 1572872 | tf_op jit(solution)/shard_map/ppermute | solution.py:12
  79.3 8.7 %collective-permute-done.4 = f32[16,64,128]{2,1,0:T(8,128)S(1)} collective-permute-done((f32[16,64,128]{2,1,0:T(8,128)S(1)}, f32[16,64,128]{2,1,0:T(8,128)S(1)}, u32[]{:S(2)}, u32[]{:S(2)}) %collective-permute-start.4) | collective-permute-done | bytes 524320 | tf_op jit(solution)/shard_map/ppermute | solution.py:12
  88.1 1.2 collective-permute-done.5
  89.4 1.9 collective-permute-start.6
  91.4 6.5 %collective-permute-start.7 = (f32[16,64,128]{2,1,0:T(8,128)S(1)}, f32[16,64,128]{2,1,0:T(8,128)S(1)}, u32[]{:S(2)}, u32[]{:S(2)}) collective-permute-start(f32[16,64,128]{2,1,0:T(8,128)S(1)} %get-tuple-element.65), channel_id=1, source_target_pairs={{8,0},{16,8},{24,16},{32,24},{40,32},{48,40},{56,48},{64,56},{72,6... | collective-permute-start | bytes 1572872 | tf_op jit(solution)/shard_map/ppermute | solution.py:12
  97.9 7.8 %collective-permute-done.6 = f32[16,64,128]{2,1,0:T(8,128)S(1)} collective-permute-done((f32[16,64,128]{2,1,0:T(8,128)S(1)}, f32[16,64,128]{2,1,0:T(8,128)S(1)}, u32[]{:S(2)}, u32[]{:S(2)}) %collective-permute-start.6) | collective-permute-done | bytes 524320 | tf_op jit(solution)/shard_map/ppermute | solution.py:12
  105.7 1.2 collective-permute-done.7
  107.0 1.9 collective-permute-start.8
  109.0 6.5 %collective-permute-start.9 = (f32[16,64,128]{2,1,0:T(8,128)S(1)}, f32[16,64,128]{2,1,0:T(8,128)S(1)}, u32[]{:S(2)}, u32[]{:S(2)}) collective-permute-start(f32[16,64,128]{2,1,0:T(8,128)S(1)} %get-tuple-element.69), channel_id=1, source_target_pairs={{8,0},{16,8},{24,16},{32,24},{40,32},{48,40},{56,48},{64,56},{72,6... | collective-permute-start | bytes 1572872 | tf_op jit(solution)/shard_map/ppermute | solution.py:12
  115.5 6.9 %collective-permute-done.8 = f32[16,64,128]{2,1,0:T(8,128)S(1)} collective-permute-done((f32[16,64,128]{2,1,0:T(8,128)S(1)}, f32[16,64,128]{2,1,0:T(8,128)S(1)}, u32[]{:S(2)}, u32[]{:S(2)}) %collective-permute-start.8) | collective-permute-done | bytes 524320 | tf_op jit(solution)/shard_map/ppermute | solution.py:12
  122.4 1.2 collective-permute-done.9
  123.7 1.9 collective-permute-start.10
  125.7 6.5 %collective-permute-start.11 = (f32[16,64,128]{2,1,0:T(8,128)S(1)}, f32[16,64,128]{2,1,0:T(8,128)S(1)}, u32[]{:S(2)}, u32[]{:S(2)}) collective-permute-start(f32[16,64,128]{2,1,0:T(8,128)S(1)} %get-tuple-element.73), channel_id=1, source_target_pairs={{8,0},{16,8},{24,16},{32,24},{40,32},{48,40},{56,48},{64,56},{72,6... | collective-permute-start | bytes 1572872 | tf_op jit(solution)/shard_map/ppermute | solution.py:12
  132.2 6.0 %collective-permute-done.10 = f32[16,64,128]{2,1,0:T(8,128)S(1)} collective-permute-done((f32[16,64,128]{2,1,0:T(8,128)S(1)}, f32[16,64,128]{2,1,0:T(8,128)S(1)}, u32[]{:S(2)}, u32[]{:S(2)}) %collective-permute-start.10) | collective-permute-done | bytes 524320 | tf_op jit(solution)/shard_map/ppermute | solution.py:12
  138.1 1.2 collective-permute-done.11
  139.5 1.9 collective-permute-start.12
  141.4 6.5 %collective-permute-start.13 = (f32[16,64,128]{2,1,0:T(8,128)S(1)}, f32[16,64,128]{2,1,0:T(8,128)S(1)}, u32[]{:S(2)}, u32[]{:S(2)}) collective-permute-start(f32[16,64,128]{2,1,0:T(8,128)S(1)} %get-tuple-element.77), channel_id=1, source_target_pairs={{8,0},{16,8},{24,16},{32,24},{40,32},{48,40},{56,48},{64,56},{72,6... | collective-permute-start | bytes 1572872 | tf_op jit(solution)/shard_map/ppermute | solution.py:12
  147.9 5.2 %collective-permute-done.12 = f32[16,64,128]{2,1,0:T(8,128)S(1)} collective-permute-done((f32[16,64,128]{2,1,0:T(8,128)S(1)}, f32[16,64,128]{2,1,0:T(8,128)S(1)}, u32[]{:S(2)}, u32[]{:S(2)}) %collective-permute-start.12) | collective-permute-done | bytes 524320 | tf_op jit(solution)/shard_map/ppermute | solution.py:12
  153.1 1.5 collective-permute-done.13
  154.8 1.9 collective-permute-start.14
  156.7 6.5 %collective-permute-start.15 = (f32[16,64,128]{2,1,0:T(8,128)S(1)}, f32[16,64,128]{2,1,0:T(8,128)S(1)}, u32[]{:S(2)}, u32[]{:S(2)}) collective-permute-start(f32[16,64,128]{2,1,0:T(8,128)S(1)} %get-tuple-element.81), channel_id=1, source_target_pairs={{8,0},{16,8},{24,16},{32,24},{40,32},{48,40},{56,48},{64,56},{72,6... | collective-permute-start | bytes 1572872 | tf_op jit(solution)/shard_map/ppermute | solution.py:12
  163.2 5.2 %collective-permute-done.14 = f32[16,64,128]{2,1,0:T(8,128)S(1)} collective-permute-done((f32[16,64,128]{2,1,0:T(8,128)S(1)}, f32[16,64,128]{2,1,0:T(8,128)S(1)}, u32[]{:S(2)}, u32[]{:S(2)}) %collective-permute-start.14) | collective-permute-done | bytes 524320 | tf_op jit(solution)/shard_map/ppermute | solution.py:12
  168.4 1.5 collective-permute-done.15
  170.1 1.9 collective-permute-start.16
  172.0 6.5 %collective-permute-start.17 = (f32[16,64,128]{2,1,0:T(8,128)S(1)}, f32[16,64,128]{2,1,0:T(8,128)S(1)}, u32[]{:S(2)}, u32[]{:S(2)}) collective-permute-start(f32[16,64,128]{2,1,0:T(8,128)S(1)} %get-tuple-element.85), channel_id=1, source_target_pairs={{8,0},{16,8},{24,16},{32,24},{40,32},{48,40},{56,48},{64,56},{72,6... | collective-permute-start | bytes 1572872 | tf_op jit(solution)/shard_map/ppermute | solution.py:12
  178.5 5.2 %collective-permute-done.16 = f32[16,64,128]{2,1,0:T(8,128)S(1)} collective-permute-done((f32[16,64,128]{2,1,0:T(8,128)S(1)}, f32[16,64,128]{2,1,0:T(8,128)S(1)}, u32[]{:S(2)}, u32[]{:S(2)}) %collective-permute-start.16) | collective-permute-done | bytes 524320 | tf_op jit(solution)/shard_map/ppermute | solution.py:12
  183.7 1.5 collective-permute-done.17
  185.3 1.9 collective-permute-start.18
  187.3 6.5 %collective-permute-start.19 = (f32[16,64,128]{2,1,0:T(8,128)S(1)}, f32[16,64,128]{2,1,0:T(8,128)S(1)}, u32[]{:S(2)}, u32[]{:S(2)}) collective-permute-start(f32[16,64,128]{2,1,0:T(8,128)S(1)} %get-tuple-element.89), channel_id=1, source_target_pairs={{8,0},{16,8},{24,16},{32,24},{40,32},{48,40},{56,48},{64,56},{72,6... | collective-permute-start | bytes 1572872 | tf_op jit(solution)/shard_map/ppermute | solution.py:12
  193.8 5.9 %collective-permute-done.18 = f32[16,64,128]{2,1,0:T(8,128)S(1)} collective-permute-done((f32[16,64,128]{2,1,0:T(8,128)S(1)}, f32[16,64,128]{2,1,0:T(8,128)S(1)}, u32[]{:S(2)}, u32[]{:S(2)}) %collective-permute-start.18) | collective-permute-done | bytes 524320 | tf_op jit(solution)/shard_map/ppermute | solution.py:12
  199.6 1.7 collective-permute-done.19
  201.6 1.9 collective-permute-start.20
  203.5 6.5 %collective-permute-start.21 = (f32[16,64,128]{2,1,0:T(8,128)S(1)}, f32[16,64,128]{2,1,0:T(8,128)S(1)}, u32[]{:S(2)}, u32[]{:S(2)}) collective-permute-start(f32[16,64,128]{2,1,0:T(8,128)S(1)} %get-tuple-element.93), channel_id=1, source_target_pairs={{8,0},{16,8},{24,16},{32,24},{40,32},{48,40},{56,48},{64,56},{72,6... | collective-permute-start | bytes 1572872 | tf_op jit(solution)/shard_map/ppermute | solution.py:12
  210.7 1.5 fusion.12
  212.2 4.7 %collective-permute-done.20 = f32[16,64,128]{2,1,0:T(8,128)S(1)} collective-permute-done((f32[16,64,128]{2,1,0:T(8,128)S(1)}, f32[16,64,128]{2,1,0:T(8,128)S(1)}, u32[]{:S(2)}, u32[]{:S(2)}) %collective-permute-start.20) | collective-permute-done | bytes 524320 | tf_op jit(solution)/shard_map/ppermute | solution.py:12
  216.9 1.7 collective-permute-done.21
  218.8 2.1 collective-permute-start.22
  221.0 6.5 %collective-permute-start.23 = (f32[16,64,128]{2,1,0:T(8,128)S(1)}, f32[16,64,128]{2,1,0:T(8,128)S(1)}, u32[]{:S(2)}, u32[]{:S(2)}) collective-permute-start(f32[16,64,128]{2,1,0:T(8,128)S(1)} %get-tuple-element.97), channel_id=1, source_target_pairs={{8,0},{16,8},{24,16},{32,24},{40,32},{48,40},{56,48},{64,56},{72,6... | collective-permute-start | bytes 1572872 | tf_op jit(solution)/shard_map/ppermute | solution.py:12
  227.6 0.9 reduce_window_sum.32
  228.5 0.9 reduce_window_sum.31
  230.3 1.3 fusion.10
  231.6 0.9 collective-permute-done.22
  232.5 1.5 collective-permute-done.23
  234.4 1.0 fusion.5
  235.4 1.0 fusion.3
  236.4 0.7 pad_maximum_fusion
  238.9 1.2 fusion.6
  240.0 1.9 fusion.7
  242.2 1.0 copy.35
  243.8 0.7 multiply_subtract_fusion
  244.5 25.7 %reduce-scatter.2.cloned.1.call-done = f32[2,16,128]{2,1,0:T(8,128)} async-done(((f32[2,128,128]{2,1,0:T(8,128)}), f32[2,16,128]{2,1,0:T(8,128)}) %reduce-scatter.2.cloned.1.call-update) | async-done | bytes 16400 | tf_op jit(solution)/shard_map/reduce_scatter | solution.py:88
  270.2 1.3 slice_bitcast_fusion
  (84 shorter events, 10.5 us)
Async XLA Ops:
  7.2 263.0 %reduce-scatter.2.cloned.1.call-start = ((), (), s32[]{:S(2)}) async-start(), calls=%async_computation.1 | async-start | bytes 147456 | tf_op jit(solution)/shard_map/reduce_scatter | solution.py:88
  7.2 0.7 copy-start.19
  8.2 1.4 copy-start
  8.9 0.7 copy-start.20
  10.0 200.3 %copy-start.5 = (f32[16,128]{1,0:T(8,128)}, f32[16,128]{1,0:T(8,128)S(1)}, u32[]{:S(2)}) copy-start(f32[16,128]{1,0:T(8,128)S(1)} %reduce_window_sum.30) | copy-start | bytes 24580
  10.0 0.7 copy-start.17
  10.0 0.7 copy-start.18
  23.9 1.4 copy-start.1
  25.1 0.8 copy-start.2
  26.3 23.8 %collective-permute-start = (f32[16,64,128]{2,1,0:T(8,128)S(1)}, f32[16,64,128]{2,1,0:T(8,128)S(1)}, u32[]{:S(2)}, u32[]{:S(2)}) collective-permute-start(f32[16,64,128]{2,1,0:T(8,128)S(1)} %get-tuple-element.52), channel_id=1, source_target_pairs={{0,8},{8,16},{16,24},{24,32},{32,40},{40,48},{48,56},{56,64},{64,7... | collective-permute-start | bytes 1572872 | tf_op jit(solution)/shard_map/ppermute | solution.py:12
  30.2 21.1 %collective-permute-start.1 = (f32[16,64,128]{2,1,0:T(8,128)S(1)}, f32[16,64,128]{2,1,0:T(8,128)S(1)}, u32[]{:S(2)}, u32[]{:S(2)}) collective-permute-start(f32[16,64,128]{2,1,0:T(8,128)S(1)} %get-tuple-element.53), channel_id=1, source_target_pairs={{8,0},{16,8},{24,16},{32,24},{40,32},{48,40},{56,48},{64,56},{72,6... | collective-permute-start | bytes 1572872 | tf_op jit(solution)/shard_map/ppermute | solution.py:12
  51.5 18.1 %collective-permute-start.2 = (f32[16,64,128]{2,1,0:T(8,128)S(1)}, f32[16,64,128]{2,1,0:T(8,128)S(1)}, u32[]{:S(2)}, u32[]{:S(2)}) collective-permute-start(f32[16,64,128]{2,1,0:T(8,128)S(1)} %get-tuple-element.56), channel_id=1, source_target_pairs={{0,8},{8,16},{16,24},{24,32},{32,40},{40,48},{48,56},{56,64},{64,7... | collective-permute-start | bytes 1572872 | tf_op jit(solution)/shard_map/ppermute | solution.py:12
  53.4 17.3 %collective-permute-start.3 = (f32[16,64,128]{2,1,0:T(8,128)S(1)}, f32[16,64,128]{2,1,0:T(8,128)S(1)}, u32[]{:S(2)}, u32[]{:S(2)}) collective-permute-start(f32[16,64,128]{2,1,0:T(8,128)S(1)} %get-tuple-element.57), channel_id=1, source_target_pairs={{8,0},{16,8},{24,16},{32,24},{40,32},{48,40},{56,48},{64,56},{72,6... | collective-permute-start | bytes 1572872 | tf_op jit(solution)/shard_map/ppermute | solution.py:12
  70.9 17.2 %collective-permute-start.4 = (f32[16,64,128]{2,1,0:T(8,128)S(1)}, f32[16,64,128]{2,1,0:T(8,128)S(1)}, u32[]{:S(2)}, u32[]{:S(2)}) collective-permute-start(f32[16,64,128]{2,1,0:T(8,128)S(1)} %get-tuple-element.60), channel_id=1, source_target_pairs={{0,8},{8,16},{16,24},{24,32},{32,40},{40,48},{48,56},{56,64},{64,7... | collective-permute-start | bytes 1572872 | tf_op jit(solution)/shard_map/ppermute | solution.py:12
  72.8 16.4 %collective-permute-start.5 = (f32[16,64,128]{2,1,0:T(8,128)S(1)}, f32[16,64,128]{2,1,0:T(8,128)S(1)}, u32[]{:S(2)}, u32[]{:S(2)}) collective-permute-start(f32[16,64,128]{2,1,0:T(8,128)S(1)} %get-tuple-element.61), channel_id=1, source_target_pairs={{8,0},{16,8},{24,16},{32,24},{40,32},{48,40},{56,48},{64,56},{72,6... | collective-permute-start | bytes 1572872 | tf_op jit(solution)/shard_map/ppermute | solution.py:12
  89.4 16.3 %collective-permute-start.6 = (f32[16,64,128]{2,1,0:T(8,128)S(1)}, f32[16,64,128]{2,1,0:T(8,128)S(1)}, u32[]{:S(2)}, u32[]{:S(2)}) collective-permute-start(f32[16,64,128]{2,1,0:T(8,128)S(1)} %get-tuple-element.64), channel_id=1, source_target_pairs={{0,8},{8,16},{16,24},{24,32},{32,40},{40,48},{48,56},{56,64},{64,7... | collective-permute-start | bytes 1572872 | tf_op jit(solution)/shard_map/ppermute | solution.py:12
  91.4 15.5 %collective-permute-start.7 = (f32[16,64,128]{2,1,0:T(8,128)S(1)}, f32[16,64,128]{2,1,0:T(8,128)S(1)}, u32[]{:S(2)}, u32[]{:S(2)}) collective-permute-start(f32[16,64,128]{2,1,0:T(8,128)S(1)} %get-tuple-element.65), channel_id=1, source_target_pairs={{8,0},{16,8},{24,16},{32,24},{40,32},{48,40},{56,48},{64,56},{72,6... | collective-permute-start | bytes 1572872 | tf_op jit(solution)/shard_map/ppermute | solution.py:12
  107.0 15.3 %collective-permute-start.8 = (f32[16,64,128]{2,1,0:T(8,128)S(1)}, f32[16,64,128]{2,1,0:T(8,128)S(1)}, u32[]{:S(2)}, u32[]{:S(2)}) collective-permute-start(f32[16,64,128]{2,1,0:T(8,128)S(1)} %get-tuple-element.68), channel_id=1, source_target_pairs={{0,8},{8,16},{16,24},{24,32},{32,40},{40,48},{48,56},{56,64},{64,7... | collective-permute-start | bytes 1572872 | tf_op jit(solution)/shard_map/ppermute | solution.py:12
  109.0 14.6 %collective-permute-start.9 = (f32[16,64,128]{2,1,0:T(8,128)S(1)}, f32[16,64,128]{2,1,0:T(8,128)S(1)}, u32[]{:S(2)}, u32[]{:S(2)}) collective-permute-start(f32[16,64,128]{2,1,0:T(8,128)S(1)} %get-tuple-element.69), channel_id=1, source_target_pairs={{8,0},{16,8},{24,16},{32,24},{40,32},{48,40},{56,48},{64,56},{72,6... | collective-permute-start | bytes 1572872 | tf_op jit(solution)/shard_map/ppermute | solution.py:12
  123.7 14.4 %collective-permute-start.10 = (f32[16,64,128]{2,1,0:T(8,128)S(1)}, f32[16,64,128]{2,1,0:T(8,128)S(1)}, u32[]{:S(2)}, u32[]{:S(2)}) collective-permute-start(f32[16,64,128]{2,1,0:T(8,128)S(1)} %get-tuple-element.72), channel_id=1, source_target_pairs={{0,8},{8,16},{16,24},{24,32},{32,40},{40,48},{48,56},{56,64},{64,7... | collective-permute-start | bytes 1572872 | tf_op jit(solution)/shard_map/ppermute | solution.py:12
  125.7 13.7 %collective-permute-start.11 = (f32[16,64,128]{2,1,0:T(8,128)S(1)}, f32[16,64,128]{2,1,0:T(8,128)S(1)}, u32[]{:S(2)}, u32[]{:S(2)}) collective-permute-start(f32[16,64,128]{2,1,0:T(8,128)S(1)} %get-tuple-element.73), channel_id=1, source_target_pairs={{8,0},{16,8},{24,16},{32,24},{40,32},{48,40},{56,48},{64,56},{72,6... | collective-permute-start | bytes 1572872 | tf_op jit(solution)/shard_map/ppermute | solution.py:12
  139.5 13.7 %collective-permute-start.12 = (f32[16,64,128]{2,1,0:T(8,128)S(1)}, f32[16,64,128]{2,1,0:T(8,128)S(1)}, u32[]{:S(2)}, u32[]{:S(2)}) collective-permute-start(f32[16,64,128]{2,1,0:T(8,128)S(1)} %get-tuple-element.76), channel_id=1, source_target_pairs={{0,8},{8,16},{16,24},{24,32},{32,40},{40,48},{48,56},{56,64},{64,7... | collective-permute-start | bytes 1572872 | tf_op jit(solution)/shard_map/ppermute | solution.py:12
  141.4 13.2 %collective-permute-start.13 = (f32[16,64,128]{2,1,0:T(8,128)S(1)}, f32[16,64,128]{2,1,0:T(8,128)S(1)}, u32[]{:S(2)}, u32[]{:S(2)}) collective-permute-start(f32[16,64,128]{2,1,0:T(8,128)S(1)} %get-tuple-element.77), channel_id=1, source_target_pairs={{8,0},{16,8},{24,16},{32,24},{40,32},{48,40},{56,48},{64,56},{72,6... | collective-permute-start | bytes 1572872 | tf_op jit(solution)/shard_map/ppermute | solution.py:12
  154.8 13.7 %collective-permute-start.14 = (f32[16,64,128]{2,1,0:T(8,128)S(1)}, f32[16,64,128]{2,1,0:T(8,128)S(1)}, u32[]{:S(2)}, u32[]{:S(2)}) collective-permute-start(f32[16,64,128]{2,1,0:T(8,128)S(1)} %get-tuple-element.80), channel_id=1, source_target_pairs={{0,8},{8,16},{16,24},{24,32},{32,40},{40,48},{48,56},{56,64},{64,7... | collective-permute-start | bytes 1572872 | tf_op jit(solution)/shard_map/ppermute | solution.py:12
  156.7 13.2 %collective-permute-start.15 = (f32[16,64,128]{2,1,0:T(8,128)S(1)}, f32[16,64,128]{2,1,0:T(8,128)S(1)}, u32[]{:S(2)}, u32[]{:S(2)}) collective-permute-start(f32[16,64,128]{2,1,0:T(8,128)S(1)} %get-tuple-element.81), channel_id=1, source_target_pairs={{8,0},{16,8},{24,16},{32,24},{40,32},{48,40},{56,48},{64,56},{72,6... | collective-permute-start | bytes 1572872 | tf_op jit(solution)/shard_map/ppermute | solution.py:12
  170.1 13.7 %collective-permute-start.16 = (f32[16,64,128]{2,1,0:T(8,128)S(1)}, f32[16,64,128]{2,1,0:T(8,128)S(1)}, u32[]{:S(2)}, u32[]{:S(2)}) collective-permute-start(f32[16,64,128]{2,1,0:T(8,128)S(1)} %get-tuple-element.84), channel_id=1, source_target_pairs={{0,8},{8,16},{16,24},{24,32},{32,40},{40,48},{48,56},{56,64},{64,7... | collective-permute-start | bytes 1572872 | tf_op jit(solution)/shard_map/ppermute | solution.py:12
  172.0 13.2 %collective-permute-start.17 = (f32[16,64,128]{2,1,0:T(8,128)S(1)}, f32[16,64,128]{2,1,0:T(8,128)S(1)}, u32[]{:S(2)}, u32[]{:S(2)}) collective-permute-start(f32[16,64,128]{2,1,0:T(8,128)S(1)} %get-tuple-element.85), channel_id=1, source_target_pairs={{8,0},{16,8},{24,16},{32,24},{40,32},{48,40},{56,48},{64,56},{72,6... | collective-permute-start | bytes 1572872 | tf_op jit(solution)/shard_map/ppermute | solution.py:12
  185.3 14.3 %collective-permute-start.18 = (f32[16,64,128]{2,1,0:T(8,128)S(1)}, f32[16,64,128]{2,1,0:T(8,128)S(1)}, u32[]{:S(2)}, u32[]{:S(2)}) collective-permute-start(f32[16,64,128]{2,1,0:T(8,128)S(1)} %get-tuple-element.88), channel_id=1, source_target_pairs={{0,8},{8,16},{16,24},{24,32},{32,40},{40,48},{48,56},{56,64},{64,7... | collective-permute-start | bytes 1572872 | tf_op jit(solution)/shard_map/ppermute | solution.py:12
  187.3 14.1 %collective-permute-start.19 = (f32[16,64,128]{2,1,0:T(8,128)S(1)}, f32[16,64,128]{2,1,0:T(8,128)S(1)}, u32[]{:S(2)}, u32[]{:S(2)}) collective-permute-start(f32[16,64,128]{2,1,0:T(8,128)S(1)} %get-tuple-element.89), channel_id=1, source_target_pairs={{8,0},{16,8},{24,16},{32,24},{40,32},{48,40},{56,48},{64,56},{72,6... | collective-permute-start | bytes 1572872 | tf_op jit(solution)/shard_map/ppermute | solution.py:12
  201.6 15.4 %collective-permute-start.20 = (f32[16,64,128]{2,1,0:T(8,128)S(1)}, f32[16,64,128]{2,1,0:T(8,128)S(1)}, u32[]{:S(2)}, u32[]{:S(2)}) collective-permute-start(f32[16,64,128]{2,1,0:T(8,128)S(1)} %get-tuple-element.92), channel_id=1, source_target_pairs={{0,8},{8,16},{16,24},{24,32},{32,40},{40,48},{48,56},{56,64},{64,7... | collective-permute-start | bytes 1572872 | tf_op jit(solution)/shard_map/ppermute | solution.py:12
  203.5 15.2 %collective-permute-start.21 = (f32[16,64,128]{2,1,0:T(8,128)S(1)}, f32[16,64,128]{2,1,0:T(8,128)S(1)}, u32[]{:S(2)}, u32[]{:S(2)}) collective-permute-start(f32[16,64,128]{2,1,0:T(8,128)S(1)} %get-tuple-element.93), channel_id=1, source_target_pairs={{8,0},{16,8},{24,16},{32,24},{40,32},{48,40},{56,48},{64,56},{72,6... | collective-permute-start | bytes 1572872 | tf_op jit(solution)/shard_map/ppermute | solution.py:12
  210.1 0.6 copy-start.14
  210.2 2.0 copy-start.8
  212.2 15.4 %copy-start.10 = (f32[16,128]{1,0:T(8,128)}, f32[16,128]{1,0:T(8,128)S(1)}, u32[]{:S(2)}) copy-start(f32[16,128]{1,0:T(8,128)S(1)} %get-tuple-element.116) | copy-start | bytes 24580
  218.8 13.7 %collective-permute-start.22 = (f32[16,64,128]{2,1,0:T(8,128)S(1)}, f32[16,64,128]{2,1,0:T(8,128)S(1)}, u32[]{:S(2)}, u32[]{:S(2)}) collective-permute-start(f32[16,64,128]{2,1,0:T(8,128)S(1)} %get-tuple-element.96), channel_id=1, source_target_pairs={{0,8},{8,16},{16,24},{24,32},{32,40},{40,48},{48,56},{56,64},{64,7... | collective-permute-start | bytes 1572872 | tf_op jit(solution)/shard_map/ppermute | solution.py:12
  221.0 13.0 %collective-permute-start.23 = (f32[16,64,128]{2,1,0:T(8,128)S(1)}, f32[16,64,128]{2,1,0:T(8,128)S(1)}, u32[]{:S(2)}, u32[]{:S(2)}) collective-permute-start(f32[16,64,128]{2,1,0:T(8,128)S(1)} %get-tuple-element.97), channel_id=1, source_target_pairs={{8,0},{16,8},{24,16},{32,24},{40,32},{48,40},{56,48},{64,56},{72,6... | collective-permute-start | bytes 1572872 | tf_op jit(solution)/shard_map/ppermute | solution.py:12
  229.4 0.7 copy-start.6
  229.4 0.9 copy-start.9
  229.4 0.9 copy-start.15
  231.6 2.8 copy-start.3
  237.1 0.7 copy-start.22
  238.1 0.7 copy-start.7
  238.1 0.7 copy-start.16
  242.1 1.0 copy-start.4
  242.1 1.0 copy-start.11
  242.2 1.0 copy-start.12
  242.2 1.0 copy-start.13
  243.2 0.7 copy-start.21
Sparse Core Ops, SparseCore 0:
  237.2 32.9 reduce-scatter.1

commit v2 on v1

--- a/solution.py
+++ b/solution.py
@@ -12,12 +12,53 @@
     return lax.ppermute(x, axis, pairs)
 
 
+def shift_pair(fwd, bwd, by):
+    fwd, bwd = lax.optimization_barrier((fwd, bwd))
+    return lax.optimization_barrier(
+        (from_behind(fwd, "context", by), from_behind(bwd, "context", -by))
+    )
+
+
+def exchange(pieces, axis):
+    count = lax.axis_size(axis)
+    pieces = lax.optimization_barrier(pieces)
+    got = [
+        lax.ppermute(pieces[s], axis, [(i, (i + s) % count) for i in range(count)])
+        for s in range(1, count)
+    ]
+    return [pieces[0]] + list(lax.optimization_barrier(got))
+
+
+def gather_rows(piece, axis):
+    count = lax.axis_size(axis)
+    me = lax.axis_index(axis)
+    got = jnp.stack(exchange([piece] * count, axis))
+    order = (me - jnp.arange(count)) % count
+    return jnp.take(got, order, axis=0)
+
+
+def scatter_sum(whole, axis):
+    count = lax.axis_size(axis)
+    me = lax.axis_index(axis)
+    size = whole.shape[1] // count
+    pieces = [
+        lax.dynamic_slice_in_dim(whole, ((me + s) % count) * size, size, axis=1)
+        for s in range(count)
+    ]
+    got = exchange(pieces, axis)
+    out = got[0]
+    for part in got[1:]:
+        out = out + part
+    return out
+
+
 def local(inputs, grads, step_size, decay_rate, skip_gain, b_rows, c_rows, doc_lengths):
     length = inputs.shape[0]
     heads = step_size.shape[0]
     width = inputs.shape[1] // heads
-    rows = lax.all_gather(jnp.stack([b_rows, c_rows]), "tensor", axis=1, tiled=True)
-    b_bf, c_bf = rows[0], rows[1]
+    rows = gather_rows(jnp.stack([b_rows, c_rows]), "tensor")
+    b_bf = rows[:, 0].reshape(length, -1)
+    c_bf = rows[:, 1].reshape(length, -1)
     bmat = b_bf.astype(jnp.float32)
     cmat = c_bf.astype(jnp.float32)
     xs = inputs.astype(jnp.float32).reshape(length, heads, width).transpose(1, 0, 2)
@@ -41,17 +82,31 @@
     local_state = jnp.einsum("hlp,ln->hpn", left_u, bmat, precision=HIGH)
     local_adj = jnp.einsum("hlp,ln->hpn", enter_dy, cmat, precision=HIGH)
 
-    turns = 3 * lax.axis_size("context") // 16
-    inc_state = jnp.zeros_like(local_state)
-    inc_adj = jnp.zeros_like(local_adj)
-    for _ in range(turns):
-        send_state, send_adj = lax.optimization_barrier(
-            (local_state + total * inc_state, local_adj + total * inc_adj)
+    reach = 3 * lax.axis_size("context") // 16
+    low = reach & -reach
+    high = reach - low
+    assert high > 0 and high & (high - 1) == 0 and low < high
+    fwd = (local_state, total)
+    bwd = (local_adj, total)
+    span = 1
+    kept = {}
+    while span < high:
+        kept[span] = (fwd, bwd)
+        got_f, got_b = shift_pair(fwd, bwd, span)
+        fwd = (fwd[0] + fwd[1] * got_f[0], fwd[1] * got_f[1])
+        bwd = (bwd[0] + bwd[1] * got_b[0], bwd[1] * got_b[1])
+        span *= 2
+    near_f, near_b = kept[low]
+    got = lax.optimization_barrier(
+        (
+            from_behind(near_f, "context", 1),
+            from_behind(fwd[0], "context", low + 1),
+            from_behind(near_b, "context", -1),
+            from_behind(bwd[0], "context", -low - 1),
         )
-        inc_state, inc_adj = lax.optimization_barrier(
-            (from_behind(send_state, "context", 1), from_behind(send_adj, "context", -1))
-        )
-    s_in, g_in = inc_state, inc_adj
+    )
+    s_in = got[0][0] + got[0][1] * got[1]
+    g_in = got[2][0] + got[2][1] * got[3]
 
     index = jnp.arange(length)
     keep = (index[:, None] >= index[None, :]) & (seg[:, None] == seg[None, :])
@@ -85,7 +140,7 @@
     gc = gc_loc + jnp.einsum("hlp,hpn->ln", enter_dy, s_in, precision=HIGH)
 
     grad_x = gx.transpose(1, 0, 2).reshape(length, heads * width)
-    grad_bc = lax.psum_scatter(jnp.stack([gb, gc]), "tensor", scatter_dimension=1, tiled=True)
+    grad_bc = scatter_sum(jnp.stack([gb, gc]), "tensor")
     return (grad_x, grad_step, grad_bc[0], grad_bc[1])
 
 

time: 280 us -> 242 us (0.86)
  the two profiles are of different devices: /device:TPU:2 before, /device:TPU:3 now
where the time goes in v2:
time: 242 us; the launch traced here: 240 us
  starting transfers between devices  120 us (50%)
  waiting for transfers between devices  88.6 us (37%)
  other arithmetic  11.8 us (5%)
  matrix products  11.3 us (5%)
  local copies, waits for them, and re-layouts  7.7 us (3%)
    ppermute x16, waiting for transfers between devices, from_behind(): return lax.ppermute(x, axis, pairs)  88 us
    ppermute x16, starting transfers between devices, from_behind(): return lax.ppermute(x, axis, pairs)  78.9 us
    ppermute x14, starting transfers between devices, exchange(): lax.ppermute(pieces[s], axis, [(i, (i + s) % count) for i in range(count)])  40.9 us
  transfers between devices with their start and end apart: 30, of which 8 were waited for; matrix products, arithmetic and copies ran while one was open for 8% of the time, Pallas kernels for 0%

profile of v2, /device:TPU:3, one launch (start us, length us, event | category | flops | bytes accessed | tf_op | source)
XLA Modules:
  0.0 240.5 jit_solution(8264799985169646566)
XLA Ops:
  0.6 0.7 pad_maximum_fusion
  1.3 1.9 collective-permute-start
  3.2 3.2 %collective-permute-start.1 = (bf16[2,16,128]{2,1,0:T(8,128)(2,1)S(1)}, bf16[2,16,128]{2,1,0:T(8,128)(2,1)S(1)}, u32[]{:S(2)}, u32[]{:S(2)}) collective-permute-start(bf16[2,16,128]{2,1,0:T(8,128)(2,1)S(1)} %pad_maximum_fusion), channel_id=1, source_target_pairs={{0,2},{1,3},{2,4},{3,5},{4,6},{5,7},{6,0},{7,1},{8,10},{9,11},{10,... | collective-permute-start | bytes 24584 | tf_op jit(solution)/shard_map/ppermute | solution.py:26
  6.4 3.5 %collective-permute-start.2 = (bf16[2,16,128]{2,1,0:T(8,128)(2,1)S(1)}, bf16[2,16,128]{2,1,0:T(8,128)(2,1)S(1)}, u32[]{:S(2)}, u32[]{:S(2)}) collective-permute-start(bf16[2,16,128]{2,1,0:T(8,128)(2,1)S(1)} %pad_maximum_fusion), channel_id=1, source_target_pairs={{0,3},{1,4},{2,5},{3,6},{4,7},{5,0},{6,1},{7,2},{8,11},{9,12},{10,... | collective-permute-start | bytes 24584 | tf_op jit(solution)/shard_map/ppermute | solution.py:26
  9.9 2.3 collective-permute-start.3
  12.2 3.9 %collective-permute-start.4 = (bf16[2,16,128]{2,1,0:T(8,128)(2,1)S(1)}, bf16[2,16,128]{2,1,0:T(8,128)(2,1)S(1)}, u32[]{:S(2)}, u32[]{:S(2)}) collective-permute-start(bf16[2,16,128]{2,1,0:T(8,128)(2,1)S(1)} %pad_maximum_fusion), channel_id=1, source_target_pairs={{0,5},{1,6},{2,7},{3,0},{4,1},{5,2},{6,3},{7,4},{8,13},{9,14},{10,... | collective-permute-start | bytes 24584 | tf_op jit(solution)/shard_map/ppermute | solution.py:26
  16.2 0.6 copy-done.14
  17.3 0.6 slice.27
  17.8 0.7 compare_convert_fusion
  19.4 2.8 %collective-permute-start.5 = (bf16[2,16,128]{2,1,0:T(8,128)(2,1)S(1)}, bf16[2,16,128]{2,1,0:T(8,128)(2,1)S(1)}, u32[]{:S(2)}, u32[]{:S(2)}) collective-permute-start(bf16[2,16,128]{2,1,0:T(8,128)(2,1)S(1)} %pad_maximum_fusion), channel_id=1, source_target_pairs={{0,6},{1,7},{2,0},{3,1},{4,2},{5,3},{6,4},{7,5},{8,14},{9,15},{10,... | collective-permute-start | bytes 24584 | tf_op jit(solution)/shard_map/ppermute | solution.py:26
  22.1 1.5 collective-permute-start.6
  23.7 1.1 copy.34
  25.0 0.5 collective-permute-done.6
  25.6 0.6 gather_fusion
  27.1 3.5 %collective-permute-start.7 = (f32[16,64,128]{2,1,0:T(8,128)S(1)}, f32[16,64,128]{2,1,0:T(8,128)S(1)}, u32[]{:S(2)}, u32[]{:S(2)}) collective-permute-start(f32[16,64,128]{2,1,0:T(8,128)S(1)} %fusion.39), channel_id=1, source_target_pairs={{0,8},{8,16},{16,24},{24,32},{32,40},{40,48},{48,56},{56,64},{64,7... | collective-permute-start | bytes 1572872 | tf_op jit(solution)/shard_map/ppermute | solution.py:12
  30.6 9.5 %collective-permute-start.9 = (f32[16,64,128]{2,1,0:T(8,128)S(1)}, f32[16,64,128]{2,1,0:T(8,128)S(1)}, u32[]{:S(2)}, u32[]{:S(2)}) collective-permute-start(f32[16,64,128]{2,1,0:T(8,128)S(1)} %fusion.16), channel_id=1, source_target_pairs={{8,0},{16,8},{24,16},{32,24},{40,32},{48,40},{56,48},{64,56},{72,6... | collective-permute-start | bytes 1572872 | tf_op jit(solution)/shard_map/ppermute | solution.py:12
  40.1 3.4 %collective-permute-start.10 = (f32[16,1,1]{0,2,1:T(1,128)S(1)}, f32[16,1,1]{0,2,1:T(1,128)S(1)}, u32[]{:S(2)}, u32[]{:S(2)}) collective-permute-start(f32[16,1,1]{0,2,1:T(1,128)S(1)} %bitcast.157), channel_id=1, source_target_pairs={{8,0},{16,8},{24,16},{32,24},{40,32},{48,40},{56,48},{64,56},{72,6... | collective-permute-start | bytes 200 | tf_op jit(solution)/shard_map/ppermute | solution.py:12
  43.5 1.9 collective-permute-start.8
  45.4 5.6 %collective-permute-done.10 = f32[16,1,1]{0,2,1:T(1,128)S(1)} collective-permute-done((f32[16,1,1]{0,2,1:T(1,128)S(1)}, f32[16,1,1]{0,2,1:T(1,128)S(1)}, u32[]{:S(2)}, u32[]{:S(2)}) %collective-permute-start.10) | collective-permute-done | bytes 96 | tf_op jit(solution)/shard_map/ppermute | solution.py:12
  51.2 1.9 collective-permute-start.11
  53.1 6.4 %collective-permute-start.13 = (f32[16,64,128]{2,1,0:T(8,128)S(1)}, f32[16,64,128]{2,1,0:T(8,128)S(1)}, u32[]{:S(2)}, u32[]{:S(2)}) collective-permute-start(f32[16,64,128]{2,1,0:T(8,128)S(1)} %get-tuple-element.85), channel_id=1, source_target_pairs={{16,0},{24,8},{32,16},{40,24},{48,32},{56,40},{64,48},{72,56},{80,... | collective-permute-start | bytes 1572872 | tf_op jit(solution)/shard_map/ppermute | solution.py:12
  59.5 1.9 collective-permute-start.12
  61.4 6.4 %collective-permute-start.14 = (f32[16,1,1]{0,2,1:T(1,128)S(1)}, f32[16,1,1]{0,2,1:T(1,128)S(1)}, u32[]{:S(2)}, u32[]{:S(2)}) collective-permute-start(f32[16,1,1]{0,2,1:T(1,128)S(1)} %get-tuple-element.86), channel_id=1, source_target_pairs={{16,0},{24,8},{32,16},{40,24},{48,32},{56,40},{64,48},{72,56},{80,... | collective-permute-start | bytes 200 | tf_op jit(solution)/shard_map/ppermute | solution.py:12
  67.8 1.8 collective-permute-done.12
  69.6 3.7 %collective-permute-done.14 = f32[16,1,1]{0,2,1:T(1,128)S(1)} collective-permute-done((f32[16,1,1]{0,2,1:T(1,128)S(1)}, f32[16,1,1]{0,2,1:T(1,128)S(1)}, u32[]{:S(2)}, u32[]{:S(2)}) %collective-permute-start.14) | collective-permute-done | bytes 96 | tf_op jit(solution)/shard_map/ppermute | solution.py:12
  73.4 0.5 mul.298
  74.2 4.4 %collective-permute-start.17 = (f32[16,64,128]{2,1,0:T(8,128)S(1)}, f32[16,64,128]{2,1,0:T(8,128)S(1)}, u32[]{:S(2)}, u32[]{:S(2)}) collective-permute-start(f32[16,64,128]{2,1,0:T(8,128)S(1)} %multiply_add_fusion.5), channel_id=1, source_target_pairs={{0,32},{8,40},{16,48},{24,56},{32,64},{40,72},{48,80},{56,88},{64,... | collective-permute-start | bytes 1572872 | tf_op jit(solution)/shard_map/ppermute | solution.py:12
  78.5 10.0 %collective-permute-start.18 = (f32[16,64,128]{2,1,0:T(8,128)S(1)}, f32[16,64,128]{2,1,0:T(8,128)}, u32[]{:S(2)}, u32[]{:S(2)}) collective-permute-start(f32[16,64,128]{2,1,0:T(8,128)S(1)} %multiply_add_fusion.4), channel_id=1, source_target_pairs={{32,0},{40,8},{48,16},{56,24},{64,32},{72,40},{80,48},{88,56},{96,... | collective-permute-start | bytes 1572872 | tf_op jit(solution)/shard_map/ppermute | solution.py:12
  89.2 2.1 fusion.12
  91.3 9.0 %collective-permute-start.20 = (f32[16,64,128]{2,1,0:T(8,128)S(1)}, f32[16,64,128]{2,1,0:T(8,128)S(1)}, u32[]{:S(2)}, u32[]{:S(2)}) collective-permute-start(f32[16,64,128]{2,1,0:T(8,128)S(1)} %multiply_add_fusion.4), channel_id=1, source_target_pairs={{8,0},{16,8},{24,16},{32,24},{40,32},{48,40},{56,48},{64,56},{72,6... | collective-permute-start | bytes 1572872 | tf_op jit(solution)/shard_map/ppermute | solution.py:12
  100.4 1.9 collective-permute-start.15
  102.3 1.5 collective-permute-done.17
  103.8 26.3 %collective-permute-done.18 = f32[16,64,128]{2,1,0:T(8,128)} collective-permute-done((f32[16,64,128]{2,1,0:T(8,128)S(1)}, f32[16,64,128]{2,1,0:T(8,128)}, u32[]{:S(2)}, u32[]{:S(2)}) %collective-permute-start.18) | collective-permute-done | bytes 524320 | tf_op jit(solution)/shard_map/ppermute | solution.py:12
  130.0 1.9 multiply_add_fusion.2
  132.0 1.9 collective-permute-start.22
  133.9 0.9 multiply_add_fusion.3
  134.8 8.2 %collective-permute-start.19 = (f32[16,64,128]{2,1,0:T(8,128)}, f32[16,64,128]{2,1,0:T(8,128)}, u32[]{:S(2)}, u32[]{:S(2)}) collective-permute-start(f32[16,64,128]{2,1,0:T(8,128)} %multiply_add_fusion.3), channel_id=1, source_target_pairs={{0,40},{8,48},{16,56},{24,64},{32,72},{40,80},{48,88},{56,96},{64,... | collective-permute-start | bytes 1572872 | tf_op jit(solution)/shard_map/ppermute | solution.py:12
  143.2 0.8 fusion.68
  144.0 1.3 fusion.10
  145.4 6.7 %collective-permute-start.21 = (f32[16,1,1]{0,2,1:T(1,128)}, f32[16,1,1]{0,2,1:T(1,128)}, u32[]{:S(2)}, u32[]{:S(2)}) collective-permute-start(f32[16,1,1]{0,2,1:T(1,128)} %mul.298), channel_id=1, source_target_pairs={{8,0},{16,8},{24,16},{32,24},{40,32},{48,40},{56,48},{64,56},{72,6... | collective-permute-start | bytes 200 | tf_op jit(solution)/shard_map/ppermute | solution.py:12
  152.1 1.6 reduce_window_sum.31
  153.7 43.8 %collective-permute-done.21 = f32[16,1,1]{0,2,1:T(1,128)} collective-permute-done((f32[16,1,1]{0,2,1:T(1,128)}, f32[16,1,1]{0,2,1:T(1,128)}, u32[]{:S(2)}, u32[]{:S(2)}) %collective-permute-start.21) | collective-permute-done | bytes 96 | tf_op jit(solution)/shard_map/ppermute | solution.py:12
  197.4 1.9 collective-permute-start.16
  199.4 1.6 reduce_window_sum.32
  200.9 5.4 %collective-permute-done.16 = f32[16,1,1]{0,2,1:T(1,128)} collective-permute-done((f32[16,1,1]{0,2,1:T(1,128)}, f32[16,1,1]{0,2,1:T(1,128)}, u32[]{:S(2)}, u32[]{:S(2)}) %collective-permute-start.16) | collective-permute-done | bytes 96 | tf_op jit(solution)/shard_map/ppermute | solution.py:12
  206.3 1.5 multiply_reduce_fusion.1
  207.9 0.4 fusion.1
  208.6 1.0 fusion.5
  209.6 1.0 fusion.3
  210.6 5.2 %collective-permute-start.23 = (f32[2,16,128]{2,1,0:T(8,128)S(1)}, f32[2,16,128]{2,1,0:T(8,128)S(1)}, u32[]{:S(2)}, u32[]{:S(2)}) collective-permute-start(f32[2,16,128]{2,1,0:T(8,128)S(1)} %get-tuple-element.102), channel_id=1, source_target_pairs={{0,1},{1,2},{2,3},{3,4},{4,5},{5,6},{6,7},{7,0},{8,9},{9,10},{10,1... | collective-permute-start | bytes 49160 | tf_op jit(solution)/shard_map/ppermute | solution.py:26
  215.9 2.5 %collective-permute-start.24 = (f32[2,16,128]{2,1,0:T(8,128)S(1)}, f32[2,16,128]{2,1,0:T(8,128)S(1)}, u32[]{:S(2)}, u32[]{:S(2)}) collective-permute-start(f32[2,16,128]{2,1,0:T(8,128)S(1)} %get-tuple-element.103), channel_id=1, source_target_pairs={{0,2},{1,3},{2,4},{3,5},{4,6},{5,7},{6,0},{7,1},{8,10},{9,11},{10,... | collective-permute-start | bytes 49160 | tf_op jit(solution)/shard_map/ppermute | solution.py:26
  218.4 3.4 %collective-permute-start.25 = (f32[2,16,128]{2,1,0:T(8,128)S(1)}, f32[2,16,128]{2,1,0:T(8,128)S(1)}, u32[]{:S(2)}, u32[]{:S(2)}) collective-permute-start(f32[2,16,128]{2,1,0:T(8,128)S(1)} %get-tuple-element.104), channel_id=1, source_target_pairs={{0,3},{1,4},{2,5},{3,6},{4,7},{5,0},{6,1},{7,2},{8,11},{9,12},{10,... | collective-permute-start | bytes 49160 | tf_op jit(solution)/shard_map/ppermute | solution.py:26
  221.8 3.1 %collective-permute-start.26 = (f32[2,16,128]{2,1,0:T(8,128)S(1)}, f32[2,16,128]{2,1,0:T(8,128)S(1)}, u32[]{:S(2)}, u32[]{:S(2)}) collective-permute-start(f32[2,16,128]{2,1,0:T(8,128)S(1)} %get-tuple-element.105), channel_id=1, source_target_pairs={{0,4},{1,5},{2,6},{3,7},{4,0},{5,1},{6,2},{7,3},{8,12},{9,13},{10,... | collective-permute-start | bytes 49160 | tf_op jit(solution)/shard_map/ppermute | solution.py:26
  224.9 3.6 %collective-permute-start.27 = (f32[2,16,128]{2,1,0:T(8,128)S(1)}, f32[2,16,128]{2,1,0:T(8,128)S(1)}, u32[]{:S(2)}, u32[]{:S(2)}) collective-permute-start(f32[2,16,128]{2,1,0:T(8,128)S(1)} %get-tuple-element.106), channel_id=1, source_target_pairs={{0,5},{1,6},{2,7},{3,0},{4,1},{5,2},{6,3},{7,4},{8,13},{9,14},{10,... | collective-permute-start | bytes 49160 | tf_op jit(solution)/shard_map/ppermute | solution.py:26
  228.5 0.6 copy-done.18
  229.8 0.4 copy-done.7
  230.3 1.2 fusion.6
  231.5 1.9 fusion.7
  233.4 2.4 collective-permute-start.28
  235.8 1.7 collective-permute-start.29
  237.5 0.6 copy-done.16
  238.1 0.7 multiply_subtract_fusion
  238.8 1.0 copy.35
  239.9 0.6 slice_bitcast_fusion
  (96 shorter events, 4.7 us)
Async XLA Ops:
  1.3 18.0 %collective-permute-start = (bf16[2,16,128]{2,1,0:T(8,128)(2,1)S(1)}, bf16[2,16,128]{2,1,0:T(8,128)(2,1)S(1)}, u32[]{:S(2)}, u32[]{:S(2)}) collective-permute-start(bf16[2,16,128]{2,1,0:T(8,128)(2,1)S(1)} %pad_maximum_fusion), channel_id=1, source_target_pairs={{0,1},{1,2},{2,3},{3,4},{4,5},{5,6},{6,7},{7,0},{8,9},{9,10},{10,1... | collective-permute-start | bytes 24584 | tf_op jit(solution)/shard_map/ppermute | solution.py:26
  3.2 18.9 %collective-permute-start.1 = (bf16[2,16,128]{2,1,0:T(8,128)(2,1)S(1)}, bf16[2,16,128]{2,1,0:T(8,128)(2,1)S(1)}, u32[]{:S(2)}, u32[]{:S(2)}) collective-permute-start(bf16[2,16,128]{2,1,0:T(8,128)(2,1)S(1)} %pad_maximum_fusion), channel_id=1, source_target_pairs={{0,2},{1,3},{2,4},{3,5},{4,6},{5,7},{6,0},{7,1},{8,10},{9,11},{10,... | collective-permute-start | bytes 24584 | tf_op jit(solution)/shard_map/ppermute | solution.py:26
  6.4 18.6 %collective-permute-start.2 = (bf16[2,16,128]{2,1,0:T(8,128)(2,1)S(1)}, bf16[2,16,128]{2,1,0:T(8,128)(2,1)S(1)}, u32[]{:S(2)}, u32[]{:S(2)}) collective-permute-start(bf16[2,16,128]{2,1,0:T(8,128)(2,1)S(1)} %pad_maximum_fusion), channel_id=1, source_target_pairs={{0,3},{1,4},{2,5},{3,6},{4,7},{5,0},{6,1},{7,2},{8,11},{9,12},{10,... | collective-permute-start | bytes 24584 | tf_op jit(solution)/shard_map/ppermute | solution.py:26
  9.9 15.1 %collective-permute-start.3 = (bf16[2,16,128]{2,1,0:T(8,128)(2,1)S(1)}, bf16[2,16,128]{2,1,0:T(8,128)(2,1)S(1)}, u32[]{:S(2)}, u32[]{:S(2)}) collective-permute-start(bf16[2,16,128]{2,1,0:T(8,128)(2,1)S(1)} %pad_maximum_fusion), channel_id=1, source_target_pairs={{0,4},{1,5},{2,6},{3,7},{4,0},{5,1},{6,2},{7,3},{8,12},{9,13},{10,... | collective-permute-start | bytes 24584 | tf_op jit(solution)/shard_map/ppermute | solution.py:26
  12.2 12.8 %collective-permute-start.4 = (bf16[2,16,128]{2,1,0:T(8,128)(2,1)S(1)}, bf16[2,16,128]{2,1,0:T(8,128)(2,1)S(1)}, u32[]{:S(2)}, u32[]{:S(2)}) collective-permute-start(bf16[2,16,128]{2,1,0:T(8,128)(2,1)S(1)} %pad_maximum_fusion), channel_id=1, source_target_pairs={{0,5},{1,6},{2,7},{3,0},{4,1},{5,2},{6,3},{7,4},{8,13},{9,14},{10,... | collective-permute-start | bytes 24584 | tf_op jit(solution)/shard_map/ppermute | solution.py:26
  16.2 0.7 copy-start.14
  17.1 1.4 copy-start
  17.8 0.7 copy-start.15
  18.9 70.0 %copy-start.5 = (f32[16,128]{1,0:T(8,128)}, f32[16,128]{1,0:T(8,128)S(1)}, u32[]{:S(2)}) copy-start(f32[16,128]{1,0:T(8,128)S(1)} %reduce_window_sum.30) | copy-start | bytes 24580
  19.2 7.1 %copy-start.3 = (f32[16,128]{1,0:T(8,128)}, f32[16,128]{1,0:T(8,128)S(1)}, u32[]{:S(2)}) copy-start(f32[16,128]{1,0:T(8,128)S(1)} %get-tuple-element.154) | copy-start | bytes 24580
  19.4 5.7 %collective-permute-start.5 = (bf16[2,16,128]{2,1,0:T(8,128)(2,1)S(1)}, bf16[2,16,128]{2,1,0:T(8,128)(2,1)S(1)}, u32[]{:S(2)}, u32[]{:S(2)}) collective-permute-start(bf16[2,16,128]{2,1,0:T(8,128)(2,1)S(1)} %pad_maximum_fusion), channel_id=1, source_target_pairs={{0,6},{1,7},{2,0},{3,1},{4,2},{5,3},{6,4},{7,5},{8,14},{9,15},{10,... | collective-permute-start | bytes 24584 | tf_op jit(solution)/shard_map/ppermute | solution.py:26
  22.1 3.4 %collective-permute-start.6 = (bf16[2,16,128]{2,1,0:T(8,128)(2,1)S(1)}, bf16[2,16,128]{2,1,0:T(8,128)(2,1)S(1)}, u32[]{:S(2)}, u32[]{:S(2)}) collective-permute-start(bf16[2,16,128]{2,1,0:T(8,128)(2,1)S(1)} %pad_maximum_fusion), channel_id=1, source_target_pairs={{0,7},{1,0},{2,1},{3,2},{4,3},{5,4},{6,5},{7,6},{8,15},{9,8},{10,9... | collective-permute-start | bytes 24584 | tf_op jit(solution)/shard_map/ppermute | solution.py:26
  23.7 1.1 copy-start.2
  27.1 24.0 %collective-permute-start.7 = (f32[16,64,128]{2,1,0:T(8,128)S(1)}, f32[16,64,128]{2,1,0:T(8,128)S(1)}, u32[]{:S(2)}, u32[]{:S(2)}) collective-permute-start(f32[16,64,128]{2,1,0:T(8,128)S(1)} %fusion.39), channel_id=1, source_target_pairs={{0,8},{8,16},{16,24},{24,32},{32,40},{40,48},{48,56},{56,64},{64,7... | collective-permute-start | bytes 1572872 | tf_op jit(solution)/shard_map/ppermute | solution.py:12
  30.6 20.4 %collective-permute-start.9 = (f32[16,64,128]{2,1,0:T(8,128)S(1)}, f32[16,64,128]{2,1,0:T(8,128)S(1)}, u32[]{:S(2)}, u32[]{:S(2)}) collective-permute-start(f32[16,64,128]{2,1,0:T(8,128)S(1)} %fusion.16), channel_id=1, source_target_pairs={{8,0},{16,8},{24,16},{32,24},{40,32},{48,40},{56,48},{64,56},{72,6... | collective-permute-start | bytes 1572872 | tf_op jit(solution)/shard_map/ppermute | solution.py:12
  40.1 10.9 %collective-permute-start.10 = (f32[16,1,1]{0,2,1:T(1,128)S(1)}, f32[16,1,1]{0,2,1:T(1,128)S(1)}, u32[]{:S(2)}, u32[]{:S(2)}) collective-permute-start(f32[16,1,1]{0,2,1:T(1,128)S(1)} %bitcast.157), channel_id=1, source_target_pairs={{8,0},{16,8},{24,16},{32,24},{40,32},{48,40},{56,48},{64,56},{72,6... | collective-permute-start | bytes 200 | tf_op jit(solution)/shard_map/ppermute | solution.py:12
  43.5 7.5 %collective-permute-start.8 = (f32[16,1,1]{0,2,1:T(1,128)S(1)}, f32[16,1,1]{0,2,1:T(1,128)S(1)}, u32[]{:S(2)}, u32[]{:S(2)}) collective-permute-start(f32[16,1,1]{0,2,1:T(1,128)S(1)} %bitcast.158), channel_id=1, source_target_pairs={{0,8},{8,16},{16,24},{24,32},{32,40},{40,48},{48,56},{56,64},{64,7... | collective-permute-start | bytes 200 | tf_op jit(solution)/shard_map/ppermute | solution.py:12
  51.2 22.2 %collective-permute-start.11 = (f32[16,64,128]{2,1,0:T(8,128)S(1)}, f32[16,64,128]{2,1,0:T(8,128)S(1)}, u32[]{:S(2)}, u32[]{:S(2)}) collective-permute-start(f32[16,64,128]{2,1,0:T(8,128)S(1)} %get-tuple-element.83), channel_id=1, source_target_pairs={{0,16},{8,24},{16,32},{24,40},{32,48},{40,56},{48,64},{56,72},{64,... | collective-permute-start | bytes 1572872 | tf_op jit(solution)/shard_map/ppermute | solution.py:12
  53.1 20.2 %collective-permute-start.13 = (f32[16,64,128]{2,1,0:T(8,128)S(1)}, f32[16,64,128]{2,1,0:T(8,128)S(1)}, u32[]{:S(2)}, u32[]{:S(2)}) collective-permute-start(f32[16,64,128]{2,1,0:T(8,128)S(1)} %get-tuple-element.85), channel_id=1, source_target_pairs={{16,0},{24,8},{32,16},{40,24},{48,32},{56,40},{64,48},{72,56},{80,... | collective-permute-start | bytes 1572872 | tf_op jit(solution)/shard_map/ppermute | solution.py:12
  59.5 10.1 %collective-permute-start.12 = (f32[16,1,1]{0,2,1:T(1,128)S(1)}, f32[16,1,1]{0,2,1:T(1,128)S(1)}, u32[]{:S(2)}, u32[]{:S(2)}) collective-permute-start(f32[16,1,1]{0,2,1:T(1,128)S(1)} %get-tuple-element.84), channel_id=1, source_target_pairs={{0,16},{8,24},{16,32},{24,40},{32,48},{40,56},{48,64},{56,72},{64,... | collective-permute-start | bytes 200 | tf_op jit(solution)/shard_map/ppermute | solution.py:12
  61.4 11.9 %collective-permute-start.14 = (f32[16,1,1]{0,2,1:T(1,128)S(1)}, f32[16,1,1]{0,2,1:T(1,128)S(1)}, u32[]{:S(2)}, u32[]{:S(2)}) collective-permute-start(f32[16,1,1]{0,2,1:T(1,128)S(1)} %get-tuple-element.86), channel_id=1, source_target_pairs={{16,0},{24,8},{32,16},{40,24},{48,32},{56,40},{64,48},{72,56},{80,... | collective-permute-start | bytes 200 | tf_op jit(solution)/shard_map/ppermute | solution.py:12
  73.9 60.0 %copy-start.17 = (f32[16,1,1]{0,2,1:T(1,128)}, f32[16,1,1]{0,2,1:T(1,128)S(1)}, u32[]{:S(2)}) copy-start(f32[16,1,1]{0,2,1:T(1,128)S(1)} %mul.292) | copy-start | bytes 196
  74.2 29.6 %collective-permute-start.17 = (f32[16,64,128]{2,1,0:T(8,128)S(1)}, f32[16,64,128]{2,1,0:T(8,128)S(1)}, u32[]{:S(2)}, u32[]{:S(2)}) collective-permute-start(f32[16,64,128]{2,1,0:T(8,128)S(1)} %multiply_add_fusion.5), channel_id=1, source_target_pairs={{0,32},{8,40},{16,48},{24,56},{32,64},{40,72},{48,80},{56,88},{64,... | collective-permute-start | bytes 1572872 | tf_op jit(solution)/shard_map/ppermute | solution.py:12
  78.5 51.5 %collective-permute-start.18 = (f32[16,64,128]{2,1,0:T(8,128)S(1)}, f32[16,64,128]{2,1,0:T(8,128)}, u32[]{:S(2)}, u32[]{:S(2)}) collective-permute-start(f32[16,64,128]{2,1,0:T(8,128)S(1)} %multiply_add_fusion.4), channel_id=1, source_target_pairs={{32,0},{40,8},{48,16},{56,24},{64,32},{72,40},{80,48},{88,56},{96,... | collective-permute-start | bytes 1572872 | tf_op jit(solution)/shard_map/ppermute | solution.py:12
  88.6 0.6 copy-start.11
  91.3 115.0 %collective-permute-start.20 = (f32[16,64,128]{2,1,0:T(8,128)S(1)}, f32[16,64,128]{2,1,0:T(8,128)S(1)}, u32[]{:S(2)}, u32[]{:S(2)}) collective-permute-start(f32[16,64,128]{2,1,0:T(8,128)S(1)} %multiply_add_fusion.4), channel_id=1, source_target_pairs={{8,0},{16,8},{24,16},{32,24},{40,32},{48,40},{56,48},{64,56},{72,6... | collective-permute-start | bytes 1572872 | tf_op jit(solution)/shard_map/ppermute | solution.py:12
  100.4 105.9 %collective-permute-start.15 = (f32[16,64,128]{2,1,0:T(8,128)S(1)}, f32[16,64,128]{2,1,0:T(8,128)S(1)}, u32[]{:S(2)}, u32[]{:S(2)}) collective-permute-start(f32[16,64,128]{2,1,0:T(8,128)S(1)} %multiply_add_fusion.5), channel_id=1, source_target_pairs={{0,8},{8,16},{16,24},{24,32},{32,40},{40,48},{48,56},{56,64},{64,7... | collective-permute-start | bytes 1572872 | tf_op jit(solution)/shard_map/ppermute | solution.py:12
  132.0 74.3 %collective-permute-start.22 = (f32[16,64,128]{2,1,0:T(8,128)}, f32[16,64,128]{2,1,0:T(8,128)}, u32[]{:S(2)}, u32[]{:S(2)}) collective-permute-start(f32[16,64,128]{2,1,0:T(8,128)} %multiply_add_fusion.2), channel_id=1, source_target_pairs={{40,0},{48,8},{56,16},{64,24},{72,32},{80,40},{88,48},{96,56},{104... | collective-permute-start | bytes 1572872 | tf_op jit(solution)/shard_map/ppermute | solution.py:12
  134.8 71.5 %collective-permute-start.19 = (f32[16,64,128]{2,1,0:T(8,128)}, f32[16,64,128]{2,1,0:T(8,128)}, u32[]{:S(2)}, u32[]{:S(2)}) collective-permute-start(f32[16,64,128]{2,1,0:T(8,128)} %multiply_add_fusion.3), channel_id=1, source_target_pairs={{0,40},{8,48},{16,56},{24,64},{32,72},{40,80},{48,88},{56,96},{64,... | collective-permute-start | bytes 1572872 | tf_op jit(solution)/shard_map/ppermute | solution.py:12
  143.2 0.8 copy-start.6
  143.2 0.8 copy-start.12
  145.4 52.1 %collective-permute-start.21 = (f32[16,1,1]{0,2,1:T(1,128)}, f32[16,1,1]{0,2,1:T(1,128)}, u32[]{:S(2)}, u32[]{:S(2)}) collective-permute-start(f32[16,1,1]{0,2,1:T(1,128)} %mul.298), channel_id=1, source_target_pairs={{8,0},{16,8},{24,16},{32,24},{40,32},{48,40},{56,48},{64,56},{72,6... | collective-permute-start | bytes 200 | tf_op jit(solution)/shard_map/ppermute | solution.py:12
  197.4 8.9 %collective-permute-start.16 = (f32[16,1,1]{0,2,1:T(1,128)}, f32[16,1,1]{0,2,1:T(1,128)}, u32[]{:S(2)}, u32[]{:S(2)}) collective-permute-start(f32[16,1,1]{0,2,1:T(1,128)} %copy-done.17), channel_id=1, source_target_pairs={{0,8},{8,16},{16,24},{24,32},{32,40},{40,48},{48,56},{56,64},{64,7... | collective-permute-start | bytes 200 | tf_op jit(solution)/shard_map/ppermute | solution.py:12
  207.8 0.7 copy-start.4
  208.6 1.0 copy-start.1
  210.6 22.7 %collective-permute-start.23 = (f32[2,16,128]{2,1,0:T(8,128)S(1)}, f32[2,16,128]{2,1,0:T(8,128)S(1)}, u32[]{:S(2)}, u32[]{:S(2)}) collective-permute-start(f32[2,16,128]{2,1,0:T(8,128)S(1)} %get-tuple-element.102), channel_id=1, source_target_pairs={{0,1},{1,2},{2,3},{3,4},{4,5},{5,6},{6,7},{7,0},{8,9},{9,10},{10,1... | collective-permute-start | bytes 49160 | tf_op jit(solution)/shard_map/ppermute | solution.py:26
  215.9 19.9 %collective-permute-start.24 = (f32[2,16,128]{2,1,0:T(8,128)S(1)}, f32[2,16,128]{2,1,0:T(8,128)S(1)}, u32[]{:S(2)}, u32[]{:S(2)}) collective-permute-start(f32[2,16,128]{2,1,0:T(8,128)S(1)} %get-tuple-element.103), channel_id=1, source_target_pairs={{0,2},{1,3},{2,4},{3,5},{4,6},{5,7},{6,0},{7,1},{8,10},{9,11},{10,... | collective-permute-start | bytes 49160 | tf_op jit(solution)/shard_map/ppermute | solution.py:26
  218.4 21.4 %collective-permute-start.25 = (f32[2,16,128]{2,1,0:T(8,128)S(1)}, f32[2,16,128]{2,1,0:T(8,128)S(1)}, u32[]{:S(2)}, u32[]{:S(2)}) collective-permute-start(f32[2,16,128]{2,1,0:T(8,128)S(1)} %get-tuple-element.104), channel_id=1, source_target_pairs={{0,3},{1,4},{2,5},{3,6},{4,7},{5,0},{6,1},{7,2},{8,11},{9,12},{10,... | collective-permute-start | bytes 49160 | tf_op jit(solution)/shard_map/ppermute | solution.py:26
  221.8 18.0 %collective-permute-start.26 = (f32[2,16,128]{2,1,0:T(8,128)S(1)}, f32[2,16,128]{2,1,0:T(8,128)S(1)}, u32[]{:S(2)}, u32[]{:S(2)}) collective-permute-start(f32[2,16,128]{2,1,0:T(8,128)S(1)} %get-tuple-element.105), channel_id=1, source_target_pairs={{0,4},{1,5},{2,6},{3,7},{4,0},{5,1},{6,2},{7,3},{8,12},{9,13},{10,... | collective-permute-start | bytes 49160 | tf_op jit(solution)/shard_map/ppermute | solution.py:26
  224.9 14.9 %collective-permute-start.27 = (f32[2,16,128]{2,1,0:T(8,128)S(1)}, f32[2,16,128]{2,1,0:T(8,128)S(1)}, u32[]{:S(2)}, u32[]{:S(2)}) collective-permute-start(f32[2,16,128]{2,1,0:T(8,128)S(1)} %get-tuple-element.106), channel_id=1, source_target_pairs={{0,5},{1,6},{2,7},{3,0},{4,1},{5,2},{6,3},{7,4},{8,13},{9,14},{10,... | collective-permute-start | bytes 49160 | tf_op jit(solution)/shard_map/ppermute | solution.py:26
  228.5 0.7 copy-start.18
  229.6 0.7 copy-start.7
  229.6 0.7 copy-start.13
  231.5 6.0 %copy-start.8 = (f32[16,128]{1,0:T(8,128)S(1)}, f32[16,128]{1,0:T(8,128)}, u32[]{:S(2)}) copy-start(f32[16,128]{1,0:T(8,128)} %get-tuple-element.132) | copy-start | bytes 24580
  231.5 6.0 %copy-start.9 = (f32[16,128]{1,0:T(8,128)S(1)}, f32[16,128]{1,0:T(8,128)}, u32[]{:S(2)}) copy-start(f32[16,128]{1,0:T(8,128)} %reduce_window_sum.31) | copy-start | bytes 24580
  231.5 6.0 %copy-start.10 = (f32[16,128]{1,0:T(8,128)S(1)}, f32[16,128]{1,0:T(8,128)}, u32[]{:S(2)}) copy-start(f32[16,128]{1,0:T(8,128)} %reduce_window_sum.32) | copy-start | bytes 24580
  233.4 6.4 %collective-permute-start.28 = (f32[2,16,128]{2,1,0:T(8,128)S(1)}, f32[2,16,128]{2,1,0:T(8,128)S(1)}, u32[]{:S(2)}, u32[]{:S(2)}) collective-permute-start(f32[2,16,128]{2,1,0:T(8,128)S(1)} %get-tuple-element.107), channel_id=1, source_target_pairs={{0,6},{1,7},{2,0},{3,1},{4,2},{5,3},{6,4},{7,5},{8,14},{9,15},{10,... | collective-permute-start | bytes 49160 | tf_op jit(solution)/shard_map/ppermute | solution.py:26
  235.8 4.0 %collective-permute-start.29 = (f32[2,16,128]{2,1,0:T(8,128)S(1)}, f32[2,16,128]{2,1,0:T(8,128)S(1)}, u32[]{:S(2)}, u32[]{:S(2)}) collective-permute-start(f32[2,16,128]{2,1,0:T(8,128)S(1)} %get-tuple-element.108), channel_id=1, source_target_pairs={{0,7},{1,0},{2,1},{3,2},{4,3},{5,4},{6,5},{7,6},{8,15},{9,8},{10,9... | collective-permute-start | bytes 49160 | tf_op jit(solution)/shard_map/ppermute | solution.py:26
  237.5 0.7 copy-start.16

commit v3 on v2

--- a/solution.py
+++ b/solution.py
@@ -12,11 +12,23 @@
     return lax.ppermute(x, axis, pairs)
 
 
+def pack(value):
+    top = jnp.max(jnp.abs(value), axis=-1, keepdims=True)
+    unit = jnp.where(top > 0, top, 1.0) / 32767.0
+    return jnp.round(value / unit).astype(jnp.int16), unit
+
+
+def unpack(packed):
+    code, unit = packed
+    return code.astype(jnp.float32) * unit
+
+
 def shift_pair(fwd, bwd, by):
-    fwd, bwd = lax.optimization_barrier((fwd, bwd))
-    return lax.optimization_barrier(
+    fwd, bwd = lax.optimization_barrier(((pack(fwd[0]), fwd[1]), (pack(bwd[0]), bwd[1])))
+    got_f, got_b = lax.optimization_barrier(
         (from_behind(fwd, "context", by), from_behind(bwd, "context", -by))
     )
+    return (unpack(got_f[0]), got_f[1]), (unpack(got_b[0]), got_b[1])
 
 
 def exchange(pieces, axis):
@@ -27,14 +39,6 @@
         for s in range(1, count)
     ]
     return [pieces[0]] + list(lax.optimization_barrier(got))
-
-
-def gather_rows(piece, axis):
-    count = lax.axis_size(axis)
-    me = lax.axis_index(axis)
-    got = jnp.stack(exchange([piece] * count, axis))
-    order = (me - jnp.arange(count)) % count
-    return jnp.take(got, order, axis=0)
 
 
 def scatter_sum(whole, axis):
@@ -56,9 +60,8 @@
     length = inputs.shape[0]
     heads = step_size.shape[0]
     width = inputs.shape[1] // heads
-    rows = gather_rows(jnp.stack([b_rows, c_rows]), "tensor")
-    b_bf = rows[:, 0].reshape(length, -1)
-    c_bf = rows[:, 1].reshape(length, -1)
+    rows = lax.all_gather(jnp.stack([b_rows, c_rows]), "tensor", axis=1, tiled=True)
+    b_bf, c_bf = rows[0], rows[1]
     bmat = b_bf.astype(jnp.float32)
     cmat = c_bf.astype(jnp.float32)
     xs = inputs.astype(jnp.float32).reshape(length, heads, width).transpose(1, 0, 2)
@@ -97,16 +100,19 @@
         bwd = (bwd[0] + bwd[1] * got_b[0], bwd[1] * got_b[1])
         span *= 2
     near_f, near_b = kept[low]
+    sends = lax.optimization_barrier(
+        ((pack(near_f[0]), near_f[1]), pack(fwd[0]), (pack(near_b[0]), near_b[1]), pack(bwd[0]))
+    )
     got = lax.optimization_barrier(
         (
-            from_behind(near_f, "context", 1),
-            from_behind(fwd[0], "context", low + 1),
-            from_behind(near_b, "context", -1),
-            from_behind(bwd[0], "context", -low - 1),
+            from_behind(sends[0], "context", 1),
+            from_behind(sends[1], "context", low + 1),
+            from_behind(sends[2], "context", -1),
+            from_behind(sends[3], "context", -low - 1),
         )
     )
-    s_in = got[0][0] + got[0][1] * got[1]
-    g_in = got[2][0] + got[2][1] * got[3]
+    s_in = unpack(got[0][0]) + got[0][1] * unpack(got[1])
+    g_in = unpack(got[2][0]) + got[2][1] * unpack(got[3])
 
     index = jnp.arange(length)
     keep = (index[:, None] >= index[None, :]) & (seg[:, None] == seg[None, :])

time: 242 us -> 246 us (1.017)
  the two profiles are of different devices: /device:TPU:3 before, /device:TPU:7 now
where the time goes in v3:
time: 246 us; the launch traced here: 244 us
  starting transfers between devices  127 us (52%)
  waiting for transfers between devices  64 us (26%)
  other arithmetic  15.5 us (6%)
  matrix products  14.9 us (6%)
  blocking collectives  13.8 us (6%)
  local copies, waits for them, and re-layouts  7.65 us (3%)
    ppermute x26, starting transfers between devices, from_behind(): return lax.ppermute(x, axis, pairs)  108 us
    ppermute x26, waiting for transfers between devices, from_behind(): return lax.ppermute(x, axis, pairs)  63.3 us
    ppermute x7, starting transfers between devices, exchange(): lax.ppermute(pieces[s], axis, [(i, (i + s) % count) for i in range(count)])  18.5 us
    all_gather x1, blocking collectives, local(): lax.all_gather(jnp.stack([b_rows, c_rows]), 'tensor', axis=1, tiled=True)  13.8 us
    unnamed x42, local copies, waits for them, and re-layouts  5.18 us
  transfers between devices with their start and end apart: 33, of which 9 were waited for; matrix products, arithmetic and copies ran while one was open for 6% of the time, Pallas kernels for 0%

profile of v3, /device:TPU:7, one launch (start us, length us, event | category | flops | bytes accessed | tf_op | source)
XLA Modules:
  0.0 244.1 jit_solution(14137068387769241198)
XLA Ops:
  0.6 0.8 copy.30
  1.6 0.7 broadcast_compare_fusion
  3.0 0.6 compare_convert_fusion.1
  3.7 0.8 negate_multiply_fusion
  4.9 0.7 pad_maximum_fusion
  5.6 13.8 %all_gather.3 = bf16[2,128,128]{2,1,0:T(8,128)(2,1)S(1)} all-gather(bf16[2,16,128]{2,1,0:T(8,128)(2,1)S(1)} %pad_maximum_fusion), channel_id=1, replica_groups=mesh['context'=64,'tensor'=8] {'tensor'}, dimensions={1}, use_global_device_ids=true | all-gather | bytes 73728 | tf_op jit(solution)/shard_map/all_gather | solution.py:63
  19.5 0.8 copy-done.1
  22.7 3.5 %collective-permute-start = (s16[16,64,128]{2,1,0:T(8,128)(2,1)S(1)}, s16[16,64,128]{2,1,0:T(8,128)(2,1)S(1)}, u32[]{:S(2)}, u32[]{:S(2)}) collective-permute-start(s16[16,64,128]{2,1,0:T(8,128)(2,1)S(1)} %get-tuple-element.71), channel_id=1, source_target_pairs={{0,8},{8,16},{16,24},{24,32},{32,40},{40,48},{48,56},{56,64},{64,7... | collective-permute-start | bytes 786440 | tf_op jit(solution)/shard_map/ppermute | solution.py:12
  26.3 9.8 %collective-permute-start.3 = (s16[16,64,128]{2,1,0:T(8,128)(2,1)S(1)}, s16[16,64,128]{2,1,0:T(8,128)(2,1)S(1)}, u32[]{:S(2)}, u32[]{:S(2)}) collective-permute-start(s16[16,64,128]{2,1,0:T(8,128)(2,1)S(1)} %get-tuple-element.74), channel_id=1, source_target_pairs={{8,0},{16,8},{24,16},{32,24},{40,32},{48,40},{56,48},{64,56},{72,6... | collective-permute-start | bytes 786440 | tf_op jit(solution)/shard_map/ppermute | solution.py:12
  36.1 1.9 collective-permute-start.1
  38.0 5.5 %collective-permute-start.4 = (f32[16,64,1]{1,0,2:T(8,128)S(1)}, f32[16,64,1]{1,0,2:T(8,128)S(1)}, u32[]{:S(2)}, u32[]{:S(2)}) collective-permute-start(f32[16,64,1]{1,0,2:T(8,128)S(1)} %get-tuple-element.75), channel_id=1, source_target_pairs={{8,0},{16,8},{24,16},{32,24},{40,32},{48,40},{56,48},{64,56},{72,6... | collective-permute-start | bytes 12296 | tf_op jit(solution)/shard_map/ppermute | solution.py:12
  43.5 1.9 collective-permute-start.2
  45.4 4.5 %collective-permute-done.2 = f32[16,1,1]{0,2,1:T(1,128)S(1)} collective-permute-done((f32[16,1,1]{0,2,1:T(1,128)S(1)}, f32[16,1,1]{0,2,1:T(1,128)S(1)}, u32[]{:S(2)}, u32[]{:S(2)}) %collective-permute-start.2) | collective-permute-done | bytes 96 | tf_op jit(solution)/shard_map/ppermute | solution.py:12
  49.9 1.9 collective-permute-start.5
  51.8 2.4 collective-permute-done.5
  54.2 0.7 abs_reduce_fusion.4
  54.9 0.8 round-nearest-even_convert_fusion.4
  55.7 1.9 collective-permute-start.6
  57.6 6.4 %collective-permute-start.9 = (s16[16,64,128]{2,1,0:T(8,128)(2,1)S(1)}, s16[16,64,128]{2,1,0:T(8,128)(2,1)S(1)}, u32[]{:S(2)}, u32[]{:S(2)}) collective-permute-start(s16[16,64,128]{2,1,0:T(8,128)(2,1)S(1)} %get-tuple-element.86), channel_id=1, source_target_pairs={{16,0},{24,8},{32,16},{40,24},{48,32},{56,40},{64,48},{72,56},{80,... | collective-permute-start | bytes 786440 | tf_op jit(solution)/shard_map/ppermute | solution.py:12
  64.0 1.9 collective-permute-start.10
  65.9 4.3 %collective-permute-start.7 = (f32[16,64,1]{1,0,2:T(8,128)S(1)}, f32[16,64,1]{1,0,2:T(8,128)S(1)}, u32[]{:S(2)}, u32[]{:S(2)}) collective-permute-start(f32[16,64,1]{1,0,2:T(8,128)S(1)} %fusion.93), channel_id=1, source_target_pairs={{0,16},{8,24},{16,32},{24,40},{32,48},{40,56},{48,64},{56,72},{64,... | collective-permute-start | bytes 12296 | tf_op jit(solution)/shard_map/ppermute | solution.py:12
  70.2 4.0 %collective-permute-start.11 = (f32[16,1,1]{0,2,1:T(1,128)S(1)}, f32[16,1,1]{0,2,1:T(1,128)S(1)}, u32[]{:S(2)}, u32[]{:S(2)}) collective-permute-start(f32[16,1,1]{0,2,1:T(1,128)S(1)} %get-tuple-element.88), channel_id=1, source_target_pairs={{16,0},{24,8},{32,16},{40,24},{48,32},{56,40},{64,48},{72,56},{80,... | collective-permute-start | bytes 200 | tf_op jit(solution)/shard_map/ppermute | solution.py:12
  74.2 1.1 collective-permute-done.11
  75.4 3.1 %collective-permute-start.8 = (f32[16,1,1]{0,2,1:T(1,128)S(1)}, f32[16,1,1]{0,2,1:T(1,128)S(1)}, u32[]{:S(2)}, u32[]{:S(2)}) collective-permute-start(f32[16,1,1]{0,2,1:T(1,128)S(1)} %get-tuple-element.85), channel_id=1, source_target_pairs={{0,16},{8,24},{16,32},{24,40},{32,48},{40,56},{48,64},{56,72},{64,... | collective-permute-start | bytes 200 | tf_op jit(solution)/shard_map/ppermute | solution.py:12
  78.5 4.3 %collective-permute-done.8 = f32[16,1,1]{0,2,1:T(1,128)S(1)} collective-permute-done((f32[16,1,1]{0,2,1:T(1,128)S(1)}, f32[16,1,1]{0,2,1:T(1,128)S(1)}, u32[]{:S(2)}, u32[]{:S(2)}) %collective-permute-start.8) | collective-permute-done | bytes 96 | tf_op jit(solution)/shard_map/ppermute | solution.py:12
  82.8 1.2 abs_reduce_fusion.2
  85.1 2.1 collective-permute-start.12
  87.2 8.0 %collective-permute-start.14 = (s16[16,64,128]{2,1,0:T(8,128)(2,1)S(1)}, s16[16,64,128]{2,1,0:T(8,128)(2,1)S(1)}, u32[]{:S(2)}, u32[]{:S(2)}) collective-permute-start(s16[16,64,128]{2,1,0:T(8,128)(2,1)S(1)} %round-nearest-even_convert_fusion.2), channel_id=1, source_target_pairs={{32,0},{40,8},{48,16},{56,24},{64,32},{72,40},{80,48},{88,56},{96,... | collective-permute-start | bytes 786440 | tf_op jit(solution)/shard_map/ppermute | solution.py:12
  95.2 1.9 collective-permute-start.13
  97.1 8.2 %collective-permute-start.15 = (f32[16,64,1]{1,0,2:T(8,128)}, f32[16,64,1]{1,0,2:T(8,128)S(1)}, u32[]{:S(2)}, u32[]{:S(2)}) collective-permute-start(f32[16,64,1]{1,0,2:T(8,128)} %fusion.99), channel_id=1, source_target_pairs={{32,0},{40,8},{48,16},{56,24},{64,32},{72,40},{80,48},{88,56},{96,... | collective-permute-start | bytes 12296 | tf_op jit(solution)/shard_map/ppermute | solution.py:12
  105.4 11.9 %collective-permute-done.15 = f32[16,64,1]{1,0,2:T(8,128)S(1)} collective-permute-done((f32[16,64,1]{1,0,2:T(8,128)}, f32[16,64,1]{1,0,2:T(8,128)S(1)}, u32[]{:S(2)}, u32[]{:S(2)}) %collective-permute-start.15) | collective-permute-done | bytes 4128 | tf_op jit(solution)/shard_map/ppermute | solution.py:12
  119.6 1.9 collective-permute-start.17
  121.6 1.9 collective-permute-start.16
  123.6 3.7 %collective-permute-start.19 = (s16[16,64,128]{2,1,0:T(8,128)(2,1)S(1)}, s16[16,64,128]{2,1,0:T(8,128)(2,1)S(1)}, u32[]{:S(2)}, u32[]{:S(2)}) collective-permute-start(s16[16,64,128]{2,1,0:T(8,128)(2,1)S(1)} %round-nearest-even_convert_fusion.1), channel_id=1, source_target_pairs={{0,40},{8,48},{16,56},{24,64},{32,72},{40,80},{48,88},{56,96},{64,... | collective-permute-start | bytes 786440 | tf_op jit(solution)/shard_map/ppermute | solution.py:12
  127.3 5.3 %collective-permute-start.18 = (f32[16,1,1]{0,2,1:T(1,128)S(1)}, f32[16,1,1]{0,2,1:T(1,128)S(1)}, u32[]{:S(2)}, u32[]{:S(2)}) collective-permute-start(f32[16,1,1]{0,2,1:T(1,128)S(1)} %mul.401), channel_id=1, source_target_pairs={{0,8},{8,16},{16,24},{24,32},{32,40},{40,48},{48,56},{56,64},{64,7... | collective-permute-start | bytes 200 | tf_op jit(solution)/shard_map/ppermute | solution.py:12
  132.5 4.1 %collective-permute-start.23 = (f32[16,1,1]{0,2,1:T(1,128)S(1)}, f32[16,1,1]{0,2,1:T(1,128)}, u32[]{:S(2)}, u32[]{:S(2)}) collective-permute-start(f32[16,1,1]{0,2,1:T(1,128)S(1)} %mul.410), channel_id=1, source_target_pairs={{8,0},{16,8},{24,16},{32,24},{40,32},{48,40},{56,48},{64,56},{72,6... | collective-permute-start | bytes 200 | tf_op jit(solution)/shard_map/ppermute | solution.py:12
  136.6 24.9 %collective-permute-done.18 = f32[16,1,1]{0,2,1:T(1,128)S(1)} collective-permute-done((f32[16,1,1]{0,2,1:T(1,128)S(1)}, f32[16,1,1]{0,2,1:T(1,128)S(1)}, u32[]{:S(2)}, u32[]{:S(2)}) %collective-permute-start.18) | collective-permute-done | bytes 96 | tf_op jit(solution)/shard_map/ppermute | solution.py:12
  161.5 1.9 collective-permute-start.21
  163.4 6.3 %collective-permute-start.24 = (s16[16,64,128]{2,1,0:T(8,128)(2,1)S(1)}, s16[16,64,128]{2,1,0:T(8,128)(2,1)S(1)}, u32[]{:S(2)}, u32[]{:S(2)}) collective-permute-start(s16[16,64,128]{2,1,0:T(8,128)(2,1)S(1)} %round-nearest-even_convert_fusion), channel_id=1, source_target_pairs={{40,0},{48,8},{56,16},{64,24},{72,32},{80,40},{88,48},{96,56},{104... | collective-permute-start | bytes 786440 | tf_op jit(solution)/shard_map/ppermute | solution.py:12
  169.7 3.8 %collective-permute-start.20 = (f32[16,64,1]{1,0,2:T(8,128)S(1)}, f32[16,64,1]{1,0,2:T(8,128)S(1)}, u32[]{:S(2)}, u32[]{:S(2)}) collective-permute-start(f32[16,64,1]{1,0,2:T(8,128)S(1)} %fusion.101), channel_id=1, source_target_pairs={{0,40},{8,48},{16,56},{24,64},{32,72},{40,80},{48,88},{56,96},{64,... | collective-permute-start | bytes 12296 | tf_op jit(solution)/shard_map/ppermute | solution.py:12
  173.5 1.3 fusion.8
  174.9 6.2 %collective-permute-done.20 = f32[16,64,1]{1,0,2:T(8,128)S(1)} collective-permute-done((f32[16,64,1]{1,0,2:T(8,128)S(1)}, f32[16,64,1]{1,0,2:T(8,128)S(1)}, u32[]{:S(2)}, u32[]{:S(2)}) %collective-permute-start.20) | collective-permute-done | bytes 4128 | tf_op jit(solution)/shard_map/ppermute | solution.py:12
  181.6 1.9 collective-permute-start.22
  183.6 2.9 %fusion.10 = (f32[16,128]{1,0:T(8,128)}, f32[16,128]{1,0:T(8,128)}, f32[128,128]{0,1:T(8,128)S(1)}) fusion(f32[128,128]{0,1:T(8,128)S(1)} %fusion.68, f32[16,128]{1,0:T(8,128)} %copy-done.5, pred[128,128]{0,1:T(8,128)(4,1)S(1)} %fusion.62, bf16[16,128,64]{1,2,0:T(8,128)(2,1)S(1)} %bitcast.149, f32[16,128,64]{1,2,0:T(8,128)S(1)} %bitcast.145, ...), kind=kOutput, calls=%fused_computation.17 | convolution fusion | flops 203534336 | bytes 966656 | tf_op jit(solution)/shard_map/hip,hjp->hij/dot_general | solution.py:123
  186.4 8.0 %collective-permute-done.22 = f32[16,64,1]{1,0,2:T(8,128)} collective-permute-done((f32[16,64,1]{1,0,2:T(8,128)}, f32[16,64,1]{1,0,2:T(8,128)}, u32[]{:S(2)}, u32[]{:S(2)}) %collective-permute-start.22) | collective-permute-done | bytes 4128 | tf_op jit(solution)/shard_map/ppermute | solution.py:12
  194.5 11.2 %collective-permute-start.25 = (f32[16,64,1]{1,0,2:T(8,128)}, f32[16,64,1]{1,0,2:T(8,128)}, u32[]{:S(2)}, u32[]{:S(2)}) collective-permute-start(f32[16,64,1]{1,0,2:T(8,128)} %fusion.103), channel_id=1, source_target_pairs={{40,0},{48,8},{56,16},{64,24},{72,32},{80,40},{88,48},{96,56},{104... | collective-permute-start | bytes 12296 | tf_op jit(solution)/shard_map/ppermute | solution.py:12
  205.7 1.6 reduce_window_sum.32
  207.3 1.6 reduce_window_sum.31
  209.5 2.1 convolution_bitcast_fusion.2
  212.5 2.0 convolution_bitcast_fusion.3
  214.8 2.7 %collective-permute-start.26 = (f32[2,16,128]{2,1,0:T(8,128)S(1)}, f32[2,16,128]{2,1,0:T(8,128)S(1)}, u32[]{:S(2)}, u32[]{:S(2)}) collective-permute-start(f32[2,16,128]{2,1,0:T(8,128)S(1)} %get-tuple-element.124), channel_id=1, source_target_pairs={{0,1},{1,2},{2,3},{3,4},{4,5},{5,6},{6,7},{7,0},{8,9},{9,10},{10,1... | collective-permute-start | bytes 49160 | tf_op jit(solution)/shard_map/ppermute | solution.py:38
  217.5 1.9 collective-permute-start.27
  219.4 4.6 %collective-permute-start.28 = (f32[2,16,128]{2,1,0:T(8,128)S(1)}, f32[2,16,128]{2,1,0:T(8,128)S(1)}, u32[]{:S(2)}, u32[]{:S(2)}) collective-permute-start(f32[2,16,128]{2,1,0:T(8,128)S(1)} %get-tuple-element.126), channel_id=1, source_target_pairs={{0,3},{1,4},{2,5},{3,6},{4,7},{5,0},{6,1},{7,2},{8,11},{9,12},{10,... | collective-permute-start | bytes 49160 | tf_op jit(solution)/shard_map/ppermute | solution.py:38
  224.0 2.5 %collective-permute-start.29 = (f32[2,16,128]{2,1,0:T(8,128)S(1)}, f32[2,16,128]{2,1,0:T(8,128)S(1)}, u32[]{:S(2)}, u32[]{:S(2)}) collective-permute-start(f32[2,16,128]{2,1,0:T(8,128)S(1)} %get-tuple-element.127), channel_id=1, source_target_pairs={{0,4},{1,5},{2,6},{3,7},{4,0},{5,1},{6,2},{7,3},{8,12},{9,13},{10,... | collective-permute-start | bytes 49160 | tf_op jit(solution)/shard_map/ppermute | solution.py:38
  226.5 4.2 %collective-permute-start.30 = (f32[2,16,128]{2,1,0:T(8,128)S(1)}, f32[2,16,128]{2,1,0:T(8,128)S(1)}, u32[]{:S(2)}, u32[]{:S(2)}) collective-permute-start(f32[2,16,128]{2,1,0:T(8,128)S(1)} %get-tuple-element.128), channel_id=1, source_target_pairs={{0,5},{1,6},{2,7},{3,0},{4,1},{5,2},{6,3},{7,4},{8,13},{9,14},{10,... | collective-permute-start | bytes 49160 | tf_op jit(solution)/shard_map/ppermute | solution.py:38
  230.7 1.9 fusion.5
  232.6 0.7 copy-done.17
  233.3 1.3 fusion.16
  234.8 1.2 fusion.4
  236.1 1.6 multiply_reduce_fusion.1
  237.7 2.2 collective-permute-start.31
  241.1 0.7 multiply_subtract_fusion
  241.7 1.0 copy.35
  242.8 0.7 collective-permute-done.32
  (111 shorter events, 11.7 us)
Async XLA Ops:
  0.6 18.7 %copy-start = (bf16[128,1024]{1,0:T(8,128)(2,1)S(1)}, bf16[128,1024]{1,0:T(8,128)(2,1)}, u32[]{:S(2)}) copy-start(bf16[128,1024]{1,0:T(8,128)(2,1)} %param.8) | copy-start | bytes 786436
  4.7 168.8 %copy-start.5 = (f32[16,128]{1,0:T(8,128)}, f32[16,128]{1,0:T(8,128)S(1)}, u32[]{:S(2)}) copy-start(f32[16,128]{1,0:T(8,128)S(1)} %reduce_window_sum.30) | copy-start | bytes 24580
  19.4 1.0 copy-start.1
  20.5 0.7 copy-start.2
  20.6 1.6 copy-start.3
  22.7 31.4 %collective-permute-start = (s16[16,64,128]{2,1,0:T(8,128)(2,1)S(1)}, s16[16,64,128]{2,1,0:T(8,128)(2,1)S(1)}, u32[]{:S(2)}, u32[]{:S(2)}) collective-permute-start(s16[16,64,128]{2,1,0:T(8,128)(2,1)S(1)} %get-tuple-element.71), channel_id=1, source_target_pairs={{0,8},{8,16},{16,24},{24,32},{32,40},{40,48},{48,56},{56,64},{64,7... | collective-permute-start | bytes 786440 | tf_op jit(solution)/shard_map/ppermute | solution.py:12
  26.3 27.9 %collective-permute-start.3 = (s16[16,64,128]{2,1,0:T(8,128)(2,1)S(1)}, s16[16,64,128]{2,1,0:T(8,128)(2,1)S(1)}, u32[]{:S(2)}, u32[]{:S(2)}) collective-permute-start(s16[16,64,128]{2,1,0:T(8,128)(2,1)S(1)} %get-tuple-element.74), channel_id=1, source_target_pairs={{8,0},{16,8},{24,16},{32,24},{40,32},{48,40},{56,48},{64,56},{72,6... | collective-permute-start | bytes 786440 | tf_op jit(solution)/shard_map/ppermute | solution.py:12
  36.1 18.1 %collective-permute-start.1 = (f32[16,64,1]{1,0,2:T(8,128)S(1)}, f32[16,64,1]{1,0,2:T(8,128)S(1)}, u32[]{:S(2)}, u32[]{:S(2)}) collective-permute-start(f32[16,64,1]{1,0,2:T(8,128)S(1)} %get-tuple-element.72), channel_id=1, source_target_pairs={{0,8},{8,16},{16,24},{24,32},{32,40},{40,48},{48,56},{56,64},{64,7... | collective-permute-start | bytes 12296 | tf_op jit(solution)/shard_map/ppermute | solution.py:12
  38.0 16.2 %collective-permute-start.4 = (f32[16,64,1]{1,0,2:T(8,128)S(1)}, f32[16,64,1]{1,0,2:T(8,128)S(1)}, u32[]{:S(2)}, u32[]{:S(2)}) collective-permute-start(f32[16,64,1]{1,0,2:T(8,128)S(1)} %get-tuple-element.75), channel_id=1, source_target_pairs={{8,0},{16,8},{24,16},{32,24},{40,32},{48,40},{56,48},{64,56},{72,6... | collective-permute-start | bytes 12296 | tf_op jit(solution)/shard_map/ppermute | solution.py:12
  43.5 6.4 %collective-permute-start.2 = (f32[16,1,1]{0,2,1:T(1,128)S(1)}, f32[16,1,1]{0,2,1:T(1,128)S(1)}, u32[]{:S(2)}, u32[]{:S(2)}) collective-permute-start(f32[16,1,1]{0,2,1:T(1,128)S(1)} %bitcast.165), channel_id=1, source_target_pairs={{0,8},{8,16},{16,24},{24,32},{32,40},{40,48},{48,56},{56,64},{64,7... | collective-permute-start | bytes 200 | tf_op jit(solution)/shard_map/ppermute | solution.py:12
  49.9 4.3 %collective-permute-start.5 = (f32[16,1,1]{0,2,1:T(1,128)S(1)}, f32[16,1,1]{0,2,1:T(1,128)S(1)}, u32[]{:S(2)}, u32[]{:S(2)}) collective-permute-start(f32[16,1,1]{0,2,1:T(1,128)S(1)} %bitcast.166), channel_id=1, source_target_pairs={{8,0},{16,8},{24,16},{32,24},{40,32},{48,40},{56,48},{64,56},{72,6... | collective-permute-start | bytes 200 | tf_op jit(solution)/shard_map/ppermute | solution.py:12
  55.7 27.2 %collective-permute-start.6 = (s16[16,64,128]{2,1,0:T(8,128)(2,1)S(1)}, s16[16,64,128]{2,1,0:T(8,128)(2,1)S(1)}, u32[]{:S(2)}, u32[]{:S(2)}) collective-permute-start(s16[16,64,128]{2,1,0:T(8,128)(2,1)S(1)} %get-tuple-element.83), channel_id=1, source_target_pairs={{0,16},{8,24},{16,32},{24,40},{32,48},{40,56},{48,64},{56,72},{64,... | collective-permute-start | bytes 786440 | tf_op jit(solution)/shard_map/ppermute | solution.py:12
  57.6 25.2 %collective-permute-start.9 = (s16[16,64,128]{2,1,0:T(8,128)(2,1)S(1)}, s16[16,64,128]{2,1,0:T(8,128)(2,1)S(1)}, u32[]{:S(2)}, u32[]{:S(2)}) collective-permute-start(s16[16,64,128]{2,1,0:T(8,128)(2,1)S(1)} %get-tuple-element.86), channel_id=1, source_target_pairs={{16,0},{24,8},{32,16},{40,24},{48,32},{56,40},{64,48},{72,56},{80,... | collective-permute-start | bytes 786440 | tf_op jit(solution)/shard_map/ppermute | solution.py:12
  64.0 18.8 %collective-permute-start.10 = (f32[16,64,1]{1,0,2:T(8,128)S(1)}, f32[16,64,1]{1,0,2:T(8,128)S(1)}, u32[]{:S(2)}, u32[]{:S(2)}) collective-permute-start(f32[16,64,1]{1,0,2:T(8,128)S(1)} %fusion.95), channel_id=1, source_target_pairs={{16,0},{24,8},{32,16},{40,24},{48,32},{56,40},{64,48},{72,56},{80,... | collective-permute-start | bytes 12296 | tf_op jit(solution)/shard_map/ppermute | solution.py:12
  65.9 16.9 %collective-permute-start.7 = (f32[16,64,1]{1,0,2:T(8,128)S(1)}, f32[16,64,1]{1,0,2:T(8,128)S(1)}, u32[]{:S(2)}, u32[]{:S(2)}) collective-permute-start(f32[16,64,1]{1,0,2:T(8,128)S(1)} %fusion.93), channel_id=1, source_target_pairs={{0,16},{8,24},{16,32},{24,40},{32,48},{40,56},{48,64},{56,72},{64,... | collective-permute-start | bytes 12296 | tf_op jit(solution)/shard_map/ppermute | solution.py:12
  70.2 5.2 %collective-permute-start.11 = (f32[16,1,1]{0,2,1:T(1,128)S(1)}, f32[16,1,1]{0,2,1:T(1,128)S(1)}, u32[]{:S(2)}, u32[]{:S(2)}) collective-permute-start(f32[16,1,1]{0,2,1:T(1,128)S(1)} %get-tuple-element.88), channel_id=1, source_target_pairs={{16,0},{24,8},{32,16},{40,24},{48,32},{56,40},{64,48},{72,56},{80,... | collective-permute-start | bytes 200 | tf_op jit(solution)/shard_map/ppermute | solution.py:12
  75.4 7.5 %collective-permute-start.8 = (f32[16,1,1]{0,2,1:T(1,128)S(1)}, f32[16,1,1]{0,2,1:T(1,128)S(1)}, u32[]{:S(2)}, u32[]{:S(2)}) collective-permute-start(f32[16,1,1]{0,2,1:T(1,128)S(1)} %get-tuple-element.85), channel_id=1, source_target_pairs={{0,16},{8,24},{16,32},{24,40},{32,48},{40,56},{48,64},{56,72},{64,... | collective-permute-start | bytes 200 | tf_op jit(solution)/shard_map/ppermute | solution.py:12
  85.1 32.3 %collective-permute-start.12 = (s16[16,64,128]{2,1,0:T(8,128)(2,1)S(1)}, s16[16,64,128]{2,1,0:T(8,128)(2,1)S(1)}, u32[]{:S(2)}, u32[]{:S(2)}) collective-permute-start(s16[16,64,128]{2,1,0:T(8,128)(2,1)S(1)} %round-nearest-even_convert_fusion.3), channel_id=1, source_target_pairs={{0,32},{8,40},{16,48},{24,56},{32,64},{40,72},{48,80},{56,88},{64,... | collective-permute-start | bytes 786440 | tf_op jit(solution)/shard_map/ppermute | solution.py:12
  87.2 30.1 %collective-permute-start.14 = (s16[16,64,128]{2,1,0:T(8,128)(2,1)S(1)}, s16[16,64,128]{2,1,0:T(8,128)(2,1)S(1)}, u32[]{:S(2)}, u32[]{:S(2)}) collective-permute-start(s16[16,64,128]{2,1,0:T(8,128)(2,1)S(1)} %round-nearest-even_convert_fusion.2), channel_id=1, source_target_pairs={{32,0},{40,8},{48,16},{56,24},{64,32},{72,40},{80,48},{88,56},{96,... | collective-permute-start | bytes 786440 | tf_op jit(solution)/shard_map/ppermute | solution.py:12
  95.2 10.2 %collective-permute-start.13 = (f32[16,64,1]{1,0,2:T(8,128)S(1)}, f32[16,64,1]{1,0,2:T(8,128)S(1)}, u32[]{:S(2)}, u32[]{:S(2)}) collective-permute-start(f32[16,64,1]{1,0,2:T(8,128)S(1)} %fusion.97), channel_id=1, source_target_pairs={{0,32},{8,40},{16,48},{24,56},{32,64},{40,72},{48,80},{56,88},{64,... | collective-permute-start | bytes 12296 | tf_op jit(solution)/shard_map/ppermute | solution.py:12
  97.1 20.2 %collective-permute-start.15 = (f32[16,64,1]{1,0,2:T(8,128)}, f32[16,64,1]{1,0,2:T(8,128)S(1)}, u32[]{:S(2)}, u32[]{:S(2)}) collective-permute-start(f32[16,64,1]{1,0,2:T(8,128)} %fusion.99), channel_id=1, source_target_pairs={{32,0},{40,8},{48,16},{56,24},{64,32},{72,40},{80,48},{88,56},{96,... | collective-permute-start | bytes 12296 | tf_op jit(solution)/shard_map/ppermute | solution.py:12
  119.6 50.1 %collective-permute-start.17 = (f32[16,64,1]{1,0,2:T(8,128)S(1)}, f32[16,64,1]{1,0,2:T(8,128)S(1)}, u32[]{:S(2)}, u32[]{:S(2)}) collective-permute-start(f32[16,64,1]{1,0,2:T(8,128)S(1)} %fusion.97), channel_id=1, source_target_pairs={{0,8},{8,16},{16,24},{24,32},{32,40},{40,48},{48,56},{56,64},{64,7... | collective-permute-start | bytes 12296 | tf_op jit(solution)/shard_map/ppermute | solution.py:12
  121.6 61.9 %copy-start.10 = (pred[128,128]{0,1:T(8,128)(4,1)}, pred[128,128]{0,1:T(8,128)(4,1)S(1)}, u32[]{:S(2)}) copy-start(pred[128,128]{0,1:T(8,128)(4,1)S(1)} %fusion.62) | copy-start | bytes 49156
  121.6 87.2 %collective-permute-start.16 = (s16[16,64,128]{2,1,0:T(8,128)(2,1)S(1)}, s16[16,64,128]{2,1,0:T(8,128)(2,1)S(1)}, u32[]{:S(2)}, u32[]{:S(2)}) collective-permute-start(s16[16,64,128]{2,1,0:T(8,128)(2,1)S(1)} %round-nearest-even_convert_fusion.3), channel_id=1, source_target_pairs={{0,8},{8,16},{16,24},{24,32},{32,40},{40,48},{48,56},{56,64},{64,7... | collective-permute-start | bytes 786440 | tf_op jit(solution)/shard_map/ppermute | solution.py:12
  123.6 85.3 %collective-permute-start.19 = (s16[16,64,128]{2,1,0:T(8,128)(2,1)S(1)}, s16[16,64,128]{2,1,0:T(8,128)(2,1)S(1)}, u32[]{:S(2)}, u32[]{:S(2)}) collective-permute-start(s16[16,64,128]{2,1,0:T(8,128)(2,1)S(1)} %round-nearest-even_convert_fusion.1), channel_id=1, source_target_pairs={{0,40},{8,48},{16,56},{24,64},{32,72},{40,80},{48,88},{56,96},{64,... | collective-permute-start | bytes 786440 | tf_op jit(solution)/shard_map/ppermute | solution.py:12
  127.3 34.2 %collective-permute-start.18 = (f32[16,1,1]{0,2,1:T(1,128)S(1)}, f32[16,1,1]{0,2,1:T(1,128)S(1)}, u32[]{:S(2)}, u32[]{:S(2)}) collective-permute-start(f32[16,1,1]{0,2,1:T(1,128)S(1)} %mul.401), channel_id=1, source_target_pairs={{0,8},{8,16},{16,24},{24,32},{32,40},{40,48},{48,56},{56,64},{64,7... | collective-permute-start | bytes 200 | tf_op jit(solution)/shard_map/ppermute | solution.py:12
  132.5 30.9 %collective-permute-start.23 = (f32[16,1,1]{0,2,1:T(1,128)S(1)}, f32[16,1,1]{0,2,1:T(1,128)}, u32[]{:S(2)}, u32[]{:S(2)}) collective-permute-start(f32[16,1,1]{0,2,1:T(1,128)S(1)} %mul.410), channel_id=1, source_target_pairs={{8,0},{16,8},{24,16},{32,24},{40,32},{48,40},{56,48},{64,56},{72,6... | collective-permute-start | bytes 200 | tf_op jit(solution)/shard_map/ppermute | solution.py:12
  161.4 13.4 %copy-start.18 = (f32[16,1,1]{0,2,1:T(1,128)}, f32[16,1,1]{0,2,1:T(1,128)S(1)}, u32[]{:S(2)}) copy-start(f32[16,1,1]{0,2,1:T(1,128)S(1)} %collective-permute-done.18) | copy-start | bytes 196
  161.5 47.4 %collective-permute-start.21 = (s16[16,64,128]{2,1,0:T(8,128)(2,1)S(1)}, s16[16,64,128]{2,1,0:T(8,128)(2,1)S(1)}, u32[]{:S(2)}, u32[]{:S(2)}) collective-permute-start(s16[16,64,128]{2,1,0:T(8,128)(2,1)S(1)} %round-nearest-even_convert_fusion.2), channel_id=1, source_target_pairs={{8,0},{16,8},{24,16},{32,24},{40,32},{48,40},{56,48},{64,56},{72,6... | collective-permute-start | bytes 786440 | tf_op jit(solution)/shard_map/ppermute | solution.py:12
  163.4 45.5 %collective-permute-start.24 = (s16[16,64,128]{2,1,0:T(8,128)(2,1)S(1)}, s16[16,64,128]{2,1,0:T(8,128)(2,1)S(1)}, u32[]{:S(2)}, u32[]{:S(2)}) collective-permute-start(s16[16,64,128]{2,1,0:T(8,128)(2,1)S(1)} %round-nearest-even_convert_fusion), channel_id=1, source_target_pairs={{40,0},{48,8},{56,16},{64,24},{72,32},{80,40},{88,48},{96,56},{104... | collective-permute-start | bytes 786440 | tf_op jit(solution)/shard_map/ppermute | solution.py:12
  169.7 3.8 %copy-start.12 = (f32[16,64,1]{1,0,2:T(8,128)}, f32[16,64,1]{1,0,2:T(8,128)S(1)}, u32[]{:S(2)}) copy-start(f32[16,64,1]{1,0,2:T(8,128)S(1)} %collective-permute-done.17) | copy-start | bytes 12292
  169.7 11.3 %collective-permute-start.20 = (f32[16,64,1]{1,0,2:T(8,128)S(1)}, f32[16,64,1]{1,0,2:T(8,128)S(1)}, u32[]{:S(2)}, u32[]{:S(2)}) collective-permute-start(f32[16,64,1]{1,0,2:T(8,128)S(1)} %fusion.101), channel_id=1, source_target_pairs={{0,40},{8,48},{16,56},{24,64},{32,72},{40,80},{48,88},{56,96},{64,... | collective-permute-start | bytes 12296 | tf_op jit(solution)/shard_map/ppermute | solution.py:12
  181.0 0.6 copy-start.14
  181.6 12.8 %collective-permute-start.22 = (f32[16,64,1]{1,0,2:T(8,128)}, f32[16,64,1]{1,0,2:T(8,128)}, u32[]{:S(2)}, u32[]{:S(2)}) collective-permute-start(f32[16,64,1]{1,0,2:T(8,128)} %fusion.99), channel_id=1, source_target_pairs={{8,0},{16,8},{24,16},{32,24},{40,32},{48,40},{56,48},{64,56},{72,6... | collective-permute-start | bytes 12296 | tf_op jit(solution)/shard_map/ppermute | solution.py:12
  194.5 14.4 %collective-permute-start.25 = (f32[16,64,1]{1,0,2:T(8,128)}, f32[16,64,1]{1,0,2:T(8,128)}, u32[]{:S(2)}, u32[]{:S(2)}) collective-permute-start(f32[16,64,1]{1,0,2:T(8,128)} %fusion.103), channel_id=1, source_target_pairs={{40,0},{48,8},{56,16},{64,24},{72,32},{80,40},{88,48},{96,56},{104... | collective-permute-start | bytes 12296 | tf_op jit(solution)/shard_map/ppermute | solution.py:12
  208.9 0.6 copy-start.19
  209.5 2.1 copy-start.13
  209.5 2.1 copy-start.15
  214.8 15.9 %copy-start.11 = (pred[128,128]{0,1:T(8,128)(4,1)S(1)}, pred[128,128]{0,1:T(8,128)(4,1)}, u32[]{:S(2)}) copy-start(pred[128,128]{0,1:T(8,128)(4,1)} %copy-done.10) | copy-start | bytes 49156
  214.8 15.9 %copy-start.6 = (f32[16,128]{1,0:T(8,128)S(1)}, f32[16,128]{1,0:T(8,128)}, u32[]{:S(2)}) copy-start(f32[16,128]{1,0:T(8,128)} %copy-done.5) | copy-start | bytes 24580
  214.8 22.8 %collective-permute-start.26 = (f32[2,16,128]{2,1,0:T(8,128)S(1)}, f32[2,16,128]{2,1,0:T(8,128)S(1)}, u32[]{:S(2)}, u32[]{:S(2)}) collective-permute-start(f32[2,16,128]{2,1,0:T(8,128)S(1)} %get-tuple-element.124), channel_id=1, source_target_pairs={{0,1},{1,2},{2,3},{3,4},{4,5},{5,6},{6,7},{7,0},{8,9},{9,10},{10,1... | collective-permute-start | bytes 49160 | tf_op jit(solution)/shard_map/ppermute | solution.py:38
  217.5 22.4 %collective-permute-start.27 = (f32[2,16,128]{2,1,0:T(8,128)S(1)}, f32[2,16,128]{2,1,0:T(8,128)S(1)}, u32[]{:S(2)}, u32[]{:S(2)}) collective-permute-start(f32[2,16,128]{2,1,0:T(8,128)S(1)} %get-tuple-element.125), channel_id=1, source_target_pairs={{0,2},{1,3},{2,4},{3,5},{4,6},{5,7},{6,0},{7,1},{8,10},{9,11},{10,... | collective-permute-start | bytes 49160 | tf_op jit(solution)/shard_map/ppermute | solution.py:38
  219.4 23.3 %collective-permute-start.28 = (f32[2,16,128]{2,1,0:T(8,128)S(1)}, f32[2,16,128]{2,1,0:T(8,128)S(1)}, u32[]{:S(2)}, u32[]{:S(2)}) collective-permute-start(f32[2,16,128]{2,1,0:T(8,128)S(1)} %get-tuple-element.126), channel_id=1, source_target_pairs={{0,3},{1,4},{2,5},{3,6},{4,7},{5,0},{6,1},{7,2},{8,11},{9,12},{10,... | collective-permute-start | bytes 49160 | tf_op jit(solution)/shard_map/ppermute | solution.py:38
  224.0 18.7 %collective-permute-start.29 = (f32[2,16,128]{2,1,0:T(8,128)S(1)}, f32[2,16,128]{2,1,0:T(8,128)S(1)}, u32[]{:S(2)}, u32[]{:S(2)}) collective-permute-start(f32[2,16,128]{2,1,0:T(8,128)S(1)} %get-tuple-element.127), channel_id=1, source_target_pairs={{0,4},{1,5},{2,6},{3,7},{4,0},{5,1},{6,2},{7,3},{8,12},{9,13},{10,... | collective-permute-start | bytes 49160 | tf_op jit(solution)/shard_map/ppermute | solution.py:38
  226.5 16.2 %collective-permute-start.30 = (f32[2,16,128]{2,1,0:T(8,128)S(1)}, f32[2,16,128]{2,1,0:T(8,128)S(1)}, u32[]{:S(2)}, u32[]{:S(2)}) collective-permute-start(f32[2,16,128]{2,1,0:T(8,128)S(1)} %get-tuple-element.128), channel_id=1, source_target_pairs={{0,5},{1,6},{2,7},{3,0},{4,1},{5,2},{6,3},{7,4},{8,13},{9,14},{10,... | collective-permute-start | bytes 49160 | tf_op jit(solution)/shard_map/ppermute | solution.py:38
  232.6 0.7 copy-start.17
  236.0 4.4 %copy-start.4 = (f32[16,128]{1,0:T(8,128)S(1)}, f32[16,128]{1,0:T(8,128)}, u32[]{:S(2)}) copy-start(f32[16,128]{1,0:T(8,128)} %copy-done.3) | copy-start | bytes 24580
  236.0 4.4 %copy-start.7 = (f32[16,128]{1,0:T(8,128)S(1)}, f32[16,128]{1,0:T(8,128)}, u32[]{:S(2)}) copy-start(f32[16,128]{1,0:T(8,128)} %get-tuple-element.154) | copy-start | bytes 24580
  236.0 4.4 %copy-start.8 = (f32[16,128]{1,0:T(8,128)S(1)}, f32[16,128]{1,0:T(8,128)}, u32[]{:S(2)}) copy-start(f32[16,128]{1,0:T(8,128)} %reduce_window_sum.32) | copy-start | bytes 24580
  236.1 4.4 %copy-start.9 = (f32[16,128]{1,0:T(8,128)S(1)}, f32[16,128]{1,0:T(8,128)}, u32[]{:S(2)}) copy-start(f32[16,128]{1,0:T(8,128)} %reduce_window_sum.31) | copy-start | bytes 24580
  237.7 5.1 %collective-permute-start.31 = (f32[2,16,128]{2,1,0:T(8,128)S(1)}, f32[2,16,128]{2,1,0:T(8,128)S(1)}, u32[]{:S(2)}, u32[]{:S(2)}) collective-permute-start(f32[2,16,128]{2,1,0:T(8,128)S(1)} %get-tuple-element.129), channel_id=1, source_target_pairs={{0,6},{1,7},{2,0},{3,1},{4,2},{5,3},{6,4},{7,5},{8,14},{9,15},{10,... | collective-permute-start | bytes 49160 | tf_op jit(solution)/shard_map/ppermute | solution.py:38
  239.9 3.5 %collective-permute-start.32 = (f32[2,16,128]{2,1,0:T(8,128)S(1)}, f32[2,16,128]{2,1,0:T(8,128)S(1)}, u32[]{:S(2)}, u32[]{:S(2)}) collective-permute-start(f32[2,16,128]{2,1,0:T(8,128)S(1)} %get-tuple-element.130), channel_id=1, source_target_pairs={{0,7},{1,0},{2,1},{3,2},{4,3},{5,4},{6,5},{7,6},{8,15},{9,8},{10,9... | collective-permute-start | bytes 49160 | tf_op jit(solution)/shard_map/ppermute | solution.py:38
  240.4 0.7 copy-start.16

commit v4 on v3

--- a/solution.py
+++ b/solution.py
@@ -12,23 +12,45 @@
     return lax.ppermute(x, axis, pairs)
 
 
-def pack(value):
-    top = jnp.max(jnp.abs(value), axis=-1, keepdims=True)
-    unit = jnp.where(top > 0, top, 1.0) / 32767.0
-    return jnp.round(value / unit).astype(jnp.int16), unit
+FLOOR = -150.0
 
 
-def unpack(packed):
-    code, unit = packed
-    return code.astype(jnp.float32) * unit
+def pack(value, decay):
+    top = jnp.max(jnp.abs(value), axis=-1, keepdims=True)
+    expo = jnp.maximum(jnp.ceil(jnp.log2(jnp.where(top > 0, top, 1.0))), -100.0)
+    code = jnp.clip(jnp.round(value / jnp.exp2(expo - 15.0)), -32767.0, 32767.0).astype(jnp.int16)
+    scaled = decay * 64.0
+    high = jnp.floor(scaled)
+    low = jnp.round((scaled - high) * 16384.0)
+    tail = jnp.zeros((1, 128), jnp.float32).at[0, : decay.shape[0]].set(high)
+    tail = tail.at[0, decay.shape[0] : 2 * decay.shape[0]].set(low)
+    lanes = value.shape[-1]
+    return jnp.concatenate(
+        [code.reshape(-1, lanes), expo.reshape(-1, lanes).astype(jnp.int16), tail.astype(jnp.int16)]
+    )
+
+
+def unpack(packed, shape):
+    body = shape[0] * shape[1]
+    code = packed[:body].astype(jnp.float32).reshape(shape)
+    expo = packed[body : body + body // shape[2]].astype(jnp.float32).reshape(shape[:2] + (1,))
+    tail = packed[-1].astype(jnp.float32)
+    decay = (tail[: shape[0]] + tail[shape[0] : 2 * shape[0]] / 16384.0) / 64.0
+    return code * jnp.exp2(expo - 15.0), decay
+
+
+def combine(own, got):
+    value = own[0] + jnp.exp(own[1])[:, None, None] * got[0]
+    return value, jnp.maximum(own[1] + got[1], FLOOR)
 
 
 def shift_pair(fwd, bwd, by):
-    fwd, bwd = lax.optimization_barrier(((pack(fwd[0]), fwd[1]), (pack(bwd[0]), bwd[1])))
+    shape = fwd[0].shape
+    fwd, bwd = lax.optimization_barrier((pack(*fwd), pack(*bwd)))
     got_f, got_b = lax.optimization_barrier(
         (from_behind(fwd, "context", by), from_behind(bwd, "context", -by))
     )
-    return (unpack(got_f[0]), got_f[1]), (unpack(got_b[0]), got_b[1])
+    return unpack(got_f, shape), unpack(got_b, shape)
 
 
 def exchange(pieces, axis):
@@ -78,7 +100,6 @@
     logc = jnp.cumsum(-step_size * rate, axis=1)
     enter = jnp.exp(logc) * (seg == 0).astype(jnp.float32)[None, :]
     leave = jnp.exp(logc[:, -1:] - logc) * (seg == seg[-1]).astype(jnp.float32)[None, :]
-    total = enter[:, -1][:, None, None]
     moved = step_size[:, :, None] * xs
     left_u = leave[:, :, None] * moved
     enter_dy = enter[:, :, None] * dys
@@ -89,20 +110,20 @@
     low = reach & -reach
     high = reach - low
     assert high > 0 and high & (high - 1) == 0 and low < high
-    fwd = (local_state, total)
-    bwd = (local_adj, total)
+    shape = local_state.shape
+    decay = jnp.where(seg[-1] == 0, jnp.maximum(logc[:, -1], FLOOR), FLOOR)
+    fwd = (local_state, decay)
+    bwd = (local_adj, decay)
     span = 1
     kept = {}
     while span < high:
         kept[span] = (fwd, bwd)
         got_f, got_b = shift_pair(fwd, bwd, span)
-        fwd = (fwd[0] + fwd[1] * got_f[0], fwd[1] * got_f[1])
-        bwd = (bwd[0] + bwd[1] * got_b[0], bwd[1] * got_b[1])
+        fwd = combine(fwd, got_f)
+        bwd = combine(bwd, got_b)
         span *= 2
     near_f, near_b = kept[low]
-    sends = lax.optimization_barrier(
-        ((pack(near_f[0]), near_f[1]), pack(fwd[0]), (pack(near_b[0]), near_b[1]), pack(bwd[0]))
-    )
+    sends = lax.optimization_barrier((pack(*near_f), pack(*fwd), pack(*near_b), pack(*bwd)))
     got = lax.optimization_barrier(
         (
             from_behind(sends[0], "context", 1),
@@ -111,8 +132,9 @@
             from_behind(sends[3], "context", -low - 1),
         )
     )
-    s_in = unpack(got[0][0]) + got[0][1] * unpack(got[1])
-    g_in = unpack(got[2][0]) + got[2][1] * unpack(got[3])
+    got = [unpack(g, shape) for g in got]
+    s_in = combine(got[0], got[1])[0]
+    g_in = combine(got[2], got[3])[0]
 
     index = jnp.arange(length)
     keep = (index[:, None] >= index[None, :]) & (seg[:, None] == seg[None, :])

time: 246 us -> 226 us (0.919)
  starting transfers between devices: 127 us -> 91.9 us
  other arithmetic: 15.5 us -> 39.7 us
  waiting for transfers between devices: 64 us -> 43 us
  local copies, waits for them, and re-layouts: 7.65 us -> 22.7 us
  matrix products: 14.9 us -> 11.3 us
    ppermute x26 -> x10, starting transfers between devices: 108 us -> 71.6 us  [from_behind(): return lax.ppermute(x, axis, pairs)]
    ppermute x26 -> x10, waiting for transfers between devices: 63.3 us -> 42.3 us  [from_behind(): return lax.ppermute(x, axis, pairs)]
    another operation x2 -> x18, other arithmetic: 0.2 us -> 15 us
    scatter x0 -> x14, local copies, waits for them, and re-layouts: none -> 6.75 us  [the longest x7 6.24 us: pack(): tail = tail.at[0, decay.shape[0]:2 * decay.shape[0]].set(low)]
    convert_element_type x7 -> x34, other arithmetic: 2.9 us -> 6.91 us  [the longest x8 2.5 us: unpack(): tail = packed[-1].astype(jnp.float32)]
    unnamed x42 -> x82, local copies, waits for them, and re-layouts: 5.18 us -> 9.09 us
    exp2 x0 -> x18, other arithmetic: none -> 3.3 us  [the longest x10 3.16 us: unpack(): return (code * jnp.exp2(expo - 15.0), decay)]
    exp x0 -> x5, other arithmetic: none -> 2.74 us  [combine(): value = own[0] + jnp.exp(own[1])[:, None, None] * got[0]]
  transfers between devices with their start and end apart: 33 -> 17, of which waited for: 9 -> 9; matrix products, arithmetic and copies ran while one was open for 6% -> 6% of each run, Pallas kernels for 0% -> 0%
where the time goes in v4:
time: 226 us; the launch traced here: 224 us
  starting transfers between devices  91.9 us (41%)
  waiting for transfers between devices  43 us (19%)
  other arithmetic  39.7 us (18%)
  local copies, waits for them, and re-layouts  22.7 us (10%)
  blocking collectives  13.8 us (6%)
  matrix products  11.3 us (5%)
    ppermute x10, starting transfers between devices, from_behind(): return lax.ppermute(x, axis, pairs)  71.6 us
    ppermute x10, waiting for transfers between devices, from_behind(): return lax.ppermute(x, axis, pairs)  42.3 us
    ppermute x7, starting transfers between devices, exchange(): lax.ppermute(pieces[s], axis, [(i, (i + s) % count) for i in range(count)])  20.3 us
    another operation x18, other arithmetic  15 us
    all_gather x1, blocking collectives, local(): lax.all_gather(jnp.stack([b_rows, c_rows]), 'tensor', axis=1, tiled=True)  13.8 us
    unnamed x82, local copies, waits for them, and re-layouts  9.09 us
    scatter x7, local copies, waits for them, and re-layouts, pack(): tail = tail.at[0, decay.shape[0]:2 * decay.shape[0]].set(low)  6.24 us
  transfers between devices with their start and end apart: 17, of which 9 were waited for; matrix products, arithmetic and copies ran while one was open for 6% of the time, Pallas kernels for 0%

profile of v4, /device:TPU:7, one launch (start us, length us, event | category | flops | bytes accessed | tf_op | source)
XLA Modules:
  0.0 224.4 jit_solution(15985088294382721301)
XLA Ops:
  0.6 0.8 copy.30
  5.6 0.7 pad_maximum_fusion
  6.3 13.8 %all_gather.3 = bf16[2,128,128]{2,1,0:T(8,128)(2,1)S(1)} all-gather(bf16[2,16,128]{2,1,0:T(8,128)(2,1)S(1)} %pad_maximum_fusion), channel_id=1, replica_groups=mesh['context'=64,'tensor'=8] {'tensor'}, dimensions={1}, use_global_device_ids=true | all-gather | bytes 73728 | tf_op jit(solution)/shard_map/all_gather | solution.py:85
  24.3 1.4 broadcast_select_fusion.12
  25.7 0.9 scatter.49
  27.1 3.5 %collective-permute-start = (s16[1033,128]{1,0:T(8,128)(2,1)S(1)}, s16[1033,128]{1,0:T(8,128)(2,1)S(1)}, u32[]{:S(2)}, u32[]{:S(2)}) collective-permute-start(s16[1033,128]{1,0:T(8,128)(2,1)S(1)} %get-tuple-element.255), channel_id=1, source_target_pairs={{0,8},{8,16},{16,24},{24,32},{32,40},{40,48},{48,56},{56,64},{64,7... | collective-permute-start | bytes 793352 | tf_op jit(solution)/shard_map/ppermute | solution.py:12
  30.7 9.8 %collective-permute-start.1 = (s16[1033,128]{1,0:T(8,128)(2,1)S(1)}, s16[1033,128]{1,0:T(8,128)(2,1)S(1)}, u32[]{:S(2)}, u32[]{:S(2)}) collective-permute-start(s16[1033,128]{1,0:T(8,128)(2,1)S(1)} %get-tuple-element.256), channel_id=1, source_target_pairs={{8,0},{16,8},{24,16},{32,24},{40,32},{48,40},{56,48},{64,56},{72,6... | collective-permute-start | bytes 793352 | tf_op jit(solution)/shard_map/ppermute | solution.py:12
  40.4 4.7 %collective-permute-done = s16[1033,128]{1,0:T(8,128)(2,1)S(1)} collective-permute-done((s16[1033,128]{1,0:T(8,128)(2,1)S(1)}, s16[1033,128]{1,0:T(8,128)(2,1)S(1)}, u32[]{:S(2)}, u32[]{:S(2)}) %collective-permute-start) | collective-permute-done | bytes 264480 | tf_op jit(solution)/shard_map/ppermute | solution.py:12
  45.2 0.9 collective-permute-done.1
  47.3 1.4 broadcast_select_fusion.10
  50.5 1.4 broadcast_select_fusion.11
  51.8 0.9 scatter.55
  52.8 0.9 scatter.51
  53.7 0.8 clamp_convert_fusion.4
  54.5 1.9 collective-permute-start.2
  56.4 6.4 %collective-permute-start.3 = (s16[1033,128]{1,0:T(8,128)(2,1)S(1)}, s16[1033,128]{1,0:T(8,128)(2,1)S(1)}, u32[]{:S(2)}, u32[]{:S(2)}) collective-permute-start(s16[1033,128]{1,0:T(8,128)(2,1)S(1)} %pad_add_fusion.3), channel_id=1, source_target_pairs={{16,0},{24,8},{32,16},{40,24},{48,32},{56,40},{64,48},{72,56},{80,... | collective-permute-start | bytes 793352 | tf_op jit(solution)/shard_map/ppermute | solution.py:12
  62.8 4.2 %collective-permute-done.2 = s16[1033,128]{1,0:T(8,128)(2,1)S(1)} collective-permute-done((s16[1033,128]{1,0:T(8,128)(2,1)S(1)}, s16[1033,128]{1,0:T(8,128)(2,1)S(1)}, u32[]{:S(2)}, u32[]{:S(2)}) %collective-permute-start.2) | collective-permute-done | bytes 264480 | tf_op jit(solution)/shard_map/ppermute | solution.py:12
  67.0 2.3 %collective-permute-done.3 = s16[1033,128]{1,0:T(8,128)(2,1)S(1)} collective-permute-done((s16[1033,128]{1,0:T(8,128)(2,1)S(1)}, s16[1033,128]{1,0:T(8,128)(2,1)S(1)}, u32[]{:S(2)}, u32[]{:S(2)}) %collective-permute-start.3) | collective-permute-done | bytes 264480 | tf_op jit(solution)/shard_map/ppermute | solution.py:12
  69.3 0.7 slice.474
  70.0 0.7 slice.479
  72.1 1.9 broadcast_select_fusion.8
  75.3 1.8 fusion.22
  77.6 0.7 slice_convert_fusion.9
  79.1 1.4 broadcast_select_fusion.9
  81.1 0.9 scatter.61
  82.3 0.9 scatter.59
  83.2 5.4 %collective-permute-start.4 = (s16[1033,128]{1,0:T(8,128)(2,1)S(1)}, s16[1033,128]{1,0:T(8,128)(2,1)S(1)}, u32[]{:S(2)}, u32[]{:S(2)}) collective-permute-start(s16[1033,128]{1,0:T(8,128)(2,1)S(1)} %pad_add_fusion.4), channel_id=1, source_target_pairs={{0,32},{8,40},{16,48},{24,56},{32,64},{40,72},{48,80},{56,88},{64,... | collective-permute-start | bytes 793352 | tf_op jit(solution)/shard_map/ppermute | solution.py:12
  88.7 4.7 %collective-permute-start.5 = (s16[1033,128]{1,0:T(8,128)(2,1)S(1)}, s16[1033,128]{1,0:T(8,128)(2,1)S(1)}, u32[]{:S(2)}, u32[]{:S(2)}) collective-permute-start(s16[1033,128]{1,0:T(8,128)(2,1)S(1)} %pad_add_fusion.5), channel_id=1, source_target_pairs={{32,0},{40,8},{48,16},{56,24},{64,32},{72,40},{80,48},{88,56},{96,... | collective-permute-start | bytes 793352 | tf_op jit(solution)/shard_map/ppermute | solution.py:12
  93.6 1.7 collective-permute-done.4
  95.3 4.7 %collective-permute-done.5 = s16[1033,128]{1,0:T(8,128)(2,1)S(1)} collective-permute-done((s16[1033,128]{1,0:T(8,128)(2,1)S(1)}, s16[1033,128]{1,0:T(8,128)(2,1)S(1)}, u32[]{:S(2)}, u32[]{:S(2)}) %collective-permute-start.5) | collective-permute-done | bytes 264480 | tf_op jit(solution)/shard_map/ppermute | solution.py:12
  102.9 0.7 fusion.223
  103.6 0.7 fusion.222
  104.3 1.4 broadcast_select_fusion.6
  105.7 0.9 scatter.69
  106.7 0.9 scatter.65
  107.6 0.8 clamp_convert_fusion
  108.3 0.7 pad_add_fusion.7
  109.1 0.7 pad_add_fusion.6
  110.1 25.6 %collective-permute-start.6 = (s16[1033,128]{1,0:T(8,128)(2,1)S(1)}, s16[1033,128]{1,0:T(8,128)(2,1)S(1)}, u32[]{:S(2)}, u32[]{:S(2)}) collective-permute-start(s16[1033,128]{1,0:T(8,128)(2,1)S(1)} %copy-done.12), channel_id=1, source_target_pairs={{0,8},{8,16},{16,24},{24,32},{32,40},{40,48},{48,56},{56,64},{64,7... | collective-permute-start | bytes 793352 | tf_op jit(solution)/shard_map/ppermute | solution.py:12
  135.7 3.8 %collective-permute-start.7 = (s16[1033,128]{1,0:T(8,128)(2,1)}, s16[1033,128]{1,0:T(8,128)(2,1)S(1)}, u32[]{:S(2)}, u32[]{:S(2)}) collective-permute-start(s16[1033,128]{1,0:T(8,128)(2,1)} %pad_add_fusion.6), channel_id=1, source_target_pairs={{0,40},{8,48},{16,56},{24,64},{32,72},{40,80},{48,88},{56,96},{64,... | collective-permute-start | bytes 793352 | tf_op jit(solution)/shard_map/ppermute | solution.py:12
  139.6 5.5 %collective-permute-start.8 = (s16[1033,128]{1,0:T(8,128)(2,1)S(1)}, s16[1033,128]{1,0:T(8,128)(2,1)S(1)}, u32[]{:S(2)}, u32[]{:S(2)}) collective-permute-start(s16[1033,128]{1,0:T(8,128)(2,1)S(1)} %copy-done.10), channel_id=1, source_target_pairs={{8,0},{16,8},{24,16},{32,24},{40,32},{48,40},{56,48},{64,56},{72,6... | collective-permute-start | bytes 793352 | tf_op jit(solution)/shard_map/ppermute | solution.py:12
  145.1 5.0 %collective-permute-start.9 = (s16[1033,128]{1,0:T(8,128)(2,1)}, s16[1033,128]{1,0:T(8,128)(2,1)}, u32[]{:S(2)}, u32[]{:S(2)}) collective-permute-start(s16[1033,128]{1,0:T(8,128)(2,1)} %pad_add_fusion.7), channel_id=1, source_target_pairs={{40,0},{48,8},{56,16},{64,24},{72,32},{80,40},{88,48},{96,56},{104... | collective-permute-start | bytes 793352 | tf_op jit(solution)/shard_map/ppermute | solution.py:12
  150.1 2.0 fusion.10
  152.3 0.9 reduce_window_sum.31
  153.2 1.3 fusion.8
  154.5 15.2 %collective-permute-done.7 = s16[1033,128]{1,0:T(8,128)(2,1)S(1)} collective-permute-done((s16[1033,128]{1,0:T(8,128)(2,1)}, s16[1033,128]{1,0:T(8,128)(2,1)S(1)}, u32[]{:S(2)}, u32[]{:S(2)}) %collective-permute-start.7) | collective-permute-done | bytes 264480 | tf_op jit(solution)/shard_map/ppermute | solution.py:12
  169.7 8.6 %collective-permute-done.9 = s16[1033,128]{1,0:T(8,128)(2,1)} collective-permute-done((s16[1033,128]{1,0:T(8,128)(2,1)}, s16[1033,128]{1,0:T(8,128)(2,1)}, u32[]{:S(2)}, u32[]{:S(2)}) %collective-permute-start.9) | collective-permute-done | bytes 264480 | tf_op jit(solution)/shard_map/ppermute | solution.py:12
  181.0 1.0 slice_convert_fusion.2
  182.0 1.3 multiply_exponential_fusion.2
  183.3 1.2 slice_convert_fusion.5
  185.9 0.8 exp2.403
  186.7 0.8 exponential_bitcast_fusion.1
  188.1 1.3 convolution_bitcast_fusion.2
  189.7 1.3 convolution_bitcast_fusion.3
  191.3 4.4 %collective-permute-start.10 = (f32[2,16,128]{2,1,0:T(8,128)S(1)}, f32[2,16,128]{2,1,0:T(8,128)S(1)}, u32[]{:S(2)}, u32[]{:S(2)}) collective-permute-start(f32[2,16,128]{2,1,0:T(8,128)S(1)} %get-tuple-element.276), channel_id=1, source_target_pairs={{0,1},{1,2},{2,3},{3,4},{4,5},{5,6},{6,7},{7,0},{8,9},{9,10},{10,1... | collective-permute-start | bytes 49160 | tf_op jit(solution)/shard_map/ppermute | solution.py:60
  195.7 1.9 collective-permute-start.11
  197.7 4.6 %collective-permute-start.12 = (f32[2,16,128]{2,1,0:T(8,128)S(1)}, f32[2,16,128]{2,1,0:T(8,128)S(1)}, u32[]{:S(2)}, u32[]{:S(2)}) collective-permute-start(f32[2,16,128]{2,1,0:T(8,128)S(1)} %get-tuple-element.278), channel_id=1, source_target_pairs={{0,3},{1,4},{2,5},{3,6},{4,7},{5,0},{6,1},{7,2},{8,11},{9,12},{10,... | collective-permute-start | bytes 49160 | tf_op jit(solution)/shard_map/ppermute | solution.py:60
  202.2 2.5 %collective-permute-start.13 = (f32[2,16,128]{2,1,0:T(8,128)S(1)}, f32[2,16,128]{2,1,0:T(8,128)S(1)}, u32[]{:S(2)}, u32[]{:S(2)}) collective-permute-start(f32[2,16,128]{2,1,0:T(8,128)S(1)} %get-tuple-element.279), channel_id=1, source_target_pairs={{0,4},{1,5},{2,6},{3,7},{4,0},{5,1},{6,2},{7,3},{8,12},{9,13},{10,... | collective-permute-start | bytes 49160 | tf_op jit(solution)/shard_map/ppermute | solution.py:60
  204.8 4.2 %collective-permute-start.14 = (f32[2,16,128]{2,1,0:T(8,128)S(1)}, f32[2,16,128]{2,1,0:T(8,128)S(1)}, u32[]{:S(2)}, u32[]{:S(2)}) collective-permute-start(f32[2,16,128]{2,1,0:T(8,128)S(1)} %get-tuple-element.280), channel_id=1, source_target_pairs={{0,5},{1,6},{2,7},{3,0},{4,1},{5,2},{6,3},{7,4},{8,13},{9,14},{10,... | collective-permute-start | bytes 49160 | tf_op jit(solution)/shard_map/ppermute | solution.py:60
  210.5 2.1 multiply_reduce_fusion.1
  214.4 1.2 fusion.4
  216.0 1.9 fusion.5
  218.0 2.2 collective-permute-start.15
  222.1 1.0 copy.35
  (221 shorter events, 32.0 us)
Async XLA Ops:
  0.6 19.4 %copy-start.14 = (bf16[128,1024]{1,0:T(8,128)(2,1)S(1)}, bf16[128,1024]{1,0:T(8,128)(2,1)}, u32[]{:S(2)}) copy-start(bf16[128,1024]{1,0:T(8,128)(2,1)} %param.48) | copy-start | bytes 786436
  20.1 0.7 copy-start.8
  20.1 0.7 copy-start.35
  21.4 1.0 copy-start.16
  27.1 18.1 %collective-permute-start = (s16[1033,128]{1,0:T(8,128)(2,1)S(1)}, s16[1033,128]{1,0:T(8,128)(2,1)S(1)}, u32[]{:S(2)}, u32[]{:S(2)}) collective-permute-start(s16[1033,128]{1,0:T(8,128)(2,1)S(1)} %get-tuple-element.255), channel_id=1, source_target_pairs={{0,8},{8,16},{16,24},{24,32},{32,40},{40,48},{48,56},{56,64},{64,7... | collective-permute-start | bytes 793352 | tf_op jit(solution)/shard_map/ppermute | solution.py:12
  30.7 15.4 %collective-permute-start.1 = (s16[1033,128]{1,0:T(8,128)(2,1)S(1)}, s16[1033,128]{1,0:T(8,128)(2,1)S(1)}, u32[]{:S(2)}, u32[]{:S(2)}) collective-permute-start(s16[1033,128]{1,0:T(8,128)(2,1)S(1)} %get-tuple-element.256), channel_id=1, source_target_pairs={{8,0},{16,8},{24,16},{32,24},{40,32},{48,40},{56,48},{64,56},{72,6... | collective-permute-start | bytes 793352 | tf_op jit(solution)/shard_map/ppermute | solution.py:12
  46.7 3.8 %copy-start.27 = (f32[16]{0:T(128)}, f32[16]{0:T(128)S(1)}, u32[]{:S(2)}) copy-start(f32[16]{0:T(128)S(1)} %get-tuple-element.357) | copy-start | bytes 196
  54.5 12.5 %collective-permute-start.2 = (s16[1033,128]{1,0:T(8,128)(2,1)S(1)}, s16[1033,128]{1,0:T(8,128)(2,1)S(1)}, u32[]{:S(2)}, u32[]{:S(2)}) collective-permute-start(s16[1033,128]{1,0:T(8,128)(2,1)S(1)} %pad_add_fusion.2), channel_id=1, source_target_pairs={{0,16},{8,24},{16,32},{24,40},{32,48},{40,56},{48,64},{56,72},{64,... | collective-permute-start | bytes 793352 | tf_op jit(solution)/shard_map/ppermute | solution.py:12
  56.4 12.9 %collective-permute-start.3 = (s16[1033,128]{1,0:T(8,128)(2,1)S(1)}, s16[1033,128]{1,0:T(8,128)(2,1)S(1)}, u32[]{:S(2)}, u32[]{:S(2)}) collective-permute-start(s16[1033,128]{1,0:T(8,128)(2,1)S(1)} %pad_add_fusion.3), channel_id=1, source_target_pairs={{16,0},{24,8},{32,16},{40,24},{48,32},{56,40},{64,48},{72,56},{80,... | collective-permute-start | bytes 793352 | tf_op jit(solution)/shard_map/ppermute | solution.py:12
  67.0 3.8 %copy-start.13 = (s16[1033,128]{1,0:T(8,128)(2,1)}, s16[1033,128]{1,0:T(8,128)(2,1)S(1)}, u32[]{:S(2)}) copy-start(s16[1033,128]{1,0:T(8,128)(2,1)S(1)} %collective-permute-done.2) | copy-start | bytes 793348
  71.4 0.7 copy-start.25
  74.6 0.6 copy-start.32
  74.6 0.6 copy-start.33
  77.6 0.7 copy-start.28
  80.4 0.7 copy-start.34
  80.4 0.7 copy-start.38
  83.2 5.5 %copy-start.9 = (s16[1033,128]{1,0:T(8,128)(2,1)}, s16[1033,128]{1,0:T(8,128)(2,1)S(1)}, u32[]{:S(2)}) copy-start(s16[1033,128]{1,0:T(8,128)(2,1)S(1)} %pad_add_fusion.5) | copy-start | bytes 793348
  83.2 16.8 %copy-start.11 = (s16[1033,128]{1,0:T(8,128)(2,1)}, s16[1033,128]{1,0:T(8,128)(2,1)S(1)}, u32[]{:S(2)}) copy-start(s16[1033,128]{1,0:T(8,128)(2,1)S(1)} %pad_add_fusion.4) | copy-start | bytes 793348
  83.2 12.1 %collective-permute-start.4 = (s16[1033,128]{1,0:T(8,128)(2,1)S(1)}, s16[1033,128]{1,0:T(8,128)(2,1)S(1)}, u32[]{:S(2)}, u32[]{:S(2)}) collective-permute-start(s16[1033,128]{1,0:T(8,128)(2,1)S(1)} %pad_add_fusion.4), channel_id=1, source_target_pairs={{0,32},{8,40},{16,48},{24,56},{32,64},{40,72},{48,80},{56,88},{64,... | collective-permute-start | bytes 793352 | tf_op jit(solution)/shard_map/ppermute | solution.py:12
  88.7 11.4 %collective-permute-start.5 = (s16[1033,128]{1,0:T(8,128)(2,1)S(1)}, s16[1033,128]{1,0:T(8,128)(2,1)S(1)}, u32[]{:S(2)}, u32[]{:S(2)}) collective-permute-start(s16[1033,128]{1,0:T(8,128)(2,1)S(1)} %pad_add_fusion.5), channel_id=1, source_target_pairs={{32,0},{40,8},{48,16},{56,24},{64,32},{72,40},{80,48},{88,56},{96,... | collective-permute-start | bytes 793352 | tf_op jit(solution)/shard_map/ppermute | solution.py:12
  93.5 59.7 %copy-start.23 = (pred[128,128]{0,1:T(8,128)(4,1)}, pred[128,128]{0,1:T(8,128)(4,1)S(1)}, u32[]{:S(2)}) copy-start(pred[128,128]{0,1:T(8,128)(4,1)S(1)} %fusion.75) | copy-start | bytes 49156
  95.3 4.8 %copy-start = (s16[1033,128]{1,0:T(8,128)(2,1)}, s16[1033,128]{1,0:T(8,128)(2,1)S(1)}, u32[]{:S(2)}) copy-start(s16[1033,128]{1,0:T(8,128)(2,1)S(1)} %collective-permute-done.4) | copy-start | bytes 793348
  100.2 0.6 copy-start.29
  100.8 0.9 slice-start
  101.8 5.8 %copy-start.1 = (s16[1033,128]{1,0:T(8,128)(2,1)S(1)}, s16[1033,128]{1,0:T(8,128)(2,1)}, u32[]{:S(2)}) copy-start(s16[1033,128]{1,0:T(8,128)(2,1)} %copy-done) | copy-start | bytes 793348
  102.2 0.7 copy-start.26
  109.1 1.0 copy-start.12
  109.1 30.5 %copy-start.10 = (s16[1033,128]{1,0:T(8,128)(2,1)S(1)}, s16[1033,128]{1,0:T(8,128)(2,1)}, u32[]{:S(2)}) copy-start(s16[1033,128]{1,0:T(8,128)(2,1)} %copy-done.9) | copy-start | bytes 793348
  110.1 44.4 %collective-permute-start.6 = (s16[1033,128]{1,0:T(8,128)(2,1)S(1)}, s16[1033,128]{1,0:T(8,128)(2,1)S(1)}, u32[]{:S(2)}, u32[]{:S(2)}) collective-permute-start(s16[1033,128]{1,0:T(8,128)(2,1)S(1)} %copy-done.12), channel_id=1, source_target_pairs={{0,8},{8,16},{16,24},{24,32},{32,40},{40,48},{48,56},{56,64},{64,7... | collective-permute-start | bytes 793352 | tf_op jit(solution)/shard_map/ppermute | solution.py:12
  135.7 34.0 %collective-permute-start.7 = (s16[1033,128]{1,0:T(8,128)(2,1)}, s16[1033,128]{1,0:T(8,128)(2,1)S(1)}, u32[]{:S(2)}, u32[]{:S(2)}) collective-permute-start(s16[1033,128]{1,0:T(8,128)(2,1)} %pad_add_fusion.6), channel_id=1, source_target_pairs={{0,40},{8,48},{16,56},{24,64},{32,72},{40,80},{48,88},{56,96},{64,... | collective-permute-start | bytes 793352 | tf_op jit(solution)/shard_map/ppermute | solution.py:12
  139.6 30.1 %collective-permute-start.8 = (s16[1033,128]{1,0:T(8,128)(2,1)S(1)}, s16[1033,128]{1,0:T(8,128)(2,1)S(1)}, u32[]{:S(2)}, u32[]{:S(2)}) collective-permute-start(s16[1033,128]{1,0:T(8,128)(2,1)S(1)} %copy-done.10), channel_id=1, source_target_pairs={{8,0},{16,8},{24,16},{32,24},{40,32},{48,40},{56,48},{64,56},{72,6... | collective-permute-start | bytes 793352 | tf_op jit(solution)/shard_map/ppermute | solution.py:12
  145.1 33.2 %collective-permute-start.9 = (s16[1033,128]{1,0:T(8,128)(2,1)}, s16[1033,128]{1,0:T(8,128)(2,1)}, u32[]{:S(2)}, u32[]{:S(2)}) collective-permute-start(s16[1033,128]{1,0:T(8,128)(2,1)} %pad_add_fusion.7), channel_id=1, source_target_pairs={{40,0},{48,8},{56,16},{64,24},{72,32},{80,40},{88,48},{96,56},{104... | collective-permute-start | bytes 793352 | tf_op jit(solution)/shard_map/ppermute | solution.py:12
  154.5 25.2 %copy-start.2 = (s16[1033,128]{1,0:T(8,128)(2,1)}, s16[1033,128]{1,0:T(8,128)(2,1)S(1)}, u32[]{:S(2)}) copy-start(s16[1033,128]{1,0:T(8,128)(2,1)S(1)} %collective-permute-done.6) | copy-start | bytes 793348
  169.7 9.3 %copy-start.4 = (s16[1033,128]{1,0:T(8,128)(2,1)}, s16[1033,128]{1,0:T(8,128)(2,1)S(1)}, u32[]{:S(2)}) copy-start(s16[1033,128]{1,0:T(8,128)(2,1)S(1)} %collective-permute-done.7) | copy-start | bytes 793348
  169.7 10.6 %copy-start.6 = (s16[1033,128]{1,0:T(8,128)(2,1)}, s16[1033,128]{1,0:T(8,128)(2,1)S(1)}, u32[]{:S(2)}) copy-start(s16[1033,128]{1,0:T(8,128)(2,1)S(1)} %collective-permute-done.8) | copy-start | bytes 793348
  184.5 0.7 copy-start.39
  184.5 1.3 copy-start.22
  187.5 0.7 copy-start.30
  188.1 1.3 copy-start.15
  189.7 20.1 %copy-start.7 = (s16[1033,128]{1,0:T(8,128)(2,1)S(1)}, s16[1033,128]{1,0:T(8,128)(2,1)}, u32[]{:S(2)}) copy-start(s16[1033,128]{1,0:T(8,128)(2,1)} %copy-done.6) | copy-start | bytes 793348
  191.1 18.7 %copy-start.5 = (s16[1033,128]{1,0:T(8,128)(2,1)S(1)}, s16[1033,128]{1,0:T(8,128)(2,1)}, u32[]{:S(2)}) copy-start(s16[1033,128]{1,0:T(8,128)(2,1)} %copy-done.4) | copy-start | bytes 793348
  191.3 18.5 %copy-start.3 = (s16[1033,128]{1,0:T(8,128)(2,1)S(1)}, s16[1033,128]{1,0:T(8,128)(2,1)}, u32[]{:S(2)}) copy-start(s16[1033,128]{1,0:T(8,128)(2,1)} %copy-done.2) | copy-start | bytes 793348
  191.3 26.7 %collective-permute-start.10 = (f32[2,16,128]{2,1,0:T(8,128)S(1)}, f32[2,16,128]{2,1,0:T(8,128)S(1)}, u32[]{:S(2)}, u32[]{:S(2)}) collective-permute-start(f32[2,16,128]{2,1,0:T(8,128)S(1)} %get-tuple-element.276), channel_id=1, source_target_pairs={{0,1},{1,2},{2,3},{3,4},{4,5},{5,6},{6,7},{7,0},{8,9},{9,10},{10,1... | collective-permute-start | bytes 49160 | tf_op jit(solution)/shard_map/ppermute | solution.py:60
  195.7 24.6 %collective-permute-start.11 = (f32[2,16,128]{2,1,0:T(8,128)S(1)}, f32[2,16,128]{2,1,0:T(8,128)S(1)}, u32[]{:S(2)}, u32[]{:S(2)}) collective-permute-start(f32[2,16,128]{2,1,0:T(8,128)S(1)} %get-tuple-element.277), channel_id=1, source_target_pairs={{0,2},{1,3},{2,4},{3,5},{4,6},{5,7},{6,0},{7,1},{8,10},{9,11},{10,... | collective-permute-start | bytes 49160 | tf_op jit(solution)/shard_map/ppermute | solution.py:60
  197.7 25.5 %collective-permute-start.12 = (f32[2,16,128]{2,1,0:T(8,128)S(1)}, f32[2,16,128]{2,1,0:T(8,128)S(1)}, u32[]{:S(2)}, u32[]{:S(2)}) collective-permute-start(f32[2,16,128]{2,1,0:T(8,128)S(1)} %get-tuple-element.278), channel_id=1, source_target_pairs={{0,3},{1,4},{2,5},{3,6},{4,7},{5,0},{6,1},{7,2},{8,11},{9,12},{10,... | collective-permute-start | bytes 49160 | tf_op jit(solution)/shard_map/ppermute | solution.py:60
  202.2 20.9 %collective-permute-start.13 = (f32[2,16,128]{2,1,0:T(8,128)S(1)}, f32[2,16,128]{2,1,0:T(8,128)S(1)}, u32[]{:S(2)}, u32[]{:S(2)}) collective-permute-start(f32[2,16,128]{2,1,0:T(8,128)S(1)} %get-tuple-element.279), channel_id=1, source_target_pairs={{0,4},{1,5},{2,6},{3,7},{4,0},{5,1},{6,2},{7,3},{8,12},{9,13},{10,... | collective-permute-start | bytes 49160 | tf_op jit(solution)/shard_map/ppermute | solution.py:60
  204.8 18.4 %collective-permute-start.14 = (f32[2,16,128]{2,1,0:T(8,128)S(1)}, f32[2,16,128]{2,1,0:T(8,128)S(1)}, u32[]{:S(2)}, u32[]{:S(2)}) collective-permute-start(f32[2,16,128]{2,1,0:T(8,128)S(1)} %get-tuple-element.280), channel_id=1, source_target_pairs={{0,5},{1,6},{2,7},{3,0},{4,1},{5,2},{6,3},{7,4},{8,13},{9,14},{10,... | collective-permute-start | bytes 49160 | tf_op jit(solution)/shard_map/ppermute | solution.py:60
  209.0 0.7 copy-start.31
  209.7 0.7 copy-start.19
  209.7 0.7 copy-start.20
  209.7 0.7 copy-start.21
  209.8 0.7 copy-start.18
  212.6 0.7 copy-start.37
  213.7 0.7 copy-start.24
  217.9 2.9 %copy-start.17 = (f32[16,128]{1,0:T(8,128)S(1)}, f32[16,128]{1,0:T(8,128)}, u32[]{:S(2)}) copy-start(f32[16,128]{1,0:T(8,128)} %reduce_window_sum.31) | copy-start | bytes 24580
  218.0 5.1 %collective-permute-start.15 = (f32[2,16,128]{2,1,0:T(8,128)S(1)}, f32[2,16,128]{2,1,0:T(8,128)S(1)}, u32[]{:S(2)}, u32[]{:S(2)}) collective-permute-start(f32[2,16,128]{2,1,0:T(8,128)S(1)} %get-tuple-element.281), channel_id=1, source_target_pairs={{0,6},{1,7},{2,0},{3,1},{4,2},{5,3},{6,4},{7,5},{8,14},{9,15},{10,... | collective-permute-start | bytes 49160 | tf_op jit(solution)/shard_map/ppermute | solution.py:60
  220.3 3.5 %collective-permute-start.16 = (f32[2,16,128]{2,1,0:T(8,128)S(1)}, f32[2,16,128]{2,1,0:T(8,128)S(1)}, u32[]{:S(2)}, u32[]{:S(2)}) collective-permute-start(f32[2,16,128]{2,1,0:T(8,128)S(1)} %get-tuple-element.282), channel_id=1, source_target_pairs={{0,7},{1,0},{2,1},{3,2},{4,3},{5,4},{6,5},{7,6},{8,15},{9,8},{10,9... | collective-permute-start | bytes 49160 | tf_op jit(solution)/shard_map/ppermute | solution.py:60
  220.8 0.7 copy-start.36

commit v5 on v4

--- a/solution.py
+++ b/solution.py
@@ -22,9 +22,8 @@
     scaled = decay * 64.0
     high = jnp.floor(scaled)
     low = jnp.round((scaled - high) * 16384.0)
-    tail = jnp.zeros((1, 128), jnp.float32).at[0, : decay.shape[0]].set(high)
-    tail = tail.at[0, decay.shape[0] : 2 * decay.shape[0]].set(low)
     lanes = value.shape[-1]
+    tail = jnp.concatenate([high, low, jnp.zeros((lanes - 2 * decay.shape[0],), jnp.float32)])[None]
     return jnp.concatenate(
         [code.reshape(-1, lanes), expo.reshape(-1, lanes).astype(jnp.int16), tail.astype(jnp.int16)]
     )
@@ -64,6 +63,14 @@
 
 
 def scatter_sum(whole, axis):
+    count = lax.axis_size(axis)
+    size = whole.shape[1] // count
+    parts = whole.reshape(whole.shape[0], count, size, whole.shape[2]).transpose(1, 0, 2, 3)
+    got = lax.all_to_all(parts, axis, 0, 0, tiled=True)
+    return jnp.sum(got, axis=0)
+
+
+def scatter_sum_by_permutes(whole, axis):
     count = lax.axis_size(axis)
     me = lax.axis_index(axis)
     size = whole.shape[1] // count
@@ -82,8 +89,11 @@
     length = inputs.shape[0]
     heads = step_size.shape[0]
     width = inputs.shape[1] // heads
-    rows = lax.all_gather(jnp.stack([b_rows, c_rows]), "tensor", axis=1, tiled=True)
-    b_bf, c_bf = rows[0], rows[1]
+    count = lax.axis_size("tensor")
+    piece = jnp.stack([b_rows, c_rows])
+    rows = lax.all_to_all(jnp.broadcast_to(piece, (count,) + piece.shape), "tensor", 0, 0, tiled=True)
+    b_bf = rows[:, 0].reshape(length, -1)
+    c_bf = rows[:, 1].reshape(length, -1)
     bmat = b_bf.astype(jnp.float32)
     cmat = c_bf.astype(jnp.float32)
     xs = inputs.astype(jnp.float32).reshape(length, heads, width).transpose(1, 0, 2)

time: 226 us -> 182 us (0.81)
  the two profiles are of different devices: /device:TPU:7 before, /device:TPU:15 now
where the time goes in v5:
time: 182 us; the launch traced here: 181 us
  starting transfers between devices  87 us (48%)
  waiting for transfers between devices  40.1 us (22%)
  other arithmetic  24.8 us (14%)
  local copies, waits for them, and re-layouts  15.7 us (9%)
  matrix products  11.9 us (7%)
  between operations  2.05 us (1%)
    ppermute x10, starting transfers between devices, from_behind(): return lax.ppermute(x, axis, pairs)  71.9 us
    ppermute x10, waiting for transfers between devices, from_behind(): return lax.ppermute(x, axis, pairs)  40.1 us
    all_to_all x1, starting transfers between devices, scatter_sum(): got = lax.all_to_all(parts, axis, 0, 0, tiled=True)  9.85 us
    unnamed x74, local copies, waits for them, and re-layouts  8.24 us
    all_to_all x1, starting transfers between devices, local(): lax.all_to_all(jnp.broadcast_to(piece, (count,) + piece.shape), 'tensor',...  5.23 us
  transfers between devices with their start and end apart: 12, of which 8 were waited for; matrix products, arithmetic and copies ran while one was open for 10% of the time, Pallas kernels for 0%

profile of v5, /device:TPU:15, one launch (start us, length us, event | category | flops | bytes accessed | tf_op | source)
XLA Modules:
  0.0 181.5 jit_solution(17335887853725225770)
XLA Ops:
  0.6 0.7 pad_maximum_fusion
  1.4 0.6 broadcast_in_dim.29
  2.0 5.2 %all-to-all-start = ((bf16[8,2,16,128]{3,2,1,0:T(8,128)(2,1)}), bf16[8,2,16,128]{3,2,1,0:T(8,128)(2,1)S(1)}, u32[]{:S(2)}, u32[]{:S(2)}) async-start(bf16[8,2,16,128]{3,2,1,0:T(8,128)(2,1)} %broadcast_in_dim.29), calls=%async_computation | async-start | bytes 131072 | tf_op jit(solution)/shard_map/all_to_all | solution.py:94
  7.3 0.7 copy.32
  8.2 0.6 copy-done.23
  9.6 0.6 compare_convert_fusion
  11.7 0.8 copy-done.11
  14.4 3.5 %collective-permute-start = (s16[1033,128]{1,0:T(8,128)(2,1)S(1)}, s16[1033,128]{1,0:T(8,128)(2,1)S(1)}, u32[]{:S(2)}, u32[]{:S(2)}) collective-permute-start(s16[1033,128]{1,0:T(8,128)(2,1)S(1)} %get-tuple-element.24), channel_id=1, source_target_pairs={{0,8},{8,16},{16,24},{24,32},{32,40},{40,48},{48,56},{56,64},{64,7... | collective-permute-start | bytes 793352 | tf_op jit(solution)/shard_map/ppermute | solution.py:12
  18.0 9.8 %collective-permute-start.1 = (s16[1033,128]{1,0:T(8,128)(2,1)S(1)}, s16[1033,128]{1,0:T(8,128)(2,1)S(1)}, u32[]{:S(2)}, u32[]{:S(2)}) collective-permute-start(s16[1033,128]{1,0:T(8,128)(2,1)S(1)} %get-tuple-element.25), channel_id=1, source_target_pairs={{8,0},{16,8},{24,16},{32,24},{40,32},{48,40},{56,48},{64,56},{72,6... | collective-permute-start | bytes 793352 | tf_op jit(solution)/shard_map/ppermute | solution.py:12
  27.7 4.5 %collective-permute-done = s16[1033,128]{1,0:T(8,128)(2,1)S(1)} collective-permute-done((s16[1033,128]{1,0:T(8,128)(2,1)S(1)}, s16[1033,128]{1,0:T(8,128)(2,1)S(1)}, u32[]{:S(2)}, u32[]{:S(2)}) %collective-permute-start) | collective-permute-done | bytes 264480 | tf_op jit(solution)/shard_map/ppermute | solution.py:12
  32.3 0.9 collective-permute-done.1
  33.4 0.7 abs_reduce_fusion.4
  34.3 0.6 fusion.232
  35.5 0.7 clamp_convert_fusion.4
  36.3 1.9 %collective-permute-start.2 = (s16[1033,128]{1,0:T(8,128)(2,1)S(1)}, s16[1033,128]{1,0:T(8,128)(2,1)S(1)}, u32[]{:S(2)}, u32[]{:S(2)}) collective-permute-start(s16[1033,128]{1,0:T(8,128)(2,1)S(1)} %get-tuple-element.28), channel_id=1, source_target_pairs={{0,16},{8,24},{16,32},{24,40},{32,48},{40,56},{48,64},{56,72},{64,... | collective-permute-start | bytes 793352 | tf_op jit(solution)/shard_map/ppermute | solution.py:12
  38.2 6.4 %collective-permute-start.3 = (s16[1033,128]{1,0:T(8,128)(2,1)S(1)}, s16[1033,128]{1,0:T(8,128)(2,1)S(1)}, u32[]{:S(2)}, u32[]{:S(2)}) collective-permute-start(s16[1033,128]{1,0:T(8,128)(2,1)S(1)} %get-tuple-element.29), channel_id=1, source_target_pairs={{16,0},{24,8},{32,16},{40,24},{48,32},{56,40},{64,48},{72,56},{80,... | collective-permute-start | bytes 793352 | tf_op jit(solution)/shard_map/ppermute | solution.py:12
  44.6 4.0 %collective-permute-done.2 = s16[1033,128]{1,0:T(8,128)(2,1)S(1)} collective-permute-done((s16[1033,128]{1,0:T(8,128)(2,1)S(1)}, s16[1033,128]{1,0:T(8,128)(2,1)S(1)}, u32[]{:S(2)}, u32[]{:S(2)}) %collective-permute-start.2) | collective-permute-done | bytes 264480 | tf_op jit(solution)/shard_map/ppermute | solution.py:12
  48.6 2.5 %collective-permute-done.3 = s16[1033,128]{1,0:T(8,128)(2,1)S(1)} collective-permute-done((s16[1033,128]{1,0:T(8,128)(2,1)S(1)}, s16[1033,128]{1,0:T(8,128)(2,1)S(1)}, u32[]{:S(2)}, u32[]{:S(2)}) %collective-permute-start.3) | collective-permute-done | bytes 264480 | tf_op jit(solution)/shard_map/ppermute | solution.py:12
  51.1 0.8 slice.185
  51.9 0.7 slice.190
  53.2 0.7 copy-done.24
  53.9 1.8 fusion.20
  56.3 0.7 slice_convert_fusion.8
  58.0 0.6 copy-done.29
  58.7 0.8 fusion.63
  59.5 5.3 %collective-permute-start.4 = (s16[1033,128]{1,0:T(8,128)(2,1)}, s16[1033,128]{1,0:T(8,128)(2,1)S(1)}, u32[]{:S(2)}, u32[]{:S(2)}) collective-permute-start(s16[1033,128]{1,0:T(8,128)(2,1)} %get-tuple-element.36), channel_id=1, source_target_pairs={{0,32},{8,40},{16,48},{24,56},{32,64},{40,72},{48,80},{56,88},{64,... | collective-permute-start | bytes 793352 | tf_op jit(solution)/shard_map/ppermute | solution.py:12
  64.8 4.9 %collective-permute-start.5 = (s16[1033,128]{1,0:T(8,128)(2,1)S(1)}, s16[1033,128]{1,0:T(8,128)(2,1)S(1)}, u32[]{:S(2)}, u32[]{:S(2)}) collective-permute-start(s16[1033,128]{1,0:T(8,128)(2,1)S(1)} %get-tuple-element.38), channel_id=1, source_target_pairs={{32,0},{40,8},{48,16},{56,24},{64,32},{72,40},{80,48},{88,56},{96,... | collective-permute-start | bytes 793352 | tf_op jit(solution)/shard_map/ppermute | solution.py:12
  69.7 0.7 fusion.79
  70.4 0.8 fusion.238
  71.1 0.9 collective-permute-done.4
  72.1 4.1 %collective-permute-done.5 = s16[1033,128]{1,0:T(8,128)(2,1)S(1)} collective-permute-done((s16[1033,128]{1,0:T(8,128)(2,1)S(1)}, s16[1033,128]{1,0:T(8,128)(2,1)S(1)}, u32[]{:S(2)}, u32[]{:S(2)}) %collective-permute-start.5) | collective-permute-done | bytes 264480 | tf_op jit(solution)/shard_map/ppermute | solution.py:12
  78.5 25.8 %collective-permute-start.6 = (s16[1033,128]{1,0:T(8,128)(2,1)}, s16[1033,128]{1,0:T(8,128)(2,1)S(1)}, u32[]{:S(2)}, u32[]{:S(2)}) collective-permute-start(s16[1033,128]{1,0:T(8,128)(2,1)} %get-tuple-element.36), channel_id=1, source_target_pairs={{0,8},{8,16},{16,24},{24,32},{32,40},{40,48},{48,56},{56,64},{64,7... | collective-permute-start | bytes 793352 | tf_op jit(solution)/shard_map/ppermute | solution.py:12
  104.3 3.8 %collective-permute-start.7 = (s16[1033,128]{1,0:T(8,128)(2,1)S(1)}, s16[1033,128]{1,0:T(8,128)(2,1)S(1)}, u32[]{:S(2)}, u32[]{:S(2)}) collective-permute-start(s16[1033,128]{1,0:T(8,128)(2,1)S(1)} %get-tuple-element.37), channel_id=1, source_target_pairs={{0,40},{8,48},{16,56},{24,64},{32,72},{40,80},{48,88},{56,96},{64,... | collective-permute-start | bytes 793352 | tf_op jit(solution)/shard_map/ppermute | solution.py:12
  108.1 5.5 %collective-permute-start.8 = (s16[1033,128]{1,0:T(8,128)(2,1)S(1)}, s16[1033,128]{1,0:T(8,128)(2,1)S(1)}, u32[]{:S(2)}, u32[]{:S(2)}) collective-permute-start(s16[1033,128]{1,0:T(8,128)(2,1)S(1)} %get-tuple-element.38), channel_id=1, source_target_pairs={{8,0},{16,8},{24,16},{32,24},{40,32},{48,40},{56,48},{64,56},{72,6... | collective-permute-start | bytes 793352 | tf_op jit(solution)/shard_map/ppermute | solution.py:12
  113.6 5.1 %collective-permute-start.9 = (s16[1033,128]{1,0:T(8,128)(2,1)S(1)}, s16[1033,128]{1,0:T(8,128)(2,1)}, u32[]{:S(2)}, u32[]{:S(2)}) collective-permute-start(s16[1033,128]{1,0:T(8,128)(2,1)S(1)} %get-tuple-element.39), channel_id=1, source_target_pairs={{40,0},{48,8},{56,16},{64,24},{72,32},{80,40},{88,48},{96,56},{104... | collective-permute-start | bytes 793352 | tf_op jit(solution)/shard_map/ppermute | solution.py:12
  118.6 2.0 %fusion.8 = (f32[16,128]{1,0:T(8,128)S(1)}, f32[16,128]{1,0:T(8,128)S(1)}, f32[128,128]{0,1:T(8,128)}) fusion(f32[128,128]{0,1:T(8,128)S(1)} %copy-done.12, f32[16,128]{1,0:T(8,128)S(1)} %reduce_window_sum.30, pred[128,128]{0,1:T(8,128)(4,1)S(1)} %copy-done.18, bf16[16,128,64]{1,2,0:T(8,128)(2,1)S(1)} %bitcast.213, f32[16,128,64]{1,2,0:T(8,128)S(1)} %bitcast.210, ...), kind=kOutput, calls=%fused_computation.22 | convolution fusion | flops 203534336 | bytes 966656 | tf_op jit(solution)/shard_map/hip,hjp->hij/dot_general | solution.py:155
  120.9 0.9 reduce_window_sum.31
  121.8 1.3 fusion.6
  123.1 13.8 %collective-permute-done.7 = s16[1033,128]{1,0:T(8,128)(2,1)S(1)} collective-permute-done((s16[1033,128]{1,0:T(8,128)(2,1)S(1)}, s16[1033,128]{1,0:T(8,128)(2,1)S(1)}, u32[]{:S(2)}, u32[]{:S(2)}) %collective-permute-start.7) | collective-permute-done | bytes 264480 | tf_op jit(solution)/shard_map/ppermute | solution.py:12
  136.9 9.4 %collective-permute-done.9 = s16[1033,128]{1,0:T(8,128)(2,1)} collective-permute-done((s16[1033,128]{1,0:T(8,128)(2,1)S(1)}, s16[1033,128]{1,0:T(8,128)(2,1)}, u32[]{:S(2)}, u32[]{:S(2)}) %collective-permute-start.9) | collective-permute-done | bytes 264480 | tf_op jit(solution)/shard_map/ppermute | solution.py:12
  146.4 0.6 multiply_exponential_fusion.3
  147.0 1.0 slice_convert_fusion.2
  148.0 1.3 multiply_exponential_fusion.2
  149.3 0.7 slice_convert_fusion.5
  150.1 0.6 multiply_exponential_fusion.1
  151.0 0.6 multiply_exponential_fusion
  151.6 1.1 slice_convert_fusion.4
  152.9 0.6 exponential_bitcast_fusion.1
  153.5 0.8 exp2.405
  154.3 0.7 exponential_bitcast_fusion
  155.0 0.6 copy-done.26
  155.6 1.3 convolution_bitcast_fusion.3
  157.2 1.3 convolution_bitcast_fusion.2
  158.8 0.7 maximum_bitcast_fusion
  159.5 9.8 %all-to-all-start.1 = ((f32[8,2,16,128]{3,2,1,0:T(8,128)}), f32[8,2,16,128]{3,2,1,0:T(8,128)S(1)}, u32[]{:S(2)}, u32[]{:S(2)}) async-start(f32[8,2,16,128]{3,2,1,0:T(8,128)} %maximum_bitcast_fusion), calls=%async_computation.1 | async-start | bytes 262144 | tf_op jit(solution)/shard_map/all_to_all | solution.py:69
  169.5 0.7 mul.480
  170.9 2.1 %multiply_reduce_fusion.1 = (f32[1024]{0:T(1024)S(1)}, f32[1024,128]{1,0:T(8,128)S(1)}, f32[1024,128]{1,0:T(8,128)S(1)}) fusion(f32[1024]{0:T(1024)S(1)} %copy-done.17, s16[1033,128]{1,0:T(8,128)(2,1)S(1)} %copy-done.4, f32[1024]{0:T(1024)S(1)} %mul.481, f32[1024]{0:T(1024)S(1)} %copy-done.16, s16[1033,128]{1,0:T(8,128)(2,1)S(1)} %copy-done.1, ...), kind=kLoop, calls=%fused_computation.64 | loop fusion | flops 1833984 | bytes 2125824 | tf_op jit(solution)/shard_map/reduce_sum | solution.py:175
  173.1 0.6 copy-done.35
  174.8 1.2 fusion.2
  176.4 1.9 %fusion.3 = f32[16,1,128]{2,1,0:T(1,128)S(1)} fusion(f32[16,128,1]{1,2,0:T(1,128)S(1)} %bitcast.251, f32[16,128]{1,0:T(8,128)S(1)} %reduce_window_sum.30, pred[128,128]{0,1:T(8,128)(4,1)S(1)} %copy-done.19), kind=kOutput, calls=%fused_computation.11 | convolution fusion | flops 3670016 | bytes 40960 | tf_op jit(solution)/shard_map/hij,hi->hj/dot_general | solution.py:169
  178.5 1.0 copy.39
  179.5 0.7 copy-done.34
  180.2 0.7 multiply_subtract_fusion
  180.9 0.6 slice_bitcast_fusion
  (172 shorter events, 13.2 us)
Async XLA Ops:
  0.6 11.0 %copy-start.9 = (bf16[128,1024]{1,0:T(8,128)(2,1)S(1)}, bf16[128,1024]{1,0:T(8,128)(2,1)}, u32[]{:S(2)}) copy-start(bf16[128,1024]{1,0:T(8,128)(2,1)} %param.8) | copy-start | bytes 786436
  2.0 10.7 %all-to-all-start = ((bf16[8,2,16,128]{3,2,1,0:T(8,128)(2,1)}), bf16[8,2,16,128]{3,2,1,0:T(8,128)(2,1)S(1)}, u32[]{:S(2)}, u32[]{:S(2)}) async-start(bf16[8,2,16,128]{3,2,1,0:T(8,128)(2,1)} %broadcast_in_dim.29), calls=%async_computation | async-start | bytes 131072 | tf_op jit(solution)/shard_map/all_to_all | solution.py:94
  8.2 0.7 copy-start.23
  8.9 2.0 %copy-start.7 = (f32[16,128]{1,0:T(8,128)S(1)}, f32[16,128]{1,0:T(8,128)}, u32[]{:S(2)}) copy-start(f32[16,128]{1,0:T(8,128)} %param.10) | copy-start | bytes 24580
  9.0 0.6 copy-start.20
  10.2 0.7 copy-start.33
  11.6 1.0 copy-start.11
  14.4 17.8 %collective-permute-start = (s16[1033,128]{1,0:T(8,128)(2,1)S(1)}, s16[1033,128]{1,0:T(8,128)(2,1)S(1)}, u32[]{:S(2)}, u32[]{:S(2)}) collective-permute-start(s16[1033,128]{1,0:T(8,128)(2,1)S(1)} %get-tuple-element.24), channel_id=1, source_target_pairs={{0,8},{8,16},{16,24},{24,32},{32,40},{40,48},{48,56},{56,64},{64,7... | collective-permute-start | bytes 793352 | tf_op jit(solution)/shard_map/ppermute | solution.py:12
  18.0 15.2 %collective-permute-start.1 = (s16[1033,128]{1,0:T(8,128)(2,1)S(1)}, s16[1033,128]{1,0:T(8,128)(2,1)S(1)}, u32[]{:S(2)}, u32[]{:S(2)}) collective-permute-start(s16[1033,128]{1,0:T(8,128)(2,1)S(1)} %get-tuple-element.25), channel_id=1, source_target_pairs={{8,0},{16,8},{24,16},{32,24},{40,32},{48,40},{56,48},{64,56},{72,6... | collective-permute-start | bytes 793352 | tf_op jit(solution)/shard_map/ppermute | solution.py:12
  34.9 0.5 copy-start.28
  34.9 0.6 copy-start.30
  36.3 12.3 %collective-permute-start.2 = (s16[1033,128]{1,0:T(8,128)(2,1)S(1)}, s16[1033,128]{1,0:T(8,128)(2,1)S(1)}, u32[]{:S(2)}, u32[]{:S(2)}) collective-permute-start(s16[1033,128]{1,0:T(8,128)(2,1)S(1)} %get-tuple-element.28), channel_id=1, source_target_pairs={{0,16},{8,24},{16,32},{24,40},{32,48},{40,56},{48,64},{56,72},{64,... | collective-permute-start | bytes 793352 | tf_op jit(solution)/shard_map/ppermute | solution.py:12
  38.2 12.9 %collective-permute-start.3 = (s16[1033,128]{1,0:T(8,128)(2,1)S(1)}, s16[1033,128]{1,0:T(8,128)(2,1)S(1)}, u32[]{:S(2)}, u32[]{:S(2)}) collective-permute-start(s16[1033,128]{1,0:T(8,128)(2,1)S(1)} %get-tuple-element.29), channel_id=1, source_target_pairs={{16,0},{24,8},{32,16},{40,24},{48,32},{56,40},{64,48},{72,56},{80,... | collective-permute-start | bytes 793352 | tf_op jit(solution)/shard_map/ppermute | solution.py:12
  51.1 1.5 copy-start.8
  53.2 0.7 copy-start.24
  53.2 0.7 copy-start.25
  57.0 0.7 copy-start.31
  57.0 0.7 copy-start.32
  58.0 0.6 copy-start.29
  59.5 10.2 %copy-start.21 = (s32[128]{0:T(128)S(1)}, s32[128]{0:T(128)}, u32[]{:S(2)}) copy-start(s32[128]{0:T(128)} %copy-done.20) | copy-start | bytes 1540
  59.5 12.6 %collective-permute-start.4 = (s16[1033,128]{1,0:T(8,128)(2,1)}, s16[1033,128]{1,0:T(8,128)(2,1)S(1)}, u32[]{:S(2)}, u32[]{:S(2)}) collective-permute-start(s16[1033,128]{1,0:T(8,128)(2,1)} %get-tuple-element.36), channel_id=1, source_target_pairs={{0,32},{8,40},{16,48},{24,56},{32,64},{40,72},{48,80},{56,88},{64,... | collective-permute-start | bytes 793352 | tf_op jit(solution)/shard_map/ppermute | solution.py:12
  64.8 11.4 %collective-permute-start.5 = (s16[1033,128]{1,0:T(8,128)(2,1)S(1)}, s16[1033,128]{1,0:T(8,128)(2,1)S(1)}, u32[]{:S(2)}, u32[]{:S(2)}) collective-permute-start(s16[1033,128]{1,0:T(8,128)(2,1)S(1)} %get-tuple-element.38), channel_id=1, source_target_pairs={{32,0},{40,8},{48,16},{56,24},{64,32},{72,40},{80,48},{88,56},{96,... | collective-permute-start | bytes 793352 | tf_op jit(solution)/shard_map/ppermute | solution.py:12
  78.4 40.2 %copy-start.12 = (f32[128,128]{0,1:T(8,128)S(1)}, f32[128,128]{0,1:T(8,128)}, u32[]{:S(2)}) copy-start(f32[128,128]{0,1:T(8,128)} %fusion.238) | copy-start | bytes 196612
  78.4 40.2 %copy-start.18 = (pred[128,128]{0,1:T(8,128)(4,1)S(1)}, pred[128,128]{0,1:T(8,128)(4,1)}, u32[]{:S(2)}) copy-start(pred[128,128]{0,1:T(8,128)(4,1)} %fusion.79) | copy-start | bytes 49156
  78.5 44.6 %collective-permute-start.6 = (s16[1033,128]{1,0:T(8,128)(2,1)}, s16[1033,128]{1,0:T(8,128)(2,1)S(1)}, u32[]{:S(2)}, u32[]{:S(2)}) collective-permute-start(s16[1033,128]{1,0:T(8,128)(2,1)} %get-tuple-element.36), channel_id=1, source_target_pairs={{0,8},{8,16},{16,24},{24,32},{32,40},{40,48},{48,56},{56,64},{64,7... | collective-permute-start | bytes 793352 | tf_op jit(solution)/shard_map/ppermute | solution.py:12
  104.3 32.6 %collective-permute-start.7 = (s16[1033,128]{1,0:T(8,128)(2,1)S(1)}, s16[1033,128]{1,0:T(8,128)(2,1)S(1)}, u32[]{:S(2)}, u32[]{:S(2)}) collective-permute-start(s16[1033,128]{1,0:T(8,128)(2,1)S(1)} %get-tuple-element.37), channel_id=1, source_target_pairs={{0,40},{8,48},{16,56},{24,64},{32,72},{40,80},{48,88},{56,96},{64,... | collective-permute-start | bytes 793352 | tf_op jit(solution)/shard_map/ppermute | solution.py:12
  108.1 28.9 %collective-permute-start.8 = (s16[1033,128]{1,0:T(8,128)(2,1)S(1)}, s16[1033,128]{1,0:T(8,128)(2,1)S(1)}, u32[]{:S(2)}, u32[]{:S(2)}) collective-permute-start(s16[1033,128]{1,0:T(8,128)(2,1)S(1)} %get-tuple-element.38), channel_id=1, source_target_pairs={{8,0},{16,8},{24,16},{32,24},{40,32},{48,40},{56,48},{64,56},{72,6... | collective-permute-start | bytes 793352 | tf_op jit(solution)/shard_map/ppermute | solution.py:12
  113.6 32.7 %collective-permute-start.9 = (s16[1033,128]{1,0:T(8,128)(2,1)S(1)}, s16[1033,128]{1,0:T(8,128)(2,1)}, u32[]{:S(2)}, u32[]{:S(2)}) collective-permute-start(s16[1033,128]{1,0:T(8,128)(2,1)S(1)} %get-tuple-element.39), channel_id=1, source_target_pairs={{40,0},{48,8},{56,16},{64,24},{72,32},{80,40},{88,48},{96,56},{104... | collective-permute-start | bytes 793352 | tf_op jit(solution)/shard_map/ppermute | solution.py:12
  123.1 27.0 %copy-start = (s16[1033,128]{1,0:T(8,128)(2,1)}, s16[1033,128]{1,0:T(8,128)(2,1)S(1)}, u32[]{:S(2)}) copy-start(s16[1033,128]{1,0:T(8,128)(2,1)S(1)} %collective-permute-done.6) | copy-start | bytes 793348
  136.9 9.4 %copy-start.2 = (s16[1033,128]{1,0:T(8,128)(2,1)}, s16[1033,128]{1,0:T(8,128)(2,1)S(1)}, u32[]{:S(2)}) copy-start(s16[1033,128]{1,0:T(8,128)(2,1)S(1)} %collective-permute-done.7) | copy-start | bytes 793348
  136.9 9.5 %copy-start.5 = (s16[1033,128]{1,0:T(8,128)(2,1)}, s16[1033,128]{1,0:T(8,128)(2,1)S(1)}, u32[]{:S(2)}) copy-start(s16[1033,128]{1,0:T(8,128)(2,1)S(1)} %collective-permute-done.8) | copy-start | bytes 793348
  150.0 1.0 copy-start.3
  155.0 2.1 %copy-start.22 = (f32[16]{0:T(128)}, f32[16]{0:T(128)S(1)}, u32[]{:S(2)}) copy-start(f32[16]{0:T(128)S(1)} %exponential_bitcast_fusion) | copy-start | bytes 196
  155.0 0.6 copy-start.26
  155.6 1.3 copy-start.10
  157.2 12.2 %copy-start.27 = (f32[16]{0:T(128)S(1)}, f32[16]{0:T(128)}, u32[]{:S(2)}) copy-start(f32[16]{0:T(128)} %exponential_bitcast_fusion.1) | copy-start | bytes 196
  157.2 13.1 %copy-start.16 = (f32[1024]{0:T(1024)S(1)}, f32[1024]{0:T(1024)}, u32[]{:S(2)}) copy-start(f32[1024]{0:T(1024)} %get-tuple-element.91) | copy-start | bytes 12292
  157.2 13.1 %copy-start.17 = (f32[1024]{0:T(1024)S(1)}, f32[1024]{0:T(1024)}, u32[]{:S(2)}) copy-start(f32[1024]{0:T(1024)} %get-tuple-element.93) | copy-start | bytes 12292
  158.5 11.7 %copy-start.6 = (s16[1033,128]{1,0:T(8,128)(2,1)S(1)}, s16[1033,128]{1,0:T(8,128)(2,1)}, u32[]{:S(2)}) copy-start(s16[1033,128]{1,0:T(8,128)(2,1)} %copy-done.5) | copy-start | bytes 793348
  158.8 11.5 %copy-start.1 = (s16[1033,128]{1,0:T(8,128)(2,1)S(1)}, s16[1033,128]{1,0:T(8,128)(2,1)}, u32[]{:S(2)}) copy-start(s16[1033,128]{1,0:T(8,128)(2,1)} %copy-done) | copy-start | bytes 793348
  158.8 11.5 %copy-start.4 = (s16[1033,128]{1,0:T(8,128)(2,1)S(1)}, s16[1033,128]{1,0:T(8,128)(2,1)}, u32[]{:S(2)}) copy-start(s16[1033,128]{1,0:T(8,128)(2,1)} %copy-done.2) | copy-start | bytes 793348
  159.5 21.4 %all-to-all-start.1 = ((f32[8,2,16,128]{3,2,1,0:T(8,128)}), f32[8,2,16,128]{3,2,1,0:T(8,128)S(1)}, u32[]{:S(2)}, u32[]{:S(2)}) async-start(f32[8,2,16,128]{3,2,1,0:T(8,128)} %maximum_bitcast_fusion), calls=%async_computation.1 | async-start | bytes 262144 | tf_op jit(solution)/shard_map/all_to_all | solution.py:69
  170.2 0.7 copy-start.15
  170.3 0.7 copy-start.14
  173.1 0.7 copy-start.35
  174.1 0.7 copy-start.19
  178.5 1.0 copy-start.13
  179.5 0.7 copy-start.34

commit v6 on v5

--- a/solution.py
+++ b/solution.py
@@ -120,31 +120,49 @@
     low = reach & -reach
     high = reach - low
     assert high > 0 and high & (high - 1) == 0 and low < high
-    shape = local_state.shape
+    spans = []
+    while 2 ** len(spans) < high:
+        spans.append(2 ** len(spans))
     decay = jnp.where(seg[-1] == 0, jnp.maximum(logc[:, -1], FLOOR), FLOOR)
-    fwd = (local_state, decay)
-    bwd = (local_adj, decay)
-    span = 1
-    kept = {}
-    while span < high:
-        kept[span] = (fwd, bwd)
-        got_f, got_b = shift_pair(fwd, bwd, span)
-        fwd = combine(fwd, got_f)
-        bwd = combine(bwd, got_b)
-        span *= 2
-    near_f, near_b = kept[low]
-    sends = lax.optimization_barrier((pack(*near_f), pack(*fwd), pack(*near_b), pack(*bwd)))
-    got = lax.optimization_barrier(
-        (
-            from_behind(sends[0], "context", 1),
-            from_behind(sends[1], "context", low + 1),
-            from_behind(sends[2], "context", -1),
-            from_behind(sends[3], "context", -low - 1),
+    groups = 2
+    size = heads // groups
+    live = []
+    for g in range(groups):
+        part = slice(g * size, (g + 1) * size)
+        live.append({"fwd": (local_state[part], decay[part]), "bwd": (local_adj[part], decay[part])})
+    shape = live[0]["fwd"][0].shape
+    for step in range(len(spans) + groups):
+        sends = []
+        for g in range(groups):
+            r = step - g
+            if 0 <= r < len(spans):
+                own = live[g]
+                own["kept" + str(spans[r])] = (own["fwd"], own["bwd"])
+                sends.append((g, r, pack(*own["fwd"]), spans[r]))
+                sends.append((g, r, pack(*own["bwd"]), -spans[r]))
+            elif r == len(spans):
+                own = live[g]
+                near_f, near_b = own["kept" + str(low)]
+                sends.append((g, r, pack(*near_f), 1))
+                sends.append((g, r, pack(*own["fwd"]), low + 1))
+                sends.append((g, r, pack(*near_b), -1))
+                sends.append((g, r, pack(*own["bwd"]), -low - 1))
+        packed = lax.optimization_barrier([item[2] for item in sends])
+        got = lax.optimization_barrier(
+            [from_behind(p, "context", item[3]) for p, item in zip(packed, sends)]
         )
-    )
-    got = [unpack(g, shape) for g in got]
-    s_in = combine(got[0], got[1])[0]
-    g_in = combine(got[2], got[3])[0]
+        got = [unpack(x, shape) for x in got]
+        for g in range(groups):
+            mine = [x for x, item in zip(got, sends) if item[0] == g]
+            r = step - g
+            if 0 <= r < len(spans):
+                live[g]["fwd"] = combine(live[g]["fwd"], mine[0])
+                live[g]["bwd"] = combine(live[g]["bwd"], mine[1])
+            elif r == len(spans):
+                live[g]["s_in"] = combine(mine[0], mine[1])[0]
+                live[g]["g_in"] = combine(mine[2], mine[3])[0]
+    s_in = jnp.concatenate([own["s_in"] for own in live])
+    g_in = jnp.concatenate([own["g_in"] for own in live])
 
     index = jnp.arange(length)
     keep = (index[:, None] >= index[None, :]) & (seg[:, None] == seg[None, :])

time: 182 us -> 208 us (1.14)
  the two profiles are of different devices: /device:TPU:15 before, /device:TPU:13 now
where the time goes in v6:
time: 208 us; the launch traced here: 206 us
  starting transfers between devices  120 us (58%)
  waiting for transfers between devices  27.5 us (13%)
  local copies, waits for them, and re-layouts  27.1 us (13%)
  other arithmetic  18.7 us (9%)
  matrix products  10.7 us (5%)
  between operations  2.6 us (1%)
    ppermute x20, starting transfers between devices, from_behind(): return lax.ppermute(x, axis, pairs)  98.1 us
    ppermute x20, waiting for transfers between devices, from_behind(): return lax.ppermute(x, axis, pairs)  27.5 us
    unnamed x128, local copies, waits for them, and re-layouts  18 us
    all_to_all x1, starting transfers between devices, scatter_sum(): got = lax.all_to_all(parts, axis, 0, 0, tiled=True)  16.5 us
    all_to_all x1, starting transfers between devices, local(): lax.all_to_all(jnp.broadcast_to(piece, (count,) + piece.shape), 'tensor',...  5.23 us
  transfers between devices with their start and end apart: 22, of which 8 were waited for; matrix products, arithmetic and copies ran while one was open for 7% of the time, Pallas kernels for 0%

profile of v6, /device:TPU:13, one launch (start us, length us, event | category | flops | bytes accessed | tf_op | source)
XLA Modules:
  0.0 206.4 jit_solution(5061761348931848558)
XLA Ops:
  0.6 0.7 pad_maximum_fusion.6
  1.4 0.6 broadcast_in_dim.39
  2.0 5.2 %all-to-all-start = ((bf16[8,2,16,128]{3,2,1,0:T(8,128)(2,1)}), bf16[8,2,16,128]{3,2,1,0:T(8,128)(2,1)S(1)}, u32[]{:S(2)}, u32[]{:S(2)}) async-start(bf16[8,2,16,128]{3,2,1,0:T(8,128)(2,1)} %broadcast_in_dim.39), calls=%async_computation | async-start | bytes 131072 | tf_op jit(solution)/shard_map/all_to_all | solution.py:94
  7.3 0.7 copy.32
  8.2 0.6 copy-done.44
  9.6 0.6 compare_convert_fusion
  11.8 0.8 copy-done.25
  14.5 3.5 %collective-permute-start = (s16[517,128]{1,0:T(8,128)(2,1)S(1)}, s16[517,128]{1,0:T(8,128)(2,1)S(1)}, u32[]{:S(2)}, u32[]{:S(2)}) collective-permute-start(s16[517,128]{1,0:T(8,128)(2,1)S(1)} %get-tuple-element.44), channel_id=1, source_target_pairs={{0,8},{8,16},{16,24},{24,32},{32,40},{40,48},{48,56},{56,64},{64,7... | collective-permute-start | bytes 397064 | tf_op jit(solution)/shard_map/ppermute | solution.py:12
  18.0 9.5 %collective-permute-start.1 = (s16[517,128]{1,0:T(8,128)(2,1)S(1)}, s16[517,128]{1,0:T(8,128)(2,1)S(1)}, u32[]{:S(2)}, u32[]{:S(2)}) collective-permute-start(s16[517,128]{1,0:T(8,128)(2,1)S(1)} %get-tuple-element.45), channel_id=1, source_target_pairs={{8,0},{16,8},{24,16},{32,24},{40,32},{48,40},{56,48},{64,56},{72,6... | collective-permute-start | bytes 397064 | tf_op jit(solution)/shard_map/ppermute | solution.py:12
  27.5 1.7 collective-permute-done
  29.2 0.9 collective-permute-done.1
  34.0 1.9 collective-permute-start.2
  36.0 6.4 %collective-permute-start.3 = (s16[517,128]{1,0:T(8,128)(2,1)S(1)}, s16[517,128]{1,0:T(8,128)(2,1)S(1)}, u32[]{:S(2)}, u32[]{:S(2)}) collective-permute-start(s16[517,128]{1,0:T(8,128)(2,1)S(1)} %fusion.81), channel_id=1, source_target_pairs={{16,0},{24,8},{32,16},{40,24},{48,32},{56,40},{64,48},{72,56},{80,... | collective-permute-start | bytes 397064 | tf_op jit(solution)/shard_map/ppermute | solution.py:12
  42.3 2.9 %collective-permute-start.4 = (s16[517,128]{1,0:T(8,128)(2,1)S(1)}, s16[517,128]{1,0:T(8,128)(2,1)S(1)}, u32[]{:S(2)}, u32[]{:S(2)}) collective-permute-start(s16[517,128]{1,0:T(8,128)(2,1)S(1)} %get-tuple-element.50), channel_id=1, source_target_pairs={{0,8},{8,16},{16,24},{24,32},{32,40},{40,48},{48,56},{56,64},{64,7... | collective-permute-start | bytes 397064 | tf_op jit(solution)/shard_map/ppermute | solution.py:12
  45.3 4.5 %collective-permute-start.5 = (s16[517,128]{1,0:T(8,128)(2,1)S(1)}, s16[517,128]{1,0:T(8,128)(2,1)S(1)}, u32[]{:S(2)}, u32[]{:S(2)}) collective-permute-start(s16[517,128]{1,0:T(8,128)(2,1)S(1)} %get-tuple-element.51), channel_id=1, source_target_pairs={{8,0},{16,8},{24,16},{32,24},{40,32},{48,40},{56,48},{64,56},{72,6... | collective-permute-start | bytes 397064 | tf_op jit(solution)/shard_map/ppermute | solution.py:12
  49.7 0.7 fusion.92
  50.5 1.2 collective-permute-done.5
  51.7 0.6 copy-done.2
  52.6 0.7 fusion.384
  54.4 0.8 copy-done.1
  57.1 0.7 copy-done.18
  59.4 0.6 copy-done.50
  60.9 4.4 %collective-permute-start.6 = (s16[517,128]{1,0:T(8,128)(2,1)S(1)}, s16[517,128]{1,0:T(8,128)(2,1)S(1)}, u32[]{:S(2)}, u32[]{:S(2)}) collective-permute-start(s16[517,128]{1,0:T(8,128)(2,1)S(1)} %get-tuple-element.64), channel_id=1, source_target_pairs={{0,32},{8,40},{16,48},{24,56},{32,64},{40,72},{48,80},{56,88},{64,... | collective-permute-start | bytes 397064 | tf_op jit(solution)/shard_map/ppermute | solution.py:12
  65.4 5.7 %collective-permute-start.7 = (s16[517,128]{1,0:T(8,128)(2,1)S(1)}, s16[517,128]{1,0:T(8,128)(2,1)S(1)}, u32[]{:S(2)}, u32[]{:S(2)}) collective-permute-start(s16[517,128]{1,0:T(8,128)(2,1)S(1)} %get-tuple-element.66), channel_id=1, source_target_pairs={{32,0},{40,8},{48,16},{56,24},{64,32},{72,40},{80,48},{88,56},{96,... | collective-permute-start | bytes 397064 | tf_op jit(solution)/shard_map/ppermute | solution.py:12
  71.0 1.9 collective-permute-start.8
  73.0 6.4 %collective-permute-start.9 = (s16[517,128]{1,0:T(8,128)(2,1)S(1)}, s16[517,128]{1,0:T(8,128)(2,1)S(1)}, u32[]{:S(2)}, u32[]{:S(2)}) collective-permute-start(s16[517,128]{1,0:T(8,128)(2,1)S(1)} %get-tuple-element.59), channel_id=1, source_target_pairs={{16,0},{24,8},{32,16},{40,24},{48,32},{56,40},{64,48},{72,56},{80,... | collective-permute-start | bytes 397064 | tf_op jit(solution)/shard_map/ppermute | solution.py:12
  79.3 0.8 fusion.399
  80.8 2.5 %collective-permute-done.9 = s16[517,128]{1,0:T(8,128)(2,1)S(1)} collective-permute-done((s16[517,128]{1,0:T(8,128)(2,1)S(1)}, s16[517,128]{1,0:T(8,128)(2,1)S(1)}, u32[]{:S(2)}, u32[]{:S(2)}) %collective-permute-start.9) | collective-permute-done | bytes 132384 | tf_op jit(solution)/shard_map/ppermute | solution.py:12
  83.3 0.7 copy-done.32
  84.4 0.7 reduce_max.215
  86.0 0.7 reduce_max.213
  89.9 0.7 copy-done.16
  91.8 0.6 copy-done.56
  92.6 0.6 copy-done.39
  93.9 0.6 copy-done.54
  96.3 0.7 fusion.88
  97.0 0.8 fusion.89
  97.9 9.1 %collective-permute-start.10 = (s16[517,128]{1,0:T(8,128)(2,1)S(1)}, s16[517,128]{1,0:T(8,128)(2,1)S(1)}, u32[]{:S(2)}, u32[]{:S(2)}) collective-permute-start(s16[517,128]{1,0:T(8,128)(2,1)S(1)} %copy-done.29), channel_id=1, source_target_pairs={{0,8},{8,16},{16,24},{24,32},{32,40},{40,48},{48,56},{56,64},{64,7... | collective-permute-start | bytes 397064 | tf_op jit(solution)/shard_map/ppermute | solution.py:12
  107.1 1.5 fusion.8
  109.1 5.5 %collective-permute-start.11 = (s16[517,128]{1,0:T(8,128)(2,1)}, s16[517,128]{1,0:T(8,128)(2,1)S(1)}, u32[]{:S(2)}, u32[]{:S(2)}) collective-permute-start(s16[517,128]{1,0:T(8,128)(2,1)} %get-tuple-element.65), channel_id=1, source_target_pairs={{0,40},{8,48},{16,56},{24,64},{32,72},{40,80},{48,88},{56,96},{64,... | collective-permute-start | bytes 397064 | tf_op jit(solution)/shard_map/ppermute | solution.py:12
  114.7 5.5 %collective-permute-start.12 = (s16[517,128]{1,0:T(8,128)(2,1)S(1)}, s16[517,128]{1,0:T(8,128)(2,1)S(1)}, u32[]{:S(2)}, u32[]{:S(2)}) collective-permute-start(s16[517,128]{1,0:T(8,128)(2,1)S(1)} %copy-done.27), channel_id=1, source_target_pairs={{8,0},{16,8},{24,16},{32,24},{40,32},{48,40},{56,48},{64,56},{72,6... | collective-permute-start | bytes 397064 | tf_op jit(solution)/shard_map/ppermute | solution.py:12
  120.2 3.1 %collective-permute-start.13 = (s16[517,128]{1,0:T(8,128)(2,1)}, s16[517,128]{1,0:T(8,128)(2,1)S(1)}, u32[]{:S(2)}, u32[]{:S(2)}) collective-permute-start(s16[517,128]{1,0:T(8,128)(2,1)} %get-tuple-element.67), channel_id=1, source_target_pairs={{40,0},{48,8},{56,16},{64,24},{72,32},{80,40},{88,48},{96,56},{104... | collective-permute-start | bytes 397064 | tf_op jit(solution)/shard_map/ppermute | solution.py:12
  123.3 6.2 %collective-permute-start.14 = (s16[517,128]{1,0:T(8,128)(2,1)}, s16[517,128]{1,0:T(8,128)(2,1)S(1)}, u32[]{:S(2)}, u32[]{:S(2)}) collective-permute-start(s16[517,128]{1,0:T(8,128)(2,1)} %fusion.88), channel_id=1, source_target_pairs={{0,32},{8,40},{16,48},{24,56},{32,64},{40,72},{48,80},{56,88},{64,... | collective-permute-start | bytes 397064 | tf_op jit(solution)/shard_map/ppermute | solution.py:12
  129.5 4.1 %collective-permute-start.15 = (s16[517,128]{1,0:T(8,128)(2,1)}, s16[517,128]{1,0:T(8,128)(2,1)S(1)}, u32[]{:S(2)}, u32[]{:S(2)}) collective-permute-start(s16[517,128]{1,0:T(8,128)(2,1)} %get-tuple-element.76), channel_id=1, source_target_pairs={{32,0},{40,8},{48,16},{56,24},{64,32},{72,40},{80,48},{88,56},{96,... | collective-permute-start | bytes 397064 | tf_op jit(solution)/shard_map/ppermute | solution.py:12
  133.6 1.3 fusion.6
  135.0 6.4 %collective-permute-done.14 = s16[517,128]{1,0:T(8,128)(2,1)S(1)} collective-permute-done((s16[517,128]{1,0:T(8,128)(2,1)}, s16[517,128]{1,0:T(8,128)(2,1)S(1)}, u32[]{:S(2)}, u32[]{:S(2)}) %collective-permute-start.14) | collective-permute-done | bytes 132384 | tf_op jit(solution)/shard_map/ppermute | solution.py:12
  141.4 11.9 %collective-permute-done.15 = s16[517,128]{1,0:T(8,128)(2,1)S(1)} collective-permute-done((s16[517,128]{1,0:T(8,128)(2,1)}, s16[517,128]{1,0:T(8,128)(2,1)S(1)}, u32[]{:S(2)}, u32[]{:S(2)}) %collective-permute-start.15) | collective-permute-done | bytes 132384 | tf_op jit(solution)/shard_map/ppermute | solution.py:12
  155.5 2.0 collective-permute-start.16
  157.5 1.9 collective-permute-start.17
  159.5 6.5 %collective-permute-start.18 = (s16[517,128]{1,0:T(8,128)(2,1)}, s16[517,128]{1,0:T(8,128)(2,1)S(1)}, u32[]{:S(2)}, u32[]{:S(2)}) collective-permute-start(s16[517,128]{1,0:T(8,128)(2,1)} %get-tuple-element.76), channel_id=1, source_target_pairs={{8,0},{16,8},{24,16},{32,24},{40,32},{48,40},{56,48},{64,56},{72,6... | collective-permute-start | bytes 397064 | tf_op jit(solution)/shard_map/ppermute | solution.py:12
  166.0 7.1 %collective-permute-start.19 = (s16[517,128]{1,0:T(8,128)(2,1)S(1)}, s16[517,128]{1,0:T(8,128)(2,1)S(1)}, u32[]{:S(2)}, u32[]{:S(2)}) collective-permute-start(s16[517,128]{1,0:T(8,128)(2,1)S(1)} %get-tuple-element.77), channel_id=1, source_target_pairs={{40,0},{48,8},{56,16},{64,24},{72,32},{80,40},{88,48},{96,56},{104... | collective-permute-start | bytes 397064 | tf_op jit(solution)/shard_map/ppermute | solution.py:12
  173.6 0.7 slice-done.6
  174.6 2.2 %collective-permute-done.19 = s16[517,128]{1,0:T(8,128)(2,1)S(1)} collective-permute-done((s16[517,128]{1,0:T(8,128)(2,1)S(1)}, s16[517,128]{1,0:T(8,128)(2,1)S(1)}, u32[]{:S(2)}, u32[]{:S(2)}) %collective-permute-start.19) | collective-permute-done | bytes 132384 | tf_op jit(solution)/shard_map/ppermute | solution.py:12
  176.8 0.6 copy-done.14
  178.7 1.0 convolution_bitcast_fusion.3
  179.9 1.0 convolution_bitcast_fusion.2
  181.9 0.7 maximum_bitcast_fusion
  182.6 16.5 %all-to-all-start.1 = ((f32[8,2,16,128]{3,2,1,0:T(8,128)}), f32[8,2,16,128]{3,2,1,0:T(8,128)S(1)}, u32[]{:S(2)}, u32[]{:S(2)}) async-start(f32[8,2,16,128]{3,2,1,0:T(8,128)} %maximum_bitcast_fusion), calls=%async_computation.1 | async-start | bytes 262144 | tf_op jit(solution)/shard_map/all_to_all | solution.py:69
  199.1 1.9 fusion.3
  201.0 0.7 copy-done.62
  202.3 1.2 fusion.2
  203.5 1.0 copy.39
  204.5 0.7 copy-done.61
  205.2 0.7 multiply_subtract_fusion
  (350 shorter events, 29.1 us)
Async XLA Ops:
  0.6 11.0 %copy-start.24 = (bf16[128,1024]{1,0:T(8,128)(2,1)S(1)}, bf16[128,1024]{1,0:T(8,128)(2,1)}, u32[]{:S(2)}) copy-start(bf16[128,1024]{1,0:T(8,128)(2,1)} %param.8) | copy-start | bytes 786436
  2.0 10.7 %all-to-all-start = ((bf16[8,2,16,128]{3,2,1,0:T(8,128)(2,1)}), bf16[8,2,16,128]{3,2,1,0:T(8,128)(2,1)S(1)}, u32[]{:S(2)}, u32[]{:S(2)}) async-start(bf16[8,2,16,128]{3,2,1,0:T(8,128)(2,1)} %broadcast_in_dim.39), calls=%async_computation | async-start | bytes 131072 | tf_op jit(solution)/shard_map/all_to_all | solution.py:94
  8.9 2.0 copy-start.23
  11.6 1.0 copy-start.25
  14.5 14.7 %collective-permute-start = (s16[517,128]{1,0:T(8,128)(2,1)S(1)}, s16[517,128]{1,0:T(8,128)(2,1)S(1)}, u32[]{:S(2)}, u32[]{:S(2)}) collective-permute-start(s16[517,128]{1,0:T(8,128)(2,1)S(1)} %get-tuple-element.44), channel_id=1, source_target_pairs={{0,8},{8,16},{16,24},{24,32},{32,40},{40,48},{48,56},{56,64},{64,7... | collective-permute-start | bytes 397064 | tf_op jit(solution)/shard_map/ppermute | solution.py:12
  18.0 12.0 %collective-permute-start.1 = (s16[517,128]{1,0:T(8,128)(2,1)S(1)}, s16[517,128]{1,0:T(8,128)(2,1)S(1)}, u32[]{:S(2)}, u32[]{:S(2)}) collective-permute-start(s16[517,128]{1,0:T(8,128)(2,1)S(1)} %get-tuple-element.45), channel_id=1, source_target_pairs={{8,0},{16,8},{24,16},{32,24},{40,32},{48,40},{56,48},{64,56},{72,6... | collective-permute-start | bytes 397064 | tf_op jit(solution)/shard_map/ppermute | solution.py:12
  30.1 0.9 slice-start.3
  31.0 1.0 copy-start.7
  32.0 1.6 copy-start.5
  34.0 16.4 %collective-permute-start.2 = (s16[517,128]{1,0:T(8,128)(2,1)S(1)}, s16[517,128]{1,0:T(8,128)(2,1)S(1)}, u32[]{:S(2)}, u32[]{:S(2)}) collective-permute-start(s16[517,128]{1,0:T(8,128)(2,1)S(1)} %get-tuple-element.48), channel_id=1, source_target_pairs={{0,16},{8,24},{16,32},{24,40},{32,48},{40,56},{48,64},{56,72},{64,... | collective-permute-start | bytes 397064 | tf_op jit(solution)/shard_map/ppermute | solution.py:12
  36.0 14.5 %collective-permute-start.3 = (s16[517,128]{1,0:T(8,128)(2,1)S(1)}, s16[517,128]{1,0:T(8,128)(2,1)S(1)}, u32[]{:S(2)}, u32[]{:S(2)}) collective-permute-start(s16[517,128]{1,0:T(8,128)(2,1)S(1)} %fusion.81), channel_id=1, source_target_pairs={{16,0},{24,8},{32,16},{40,24},{48,32},{56,40},{64,48},{72,56},{80,... | collective-permute-start | bytes 397064 | tf_op jit(solution)/shard_map/ppermute | solution.py:12
  42.3 8.1 %collective-permute-start.4 = (s16[517,128]{1,0:T(8,128)(2,1)S(1)}, s16[517,128]{1,0:T(8,128)(2,1)S(1)}, u32[]{:S(2)}, u32[]{:S(2)}) collective-permute-start(s16[517,128]{1,0:T(8,128)(2,1)S(1)} %get-tuple-element.50), channel_id=1, source_target_pairs={{0,8},{8,16},{16,24},{24,32},{32,40},{40,48},{48,56},{56,64},{64,7... | collective-permute-start | bytes 397064 | tf_op jit(solution)/shard_map/ppermute | solution.py:12
  45.3 6.4 %collective-permute-start.5 = (s16[517,128]{1,0:T(8,128)(2,1)S(1)}, s16[517,128]{1,0:T(8,128)(2,1)S(1)}, u32[]{:S(2)}, u32[]{:S(2)}) collective-permute-start(s16[517,128]{1,0:T(8,128)(2,1)S(1)} %get-tuple-element.51), channel_id=1, source_target_pairs={{8,0},{16,8},{24,16},{32,24},{40,32},{48,40},{56,48},{64,56},{72,6... | collective-permute-start | bytes 397064 | tf_op jit(solution)/shard_map/ppermute | solution.py:12
  50.4 2.0 copy-start.17
  50.4 1.9 copy-start.30
  50.5 1.9 copy-start
  52.4 0.9 slice-start
  52.4 1.0 slice-start.1
  53.3 4.6 %copy-start.45 = (f32[8]{0:T(128)}, f32[8]{0:T(128)S(1)}, u32[]{:S(2)}) copy-start(f32[8]{0:T(128)S(1)} %get-tuple-element.175) | copy-start | bytes 100
  53.3 7.5 %copy-start.47 = (f32[8]{0:T(128)}, f32[8]{0:T(128)S(1)}, u32[]{:S(2)}) copy-start(f32[8]{0:T(128)S(1)} %get-tuple-element.120) | copy-start | bytes 100
  54.3 1.0 slice-start.12
  55.6 0.9 copy-start.3
  58.6 25.4 %copy-start.40 = (f32[8]{0:T(128)}, f32[8]{0:T(128)S(1)}, u32[]{:S(2)}) copy-start(f32[8]{0:T(128)S(1)} %get-tuple-element.121) | copy-start | bytes 100
  60.1 25.6 %copy-start.38 = (f32[8]{0:T(128)}, f32[8]{0:T(128)S(1)}, u32[]{:S(2)}) copy-start(f32[8]{0:T(128)S(1)} %get-tuple-element.125) | copy-start | bytes 100
  60.9 23.0 %copy-start.26 = (s16[517,128]{1,0:T(8,128)(2,1)}, s16[517,128]{1,0:T(8,128)(2,1)S(1)}, u32[]{:S(2)}) copy-start(s16[517,128]{1,0:T(8,128)(2,1)S(1)} %get-tuple-element.66) | copy-start | bytes 397060
  60.9 23.0 %copy-start.28 = (s16[517,128]{1,0:T(8,128)(2,1)}, s16[517,128]{1,0:T(8,128)(2,1)S(1)}, u32[]{:S(2)}) copy-start(s16[517,128]{1,0:T(8,128)(2,1)S(1)} %get-tuple-element.64) | copy-start | bytes 397060
  60.9 19.2 %collective-permute-start.6 = (s16[517,128]{1,0:T(8,128)(2,1)S(1)}, s16[517,128]{1,0:T(8,128)(2,1)S(1)}, u32[]{:S(2)}, u32[]{:S(2)}) collective-permute-start(s16[517,128]{1,0:T(8,128)(2,1)S(1)} %get-tuple-element.64), channel_id=1, source_target_pairs={{0,32},{8,40},{16,48},{24,56},{32,64},{40,72},{48,80},{56,88},{64,... | collective-permute-start | bytes 397064 | tf_op jit(solution)/shard_map/ppermute | solution.py:12
  65.4 14.8 %collective-permute-start.7 = (s16[517,128]{1,0:T(8,128)(2,1)S(1)}, s16[517,128]{1,0:T(8,128)(2,1)S(1)}, u32[]{:S(2)}, u32[]{:S(2)}) collective-permute-start(s16[517,128]{1,0:T(8,128)(2,1)S(1)} %get-tuple-element.66), channel_id=1, source_target_pairs={{32,0},{40,8},{48,16},{56,24},{64,32},{72,40},{80,48},{88,56},{96,... | collective-permute-start | bytes 397064 | tf_op jit(solution)/shard_map/ppermute | solution.py:12
  71.0 9.7 %collective-permute-start.8 = (s16[517,128]{1,0:T(8,128)(2,1)S(1)}, s16[517,128]{1,0:T(8,128)(2,1)S(1)}, u32[]{:S(2)}, u32[]{:S(2)}) collective-permute-start(s16[517,128]{1,0:T(8,128)(2,1)S(1)} %fusion.84), channel_id=1, source_target_pairs={{0,16},{8,24},{16,32},{24,40},{32,48},{40,56},{48,64},{56,72},{64,... | collective-permute-start | bytes 397064 | tf_op jit(solution)/shard_map/ppermute | solution.py:12
  73.0 10.3 %collective-permute-start.9 = (s16[517,128]{1,0:T(8,128)(2,1)S(1)}, s16[517,128]{1,0:T(8,128)(2,1)S(1)}, u32[]{:S(2)}, u32[]{:S(2)}) collective-permute-start(s16[517,128]{1,0:T(8,128)(2,1)S(1)} %get-tuple-element.59), channel_id=1, source_target_pairs={{16,0},{24,8},{32,16},{40,24},{48,32},{56,40},{64,48},{72,56},{80,... | collective-permute-start | bytes 397064 | tf_op jit(solution)/shard_map/ppermute | solution.py:12
  80.1 6.6 %copy-start.19 = (s16[517,128]{1,0:T(8,128)(2,1)}, s16[517,128]{1,0:T(8,128)(2,1)S(1)}, u32[]{:S(2)}) copy-start(s16[517,128]{1,0:T(8,128)(2,1)S(1)} %collective-permute-done.6) | copy-start | bytes 397060
  80.1 4.9 %copy-start.21 = (s16[517,128]{1,0:T(8,128)(2,1)}, s16[517,128]{1,0:T(8,128)(2,1)S(1)}, u32[]{:S(2)}) copy-start(s16[517,128]{1,0:T(8,128)(2,1)S(1)} %collective-permute-done.7) | copy-start | bytes 397060
  80.8 6.5 %copy-start.15 = (s16[517,128]{1,0:T(8,128)(2,1)}, s16[517,128]{1,0:T(8,128)(2,1)S(1)}, u32[]{:S(2)}) copy-start(s16[517,128]{1,0:T(8,128)(2,1)S(1)} %collective-permute-done.8) | copy-start | bytes 397060
  86.7 0.9 copy-start.33
  87.6 0.9 slice-start.11
  89.6 0.9 copy-start.16
  89.6 1.0 copy-start.22
  91.1 1.4 copy-start.20
  97.0 10.0 %copy-start.34 = (f32[128,128]{0,1:T(8,128)S(1)}, f32[128,128]{0,1:T(8,128)}, u32[]{:S(2)}) copy-start(f32[128,128]{0,1:T(8,128)} %fusion.399) | copy-start | bytes 196612
  97.0 10.0 %copy-start.35 = (pred[128,128]{0,1:T(8,128)(4,1)S(1)}, pred[128,128]{0,1:T(8,128)(4,1)}, u32[]{:S(2)}) copy-start(pred[128,128]{0,1:T(8,128)(4,1)} %fusion.92) | copy-start | bytes 49156
  97.9 31.6 %collective-permute-start.10 = (s16[517,128]{1,0:T(8,128)(2,1)S(1)}, s16[517,128]{1,0:T(8,128)(2,1)S(1)}, u32[]{:S(2)}, u32[]{:S(2)}) collective-permute-start(s16[517,128]{1,0:T(8,128)(2,1)S(1)} %copy-done.29), channel_id=1, source_target_pairs={{0,8},{8,16},{16,24},{24,32},{32,40},{40,48},{48,56},{56,64},{64,7... | collective-permute-start | bytes 397064 | tf_op jit(solution)/shard_map/ppermute | solution.py:12
  107.0 7.7 %copy-start.27 = (s16[517,128]{1,0:T(8,128)(2,1)S(1)}, s16[517,128]{1,0:T(8,128)(2,1)}, u32[]{:S(2)}) copy-start(s16[517,128]{1,0:T(8,128)(2,1)} %copy-done.26) | copy-start | bytes 397060
  109.1 25.8 %collective-permute-start.11 = (s16[517,128]{1,0:T(8,128)(2,1)}, s16[517,128]{1,0:T(8,128)(2,1)S(1)}, u32[]{:S(2)}, u32[]{:S(2)}) collective-permute-start(s16[517,128]{1,0:T(8,128)(2,1)} %get-tuple-element.65), channel_id=1, source_target_pairs={{0,40},{8,48},{16,56},{24,64},{32,72},{40,80},{48,88},{56,96},{64,... | collective-permute-start | bytes 397064 | tf_op jit(solution)/shard_map/ppermute | solution.py:12
  114.7 20.2 %collective-permute-start.12 = (s16[517,128]{1,0:T(8,128)(2,1)S(1)}, s16[517,128]{1,0:T(8,128)(2,1)S(1)}, u32[]{:S(2)}, u32[]{:S(2)}) collective-permute-start(s16[517,128]{1,0:T(8,128)(2,1)S(1)} %copy-done.27), channel_id=1, source_target_pairs={{8,0},{16,8},{24,16},{32,24},{40,32},{48,40},{56,48},{64,56},{72,6... | collective-permute-start | bytes 397064 | tf_op jit(solution)/shard_map/ppermute | solution.py:12
  120.2 14.8 %collective-permute-start.13 = (s16[517,128]{1,0:T(8,128)(2,1)}, s16[517,128]{1,0:T(8,128)(2,1)S(1)}, u32[]{:S(2)}, u32[]{:S(2)}) collective-permute-start(s16[517,128]{1,0:T(8,128)(2,1)} %get-tuple-element.67), channel_id=1, source_target_pairs={{40,0},{48,8},{56,16},{64,24},{72,32},{80,40},{88,48},{96,56},{104... | collective-permute-start | bytes 397064 | tf_op jit(solution)/shard_map/ppermute | solution.py:12
  123.3 18.1 %collective-permute-start.14 = (s16[517,128]{1,0:T(8,128)(2,1)}, s16[517,128]{1,0:T(8,128)(2,1)S(1)}, u32[]{:S(2)}, u32[]{:S(2)}) collective-permute-start(s16[517,128]{1,0:T(8,128)(2,1)} %fusion.88), channel_id=1, source_target_pairs={{0,32},{8,40},{16,48},{24,56},{32,64},{40,72},{48,80},{56,88},{64,... | collective-permute-start | bytes 397064 | tf_op jit(solution)/shard_map/ppermute | solution.py:12
  129.5 24.9 %copy-start.10 = (s16[517,128]{1,0:T(8,128)(2,1)}, s16[517,128]{1,0:T(8,128)(2,1)S(1)}, u32[]{:S(2)}) copy-start(s16[517,128]{1,0:T(8,128)(2,1)S(1)} %collective-permute-done.10) | copy-start | bytes 397060
  129.5 23.8 %collective-permute-start.15 = (s16[517,128]{1,0:T(8,128)(2,1)}, s16[517,128]{1,0:T(8,128)(2,1)S(1)}, u32[]{:S(2)}, u32[]{:S(2)}) collective-permute-start(s16[517,128]{1,0:T(8,128)(2,1)} %get-tuple-element.76), channel_id=1, source_target_pairs={{32,0},{40,8},{48,16},{56,24},{64,32},{72,40},{80,48},{88,56},{96,... | collective-permute-start | bytes 397064 | tf_op jit(solution)/shard_map/ppermute | solution.py:12
  134.9 19.5 %copy-start.11 = (s16[517,128]{1,0:T(8,128)(2,1)}, s16[517,128]{1,0:T(8,128)(2,1)S(1)}, u32[]{:S(2)}) copy-start(s16[517,128]{1,0:T(8,128)(2,1)S(1)} %collective-permute-done.11) | copy-start | bytes 397060
  135.0 18.4 %copy-start.8 = (s16[517,128]{1,0:T(8,128)(2,1)}, s16[517,128]{1,0:T(8,128)(2,1)S(1)}, u32[]{:S(2)}) copy-start(s16[517,128]{1,0:T(8,128)(2,1)S(1)} %collective-permute-done.12) | copy-start | bytes 397060
  135.0 18.4 %copy-start.9 = (s16[517,128]{1,0:T(8,128)(2,1)}, s16[517,128]{1,0:T(8,128)(2,1)S(1)}, u32[]{:S(2)}) copy-start(s16[517,128]{1,0:T(8,128)(2,1)S(1)} %collective-permute-done.13) | copy-start | bytes 397060
  155.4 18.0 %slice-start.4 = ((s16[517,128]{1,0:T(8,128)(2,1)}), s16[512,128]{1,0:T(8,128)(2,1)S(1)}, s32[]{:S(2)}) async-start(s16[517,128]{1,0:T(8,128)(2,1)} %copy-done.8), calls=%async_computation.6 | async-start | bytes 262144 | tf_op jit(solution)/shard_map/slice | solution.py:34
  155.4 18.0 %slice-start.5 = ((s16[517,128]{1,0:T(8,128)(2,1)}), s16[512,128]{1,0:T(8,128)(2,1)S(1)}, s32[]{:S(2)}) async-start(s16[517,128]{1,0:T(8,128)(2,1)} %copy-done.9), calls=%async_computation.7 | async-start | bytes 262144 | tf_op jit(solution)/shard_map/slice | solution.py:34
  155.5 19.1 %collective-permute-start.16 = (s16[517,128]{1,0:T(8,128)(2,1)}, s16[517,128]{1,0:T(8,128)(2,1)S(1)}, u32[]{:S(2)}, u32[]{:S(2)}) collective-permute-start(s16[517,128]{1,0:T(8,128)(2,1)} %fusion.88), channel_id=1, source_target_pairs={{0,8},{8,16},{16,24},{24,32},{32,40},{40,48},{48,56},{56,64},{64,7... | collective-permute-start | bytes 397064 | tf_op jit(solution)/shard_map/ppermute | solution.py:12
  157.5 17.0 %collective-permute-start.17 = (s16[517,128]{1,0:T(8,128)(2,1)S(1)}, s16[517,128]{1,0:T(8,128)(2,1)S(1)}, u32[]{:S(2)}, u32[]{:S(2)}) collective-permute-start(s16[517,128]{1,0:T(8,128)(2,1)S(1)} %get-tuple-element.75), channel_id=1, source_target_pairs={{0,40},{8,48},{16,56},{24,64},{32,72},{40,80},{48,88},{56,96},{64,... | collective-permute-start | bytes 397064 | tf_op jit(solution)/shard_map/ppermute | solution.py:12
  159.5 15.1 %collective-permute-start.18 = (s16[517,128]{1,0:T(8,128)(2,1)}, s16[517,128]{1,0:T(8,128)(2,1)S(1)}, u32[]{:S(2)}, u32[]{:S(2)}) collective-permute-start(s16[517,128]{1,0:T(8,128)(2,1)} %get-tuple-element.76), channel_id=1, source_target_pairs={{8,0},{16,8},{24,16},{32,24},{40,32},{48,40},{56,48},{64,56},{72,6... | collective-permute-start | bytes 397064 | tf_op jit(solution)/shard_map/ppermute | solution.py:12
  166.0 10.8 %collective-permute-start.19 = (s16[517,128]{1,0:T(8,128)(2,1)S(1)}, s16[517,128]{1,0:T(8,128)(2,1)S(1)}, u32[]{:S(2)}, u32[]{:S(2)}) collective-permute-start(s16[517,128]{1,0:T(8,128)(2,1)S(1)} %get-tuple-element.77), channel_id=1, source_target_pairs={{40,0},{48,8},{56,16},{64,24},{72,32},{80,40},{88,48},{96,56},{104... | collective-permute-start | bytes 397064 | tf_op jit(solution)/shard_map/ppermute | solution.py:12
  173.3 0.9 slice-start.6
  173.3 1.0 slice-start.7
  174.5 3.0 %copy-start.13 = (s16[517,128]{1,0:T(8,128)(2,1)}, s16[517,128]{1,0:T(8,128)(2,1)S(1)}, u32[]{:S(2)}) copy-start(s16[517,128]{1,0:T(8,128)(2,1)S(1)} %collective-permute-done.16) | copy-start | bytes 397060
  174.6 2.9 %copy-start.12 = (s16[517,128]{1,0:T(8,128)(2,1)}, s16[517,128]{1,0:T(8,128)(2,1)S(1)}, u32[]{:S(2)}) copy-start(s16[517,128]{1,0:T(8,128)(2,1)S(1)} %collective-permute-done.18) | copy-start | bytes 397060
  177.5 1.0 slice-start.10
  178.6 1.0 slice-start.9
  182.6 23.2 %all-to-all-start.1 = ((f32[8,2,16,128]{3,2,1,0:T(8,128)}), f32[8,2,16,128]{3,2,1,0:T(8,128)S(1)}, u32[]{:S(2)}, u32[]{:S(2)}) async-start(f32[8,2,16,128]{3,2,1,0:T(8,128)} %maximum_bitcast_fusion), calls=%async_computation.1 | async-start | bytes 262144 | tf_op jit(solution)/shard_map/all_to_all | solution.py:69
  (34 other events, 23.7 us)

commit v7 on v5

--- a/solution.py
+++ b/solution.py
@@ -10,6 +10,18 @@
     peers = lax.axis_size(axis)
     pairs = [(i, i + by) for i in range(peers) if 0 <= i + by < peers]
     return lax.ppermute(x, axis, pairs)
+
+
+def around(x, axis, by):
+    peers = lax.axis_size(axis)
+    return lax.ppermute(x, axis, [(i, (i + by) % peers) for i in range(peers)])
+
+
+def arrived(got, axis, by):
+    peers = lax.axis_size(axis)
+    source = lax.axis_index(axis) - by
+    real = (source >= 0) & (source < peers)
+    return jnp.where(real, got[0], 0.0), jnp.where(real, got[1], 0.0)
 
 
 FLOOR = -150.0
@@ -47,9 +59,12 @@
     shape = fwd[0].shape
     fwd, bwd = lax.optimization_barrier((pack(*fwd), pack(*bwd)))
     got_f, got_b = lax.optimization_barrier(
-        (from_behind(fwd, "context", by), from_behind(bwd, "context", -by))
-    )
-    return unpack(got_f, shape), unpack(got_b, shape)
+        (around(fwd, "context", by), around(bwd, "context", -by))
+    )
+    return (
+        arrived(unpack(got_f, shape), "context", by),
+        arrived(unpack(got_b, shape), "context", -by),
+    )
 
 
 def exchange(pieces, axis):
@@ -134,15 +149,11 @@
         span *= 2
     near_f, near_b = kept[low]
     sends = lax.optimization_barrier((pack(*near_f), pack(*fwd), pack(*near_b), pack(*bwd)))
+    moves = (1, low + 1, -1, -low - 1)
     got = lax.optimization_barrier(
-        (
-            from_behind(sends[0], "context", 1),
-            from_behind(sends[1], "context", low + 1),
-            from_behind(sends[2], "context", -1),
-            from_behind(sends[3], "context", -low - 1),
-        )
-    )
-    got = [unpack(g, shape) for g in got]
+        tuple(around(p, "context", by) for p, by in zip(sends, moves))
+    )
+    got = [arrived(unpack(g, shape), "context", by) for g, by in zip(got, moves)]
     s_in = combine(got[0], got[1])[0]
     g_in = combine(got[2], got[3])[0]
 

time: 182 us -> 187 us (1.027)
  the two profiles are of different devices: /device:TPU:15 before, /device:TPU:79 now
where the time goes in v7:
time: 187 us; the launch traced here: 186 us
  starting transfers between devices  74.6 us (40%)
  waiting for transfers between devices  52.1 us (28%)
  other arithmetic  26 us (14%)
  local copies, waits for them, and re-layouts  19.4 us (10%)
  matrix products  11.9 us (6%)
  between operations  1.99 us (1%)
    ppermute x10, starting transfers between devices, around(): return lax.ppermute(x, axis, [(i, (i + by) % peers) for i in range(peers)])  52.2 us
    ppermute x10, waiting for transfers between devices, around(): return lax.ppermute(x, axis, [(i, (i + by) % peers) for i in range(peers)])  52.1 us
    all_to_all x1, starting transfers between devices, scatter_sum(): got = lax.all_to_all(parts, axis, 0, 0, tiled=True)  17.2 us
    unnamed x70, local copies, waits for them, and re-layouts  9.14 us
    all_to_all x1, starting transfers between devices, local(): lax.all_to_all(jnp.broadcast_to(piece, (count,) + piece.shape), 'tensor',...  5.23 us
    exp2 x10, local copies, waits for them, and re-layouts, unpack(): return (code * jnp.exp2(expo - 15.0), decay)  3.93 us
  transfers between devices with their start and end apart: 12, of which 7 were waited for; matrix products, arithmetic and copies ran while one was open for 9% of the time, Pallas kernels for 0%

profile of v7, /device:TPU:79, one launch (start us, length us, event | category | flops | bytes accessed | tf_op | source)
XLA Modules:
  0.0 186.1 jit_solution(8976481094163665116)
XLA Ops:
  0.6 0.7 pad_maximum_fusion
  1.4 0.6 broadcast_in_dim.54
  2.0 5.2 %all-to-all-start = ((bf16[8,2,16,128]{3,2,1,0:T(8,128)(2,1)}), bf16[8,2,16,128]{3,2,1,0:T(8,128)(2,1)S(1)}, u32[]{:S(2)}, u32[]{:S(2)}) async-start(bf16[8,2,16,128]{3,2,1,0:T(8,128)(2,1)} %broadcast_in_dim.54), calls=%async_computation | async-start | bytes 131072 | tf_op jit(solution)/shard_map/all_to_all | solution.py:109
  7.3 0.7 copy.32
  8.2 0.6 copy-done.21
  9.6 0.6 compare_convert_fusion
  11.7 0.8 copy-done.6
  14.4 3.5 %collective-permute-start = (s16[1033,128]{1,0:T(8,128)(2,1)S(1)}, s16[1033,128]{1,0:T(8,128)(2,1)S(1)}, u32[]{:S(2)}, u32[]{:S(2)}) collective-permute-start(s16[1033,128]{1,0:T(8,128)(2,1)S(1)} %get-tuple-element.24), channel_id=1, source_target_pairs={{0,8},{8,16},{16,24},{24,32},{32,40},{40,48},{48,56},{56,64},{64,7... | collective-permute-start | bytes 793352 | tf_op jit(solution)/shard_map/ppermute | solution.py:17
  18.0 1.9 %collective-permute-start.1 = (s16[1033,128]{1,0:T(8,128)(2,1)S(1)}, s16[1033,128]{1,0:T(8,128)(2,1)S(1)}, u32[]{:S(2)}, u32[]{:S(2)}) collective-permute-start(s16[1033,128]{1,0:T(8,128)(2,1)S(1)} %get-tuple-element.25), channel_id=1, source_target_pairs={{0,504},{8,0},{16,8},{24,16},{32,24},{40,32},{48,40},{56,48},{64,5... | collective-permute-start | bytes 793352 | tf_op jit(solution)/shard_map/ppermute | solution.py:17
  19.9 4.0 %collective-permute-done = s16[1033,128]{1,0:T(8,128)(2,1)S(1)} collective-permute-done((s16[1033,128]{1,0:T(8,128)(2,1)S(1)}, s16[1033,128]{1,0:T(8,128)(2,1)S(1)}, u32[]{:S(2)}, u32[]{:S(2)}) %collective-permute-start) | collective-permute-done | bytes 264480 | tf_op jit(solution)/shard_map/ppermute | solution.py:17
  23.9 4.9 %collective-permute-done.1 = s16[1033,128]{1,0:T(8,128)(2,1)S(1)} collective-permute-done((s16[1033,128]{1,0:T(8,128)(2,1)S(1)}, s16[1033,128]{1,0:T(8,128)(2,1)S(1)}, u32[]{:S(2)}, u32[]{:S(2)}) %collective-permute-start.1) | collective-permute-done | bytes 264480 | tf_op jit(solution)/shard_map/ppermute | solution.py:17
  29.1 0.7 abs_reduce_fusion.4
  30.0 0.6 fusion.266
  31.2 0.8 clamp_convert_fusion.4
  32.0 0.8 fusion.71
  32.8 4.8 %collective-permute-start.2 = (s16[1033,128]{1,0:T(8,128)(2,1)}, s16[1033,128]{1,0:T(8,128)(2,1)}, u32[]{:S(2)}, u32[]{:S(2)}) collective-permute-start(s16[1033,128]{1,0:T(8,128)(2,1)} %get-tuple-element.28), channel_id=1, source_target_pairs={{0,16},{8,24},{16,32},{24,40},{32,48},{40,56},{48,64},{56,72},{64,... | collective-permute-start | bytes 793352 | tf_op jit(solution)/shard_map/ppermute | solution.py:17
  37.6 2.7 %collective-permute-start.3 = (s16[1033,128]{1,0:T(8,128)(2,1)S(1)}, s16[1033,128]{1,0:T(8,128)(2,1)S(1)}, u32[]{:S(2)}, u32[]{:S(2)}) collective-permute-start(s16[1033,128]{1,0:T(8,128)(2,1)S(1)} %get-tuple-element.29), channel_id=1, source_target_pairs={{0,496},{8,504},{16,0},{24,8},{32,16},{40,24},{48,32},{56,40},{64,... | collective-permute-start | bytes 793352 | tf_op jit(solution)/shard_map/ppermute | solution.py:17
  40.3 4.0 %collective-permute-done.2 = s16[1033,128]{1,0:T(8,128)(2,1)} collective-permute-done((s16[1033,128]{1,0:T(8,128)(2,1)}, s16[1033,128]{1,0:T(8,128)(2,1)}, u32[]{:S(2)}, u32[]{:S(2)}) %collective-permute-start.2) | collective-permute-done | bytes 264480 | tf_op jit(solution)/shard_map/ppermute | solution.py:17
  44.2 4.9 %collective-permute-done.3 = s16[1033,128]{1,0:T(8,128)(2,1)S(1)} collective-permute-done((s16[1033,128]{1,0:T(8,128)(2,1)S(1)}, s16[1033,128]{1,0:T(8,128)(2,1)S(1)}, u32[]{:S(2)}, u32[]{:S(2)}) %collective-permute-start.3) | collective-permute-done | bytes 264480 | tf_op jit(solution)/shard_map/ppermute | solution.py:17
  49.1 1.8 slice.185
  50.9 0.7 multiply_exponential_fusion.7
  51.6 0.7 slice.190
  52.3 1.2 slice_convert_fusion.9
  54.3 1.8 fusion.23
  56.7 0.7 slice_convert_fusion.8
  58.4 0.6 copy-done.26
  59.1 0.8 fusion.73
  59.9 7.4 %collective-permute-start.4 = (s16[1033,128]{1,0:T(8,128)(2,1)}, s16[1033,128]{1,0:T(8,128)(2,1)S(1)}, u32[]{:S(2)}, u32[]{:S(2)}) collective-permute-start(s16[1033,128]{1,0:T(8,128)(2,1)} %get-tuple-element.36), channel_id=1, source_target_pairs={{0,32},{8,40},{16,48},{24,56},{32,64},{40,72},{48,80},{56,88},{64,... | collective-permute-start | bytes 793352 | tf_op jit(solution)/shard_map/ppermute | solution.py:17
  67.3 2.7 %collective-permute-start.5 = (s16[1033,128]{1,0:T(8,128)(2,1)S(1)}, s16[1033,128]{1,0:T(8,128)(2,1)S(1)}, u32[]{:S(2)}, u32[]{:S(2)}) collective-permute-start(s16[1033,128]{1,0:T(8,128)(2,1)S(1)} %get-tuple-element.38), channel_id=1, source_target_pairs={{0,480},{8,488},{16,496},{24,504},{32,0},{40,8},{48,16},{56,24},{6... | collective-permute-start | bytes 793352 | tf_op jit(solution)/shard_map/ppermute | solution.py:17
  70.0 0.7 fusion.95
  70.7 0.8 fusion.272
  71.5 12.6 %collective-permute-done.4 = s16[1033,128]{1,0:T(8,128)(2,1)S(1)} collective-permute-done((s16[1033,128]{1,0:T(8,128)(2,1)}, s16[1033,128]{1,0:T(8,128)(2,1)S(1)}, u32[]{:S(2)}, u32[]{:S(2)}) %collective-permute-start.4) | collective-permute-done | bytes 264480 | tf_op jit(solution)/shard_map/ppermute | solution.py:17
  86.4 14.2 %collective-permute-start.6 = (s16[1033,128]{1,0:T(8,128)(2,1)}, s16[1033,128]{1,0:T(8,128)(2,1)S(1)}, u32[]{:S(2)}, u32[]{:S(2)}) collective-permute-start(s16[1033,128]{1,0:T(8,128)(2,1)} %get-tuple-element.36), channel_id=1, source_target_pairs={{0,8},{8,16},{16,24},{24,32},{32,40},{40,48},{48,56},{56,64},{64,7... | collective-permute-start | bytes 793352 | tf_op jit(solution)/shard_map/ppermute | solution.py:17
  100.6 6.9 %collective-permute-start.7 = (s16[1033,128]{1,0:T(8,128)(2,1)S(1)}, s16[1033,128]{1,0:T(8,128)(2,1)S(1)}, u32[]{:S(2)}, u32[]{:S(2)}) collective-permute-start(s16[1033,128]{1,0:T(8,128)(2,1)S(1)} %get-tuple-element.37), channel_id=1, source_target_pairs={{0,40},{8,48},{16,56},{24,64},{32,72},{40,80},{48,88},{56,96},{64,... | collective-permute-start | bytes 793352 | tf_op jit(solution)/shard_map/ppermute | solution.py:17
  107.5 3.4 %collective-permute-start.8 = (s16[1033,128]{1,0:T(8,128)(2,1)S(1)}, s16[1033,128]{1,0:T(8,128)(2,1)S(1)}, u32[]{:S(2)}, u32[]{:S(2)}) collective-permute-start(s16[1033,128]{1,0:T(8,128)(2,1)S(1)} %get-tuple-element.38), channel_id=1, source_target_pairs={{0,504},{8,0},{16,8},{24,16},{32,24},{40,32},{48,40},{56,48},{64,5... | collective-permute-start | bytes 793352 | tf_op jit(solution)/shard_map/ppermute | solution.py:17
  110.9 4.7 %collective-permute-start.9 = (s16[1033,128]{1,0:T(8,128)(2,1)S(1)}, s16[1033,128]{1,0:T(8,128)(2,1)S(1)}, u32[]{:S(2)}, u32[]{:S(2)}) collective-permute-start(s16[1033,128]{1,0:T(8,128)(2,1)S(1)} %get-tuple-element.39), channel_id=1, source_target_pairs={{0,472},{8,480},{16,488},{24,496},{32,504},{40,0},{48,8},{56,16},{... | collective-permute-start | bytes 793352 | tf_op jit(solution)/shard_map/ppermute | solution.py:17
  115.7 2.0 %fusion.8 = (f32[16,128]{1,0:T(8,128)S(1)}, f32[16,128]{1,0:T(8,128)S(1)}, f32[128,128]{0,1:T(8,128)}) fusion(f32[128,128]{0,1:T(8,128)S(1)} %copy-done.7, f32[16,128]{1,0:T(8,128)S(1)} %reduce_window_sum.30, pred[128,128]{0,1:T(8,128)(4,1)S(1)} %copy-done.13, bf16[16,128,64]{1,2,0:T(8,128)(2,1)S(1)} %bitcast.225, f32[16,128,64]{1,2,0:T(8,128)S(1)} %bitcast.222, ...), kind=kOutput, calls=%fused_computation.22 | convolution fusion | flops 203534336 | bytes 966656 | tf_op jit(solution)/shard_map/hip,hjp->hij/dot_general | solution.py:166
  117.9 0.9 reduce_window_sum.31
  118.8 1.3 fusion.6
  120.1 5.5 %collective-permute-done.7 = s16[1033,128]{1,0:T(8,128)(2,1)S(1)} collective-permute-done((s16[1033,128]{1,0:T(8,128)(2,1)S(1)}, s16[1033,128]{1,0:T(8,128)(2,1)S(1)}, u32[]{:S(2)}, u32[]{:S(2)}) %collective-permute-start.7) | collective-permute-done | bytes 264480 | tf_op jit(solution)/shard_map/ppermute | solution.py:17
  125.6 16.2 %collective-permute-done.9 = s16[1033,128]{1,0:T(8,128)(2,1)S(1)} collective-permute-done((s16[1033,128]{1,0:T(8,128)(2,1)S(1)}, s16[1033,128]{1,0:T(8,128)(2,1)S(1)}, u32[]{:S(2)}, u32[]{:S(2)}) %collective-permute-start.9) | collective-permute-done | bytes 264480 | tf_op jit(solution)/shard_map/ppermute | solution.py:17
  142.5 0.6 multiply_exponential_fusion.2
  143.7 0.9 slice_convert_fusion.1
  144.5 0.6 multiply_exponential_fusion.1
  145.1 0.9 slice_convert_fusion
  146.0 0.6 multiply_exponential_fusion
  147.3 0.8 exp2.403
  148.0 1.3 fusion.236
  149.3 1.4 exp2.404
  150.7 1.3 exp2.405
  152.0 0.8 fusion.231
  152.8 0.7 copy-done.19
  153.5 1.3 convolution_bitcast_fusion.3
  155.6 1.3 convolution_bitcast_fusion.2
  157.1 0.7 maximum_bitcast_fusion
  157.8 17.2 %all-to-all-start.1 = ((f32[8,2,16,128]{3,2,1,0:T(8,128)}), f32[8,2,16,128]{3,2,1,0:T(8,128)S(1)}, u32[]{:S(2)}, u32[]{:S(2)}) async-start(f32[8,2,16,128]{3,2,1,0:T(8,128)} %maximum_bitcast_fusion), calls=%async_computation.1 | async-start | bytes 262144 | tf_op jit(solution)/shard_map/all_to_all | solution.py:84
  176.5 1.2 multiply_reduce_fusion.1
  177.7 0.6 copy-done.33
  179.5 1.2 fusion.2
  181.1 1.9 %fusion.3 = f32[16,1,128]{2,1,0:T(1,128)S(1)} fusion(f32[16,128,1]{1,2,0:T(1,128)S(1)} %bitcast.263, f32[16,128]{1,0:T(8,128)S(1)} %reduce_window_sum.30, pred[128,128]{0,1:T(8,128)(4,1)S(1)} %copy-done.14), kind=kOutput, calls=%fused_computation.11 | convolution fusion | flops 3670016 | bytes 40960 | tf_op jit(solution)/shard_map/hij,hi->hj/dot_general | solution.py:180
  183.1 1.0 copy.39
  184.1 0.7 copy-done.30
  184.8 0.7 multiply_subtract_fusion
  185.5 0.6 slice_bitcast_fusion
  (168 shorter events, 15.6 us)
Async XLA Ops:
  0.6 10.9 %copy-start.4 = (bf16[128,1024]{1,0:T(8,128)(2,1)S(1)}, bf16[128,1024]{1,0:T(8,128)(2,1)}, u32[]{:S(2)}) copy-start(bf16[128,1024]{1,0:T(8,128)(2,1)} %param.8) | copy-start | bytes 786436
  2.0 10.7 %all-to-all-start = ((bf16[8,2,16,128]{3,2,1,0:T(8,128)(2,1)}), bf16[8,2,16,128]{3,2,1,0:T(8,128)(2,1)S(1)}, u32[]{:S(2)}, u32[]{:S(2)}) async-start(bf16[8,2,16,128]{3,2,1,0:T(8,128)(2,1)} %broadcast_in_dim.54), calls=%async_computation | async-start | bytes 131072 | tf_op jit(solution)/shard_map/all_to_all | solution.py:109
  8.2 0.7 copy-start.21
  8.9 2.0 %copy-start.2 = (f32[16,128]{1,0:T(8,128)S(1)}, f32[16,128]{1,0:T(8,128)}, u32[]{:S(2)}) copy-start(f32[16,128]{1,0:T(8,128)} %param.10) | copy-start | bytes 24580
  10.2 0.7 copy-start.29
  11.5 19.8 %copy-start.17 = (f32[16]{0:T(128)}, f32[16]{0:T(128)S(1)}, u32[]{:S(2)}) copy-start(f32[16]{0:T(128)S(1)} %get-tuple-element.82) | copy-start | bytes 196
  11.6 1.0 copy-start.6
  14.4 9.5 %collective-permute-start = (s16[1033,128]{1,0:T(8,128)(2,1)S(1)}, s16[1033,128]{1,0:T(8,128)(2,1)S(1)}, u32[]{:S(2)}, u32[]{:S(2)}) collective-permute-start(s16[1033,128]{1,0:T(8,128)(2,1)S(1)} %get-tuple-element.24), channel_id=1, source_target_pairs={{0,8},{8,16},{16,24},{24,32},{32,40},{40,48},{48,56},{56,64},{64,7... | collective-permute-start | bytes 793352 | tf_op jit(solution)/shard_map/ppermute | solution.py:17
  18.0 10.9 %collective-permute-start.1 = (s16[1033,128]{1,0:T(8,128)(2,1)S(1)}, s16[1033,128]{1,0:T(8,128)(2,1)S(1)}, u32[]{:S(2)}, u32[]{:S(2)}) collective-permute-start(s16[1033,128]{1,0:T(8,128)(2,1)S(1)} %get-tuple-element.25), channel_id=1, source_target_pairs={{0,504},{8,0},{16,8},{24,16},{32,24},{40,32},{48,40},{56,48},{64,5... | collective-permute-start | bytes 793352 | tf_op jit(solution)/shard_map/ppermute | solution.py:17
  30.7 0.5 copy-start.25
  30.7 0.6 copy-start.27
  32.8 11.5 %collective-permute-start.2 = (s16[1033,128]{1,0:T(8,128)(2,1)}, s16[1033,128]{1,0:T(8,128)(2,1)}, u32[]{:S(2)}, u32[]{:S(2)}) collective-permute-start(s16[1033,128]{1,0:T(8,128)(2,1)} %get-tuple-element.28), channel_id=1, source_target_pairs={{0,16},{8,24},{16,32},{24,40},{32,48},{40,56},{48,64},{56,72},{64,... | collective-permute-start | bytes 793352 | tf_op jit(solution)/shard_map/ppermute | solution.py:17
  37.6 11.6 %collective-permute-start.3 = (s16[1033,128]{1,0:T(8,128)(2,1)S(1)}, s16[1033,128]{1,0:T(8,128)(2,1)S(1)}, u32[]{:S(2)}, u32[]{:S(2)}) collective-permute-start(s16[1033,128]{1,0:T(8,128)(2,1)S(1)} %get-tuple-element.29), channel_id=1, source_target_pairs={{0,496},{8,504},{16,0},{24,8},{32,16},{40,24},{48,32},{56,40},{64,... | collective-permute-start | bytes 793352 | tf_op jit(solution)/shard_map/ppermute | solution.py:17
  49.1 3.2 %copy-start.3 = (s16[1033,128]{1,0:T(8,128)(2,1)}, s16[1033,128]{1,0:T(8,128)(2,1)S(1)}, u32[]{:S(2)}) copy-start(s16[1033,128]{1,0:T(8,128)(2,1)S(1)} %collective-permute-done.3) | copy-start | bytes 793348
  53.6 0.6 copy-start.18
  53.7 0.7 copy-start.31
  53.7 0.7 copy-start.32
  57.4 0.6 copy-start.22
  57.4 0.7 copy-start.28
  58.4 0.7 copy-start.26
  59.9 24.1 %collective-permute-start.4 = (s16[1033,128]{1,0:T(8,128)(2,1)}, s16[1033,128]{1,0:T(8,128)(2,1)S(1)}, u32[]{:S(2)}, u32[]{:S(2)}) collective-permute-start(s16[1033,128]{1,0:T(8,128)(2,1)} %get-tuple-element.36), channel_id=1, source_target_pairs={{0,32},{8,40},{16,48},{24,56},{32,64},{40,72},{48,80},{56,88},{64,... | collective-permute-start | bytes 793352 | tf_op jit(solution)/shard_map/ppermute | solution.py:17
  67.3 16.7 %collective-permute-start.5 = (s16[1033,128]{1,0:T(8,128)(2,1)S(1)}, s16[1033,128]{1,0:T(8,128)(2,1)S(1)}, u32[]{:S(2)}, u32[]{:S(2)}) collective-permute-start(s16[1033,128]{1,0:T(8,128)(2,1)S(1)} %get-tuple-element.38), channel_id=1, source_target_pairs={{0,480},{8,488},{16,496},{24,504},{32,0},{40,8},{48,16},{56,24},{6... | collective-permute-start | bytes 793352 | tf_op jit(solution)/shard_map/ppermute | solution.py:17
  86.3 29.4 %copy-start.7 = (f32[128,128]{0,1:T(8,128)S(1)}, f32[128,128]{0,1:T(8,128)}, u32[]{:S(2)}) copy-start(f32[128,128]{0,1:T(8,128)} %fusion.272) | copy-start | bytes 196612
  86.3 29.4 %copy-start.13 = (pred[128,128]{0,1:T(8,128)(4,1)S(1)}, pred[128,128]{0,1:T(8,128)(4,1)}, u32[]{:S(2)}) copy-start(pred[128,128]{0,1:T(8,128)(4,1)} %fusion.95) | copy-start | bytes 49156
  86.4 33.7 %collective-permute-start.6 = (s16[1033,128]{1,0:T(8,128)(2,1)}, s16[1033,128]{1,0:T(8,128)(2,1)S(1)}, u32[]{:S(2)}, u32[]{:S(2)}) collective-permute-start(s16[1033,128]{1,0:T(8,128)(2,1)} %get-tuple-element.36), channel_id=1, source_target_pairs={{0,8},{8,16},{16,24},{24,32},{32,40},{40,48},{48,56},{56,64},{64,7... | collective-permute-start | bytes 793352 | tf_op jit(solution)/shard_map/ppermute | solution.py:17
  100.6 25.0 %collective-permute-start.7 = (s16[1033,128]{1,0:T(8,128)(2,1)S(1)}, s16[1033,128]{1,0:T(8,128)(2,1)S(1)}, u32[]{:S(2)}, u32[]{:S(2)}) collective-permute-start(s16[1033,128]{1,0:T(8,128)(2,1)S(1)} %get-tuple-element.37), channel_id=1, source_target_pairs={{0,40},{8,48},{16,56},{24,64},{32,72},{40,80},{48,88},{56,96},{64,... | collective-permute-start | bytes 793352 | tf_op jit(solution)/shard_map/ppermute | solution.py:17
  107.5 18.1 %collective-permute-start.8 = (s16[1033,128]{1,0:T(8,128)(2,1)S(1)}, s16[1033,128]{1,0:T(8,128)(2,1)S(1)}, u32[]{:S(2)}, u32[]{:S(2)}) collective-permute-start(s16[1033,128]{1,0:T(8,128)(2,1)S(1)} %get-tuple-element.38), channel_id=1, source_target_pairs={{0,504},{8,0},{16,8},{24,16},{32,24},{40,32},{48,40},{56,48},{64,5... | collective-permute-start | bytes 793352 | tf_op jit(solution)/shard_map/ppermute | solution.py:17
  110.9 30.9 %collective-permute-start.9 = (s16[1033,128]{1,0:T(8,128)(2,1)S(1)}, s16[1033,128]{1,0:T(8,128)(2,1)S(1)}, u32[]{:S(2)}, u32[]{:S(2)}) collective-permute-start(s16[1033,128]{1,0:T(8,128)(2,1)S(1)} %get-tuple-element.39), channel_id=1, source_target_pairs={{0,472},{8,480},{16,488},{24,496},{32,504},{40,0},{48,8},{56,16},{... | collective-permute-start | bytes 793352 | tf_op jit(solution)/shard_map/ppermute | solution.py:17
  152.8 2.2 %copy-start.23 = (f32[16]{0:T(128)}, f32[16]{0:T(128)S(1)}, u32[]{:S(2)}) copy-start(f32[16]{0:T(128)S(1)} %fusion.231) | copy-start | bytes 196
  152.8 0.7 copy-start.19
  153.5 1.3 copy-start.5
  153.5 1.6 copy-start
  153.5 1.6 copy-start.1
  154.8 0.7 copy-start.15
  154.9 0.7 copy-start.16
  157.8 17.2 %copy-start.20 = (f32[16]{0:T(128)S(1)}, f32[16]{0:T(128)}, u32[]{:S(2)}) copy-start(f32[16]{0:T(128)} %fusion.236) | copy-start | bytes 196
  157.8 27.7 %all-to-all-start.1 = ((f32[8,2,16,128]{3,2,1,0:T(8,128)}), f32[8,2,16,128]{3,2,1,0:T(8,128)S(1)}, u32[]{:S(2)}, u32[]{:S(2)}) async-start(f32[8,2,16,128]{3,2,1,0:T(8,128)} %maximum_bitcast_fusion), calls=%async_computation.1 | async-start | bytes 262144 | tf_op jit(solution)/shard_map/all_to_all | solution.py:84
  175.1 0.6 copy-start.24
  175.8 0.7 copy-start.10
  175.8 0.7 copy-start.11
  175.8 0.7 copy-start.12
  175.8 0.7 copy-start.9
  177.7 0.7 copy-start.33
  178.7 0.7 copy-start.14
  183.1 1.0 copy-start.8
  184.1 0.7 copy-start.30

commit v8 on v5

--- a/solution.py
+++ b/solution.py
@@ -134,13 +134,11 @@
         span *= 2
     near_f, near_b = kept[low]
     sends = lax.optimization_barrier((pack(*near_f), pack(*fwd), pack(*near_b), pack(*bwd)))
-    got = lax.optimization_barrier(
-        (
-            from_behind(sends[0], "context", 1),
-            from_behind(sends[1], "context", low + 1),
-            from_behind(sends[2], "context", -1),
-            from_behind(sends[3], "context", -low - 1),
-        )
+    got = (
+        from_behind(sends[0], "context", 1),
+        from_behind(sends[1], "context", low + 1),
+        from_behind(sends[2], "context", -1),
+        from_behind(sends[3], "context", -low - 1),
     )
     got = [unpack(g, shape) for g in got]
     s_in = combine(got[0], got[1])[0]

time: 182 us -> 175 us (0.962)
  the two profiles are of different devices: /device:TPU:15 before, /device:TPU:75 now
where the time goes in v8:
time: 175 us; the launch traced here: 174 us
  starting transfers between devices  69 us (39%)
  waiting for transfers between devices  59.8 us (34%)
  other arithmetic  15.8 us (9%)
  local copies, waits for them, and re-layouts  14.3 us (8%)
  matrix products  12.8 us (7%)
  between operations  2.03 us (1%)
    ppermute x10, waiting for transfers between devices, from_behind(): return lax.ppermute(x, axis, pairs)  59.8 us
    ppermute x10, starting transfers between devices, from_behind(): return lax.ppermute(x, axis, pairs)  57 us
    unnamed x54, local copies, waits for them, and re-layouts  8.23 us
    all_to_all x1, starting transfers between devices, scatter_sum(): got = lax.all_to_all(parts, axis, 0, 0, tiled=True)  6.75 us
    all_to_all x1, starting transfers between devices, local(): lax.all_to_all(jnp.broadcast_to(piece, (count,) + piece.shape), 'tensor',...  5.23 us
  transfers between devices with their start and end apart: 12, of which 7 were waited for; matrix products, arithmetic and copies ran while one was open for 10% of the time, Pallas kernels for 0%

profile of v8, /device:TPU:75, one launch (start us, length us, event | category | flops | bytes accessed | tf_op | source)
XLA Modules:
  0.0 173.7 jit_solution(14910294841260704680)
XLA Ops:
  0.6 0.7 pad_maximum_fusion
  1.4 0.6 broadcast_in_dim.29
  2.0 5.2 %all-to-all-start = ((bf16[8,2,16,128]{3,2,1,0:T(8,128)(2,1)}), bf16[8,2,16,128]{3,2,1,0:T(8,128)(2,1)S(1)}, u32[]{:S(2)}, u32[]{:S(2)}) async-start(bf16[8,2,16,128]{3,2,1,0:T(8,128)(2,1)} %broadcast_in_dim.29), calls=%async_computation | async-start | bytes 131072 | tf_op jit(solution)/shard_map/all_to_all | solution.py:94
  7.3 0.7 copy.32
  8.2 0.6 copy-done.15
  9.0 0.6 slice.174
  9.6 0.6 compare_convert_fusion
  11.7 0.8 copy-done.6
  12.7 0.5 abs_reduce_fusion.7
  13.3 0.5 abs_reduce_fusion.6
  14.4 3.5 %collective-permute-start = (s16[1033,128]{1,0:T(8,128)(2,1)S(1)}, s16[1033,128]{1,0:T(8,128)(2,1)S(1)}, u32[]{:S(2)}, u32[]{:S(2)}) collective-permute-start(s16[1033,128]{1,0:T(8,128)(2,1)S(1)} %get-tuple-element.20), channel_id=1, source_target_pairs={{0,8},{8,16},{16,24},{24,32},{32,40},{40,48},{48,56},{56,64},{64,7... | collective-permute-start | bytes 793352 | tf_op jit(solution)/shard_map/ppermute | solution.py:12
  18.0 1.9 %collective-permute-start.1 = (s16[1033,128]{1,0:T(8,128)(2,1)S(1)}, s16[1033,128]{1,0:T(8,128)(2,1)S(1)}, u32[]{:S(2)}, u32[]{:S(2)}) collective-permute-start(s16[1033,128]{1,0:T(8,128)(2,1)S(1)} %get-tuple-element.21), channel_id=1, source_target_pairs={{8,0},{16,8},{24,16},{32,24},{40,32},{48,40},{56,48},{64,56},{72,6... | collective-permute-start | bytes 793352 | tf_op jit(solution)/shard_map/ppermute | solution.py:12
  19.9 4.0 %collective-permute-done = s16[1033,128]{1,0:T(8,128)(2,1)S(1)} collective-permute-done((s16[1033,128]{1,0:T(8,128)(2,1)S(1)}, s16[1033,128]{1,0:T(8,128)(2,1)S(1)}, u32[]{:S(2)}, u32[]{:S(2)}) %collective-permute-start) | collective-permute-done | bytes 264480 | tf_op jit(solution)/shard_map/ppermute | solution.py:12
  23.9 4.9 %collective-permute-done.1 = s16[1033,128]{1,0:T(8,128)(2,1)S(1)} collective-permute-done((s16[1033,128]{1,0:T(8,128)(2,1)S(1)}, s16[1033,128]{1,0:T(8,128)(2,1)S(1)}, u32[]{:S(2)}, u32[]{:S(2)}) %collective-permute-start.1) | collective-permute-done | bytes 264480 | tf_op jit(solution)/shard_map/ppermute | solution.py:12
  29.1 0.7 abs_reduce_fusion.4
  30.0 0.7 fusion.232
  30.7 0.5 copy-done.18
  31.3 0.8 clamp_convert_fusion.4
  32.1 4.8 %collective-permute-start.2 = (s16[1033,128]{1,0:T(8,128)(2,1)S(1)}, s16[1033,128]{1,0:T(8,128)(2,1)S(1)}, u32[]{:S(2)}, u32[]{:S(2)}) collective-permute-start(s16[1033,128]{1,0:T(8,128)(2,1)S(1)} %get-tuple-element.24), channel_id=1, source_target_pairs={{0,16},{8,24},{16,32},{24,40},{32,48},{40,56},{48,64},{56,72},{64,... | collective-permute-start | bytes 793352 | tf_op jit(solution)/shard_map/ppermute | solution.py:12
  36.9 2.4 %collective-permute-start.3 = (s16[1033,128]{1,0:T(8,128)(2,1)S(1)}, s16[1033,128]{1,0:T(8,128)(2,1)S(1)}, u32[]{:S(2)}, u32[]{:S(2)}) collective-permute-start(s16[1033,128]{1,0:T(8,128)(2,1)S(1)} %get-tuple-element.25), channel_id=1, source_target_pairs={{16,0},{24,8},{32,16},{40,24},{48,32},{56,40},{64,48},{72,56},{80,... | collective-permute-start | bytes 793352 | tf_op jit(solution)/shard_map/ppermute | solution.py:12
  39.3 3.9 %collective-permute-done.2 = s16[1033,128]{1,0:T(8,128)(2,1)S(1)} collective-permute-done((s16[1033,128]{1,0:T(8,128)(2,1)S(1)}, s16[1033,128]{1,0:T(8,128)(2,1)S(1)}, u32[]{:S(2)}, u32[]{:S(2)}) %collective-permute-start.2) | collective-permute-done | bytes 264480 | tf_op jit(solution)/shard_map/ppermute | solution.py:12
  43.2 5.3 %collective-permute-done.3 = s16[1033,128]{1,0:T(8,128)(2,1)S(1)} collective-permute-done((s16[1033,128]{1,0:T(8,128)(2,1)S(1)}, s16[1033,128]{1,0:T(8,128)(2,1)S(1)}, u32[]{:S(2)}, u32[]{:S(2)}) %collective-permute-start.3) | collective-permute-done | bytes 264480 | tf_op jit(solution)/shard_map/ppermute | solution.py:12
  48.4 0.8 slice.185
  49.2 0.7 slice.190
  50.0 0.6 slice_convert_fusion.9
  50.7 0.7 copy-done.16
  51.4 1.8 %fusion.20 = (f32[16,64,128]{2,1,0:T(8,128)S(1)}, f32[16,64,128]{2,1,0:T(8,128)S(1)}) fusion(s16[16,64,128]{2,1,0:T(8,128)(2,1)} %bitcast.227, f32[16,64]{1,0:T(8,128)S(1)} %exp2.377, f32[16]{0:T(128)S(1)} %copy-done.16, f32[16,64,128]{2,1,0:T(8,128)S(1)} %get-tuple-element.119, f32[16,64]{1,0:T(8,128)S(1)} %exp2.367, f32[16]{0:T(128)S(1)} %get-tuple-element.74, ...), kind=kLoop, calls=%fused_computation.37 | loop fusion | flops 2097152 | bytes 3162304 | tf_op jit(solution)/shard_map/add | solution.py:42
  53.8 0.7 slice_convert_fusion.8
  54.7 0.4 copy-done.21
  55.5 0.6 copy-done.19
  56.3 7.6 %collective-permute-start.4 = (s16[1033,128]{1,0:T(8,128)(2,1)S(1)}, s16[1033,128]{1,0:T(8,128)(2,1)S(1)}, u32[]{:S(2)}, u32[]{:S(2)}) collective-permute-start(s16[1033,128]{1,0:T(8,128)(2,1)S(1)} %get-tuple-element.34), channel_id=1, source_target_pairs={{0,32},{8,40},{16,48},{24,56},{32,64},{40,72},{48,80},{56,88},{64,... | collective-permute-start | bytes 793352 | tf_op jit(solution)/shard_map/ppermute | solution.py:12
  63.9 2.6 %collective-permute-start.5 = (s16[1033,128]{1,0:T(8,128)(2,1)S(1)}, s16[1033,128]{1,0:T(8,128)(2,1)S(1)}, u32[]{:S(2)}, u32[]{:S(2)}) collective-permute-start(s16[1033,128]{1,0:T(8,128)(2,1)S(1)} %get-tuple-element.32), channel_id=1, source_target_pairs={{32,0},{40,8},{48,16},{56,24},{64,32},{72,40},{80,48},{88,56},{96,... | collective-permute-start | bytes 793352 | tf_op jit(solution)/shard_map/ppermute | solution.py:12
  66.6 0.8 fusion.238
  67.4 4.2 %collective-permute-done.4 = s16[1033,128]{1,0:T(8,128)(2,1)S(1)} collective-permute-done((s16[1033,128]{1,0:T(8,128)(2,1)S(1)}, s16[1033,128]{1,0:T(8,128)(2,1)S(1)}, u32[]{:S(2)}, u32[]{:S(2)}) %collective-permute-start.4) | collective-permute-done | bytes 264480 | tf_op jit(solution)/shard_map/ppermute | solution.py:12
  71.6 6.0 %collective-permute-done.5 = s16[1033,128]{1,0:T(8,128)(2,1)S(1)} collective-permute-done((s16[1033,128]{1,0:T(8,128)(2,1)S(1)}, s16[1033,128]{1,0:T(8,128)(2,1)S(1)}, u32[]{:S(2)}, u32[]{:S(2)}) %collective-permute-start.5) | collective-permute-done | bytes 264480 | tf_op jit(solution)/shard_map/ppermute | solution.py:12
  77.7 0.4 abs_reduce_fusion.1
  78.4 0.4 abs_reduce_fusion
  78.9 0.4 clamp_convert_fusion.1
  79.4 0.4 clamp_convert_fusion
  79.9 0.6 copy-done.12
  80.6 0.9 copy-done.2
  81.5 14.4 %collective-permute-start.6 = (s16[1033,128]{1,0:T(8,128)(2,1)S(1)}, s16[1033,128]{1,0:T(8,128)(2,1)S(1)}, u32[]{:S(2)}, u32[]{:S(2)}) collective-permute-start(s16[1033,128]{1,0:T(8,128)(2,1)S(1)} %copy-done.2), channel_id=1, source_target_pairs={{8,0},{16,8},{24,16},{32,24},{40,32},{48,40},{56,48},{64,56},{72,6... | collective-permute-start | bytes 793352 | tf_op jit(solution)/shard_map/ppermute | solution.py:12
  95.9 1.3 fusion.6
  97.2 9.1 %collective-permute-start.7 = (s16[1033,128]{1,0:T(8,128)(2,1)S(1)}, s16[1033,128]{1,0:T(8,128)(2,1)S(1)}, u32[]{:S(2)}, u32[]{:S(2)}) collective-permute-start(s16[1033,128]{1,0:T(8,128)(2,1)S(1)} %get-tuple-element.33), channel_id=1, source_target_pairs={{40,0},{48,8},{56,16},{64,24},{72,32},{80,40},{88,48},{96,56},{104... | collective-permute-start | bytes 793352 | tf_op jit(solution)/shard_map/ppermute | solution.py:12
  106.3 2.9 %fusion.8 = (f32[16,128]{1,0:T(8,128)S(1)}, f32[16,128]{1,0:T(8,128)S(1)}, f32[128,128]{0,1:T(8,128)}) fusion(f32[128,128]{0,1:T(8,128)S(1)} %copy-done.7, f32[16,128]{1,0:T(8,128)S(1)} %reduce_window_sum.30, pred[128,128]{0,1:T(8,128)(4,1)} %copy-done.9, bf16[16,128,64]{1,2,0:T(8,128)(2,1)S(1)} %bitcast.214, f32[16,128,64]{1,2,0:T(8,128)S(1)} %bitcast.210, ...), kind=kOutput, calls=%fused_computation.22 | convolution fusion | flops 203534336 | bytes 966656 | tf_op jit(solution)/shard_map/hip,hjp->hij/dot_general | solution.py:153
  109.4 0.9 reduce_window_sum.31
  110.3 1.9 %collective-permute-start.8 = (s16[1033,128]{1,0:T(8,128)(2,1)S(1)}, s16[1033,128]{1,0:T(8,128)(2,1)S(1)}, u32[]{:S(2)}, u32[]{:S(2)}) collective-permute-start(s16[1033,128]{1,0:T(8,128)(2,1)S(1)} %get-tuple-element.34), channel_id=1, source_target_pairs={{0,8},{8,16},{16,24},{24,32},{32,40},{40,48},{48,56},{56,64},{64,7... | collective-permute-start | bytes 793352 | tf_op jit(solution)/shard_map/ppermute | solution.py:12
  112.2 8.8 %collective-permute-start.9 = (s16[1033,128]{1,0:T(8,128)(2,1)S(1)}, s16[1033,128]{1,0:T(8,128)(2,1)S(1)}, u32[]{:S(2)}, u32[]{:S(2)}) collective-permute-start(s16[1033,128]{1,0:T(8,128)(2,1)S(1)} %get-tuple-element.35), channel_id=1, source_target_pairs={{0,40},{8,48},{16,56},{24,64},{32,72},{40,80},{48,88},{56,96},{64,... | collective-permute-start | bytes 793352 | tf_op jit(solution)/shard_map/ppermute | solution.py:12
  121.4 31.4 %collective-permute-done.9 = s16[1033,128]{1,0:T(8,128)(2,1)S(1)} collective-permute-done((s16[1033,128]{1,0:T(8,128)(2,1)S(1)}, s16[1033,128]{1,0:T(8,128)(2,1)S(1)}, u32[]{:S(2)}, u32[]{:S(2)}) %collective-permute-start.9) | collective-permute-done | bytes 264480 | tf_op jit(solution)/shard_map/ppermute | solution.py:12
  153.1 1.3 convolution_bitcast_fusion.3
  154.8 1.3 convolution_bitcast_fusion.2
  156.4 0.7 maximum_bitcast_fusion
  157.1 6.8 %all-to-all-start.1 = ((f32[8,2,16,128]{3,2,1,0:T(8,128)}), f32[8,2,16,128]{3,2,1,0:T(8,128)S(1)}, u32[]{:S(2)}, u32[]{:S(2)}) async-start(f32[8,2,16,128]{3,2,1,0:T(8,128)} %maximum_bitcast_fusion), calls=%async_computation.1 | async-start | bytes 262144 | tf_op jit(solution)/shard_map/all_to_all | solution.py:69
  164.1 1.2 multiply_reduce_fusion.1
  165.3 0.6 copy-done.25
  166.0 0.4 fusion.14
  166.6 0.5 copy-done.10
  167.1 1.2 fusion.2
  168.3 0.4 fusion.1
  168.7 1.9 %fusion.3 = f32[16,1,128]{2,1,0:T(1,128)S(1)} fusion(f32[16,128,1]{1,2,0:T(1,128)S(1)} %bitcast.251, f32[16,128]{1,0:T(8,128)S(1)} %reduce_window_sum.30, pred[128,128]{0,1:T(8,128)(4,1)S(1)} %copy-done.10), kind=kOutput, calls=%fused_computation.11 | convolution fusion | flops 3670016 | bytes 40960 | tf_op jit(solution)/shard_map/hij,hi->hj/dot_general | solution.py:167
  170.8 1.0 copy.39
  171.8 0.7 copy-done.24
  172.4 0.7 multiply_subtract_fusion
  173.1 0.6 slice_bitcast_fusion
  (152 shorter events, 7.1 us)
Async XLA Ops:
  0.6 11.0 %copy-start.4 = (bf16[128,1024]{1,0:T(8,128)(2,1)S(1)}, bf16[128,1024]{1,0:T(8,128)(2,1)}, u32[]{:S(2)}) copy-start(bf16[128,1024]{1,0:T(8,128)(2,1)} %param.8) | copy-start | bytes 786436
  2.0 10.7 %all-to-all-start = ((bf16[8,2,16,128]{3,2,1,0:T(8,128)(2,1)}), bf16[8,2,16,128]{3,2,1,0:T(8,128)(2,1)S(1)}, u32[]{:S(2)}, u32[]{:S(2)}) async-start(bf16[8,2,16,128]{3,2,1,0:T(8,128)(2,1)} %broadcast_in_dim.29), calls=%async_computation | async-start | bytes 131072 | tf_op jit(solution)/shard_map/all_to_all | solution.py:94
  8.2 0.7 copy-start.15
  8.9 2.0 %copy-start = (f32[16,128]{1,0:T(8,128)S(1)}, f32[16,128]{1,0:T(8,128)}, u32[]{:S(2)}) copy-start(f32[16,128]{1,0:T(8,128)} %param.10) | copy-start | bytes 24580
  9.0 0.6 copy-start.13
  10.2 0.7 copy-start.23
  11.6 1.0 copy-start.6
  14.3 41.8 %copy-start.11 = (s16[1,96]{1,0:T(2,128)(2,1)}, s16[1,96]{1,0:T(2,128)(2,1)S(1)}, u32[]{:S(2)}) copy-start(s16[1,96]{1,0:T(2,128)(2,1)S(1)} %concatenate.139) | copy-start | bytes 580
  14.4 9.5 %collective-permute-start = (s16[1033,128]{1,0:T(8,128)(2,1)S(1)}, s16[1033,128]{1,0:T(8,128)(2,1)S(1)}, u32[]{:S(2)}, u32[]{:S(2)}) collective-permute-start(s16[1033,128]{1,0:T(8,128)(2,1)S(1)} %get-tuple-element.20), channel_id=1, source_target_pairs={{0,8},{8,16},{16,24},{24,32},{32,40},{40,48},{48,56},{56,64},{64,7... | collective-permute-start | bytes 793352 | tf_op jit(solution)/shard_map/ppermute | solution.py:12
  18.0 10.9 %collective-permute-start.1 = (s16[1033,128]{1,0:T(8,128)(2,1)S(1)}, s16[1033,128]{1,0:T(8,128)(2,1)S(1)}, u32[]{:S(2)}, u32[]{:S(2)}) collective-permute-start(s16[1033,128]{1,0:T(8,128)(2,1)S(1)} %get-tuple-element.21), channel_id=1, source_target_pairs={{8,0},{16,8},{24,16},{32,24},{40,32},{48,40},{56,48},{64,56},{72,6... | collective-permute-start | bytes 793352 | tf_op jit(solution)/shard_map/ppermute | solution.py:12
  30.7 0.5 copy-start.18
  30.7 0.6 copy-start.20
  32.1 11.1 %collective-permute-start.2 = (s16[1033,128]{1,0:T(8,128)(2,1)S(1)}, s16[1033,128]{1,0:T(8,128)(2,1)S(1)}, u32[]{:S(2)}, u32[]{:S(2)}) collective-permute-start(s16[1033,128]{1,0:T(8,128)(2,1)S(1)} %get-tuple-element.24), channel_id=1, source_target_pairs={{0,16},{8,24},{16,32},{24,40},{32,48},{40,56},{48,64},{56,72},{64,... | collective-permute-start | bytes 793352 | tf_op jit(solution)/shard_map/ppermute | solution.py:12
  36.9 11.6 %collective-permute-start.3 = (s16[1033,128]{1,0:T(8,128)(2,1)S(1)}, s16[1033,128]{1,0:T(8,128)(2,1)S(1)}, u32[]{:S(2)}, u32[]{:S(2)}) collective-permute-start(s16[1033,128]{1,0:T(8,128)(2,1)S(1)} %get-tuple-element.25), channel_id=1, source_target_pairs={{16,0},{24,8},{32,16},{40,24},{48,32},{56,40},{64,48},{72,56},{80,... | collective-permute-start | bytes 793352 | tf_op jit(solution)/shard_map/ppermute | solution.py:12
  48.4 1.5 copy-start.3
  50.7 0.7 copy-start.16
  50.7 0.7 copy-start.17
  54.4 0.6 copy-start.21
  54.4 0.7 copy-start.22
  55.4 0.6 copy-start.19
  56.3 21.4 %copy-start.1 = (s16[1033,128]{1,0:T(8,128)(2,1)}, s16[1033,128]{1,0:T(8,128)(2,1)S(1)}, u32[]{:S(2)}) copy-start(s16[1033,128]{1,0:T(8,128)(2,1)S(1)} %get-tuple-element.32) | copy-start | bytes 793348
  56.3 10.2 %copy-start.14 = (s32[128]{0:T(128)S(1)}, s32[128]{0:T(128)}, u32[]{:S(2)}) copy-start(s32[128]{0:T(128)} %copy-done.13) | copy-start | bytes 1540
  56.3 15.3 %collective-permute-start.4 = (s16[1033,128]{1,0:T(8,128)(2,1)S(1)}, s16[1033,128]{1,0:T(8,128)(2,1)S(1)}, u32[]{:S(2)}, u32[]{:S(2)}) collective-permute-start(s16[1033,128]{1,0:T(8,128)(2,1)S(1)} %get-tuple-element.34), channel_id=1, source_target_pairs={{0,32},{8,40},{16,48},{24,56},{32,64},{40,72},{48,80},{56,88},{64,... | collective-permute-start | bytes 793352 | tf_op jit(solution)/shard_map/ppermute | solution.py:12
  63.9 13.7 %collective-permute-start.5 = (s16[1033,128]{1,0:T(8,128)(2,1)S(1)}, s16[1033,128]{1,0:T(8,128)(2,1)S(1)}, u32[]{:S(2)}, u32[]{:S(2)}) collective-permute-start(s16[1033,128]{1,0:T(8,128)(2,1)S(1)} %get-tuple-element.32), channel_id=1, source_target_pairs={{32,0},{40,8},{48,16},{56,24},{64,32},{72,40},{80,48},{88,56},{96,... | collective-permute-start | bytes 793352 | tf_op jit(solution)/shard_map/ppermute | solution.py:12
  66.6 29.3 %copy-start.9 = (pred[128,128]{0,1:T(8,128)(4,1)}, pred[128,128]{0,1:T(8,128)(4,1)S(1)}, u32[]{:S(2)}) copy-start(pred[128,128]{0,1:T(8,128)(4,1)S(1)} %fusion.79) | copy-start | bytes 49156
  79.9 0.7 copy-start.12
  80.5 1.0 copy-start.2
  80.5 15.3 %copy-start.7 = (f32[128,128]{0,1:T(8,128)S(1)}, f32[128,128]{0,1:T(8,128)}, u32[]{:S(2)}) copy-start(f32[128,128]{0,1:T(8,128)} %fusion.238) | copy-start | bytes 196612
  81.5 39.6 %collective-permute-start.6 = (s16[1033,128]{1,0:T(8,128)(2,1)S(1)}, s16[1033,128]{1,0:T(8,128)(2,1)S(1)}, u32[]{:S(2)}, u32[]{:S(2)}) collective-permute-start(s16[1033,128]{1,0:T(8,128)(2,1)S(1)} %copy-done.2), channel_id=1, source_target_pairs={{8,0},{16,8},{24,16},{32,24},{40,32},{48,40},{56,48},{64,56},{72,6... | collective-permute-start | bytes 793352 | tf_op jit(solution)/shard_map/ppermute | solution.py:12
  97.2 23.9 %collective-permute-start.7 = (s16[1033,128]{1,0:T(8,128)(2,1)S(1)}, s16[1033,128]{1,0:T(8,128)(2,1)S(1)}, u32[]{:S(2)}, u32[]{:S(2)}) collective-permute-start(s16[1033,128]{1,0:T(8,128)(2,1)S(1)} %get-tuple-element.33), channel_id=1, source_target_pairs={{40,0},{48,8},{56,16},{64,24},{72,32},{80,40},{88,48},{96,56},{104... | collective-permute-start | bytes 793352 | tf_op jit(solution)/shard_map/ppermute | solution.py:12
  110.3 10.8 %collective-permute-start.8 = (s16[1033,128]{1,0:T(8,128)(2,1)S(1)}, s16[1033,128]{1,0:T(8,128)(2,1)S(1)}, u32[]{:S(2)}, u32[]{:S(2)}) collective-permute-start(s16[1033,128]{1,0:T(8,128)(2,1)S(1)} %get-tuple-element.34), channel_id=1, source_target_pairs={{0,8},{8,16},{16,24},{24,32},{32,40},{40,48},{48,56},{56,64},{64,7... | collective-permute-start | bytes 793352 | tf_op jit(solution)/shard_map/ppermute | solution.py:12
  112.2 40.5 %collective-permute-start.9 = (s16[1033,128]{1,0:T(8,128)(2,1)S(1)}, s16[1033,128]{1,0:T(8,128)(2,1)S(1)}, u32[]{:S(2)}, u32[]{:S(2)}) collective-permute-start(s16[1033,128]{1,0:T(8,128)(2,1)S(1)} %get-tuple-element.35), channel_id=1, source_target_pairs={{0,40},{8,48},{16,56},{24,64},{32,72},{40,80},{48,88},{56,96},{64,... | collective-permute-start | bytes 793352 | tf_op jit(solution)/shard_map/ppermute | solution.py:12
  153.1 1.4 copy-start.5
  157.1 16.0 %all-to-all-start.1 = ((f32[8,2,16,128]{3,2,1,0:T(8,128)}), f32[8,2,16,128]{3,2,1,0:T(8,128)S(1)}, u32[]{:S(2)}, u32[]{:S(2)}) async-start(f32[8,2,16,128]{3,2,1,0:T(8,128)} %maximum_bitcast_fusion), calls=%async_computation.1 | async-start | bytes 262144 | tf_op jit(solution)/shard_map/all_to_all | solution.py:69
  165.3 0.7 copy-start.25
  166.4 0.7 copy-start.10
  170.8 1.0 copy-start.8
  171.8 0.7 copy-start.24

commit v9 on v8

--- a/solution.py
+++ b/solution.py
@@ -46,9 +46,7 @@
 def shift_pair(fwd, bwd, by):
     shape = fwd[0].shape
     fwd, bwd = lax.optimization_barrier((pack(*fwd), pack(*bwd)))
-    got_f, got_b = lax.optimization_barrier(
-        (from_behind(fwd, "context", by), from_behind(bwd, "context", -by))
-    )
+    got_f, got_b = from_behind(fwd, "context", by), from_behind(bwd, "context", -by)
     return unpack(got_f, shape), unpack(got_b, shape)
 
 

time: 175 us -> 171 us (0.977)
  matrix products: 12.8 us -> 10.9 us
    unnamed x54 -> x40, local copies, waits for them, and re-layouts: 8.23 us -> 7.32 us
  transfers between devices with their start and end apart: 12 -> 12, of which waited for: 7 -> 7; matrix products, arithmetic and copies ran while one was open for 10% -> 9% of each run, Pallas kernels for 0% -> 0%
where the time goes in v9:
time: 171 us; the launch traced here: 170 us
  starting transfers between devices  69.2 us (40%)
  waiting for transfers between devices  59.3 us (35%)
  other arithmetic  15.9 us (9%)
  local copies, waits for them, and re-layouts  12.9 us (8%)
  matrix products  10.9 us (6%)
  between operations  2 us (1%)
    ppermute x10, waiting for transfers between devices, from_behind(): return lax.ppermute(x, axis, pairs)  59.3 us
    ppermute x10, starting transfers between devices, from_behind(): return lax.ppermute(x, axis, pairs)  57 us
    unnamed x40, local copies, waits for them, and re-layouts  7.32 us
    all_to_all x1, starting transfers between devices, scatter_sum(): got = lax.all_to_all(parts, axis, 0, 0, tiled=True)  6.99 us
    all_to_all x1, starting transfers between devices, local(): lax.all_to_all(jnp.broadcast_to(piece, (count,) + piece.shape), 'tensor',...  5.23 us
  transfers between devices with their start and end apart: 12, of which 7 were waited for; matrix products, arithmetic and copies ran while one was open for 9% of the time, Pallas kernels for 0%

profile of v9, /device:TPU:75, one launch (start us, length us, event | category | flops | bytes accessed | tf_op | source)
XLA Modules:
  0.0 170.3 jit_solution(18118045791986346466)
XLA Ops:
  0.6 0.7 pad_maximum_fusion
  1.4 0.6 broadcast_in_dim.29
  2.0 5.2 %all-to-all-start = ((bf16[8,2,16,128]{3,2,1,0:T(8,128)(2,1)}), bf16[8,2,16,128]{3,2,1,0:T(8,128)(2,1)S(1)}, u32[]{:S(2)}, u32[]{:S(2)}) async-start(bf16[8,2,16,128]{3,2,1,0:T(8,128)(2,1)} %broadcast_in_dim.29), calls=%async_computation | async-start | bytes 131072 | tf_op jit(solution)/shard_map/all_to_all | solution.py:92
  7.3 0.7 copy.32
  8.2 0.6 copy-done.9
  9.0 0.6 slice.174
  9.6 0.6 compare_convert_fusion
  11.0 0.3 reduce_window_sum.30
  11.7 0.8 copy-done.6
  12.7 0.5 abs_reduce_fusion.7
  13.3 0.5 abs_reduce_fusion.6
  14.4 3.5 %collective-permute-start = (s16[1033,128]{1,0:T(8,128)(2,1)S(1)}, s16[1033,128]{1,0:T(8,128)(2,1)S(1)}, u32[]{:S(2)}, u32[]{:S(2)}) collective-permute-start(s16[1033,128]{1,0:T(8,128)(2,1)S(1)} %get-tuple-element.14), channel_id=1, source_target_pairs={{0,8},{8,16},{16,24},{24,32},{32,40},{40,48},{48,56},{56,64},{64,7... | collective-permute-start | bytes 793352 | tf_op jit(solution)/shard_map/ppermute | solution.py:12
  18.0 1.9 %collective-permute-start.1 = (s16[1033,128]{1,0:T(8,128)(2,1)S(1)}, s16[1033,128]{1,0:T(8,128)(2,1)S(1)}, u32[]{:S(2)}, u32[]{:S(2)}) collective-permute-start(s16[1033,128]{1,0:T(8,128)(2,1)S(1)} %get-tuple-element.15), channel_id=1, source_target_pairs={{8,0},{16,8},{24,16},{32,24},{40,32},{48,40},{56,48},{64,56},{72,6... | collective-permute-start | bytes 793352 | tf_op jit(solution)/shard_map/ppermute | solution.py:12
  19.9 4.0 %collective-permute-done = s16[1033,128]{1,0:T(8,128)(2,1)S(1)} collective-permute-done((s16[1033,128]{1,0:T(8,128)(2,1)S(1)}, s16[1033,128]{1,0:T(8,128)(2,1)S(1)}, u32[]{:S(2)}, u32[]{:S(2)}) %collective-permute-start) | collective-permute-done | bytes 264480 | tf_op jit(solution)/shard_map/ppermute | solution.py:12
  24.0 4.9 %collective-permute-done.1 = s16[1033,128]{1,0:T(8,128)(2,1)S(1)} collective-permute-done((s16[1033,128]{1,0:T(8,128)(2,1)S(1)}, s16[1033,128]{1,0:T(8,128)(2,1)S(1)}, u32[]{:S(2)}, u32[]{:S(2)}) %collective-permute-start.1) | collective-permute-done | bytes 264480 | tf_op jit(solution)/shard_map/ppermute | solution.py:12
  29.0 0.7 abs_reduce_fusion.4
  29.9 0.6 fusion.232
  30.5 0.5 copy-done.14
  31.1 0.7 clamp_convert_fusion.4
  31.9 4.8 %collective-permute-start.2 = (s16[1033,128]{1,0:T(8,128)(2,1)S(1)}, s16[1033,128]{1,0:T(8,128)(2,1)S(1)}, u32[]{:S(2)}, u32[]{:S(2)}) collective-permute-start(s16[1033,128]{1,0:T(8,128)(2,1)S(1)} %get-tuple-element.16), channel_id=1, source_target_pairs={{0,16},{8,24},{16,32},{24,40},{32,48},{40,56},{48,64},{56,72},{64,... | collective-permute-start | bytes 793352 | tf_op jit(solution)/shard_map/ppermute | solution.py:12
  36.7 2.4 %collective-permute-start.3 = (s16[1033,128]{1,0:T(8,128)(2,1)S(1)}, s16[1033,128]{1,0:T(8,128)(2,1)S(1)}, u32[]{:S(2)}, u32[]{:S(2)}) collective-permute-start(s16[1033,128]{1,0:T(8,128)(2,1)S(1)} %get-tuple-element.17), channel_id=1, source_target_pairs={{16,0},{24,8},{32,16},{40,24},{48,32},{56,40},{64,48},{72,56},{80,... | collective-permute-start | bytes 793352 | tf_op jit(solution)/shard_map/ppermute | solution.py:12
  39.1 3.9 %collective-permute-done.2 = s16[1033,128]{1,0:T(8,128)(2,1)S(1)} collective-permute-done((s16[1033,128]{1,0:T(8,128)(2,1)S(1)}, s16[1033,128]{1,0:T(8,128)(2,1)S(1)}, u32[]{:S(2)}, u32[]{:S(2)}) %collective-permute-start.2) | collective-permute-done | bytes 264480 | tf_op jit(solution)/shard_map/ppermute | solution.py:12
  43.0 0.7 copy-done.4
  43.8 4.5 %collective-permute-done.3 = s16[1033,128]{1,0:T(8,128)(2,1)S(1)} collective-permute-done((s16[1033,128]{1,0:T(8,128)(2,1)S(1)}, s16[1033,128]{1,0:T(8,128)(2,1)S(1)}, u32[]{:S(2)}, u32[]{:S(2)}) %collective-permute-start.3) | collective-permute-done | bytes 264480 | tf_op jit(solution)/shard_map/ppermute | solution.py:12
  48.3 1.0 slice.230
  49.4 0.6 copy-done.10
  50.0 0.8 fusion.20
  51.7 0.7 slice_convert_fusion.9
  52.7 0.7 slice_convert_fusion.8
  53.5 0.9 fusion.63
  54.4 7.6 %collective-permute-start.4 = (s16[1033,128]{1,0:T(8,128)(2,1)}, s16[1033,128]{1,0:T(8,128)(2,1)S(1)}, u32[]{:S(2)}, u32[]{:S(2)}) collective-permute-start(s16[1033,128]{1,0:T(8,128)(2,1)} %get-tuple-element.22), channel_id=1, source_target_pairs={{0,32},{8,40},{16,48},{24,56},{32,64},{40,72},{48,80},{56,88},{64,... | collective-permute-start | bytes 793352 | tf_op jit(solution)/shard_map/ppermute | solution.py:12
  62.2 2.6 %collective-permute-start.5 = (s16[1033,128]{1,0:T(8,128)(2,1)}, s16[1033,128]{1,0:T(8,128)(2,1)S(1)}, u32[]{:S(2)}, u32[]{:S(2)}) collective-permute-start(s16[1033,128]{1,0:T(8,128)(2,1)} %get-tuple-element.20), channel_id=1, source_target_pairs={{32,0},{40,8},{48,16},{56,24},{64,32},{72,40},{80,48},{88,56},{96,... | collective-permute-start | bytes 793352 | tf_op jit(solution)/shard_map/ppermute | solution.py:12
  64.8 4.8 %collective-permute-done.4 = s16[1033,128]{1,0:T(8,128)(2,1)S(1)} collective-permute-done((s16[1033,128]{1,0:T(8,128)(2,1)}, s16[1033,128]{1,0:T(8,128)(2,1)S(1)}, u32[]{:S(2)}, u32[]{:S(2)}) %collective-permute-start.4) | collective-permute-done | bytes 264480 | tf_op jit(solution)/shard_map/ppermute | solution.py:12
  69.8 0.4 abs_reduce_fusion.1
  70.3 5.9 %collective-permute-done.5 = s16[1033,128]{1,0:T(8,128)(2,1)S(1)} collective-permute-done((s16[1033,128]{1,0:T(8,128)(2,1)}, s16[1033,128]{1,0:T(8,128)(2,1)S(1)}, u32[]{:S(2)}, u32[]{:S(2)}) %collective-permute-start.5) | collective-permute-done | bytes 264480 | tf_op jit(solution)/shard_map/ppermute | solution.py:12
  76.3 0.4 abs_reduce_fusion
  77.0 0.4 clamp_convert_fusion.1
  77.4 0.4 clamp_convert_fusion
  77.9 14.4 %collective-permute-start.6 = (s16[1033,128]{1,0:T(8,128)(2,1)}, s16[1033,128]{1,0:T(8,128)(2,1)S(1)}, u32[]{:S(2)}, u32[]{:S(2)}) collective-permute-start(s16[1033,128]{1,0:T(8,128)(2,1)} %get-tuple-element.20), channel_id=1, source_target_pairs={{8,0},{16,8},{24,16},{32,24},{40,32},{48,40},{56,48},{64,56},{72,6... | collective-permute-start | bytes 793352 | tf_op jit(solution)/shard_map/ppermute | solution.py:12
  92.3 1.3 fusion.6
  93.6 9.2 %collective-permute-start.7 = (s16[1033,128]{1,0:T(8,128)(2,1)S(1)}, s16[1033,128]{1,0:T(8,128)(2,1)S(1)}, u32[]{:S(2)}, u32[]{:S(2)}) collective-permute-start(s16[1033,128]{1,0:T(8,128)(2,1)S(1)} %get-tuple-element.21), channel_id=1, source_target_pairs={{40,0},{48,8},{56,16},{64,24},{72,32},{80,40},{88,48},{96,56},{104... | collective-permute-start | bytes 793352 | tf_op jit(solution)/shard_map/ppermute | solution.py:12
  102.8 1.5 fusion.8
  104.3 0.3 reduce_window_sum.32
  104.6 0.3 reduce_window_sum.31
  104.9 1.9 %collective-permute-start.8 = (s16[1033,128]{1,0:T(8,128)(2,1)}, s16[1033,128]{1,0:T(8,128)(2,1)S(1)}, u32[]{:S(2)}, u32[]{:S(2)}) collective-permute-start(s16[1033,128]{1,0:T(8,128)(2,1)} %get-tuple-element.22), channel_id=1, source_target_pairs={{0,8},{8,16},{16,24},{24,32},{32,40},{40,48},{48,56},{56,64},{64,7... | collective-permute-start | bytes 793352 | tf_op jit(solution)/shard_map/ppermute | solution.py:12
  106.8 8.7 %collective-permute-start.9 = (s16[1033,128]{1,0:T(8,128)(2,1)S(1)}, s16[1033,128]{1,0:T(8,128)(2,1)S(1)}, u32[]{:S(2)}, u32[]{:S(2)}) collective-permute-start(s16[1033,128]{1,0:T(8,128)(2,1)S(1)} %get-tuple-element.23), channel_id=1, source_target_pairs={{0,40},{8,48},{16,56},{24,64},{32,72},{40,80},{48,88},{56,96},{64,... | collective-permute-start | bytes 793352 | tf_op jit(solution)/shard_map/ppermute | solution.py:12
  115.9 31.3 %collective-permute-done.9 = s16[1033,128]{1,0:T(8,128)(2,1)S(1)} collective-permute-done((s16[1033,128]{1,0:T(8,128)(2,1)S(1)}, s16[1033,128]{1,0:T(8,128)(2,1)S(1)}, u32[]{:S(2)}, u32[]{:S(2)}) %collective-permute-start.9) | collective-permute-done | bytes 264480 | tf_op jit(solution)/shard_map/ppermute | solution.py:12
  147.3 0.6 copy-done
  148.1 1.3 convolution_bitcast_fusion.3
  149.8 0.9 copy-done.1
  150.7 1.3 convolution_bitcast_fusion.2
  152.3 0.7 maximum_bitcast_fusion
  153.0 7.0 %all-to-all-start.1 = ((f32[8,2,16,128]{3,2,1,0:T(8,128)}), f32[8,2,16,128]{3,2,1,0:T(8,128)}, u32[]{:S(2)}, u32[]{:S(2)}) async-start(f32[8,2,16,128]{3,2,1,0:T(8,128)} %maximum_bitcast_fusion), calls=%async_computation.1 | async-start | bytes 262144 | tf_op jit(solution)/shard_map/all_to_all | solution.py:67
  160.2 1.2 multiply_reduce_fusion.1
  161.4 0.6 copy-done.18
  162.1 0.4 fusion.14
  162.7 1.2 fusion.2
  163.9 0.4 fusion.1
  164.3 1.9 %fusion.3 = f32[16,1,128]{2,1,0:T(1,128)S(1)} fusion(f32[16,128,1]{1,2,0:T(1,128)S(1)} %bitcast.251, f32[16,128]{1,0:T(8,128)S(1)} %reduce_window_sum.30, pred[128,128]{0,1:T(8,128)(4,1)S(1)} %fusion.79), kind=kOutput, calls=%fused_computation.11 | convolution fusion | flops 3670016 | bytes 40960 | tf_op jit(solution)/shard_map/hij,hi->hj/dot_general | solution.py:165
  166.4 1.0 copy.39
  167.4 0.7 copy-done.17
  168.1 0.7 multiply_subtract_fusion
  168.7 0.9 reduce_sum.98
  169.6 0.6 slice_bitcast_fusion
  (138 shorter events, 6.5 us)
Async XLA Ops:
  0.6 11.0 %copy-start.5 = (bf16[128,1024]{1,0:T(8,128)(2,1)S(1)}, bf16[128,1024]{1,0:T(8,128)(2,1)}, u32[]{:S(2)}) copy-start(bf16[128,1024]{1,0:T(8,128)(2,1)} %param.8) | copy-start | bytes 786436
  2.0 10.7 %all-to-all-start = ((bf16[8,2,16,128]{3,2,1,0:T(8,128)(2,1)}), bf16[8,2,16,128]{3,2,1,0:T(8,128)(2,1)S(1)}, u32[]{:S(2)}, u32[]{:S(2)}) async-start(bf16[8,2,16,128]{3,2,1,0:T(8,128)(2,1)} %broadcast_in_dim.29), calls=%async_computation | async-start | bytes 131072 | tf_op jit(solution)/shard_map/all_to_all | solution.py:92
  8.2 0.7 copy-start.9
  8.9 2.0 %copy-start.2 = (f32[16,128]{1,0:T(8,128)S(1)}, f32[16,128]{1,0:T(8,128)}, u32[]{:S(2)}) copy-start(f32[16,128]{1,0:T(8,128)} %param.10) | copy-start | bytes 24580
  9.0 0.6 copy-start.7
  10.2 0.7 copy-start.16
  11.6 1.0 copy-start.6
  14.4 9.5 %collective-permute-start = (s16[1033,128]{1,0:T(8,128)(2,1)S(1)}, s16[1033,128]{1,0:T(8,128)(2,1)S(1)}, u32[]{:S(2)}, u32[]{:S(2)}) collective-permute-start(s16[1033,128]{1,0:T(8,128)(2,1)S(1)} %get-tuple-element.14), channel_id=1, source_target_pairs={{0,8},{8,16},{16,24},{24,32},{32,40},{40,48},{48,56},{56,64},{64,7... | collective-permute-start | bytes 793352 | tf_op jit(solution)/shard_map/ppermute | solution.py:12
  18.0 10.9 %collective-permute-start.1 = (s16[1033,128]{1,0:T(8,128)(2,1)S(1)}, s16[1033,128]{1,0:T(8,128)(2,1)S(1)}, u32[]{:S(2)}, u32[]{:S(2)}) collective-permute-start(s16[1033,128]{1,0:T(8,128)(2,1)S(1)} %get-tuple-element.15), channel_id=1, source_target_pairs={{8,0},{16,8},{24,16},{32,24},{40,32},{48,40},{56,48},{64,56},{72,6... | collective-permute-start | bytes 793352 | tf_op jit(solution)/shard_map/ppermute | solution.py:12
  30.5 0.5 copy-start.14
  30.5 0.5 copy-start.12
  31.9 11.1 %collective-permute-start.2 = (s16[1033,128]{1,0:T(8,128)(2,1)S(1)}, s16[1033,128]{1,0:T(8,128)(2,1)S(1)}, u32[]{:S(2)}, u32[]{:S(2)}) collective-permute-start(s16[1033,128]{1,0:T(8,128)(2,1)S(1)} %get-tuple-element.16), channel_id=1, source_target_pairs={{0,16},{8,24},{16,32},{24,40},{32,48},{40,56},{48,64},{56,72},{64,... | collective-permute-start | bytes 793352 | tf_op jit(solution)/shard_map/ppermute | solution.py:12
  36.7 11.6 %collective-permute-start.3 = (s16[1033,128]{1,0:T(8,128)(2,1)S(1)}, s16[1033,128]{1,0:T(8,128)(2,1)S(1)}, u32[]{:S(2)}, u32[]{:S(2)}) collective-permute-start(s16[1033,128]{1,0:T(8,128)(2,1)S(1)} %get-tuple-element.17), channel_id=1, source_target_pairs={{16,0},{24,8},{32,16},{40,24},{48,32},{56,40},{64,48},{72,56},{80,... | collective-permute-start | bytes 793352 | tf_op jit(solution)/shard_map/ppermute | solution.py:12
  43.0 0.7 copy-start.4
  48.2 1.1 copy-start.3
  49.4 0.7 copy-start.10
  49.4 0.7 copy-start.11
  51.6 0.7 copy-start.15
  52.7 0.7 copy-start.13
  54.4 7.6 %copy-start.8 = (s32[128]{0:T(128)S(1)}, s32[128]{0:T(128)}, u32[]{:S(2)}) copy-start(s32[128]{0:T(128)} %copy-done.7) | copy-start | bytes 1540
  54.4 15.3 %collective-permute-start.4 = (s16[1033,128]{1,0:T(8,128)(2,1)}, s16[1033,128]{1,0:T(8,128)(2,1)S(1)}, u32[]{:S(2)}, u32[]{:S(2)}) collective-permute-start(s16[1033,128]{1,0:T(8,128)(2,1)} %get-tuple-element.22), channel_id=1, source_target_pairs={{0,32},{8,40},{16,48},{24,56},{32,64},{40,72},{48,80},{56,88},{64,... | collective-permute-start | bytes 793352 | tf_op jit(solution)/shard_map/ppermute | solution.py:12
  62.2 14.0 %collective-permute-start.5 = (s16[1033,128]{1,0:T(8,128)(2,1)}, s16[1033,128]{1,0:T(8,128)(2,1)S(1)}, u32[]{:S(2)}, u32[]{:S(2)}) collective-permute-start(s16[1033,128]{1,0:T(8,128)(2,1)} %get-tuple-element.20), channel_id=1, source_target_pairs={{32,0},{40,8},{48,16},{56,24},{64,32},{72,40},{80,48},{88,56},{96,... | collective-permute-start | bytes 793352 | tf_op jit(solution)/shard_map/ppermute | solution.py:12
  77.9 37.6 %collective-permute-start.6 = (s16[1033,128]{1,0:T(8,128)(2,1)}, s16[1033,128]{1,0:T(8,128)(2,1)S(1)}, u32[]{:S(2)}, u32[]{:S(2)}) collective-permute-start(s16[1033,128]{1,0:T(8,128)(2,1)} %get-tuple-element.20), channel_id=1, source_target_pairs={{8,0},{16,8},{24,16},{32,24},{40,32},{48,40},{56,48},{64,56},{72,6... | collective-permute-start | bytes 793352 | tf_op jit(solution)/shard_map/ppermute | solution.py:12
  93.6 21.9 %collective-permute-start.7 = (s16[1033,128]{1,0:T(8,128)(2,1)S(1)}, s16[1033,128]{1,0:T(8,128)(2,1)S(1)}, u32[]{:S(2)}, u32[]{:S(2)}) collective-permute-start(s16[1033,128]{1,0:T(8,128)(2,1)S(1)} %get-tuple-element.21), channel_id=1, source_target_pairs={{40,0},{48,8},{56,16},{64,24},{72,32},{80,40},{88,48},{96,56},{104... | collective-permute-start | bytes 793352 | tf_op jit(solution)/shard_map/ppermute | solution.py:12
  104.9 10.7 %collective-permute-start.8 = (s16[1033,128]{1,0:T(8,128)(2,1)}, s16[1033,128]{1,0:T(8,128)(2,1)S(1)}, u32[]{:S(2)}, u32[]{:S(2)}) collective-permute-start(s16[1033,128]{1,0:T(8,128)(2,1)} %get-tuple-element.22), channel_id=1, source_target_pairs={{0,8},{8,16},{16,24},{24,32},{32,40},{40,48},{48,56},{56,64},{64,7... | collective-permute-start | bytes 793352 | tf_op jit(solution)/shard_map/ppermute | solution.py:12
  106.8 40.4 %collective-permute-start.9 = (s16[1033,128]{1,0:T(8,128)(2,1)S(1)}, s16[1033,128]{1,0:T(8,128)(2,1)S(1)}, u32[]{:S(2)}, u32[]{:S(2)}) collective-permute-start(s16[1033,128]{1,0:T(8,128)(2,1)S(1)} %get-tuple-element.23), channel_id=1, source_target_pairs={{0,40},{8,48},{16,56},{24,64},{32,72},{40,80},{48,88},{56,96},{64,... | collective-permute-start | bytes 793352 | tf_op jit(solution)/shard_map/ppermute | solution.py:12
  147.2 0.7 copy-start
  149.7 1.0 copy-start.1
  153.0 15.8 %all-to-all-start.1 = ((f32[8,2,16,128]{3,2,1,0:T(8,128)}), f32[8,2,16,128]{3,2,1,0:T(8,128)}, u32[]{:S(2)}, u32[]{:S(2)}) async-start(f32[8,2,16,128]{3,2,1,0:T(8,128)} %maximum_bitcast_fusion), calls=%async_computation.1 | async-start | bytes 262144 | tf_op jit(solution)/shard_map/all_to_all | solution.py:67
  161.4 0.7 copy-start.18
  167.4 0.7 copy-start.17

commit v10 on v9

--- a/solution.py
+++ b/solution.py
@@ -113,6 +113,25 @@
     enter_dy = enter[:, :, None] * dys
     local_state = jnp.einsum("hlp,ln->hpn", left_u, bmat, precision=HIGH)
     local_adj = jnp.einsum("hlp,ln->hpn", enter_dy, cmat, precision=HIGH)
+
+    index = jnp.arange(length)
+    keep = (index[:, None] >= index[None, :]) & (seg[:, None] == seg[None, :])
+    weights = jnp.exp(jnp.where(keep[None], logc[:, :, None] - logc[:, None, :], -1e30))
+    scores = jnp.dot(c_bf, b_bf.T, preferred_element_type=jnp.float32)
+    mixed = weights * scores[None]
+    core_loc = jnp.einsum("hij,hip->hjp", mixed, dys, precision=HIGH)
+    pairs = jnp.einsum("hip,hjp->hij", dys, moved, precision=HIGH)
+    paired = mixed * pairs
+    col_total = jnp.sum(paired, axis=1)
+    row_total = jnp.sum(paired, axis=2)
+    inner = jnp.cumsum(col_total, axis=1) - (jnp.cumsum(row_total, axis=1) - row_total)
+    weighted = jnp.sum(weights * pairs, axis=0)
+    gb_loc = jnp.dot(weighted.T, cmat, precision=HIGH)
+    gc_loc = jnp.dot(weighted, bmat, precision=HIGH)
+
+    local_state, local_adj, weights, core_loc, inner, gb_loc, gc_loc = lax.optimization_barrier(
+        (local_state, local_adj, weights, core_loc, inner, gb_loc, gc_loc)
+    )
 
     reach = 3 * lax.axis_size("context") // 16
     low = reach & -reach
@@ -142,21 +161,6 @@
     s_in = combine(got[0], got[1])[0]
     g_in = combine(got[2], got[3])[0]
 
-    index = jnp.arange(length)
-    keep = (index[:, None] >= index[None, :]) & (seg[:, None] == seg[None, :])
-    weights = jnp.exp(jnp.where(keep[None], logc[:, :, None] - logc[:, None, :], -1e30))
-    scores = jnp.dot(c_bf, b_bf.T, preferred_element_type=jnp.float32)
-    mixed = weights * scores[None]
-    core_loc = jnp.einsum("hij,hip->hjp", mixed, dys, precision=HIGH)
-    pairs = jnp.einsum("hip,hjp->hij", dys, moved, precision=HIGH)
-    paired = mixed * pairs
-    col_total = jnp.sum(paired, axis=1)
-    row_total = jnp.sum(paired, axis=2)
-    inner = jnp.cumsum(col_total, axis=1) - (jnp.cumsum(row_total, axis=1) - row_total)
-    weighted = jnp.sum(weights * pairs, axis=0)
-    gb_loc = jnp.dot(weighted.T, cmat, precision=HIGH)
-    gc_loc = jnp.dot(weighted, bmat, precision=HIGH)
-
     b_adj = jnp.einsum("ln,hpn->hlp", bmat, g_in, precision=HIGH)
     c_state = jnp.einsum("ln,hpn->hlp", cmat, s_in, precision=HIGH)
     core = core_loc + leave[:, :, None] * b_adj

time: 171 us -> 176 us (1.029)
  the two profiles are of different devices: /device:TPU:75 before, /device:TPU:66 now
where the time goes in v10:
time: 176 us; the launch traced here: 175 us
  waiting for transfers between devices  69.1 us (39%)
  starting transfers between devices  61 us (35%)
  local copies, waits for them, and re-layouts  15.4 us (9%)
  other arithmetic  14.9 us (8%)
  matrix products  12.7 us (7%)
  between operations  2.06 us (1%)
    ppermute x10, waiting for transfers between devices, from_behind(): return lax.ppermute(x, axis, pairs)  65.3 us
    ppermute x10, starting transfers between devices, from_behind(): return lax.ppermute(x, axis, pairs)  52.9 us
    unnamed x68, local copies, waits for them, and re-layouts  8.53 us
    all_to_all x1, starting transfers between devices, local(): lax.all_to_all(jnp.broadcast_to(piece, (count,) + piece.shape), 'tensor',...  4.47 us
    all_to_all x1, waiting for transfers between devices, scatter_sum(): got = lax.all_to_all(parts, axis, 0, 0, tiled=True)  3.81 us
    all_to_all x1, starting transfers between devices, scatter_sum(): got = lax.all_to_all(parts, axis, 0, 0, tiled=True)  3.54 us
  transfers between devices with their start and end apart: 12, of which 9 were waited for; matrix products, arithmetic and copies ran while one was open for 4% of the time, Pallas kernels for 0%

profile of v10, /device:TPU:66, one launch (start us, length us, event | category | flops | bytes accessed | tf_op | source)
XLA Modules:
  0.0 175.1 jit_solution(16239450389133994742)
XLA Ops:
  0.6 0.7 pad_maximum_fusion
  1.4 0.6 broadcast_in_dim.31
  2.0 4.5 %all-to-all-start = ((bf16[8,2,16,128]{3,2,1,0:T(8,128)(2,1)}), bf16[8,2,16,128]{3,2,1,0:T(8,128)(2,1)S(1)}, u32[]{:S(2)}, u32[]{:S(2)}) async-start(bf16[8,2,16,128]{3,2,1,0:T(8,128)(2,1)} %broadcast_in_dim.31), calls=%async_computation | async-start | bytes 131072 | tf_op jit(solution)/shard_map/all_to_all | solution.py:92
  6.5 0.7 copy.32
  7.5 0.5 copy-done.23
  8.1 0.6 slice.172
  9.4 0.6 compare_convert_fusion
  10.1 0.6 copy-done.7
  11.6 0.8 copy-done.4
  12.6 2.1 %fusion.4 = f32[16,128,64]{1,2,0:T(8,128)} fusion(bf16[16,128,64]{1,2,0:T(8,128)(2,1)S(1)} %bitcast.189, f32[128,128]{0,1:T(8,128)S(1)} %fusion.217, f32[16,128]{1,0:T(8,128)S(1)} %reduce_window_sum.30, pred[128,128]{0,1:T(8,128)(4,1)S(1)} %fusion.60), kind=kOutput, calls=%fused_computation.12 | convolution fusion | flops 202113024 | bytes 876544 | tf_op jit(solution)/shard_map/hij,hip->hjp/dot_general | solution.py:122
  14.8 2.3 %fusion.6 = (f32[16,128]{1,0:T(8,128)S(1)}, f32[16,128]{1,0:T(8,128)S(1)}, f32[128,128]{0,1:T(8,128)S(1)}, f32[16,128,128]{1,2,0:T(8,128)}) fusion(f32[128,128]{0,1:T(8,128)S(1)} %fusion.217, f32[16,128]{1,0:T(8,128)S(1)} %reduce_window_sum.30, pred[128,128]{0,1:T(8,128)(4,1)S(1)} %fusion.60, bf16[16,128,64]{1,2,0:T(8,128)(2,1)S(1)} %bitcast.190, ...), kind=kOutput, calls=%fused_computation.23 | convolution fusion | flops 203534336 | bytes 2015232 | tf_op jit(solution)/shard_map/hip,hjp->hij/dot_general | solution.py:123
  17.1 0.9 fusion.219
  18.7 0.4 fusion.36
  19.5 0.6 subtract_subtract_fusion
  21.2 3.8 %collective-permute-start = (s16[1033,128]{1,0:T(8,128)(2,1)S(1)}, s16[1033,128]{1,0:T(8,128)(2,1)S(1)}, u32[]{:S(2)}, u32[]{:S(2)}) collective-permute-start(s16[1033,128]{1,0:T(8,128)(2,1)S(1)} %get-tuple-element.24), channel_id=1, source_target_pairs={{0,8},{8,16},{16,24},{24,32},{32,40},{40,48},{48,56},{56,64},{64,7... | collective-permute-start | bytes 793352 | tf_op jit(solution)/shard_map/ppermute | solution.py:12
  25.0 2.0 %collective-permute-start.1 = (s16[1033,128]{1,0:T(8,128)(2,1)S(1)}, s16[1033,128]{1,0:T(8,128)(2,1)S(1)}, u32[]{:S(2)}, u32[]{:S(2)}) collective-permute-start(s16[1033,128]{1,0:T(8,128)(2,1)S(1)} %get-tuple-element.25), channel_id=1, source_target_pairs={{8,0},{16,8},{24,16},{32,24},{40,32},{48,40},{56,48},{64,56},{72,6... | collective-permute-start | bytes 793352 | tf_op jit(solution)/shard_map/ppermute | solution.py:12
  27.0 4.8 %collective-permute-done = s16[1033,128]{1,0:T(8,128)(2,1)S(1)} collective-permute-done((s16[1033,128]{1,0:T(8,128)(2,1)S(1)}, s16[1033,128]{1,0:T(8,128)(2,1)S(1)}, u32[]{:S(2)}, u32[]{:S(2)}) %collective-permute-start) | collective-permute-done | bytes 264480 | tf_op jit(solution)/shard_map/ppermute | solution.py:12
  32.0 4.9 %collective-permute-done.1 = s16[1033,128]{1,0:T(8,128)(2,1)S(1)} collective-permute-done((s16[1033,128]{1,0:T(8,128)(2,1)S(1)}, s16[1033,128]{1,0:T(8,128)(2,1)S(1)}, u32[]{:S(2)}, u32[]{:S(2)}) %collective-permute-start.1) | collective-permute-done | bytes 264480 | tf_op jit(solution)/shard_map/ppermute | solution.py:12
  37.0 0.7 abs_reduce_fusion.4
  37.8 0.6 fusion.211
  38.5 0.6 copy-done.28
  39.1 0.8 clamp_convert_fusion.4
  40.0 5.2 %collective-permute-start.2 = (s16[1033,128]{1,0:T(8,128)(2,1)S(1)}, s16[1033,128]{1,0:T(8,128)(2,1)S(1)}, u32[]{:S(2)}, u32[]{:S(2)}) collective-permute-start(s16[1033,128]{1,0:T(8,128)(2,1)S(1)} %get-tuple-element.26), channel_id=1, source_target_pairs={{0,16},{8,24},{16,32},{24,40},{32,48},{40,56},{48,64},{56,72},{64,... | collective-permute-start | bytes 793352 | tf_op jit(solution)/shard_map/ppermute | solution.py:12
  45.2 2.3 %collective-permute-start.3 = (s16[1033,128]{1,0:T(8,128)(2,1)S(1)}, s16[1033,128]{1,0:T(8,128)(2,1)S(1)}, u32[]{:S(2)}, u32[]{:S(2)}) collective-permute-start(s16[1033,128]{1,0:T(8,128)(2,1)S(1)} %get-tuple-element.27), channel_id=1, source_target_pairs={{16,0},{24,8},{32,16},{40,24},{48,32},{56,40},{64,48},{72,56},{80,... | collective-permute-start | bytes 793352 | tf_op jit(solution)/shard_map/ppermute | solution.py:12
  47.4 4.6 %collective-permute-done.2 = s16[1033,128]{1,0:T(8,128)(2,1)S(1)} collective-permute-done((s16[1033,128]{1,0:T(8,128)(2,1)S(1)}, s16[1033,128]{1,0:T(8,128)(2,1)S(1)}, u32[]{:S(2)}, u32[]{:S(2)}) %collective-permute-start.2) | collective-permute-done | bytes 264480 | tf_op jit(solution)/shard_map/ppermute | solution.py:12
  52.1 0.7 copy-done.3
  52.8 0.7 exp2.372
  53.4 4.9 %collective-permute-done.3 = s16[1033,128]{1,0:T(8,128)(2,1)S(1)} collective-permute-done((s16[1033,128]{1,0:T(8,128)(2,1)S(1)}, s16[1033,128]{1,0:T(8,128)(2,1)S(1)}, u32[]{:S(2)}, u32[]{:S(2)}) %collective-permute-start.3) | collective-permute-done | bytes 264480 | tf_op jit(solution)/shard_map/ppermute | solution.py:12
  58.4 0.7 exp2.377
  59.0 1.0 slice.230
  60.1 0.6 copy-done.11
  60.8 0.8 fusion.15
  62.2 0.7 slice_convert_fusion.9
  63.0 0.7 slice_convert_fusion.8
  64.2 0.7 copy-done.20
  65.0 11.9 %collective-permute-start.4 = (s16[1033,128]{1,0:T(8,128)(2,1)S(1)}, s16[1033,128]{1,0:T(8,128)(2,1)S(1)}, u32[]{:S(2)}, u32[]{:S(2)}) collective-permute-start(s16[1033,128]{1,0:T(8,128)(2,1)S(1)} %get-tuple-element.34), channel_id=1, source_target_pairs={{0,32},{8,40},{16,48},{24,56},{32,64},{40,72},{48,80},{56,88},{64,... | collective-permute-start | bytes 793352 | tf_op jit(solution)/shard_map/ppermute | solution.py:12
  76.9 1.9 %collective-permute-start.5 = (s16[1033,128]{1,0:T(8,128)(2,1)S(1)}, s16[1033,128]{1,0:T(8,128)(2,1)S(1)}, u32[]{:S(2)}, u32[]{:S(2)}) collective-permute-start(s16[1033,128]{1,0:T(8,128)(2,1)S(1)} %get-tuple-element.30), channel_id=1, source_target_pairs={{32,0},{40,8},{48,16},{56,24},{64,32},{72,40},{80,48},{88,56},{96,... | collective-permute-start | bytes 793352 | tf_op jit(solution)/shard_map/ppermute | solution.py:12
  78.9 10.4 %collective-permute-done.4 = s16[1033,128]{1,0:T(8,128)(2,1)S(1)} collective-permute-done((s16[1033,128]{1,0:T(8,128)(2,1)S(1)}, s16[1033,128]{1,0:T(8,128)(2,1)S(1)}, u32[]{:S(2)}, u32[]{:S(2)}) %collective-permute-start.4) | collective-permute-done | bytes 264480 | tf_op jit(solution)/shard_map/ppermute | solution.py:12
  89.4 0.4 abs_reduce_fusion.1
  89.9 3.6 %collective-permute-done.5 = s16[1033,128]{1,0:T(8,128)(2,1)S(1)} collective-permute-done((s16[1033,128]{1,0:T(8,128)(2,1)S(1)}, s16[1033,128]{1,0:T(8,128)(2,1)S(1)}, u32[]{:S(2)}, u32[]{:S(2)}) %collective-permute-start.5) | collective-permute-done | bytes 264480 | tf_op jit(solution)/shard_map/ppermute | solution.py:12
  93.6 0.4 abs_reduce_fusion
  95.2 6.3 %collective-permute-start.6 = (s16[1033,128]{1,0:T(8,128)(2,1)S(1)}, s16[1033,128]{1,0:T(8,128)(2,1)S(1)}, u32[]{:S(2)}, u32[]{:S(2)}) collective-permute-start(s16[1033,128]{1,0:T(8,128)(2,1)S(1)} %get-tuple-element.30), channel_id=1, source_target_pairs={{8,0},{16,8},{24,16},{32,24},{40,32},{48,40},{56,48},{64,56},{72,6... | collective-permute-start | bytes 793352 | tf_op jit(solution)/shard_map/ppermute | solution.py:12
  101.5 8.7 %collective-permute-start.7 = (s16[1033,128]{1,0:T(8,128)(2,1)S(1)}, s16[1033,128]{1,0:T(8,128)(2,1)S(1)}, u32[]{:S(2)}, u32[]{:S(2)}) collective-permute-start(s16[1033,128]{1,0:T(8,128)(2,1)S(1)} %get-tuple-element.31), channel_id=1, source_target_pairs={{40,0},{48,8},{56,16},{64,24},{72,32},{80,40},{88,48},{96,56},{104... | collective-permute-start | bytes 793352 | tf_op jit(solution)/shard_map/ppermute | solution.py:12
  110.2 1.9 %collective-permute-start.8 = (s16[1033,128]{1,0:T(8,128)(2,1)S(1)}, s16[1033,128]{1,0:T(8,128)(2,1)S(1)}, u32[]{:S(2)}, u32[]{:S(2)}) collective-permute-start(s16[1033,128]{1,0:T(8,128)(2,1)S(1)} %get-tuple-element.34), channel_id=1, source_target_pairs={{0,8},{8,16},{16,24},{24,32},{32,40},{40,48},{48,56},{56,64},{64,7... | collective-permute-start | bytes 793352 | tf_op jit(solution)/shard_map/ppermute | solution.py:12
  112.2 8.9 %collective-permute-start.9 = (s16[1033,128]{1,0:T(8,128)(2,1)S(1)}, s16[1033,128]{1,0:T(8,128)(2,1)S(1)}, u32[]{:S(2)}, u32[]{:S(2)}) collective-permute-start(s16[1033,128]{1,0:T(8,128)(2,1)S(1)} %get-tuple-element.35), channel_id=1, source_target_pairs={{0,40},{8,48},{16,56},{24,64},{32,72},{40,80},{48,88},{56,96},{64,... | collective-permute-start | bytes 793352 | tf_op jit(solution)/shard_map/ppermute | solution.py:12
  121.2 15.2 %collective-permute-done.7 = s16[1033,128]{1,0:T(8,128)(2,1)S(1)} collective-permute-done((s16[1033,128]{1,0:T(8,128)(2,1)S(1)}, s16[1033,128]{1,0:T(8,128)(2,1)S(1)}, u32[]{:S(2)}, u32[]{:S(2)}) %collective-permute-start.7) | collective-permute-done | bytes 264480 | tf_op jit(solution)/shard_map/ppermute | solution.py:12
  137.0 16.9 %collective-permute-done.9 = s16[1033,128]{1,0:T(8,128)(2,1)S(1)} collective-permute-done((s16[1033,128]{1,0:T(8,128)(2,1)S(1)}, s16[1033,128]{1,0:T(8,128)(2,1)S(1)}, u32[]{:S(2)}, u32[]{:S(2)}) %collective-permute-start.9) | collective-permute-done | bytes 264480 | tf_op jit(solution)/shard_map/ppermute | solution.py:12
  153.9 1.2 multiply_reduce_fusion.1
  155.2 0.4 fusion.1
  155.6 0.6 copy-done.1
  156.3 0.5 multiply_reduce_fusion.3
  156.8 0.7 copy-done
  157.5 1.0 fusion.221
  158.5 1.7 fusion.220
  160.6 0.7 copy-done.6
  161.3 1.3 fusion.3
  162.8 1.3 fusion.2
  164.2 0.7 maximum_bitcast_fusion
  164.8 3.5 %all-to-all-start.1 = ((f32[8,2,16,128]{3,2,1,0:T(8,128)}), f32[8,2,16,128]{3,2,1,0:T(8,128)S(1)}, u32[]{:S(2)}, u32[]{:S(2)}) async-start(f32[8,2,16,128]{3,2,1,0:T(8,128)} %maximum_bitcast_fusion), calls=%async_computation.1 | async-start | bytes 262144 | tf_op jit(solution)/shard_map/all_to_all | solution.py:67
  168.4 1.0 copy.39
  169.4 0.7 copy-done.25
  170.0 0.7 multiply_subtract_fusion
  170.7 3.8 %all-to-all-done.1 = f32[8,2,16,128]{3,2,1,0:T(8,128)S(1)} async-done(((f32[8,2,16,128]{3,2,1,0:T(8,128)}), f32[8,2,16,128]{3,2,1,0:T(8,128)S(1)}, u32[]{:S(2)}, u32[]{:S(2)}) %all-to-all-start.1) | async-done | bytes 131104 | tf_op jit(solution)/shard_map/all_to_all | solution.py:67
  174.5 0.6 slice_bitcast_fusion
  (167 shorter events, 8.4 us)
Async XLA Ops:
  0.6 10.7 %copy-start.5 = (bf16[128,1024]{1,0:T(8,128)(2,1)S(1)}, bf16[128,1024]{1,0:T(8,128)(2,1)}, u32[]{:S(2)}) copy-start(bf16[128,1024]{1,0:T(8,128)(2,1)} %param.9) | copy-start | bytes 786436
  2.0 10.4 %all-to-all-start = ((bf16[8,2,16,128]{3,2,1,0:T(8,128)(2,1)}), bf16[8,2,16,128]{3,2,1,0:T(8,128)(2,1)S(1)}, u32[]{:S(2)}, u32[]{:S(2)}) async-start(bf16[8,2,16,128]{3,2,1,0:T(8,128)(2,1)} %broadcast_in_dim.31), calls=%async_computation | async-start | bytes 131072 | tf_op jit(solution)/shard_map/all_to_all | solution.py:92
  7.3 0.7 copy-start.23
  10.0 0.7 copy-start.7
  10.0 0.7 copy-start.24
  11.3 27.8 %copy-start.21 = (f32[16]{0:T(128)}, f32[16]{0:T(128)S(1)}, u32[]{:S(2)}) copy-start(f32[16]{0:T(128)S(1)} %get-tuple-element.76) | copy-start | bytes 196
  11.3 7.3 %copy-start.8 = (f32[16,128]{1,0:T(8,128)}, f32[16,128]{1,0:T(8,128)S(1)}, u32[]{:S(2)}) copy-start(f32[16,128]{1,0:T(8,128)S(1)} %get-tuple-element.95) | copy-start | bytes 24580
  11.4 7.7 %copy-start.14 = (f32[16,128]{1,0:T(8,128)}, f32[16,128]{1,0:T(8,128)S(1)}, u32[]{:S(2)}) copy-start(f32[16,128]{1,0:T(8,128)S(1)} %get-tuple-element.94) | copy-start | bytes 24580
  11.4 1.0 copy-start.4
  21.1 18.8 %copy-start.19 = (s16[1,96]{1,0:T(2,128)(2,1)}, s16[1,96]{1,0:T(2,128)(2,1)S(1)}, u32[]{:S(2)}) copy-start(s16[1,96]{1,0:T(2,128)(2,1)S(1)} %concatenate.139) | copy-start | bytes 580
  21.2 10.7 %collective-permute-start = (s16[1033,128]{1,0:T(8,128)(2,1)S(1)}, s16[1033,128]{1,0:T(8,128)(2,1)S(1)}, u32[]{:S(2)}, u32[]{:S(2)}) collective-permute-start(s16[1033,128]{1,0:T(8,128)(2,1)S(1)} %get-tuple-element.24), channel_id=1, source_target_pairs={{0,8},{8,16},{16,24},{24,32},{32,40},{40,48},{48,56},{56,64},{64,7... | collective-permute-start | bytes 793352 | tf_op jit(solution)/shard_map/ppermute | solution.py:12
  25.0 11.8 %collective-permute-start.1 = (s16[1033,128]{1,0:T(8,128)(2,1)S(1)}, s16[1033,128]{1,0:T(8,128)(2,1)S(1)}, u32[]{:S(2)}, u32[]{:S(2)}) collective-permute-start(s16[1033,128]{1,0:T(8,128)(2,1)S(1)} %get-tuple-element.25), channel_id=1, source_target_pairs={{8,0},{16,8},{24,16},{32,24},{40,32},{48,40},{56,48},{64,56},{72,6... | collective-permute-start | bytes 793352 | tf_op jit(solution)/shard_map/ppermute | solution.py:12
  32.0 7.1 %copy-start.10 = (f32[16,64]{1,0:T(8,128)}, f32[16,64]{1,0:T(8,128)S(1)}, u32[]{:S(2)}) copy-start(f32[16,64]{1,0:T(8,128)S(1)} %exp2.362) | copy-start | bytes 12292
  36.9 2.2 %copy-start.12 = (f32[16,64]{1,0:T(8,128)}, f32[16,64]{1,0:T(8,128)S(1)}, u32[]{:S(2)}) copy-start(f32[16,64]{1,0:T(8,128)S(1)} %exp2.367) | copy-start | bytes 12292
  38.5 0.6 copy-start.28
  38.5 0.6 copy-start.30
  40.0 12.1 %collective-permute-start.2 = (s16[1033,128]{1,0:T(8,128)(2,1)S(1)}, s16[1033,128]{1,0:T(8,128)(2,1)S(1)}, u32[]{:S(2)}, u32[]{:S(2)}) collective-permute-start(s16[1033,128]{1,0:T(8,128)(2,1)S(1)} %get-tuple-element.26), channel_id=1, source_target_pairs={{0,16},{8,24},{16,32},{24,40},{32,48},{40,56},{48,64},{56,72},{64,... | collective-permute-start | bytes 793352 | tf_op jit(solution)/shard_map/ppermute | solution.py:12
  45.2 13.2 %collective-permute-start.3 = (s16[1033,128]{1,0:T(8,128)(2,1)S(1)}, s16[1033,128]{1,0:T(8,128)(2,1)S(1)}, u32[]{:S(2)}, u32[]{:S(2)}) collective-permute-start(s16[1033,128]{1,0:T(8,128)(2,1)S(1)} %get-tuple-element.27), channel_id=1, source_target_pairs={{16,0},{24,8},{32,16},{40,24},{48,32},{56,40},{64,48},{72,56},{80,... | collective-permute-start | bytes 793352 | tf_op jit(solution)/shard_map/ppermute | solution.py:12
  52.1 0.7 copy-start.3
  58.3 1.7 copy-start.2
  60.0 0.7 copy-start.11
  60.0 0.7 copy-start.13
  60.0 0.7 copy-start.16
  60.1 0.7 copy-start.17
  60.1 0.7 copy-start.22
  60.1 0.7 copy-start.26
  60.1 0.7 copy-start.27
  62.2 0.7 copy-start.31
  63.0 0.7 copy-start.29
  64.2 0.7 copy-start.20
  65.0 24.3 %collective-permute-start.4 = (s16[1033,128]{1,0:T(8,128)(2,1)S(1)}, s16[1033,128]{1,0:T(8,128)(2,1)S(1)}, u32[]{:S(2)}, u32[]{:S(2)}) collective-permute-start(s16[1033,128]{1,0:T(8,128)(2,1)S(1)} %get-tuple-element.34), channel_id=1, source_target_pairs={{0,32},{8,40},{16,48},{24,56},{32,64},{40,72},{48,80},{56,88},{64,... | collective-permute-start | bytes 793352 | tf_op jit(solution)/shard_map/ppermute | solution.py:12
  76.9 16.6 %collective-permute-start.5 = (s16[1033,128]{1,0:T(8,128)(2,1)S(1)}, s16[1033,128]{1,0:T(8,128)(2,1)S(1)}, u32[]{:S(2)}, u32[]{:S(2)}) collective-permute-start(s16[1033,128]{1,0:T(8,128)(2,1)S(1)} %get-tuple-element.30), channel_id=1, source_target_pairs={{32,0},{40,8},{48,16},{56,24},{64,32},{72,40},{80,48},{88,56},{96,... | collective-permute-start | bytes 793352 | tf_op jit(solution)/shard_map/ppermute | solution.py:12
  95.2 25.8 %collective-permute-start.6 = (s16[1033,128]{1,0:T(8,128)(2,1)S(1)}, s16[1033,128]{1,0:T(8,128)(2,1)S(1)}, u32[]{:S(2)}, u32[]{:S(2)}) collective-permute-start(s16[1033,128]{1,0:T(8,128)(2,1)S(1)} %get-tuple-element.30), channel_id=1, source_target_pairs={{8,0},{16,8},{24,16},{32,24},{40,32},{48,40},{56,48},{64,56},{72,6... | collective-permute-start | bytes 793352 | tf_op jit(solution)/shard_map/ppermute | solution.py:12
  101.5 34.9 %collective-permute-start.7 = (s16[1033,128]{1,0:T(8,128)(2,1)S(1)}, s16[1033,128]{1,0:T(8,128)(2,1)S(1)}, u32[]{:S(2)}, u32[]{:S(2)}) collective-permute-start(s16[1033,128]{1,0:T(8,128)(2,1)S(1)} %get-tuple-element.31), channel_id=1, source_target_pairs={{40,0},{48,8},{56,16},{64,24},{72,32},{80,40},{88,48},{96,56},{104... | collective-permute-start | bytes 793352 | tf_op jit(solution)/shard_map/ppermute | solution.py:12
  110.2 26.2 %collective-permute-start.8 = (s16[1033,128]{1,0:T(8,128)(2,1)S(1)}, s16[1033,128]{1,0:T(8,128)(2,1)S(1)}, u32[]{:S(2)}, u32[]{:S(2)}) collective-permute-start(s16[1033,128]{1,0:T(8,128)(2,1)S(1)} %get-tuple-element.34), channel_id=1, source_target_pairs={{0,8},{8,16},{16,24},{24,32},{32,40},{40,48},{48,56},{56,64},{64,7... | collective-permute-start | bytes 793352 | tf_op jit(solution)/shard_map/ppermute | solution.py:12
  112.2 41.7 %collective-permute-start.9 = (s16[1033,128]{1,0:T(8,128)(2,1)S(1)}, s16[1033,128]{1,0:T(8,128)(2,1)S(1)}, u32[]{:S(2)}, u32[]{:S(2)}) collective-permute-start(s16[1033,128]{1,0:T(8,128)(2,1)S(1)} %get-tuple-element.35), channel_id=1, source_target_pairs={{0,40},{8,48},{16,56},{24,64},{32,72},{40,80},{48,88},{56,96},{64,... | collective-permute-start | bytes 793352 | tf_op jit(solution)/shard_map/ppermute | solution.py:12
  155.1 1.0 copy-start.1
  155.2 1.0 copy-start.9
  155.6 0.7 copy-start.32
  156.3 1.2 copy-start
  160.5 0.8 copy-start.6
  160.5 0.8 copy-start.15
  164.8 9.7 %all-to-all-start.1 = ((f32[8,2,16,128]{3,2,1,0:T(8,128)}), f32[8,2,16,128]{3,2,1,0:T(8,128)S(1)}, u32[]{:S(2)}, u32[]{:S(2)}) async-start(f32[8,2,16,128]{3,2,1,0:T(8,128)} %maximum_bitcast_fusion), calls=%async_computation.1 | async-start | bytes 262144 | tf_op jit(solution)/shard_map/all_to_all | solution.py:67
  168.4 1.0 copy-start.18
  169.4 0.7 copy-start.25

commit v11 on v9

--- a/solution.py
+++ b/solution.py
@@ -43,11 +43,11 @@
     return value, jnp.maximum(own[1] + got[1], FLOOR)
 
 
-def shift_pair(fwd, bwd, by):
+def shift_pair(fwd, bwd, by, held=()):
     shape = fwd[0].shape
-    fwd, bwd = lax.optimization_barrier((pack(*fwd), pack(*bwd)))
+    fwd, bwd, held = lax.optimization_barrier((pack(*fwd), pack(*bwd), held))
     got_f, got_b = from_behind(fwd, "context", by), from_behind(bwd, "context", -by)
-    return unpack(got_f, shape), unpack(got_b, shape)
+    return unpack(got_f, shape), unpack(got_b, shape), held
 
 
 def exchange(pieces, axis):
@@ -124,9 +124,13 @@
     bwd = (local_adj, decay)
     span = 1
     kept = {}
+    held = (logc, dys, moved, b_bf, c_bf)
     while span < high:
         kept[span] = (fwd, bwd)
-        got_f, got_b = shift_pair(fwd, bwd, span)
+        if 2 * span < high:
+            got_f, got_b, _ = shift_pair(fwd, bwd, span)
+        else:
+            got_f, got_b, held = shift_pair(fwd, bwd, span, held)
         fwd = combine(fwd, got_f)
         bwd = combine(bwd, got_b)
         span *= 2
@@ -142,13 +146,16 @@
     s_in = combine(got[0], got[1])[0]
     g_in = combine(got[2], got[3])[0]
 
+    late_logc, late_dys, late_moved, late_b, late_c = held
     index = jnp.arange(length)
     keep = (index[:, None] >= index[None, :]) & (seg[:, None] == seg[None, :])
-    weights = jnp.exp(jnp.where(keep[None], logc[:, :, None] - logc[:, None, :], -1e30))
-    scores = jnp.dot(c_bf, b_bf.T, preferred_element_type=jnp.float32)
+    weights = jnp.exp(
+        jnp.where(keep[None], late_logc[:, :, None] - late_logc[:, None, :], -1e30)
+    )
+    scores = jnp.dot(late_c, late_b.T, preferred_element_type=jnp.float32)
     mixed = weights * scores[None]
-    core_loc = jnp.einsum("hij,hip->hjp", mixed, dys, precision=HIGH)
-    pairs = jnp.einsum("hip,hjp->hij", dys, moved, precision=HIGH)
+    core_loc = jnp.einsum("hij,hip->hjp", mixed, late_dys, precision=HIGH)
+    pairs = jnp.einsum("hip,hjp->hij", late_dys, late_moved, precision=HIGH)
     paired = mixed * pairs
     col_total = jnp.sum(paired, axis=1)
     row_total = jnp.sum(paired, axis=2)

time: 171 us -> 171 us (level)
    unnamed x40 -> x45, local copies, waits for them, and re-layouts: 7.32 us -> 6.63 us
  transfers between devices with their start and end apart: 12 -> 12, of which waited for: 7 -> 8; matrix products, arithmetic and copies ran while one was open for 9% -> 8% of each run, Pallas kernels for 0% -> 0%
where the time goes in v11:
time: 171 us; the launch traced here: 170 us
  starting transfers between devices  68.7 us (40%)
  waiting for transfers between devices  59.9 us (35%)
  other arithmetic  16.4 us (10%)
  matrix products  11.6 us (7%)
  local copies, waits for them, and re-layouts  11.4 us (7%)
  between operations  1.98 us (1%)
    ppermute x10, waiting for transfers between devices, from_behind(): return lax.ppermute(x, axis, pairs)  59.9 us
    ppermute x10, starting transfers between devices, from_behind(): return lax.ppermute(x, axis, pairs)  56.8 us
    all_to_all x1, starting transfers between devices, scatter_sum(): got = lax.all_to_all(parts, axis, 0, 0, tiled=True)  6.63 us
    unnamed x45, local copies, waits for them, and re-layouts  6.63 us
    all_to_all x1, starting transfers between devices, local(): lax.all_to_all(jnp.broadcast_to(piece, (count,) + piece.shape), 'tensor',...  5.23 us
  transfers between devices with their start and end apart: 12, of which 8 were waited for; matrix products, arithmetic and copies ran while one was open for 8% of the time, Pallas kernels for 0%

profile of v11, /device:TPU:75, one launch (start us, length us, event | category | flops | bytes accessed | tf_op | source)
XLA Modules:
  0.0 170.1 jit_solution(5964138901606878401)
XLA Ops:
  0.6 0.7 pad_maximum_fusion
  1.4 0.6 broadcast_in_dim.28
  2.0 5.2 %all-to-all-start = ((bf16[8,2,16,128]{3,2,1,0:T(8,128)(2,1)}), bf16[8,2,16,128]{3,2,1,0:T(8,128)(2,1)S(1)}, u32[]{:S(2)}, u32[]{:S(2)}) async-start(bf16[8,2,16,128]{3,2,1,0:T(8,128)(2,1)} %broadcast_in_dim.28), calls=%async_computation | async-start | bytes 131072 | tf_op jit(solution)/shard_map/all_to_all | solution.py:92
  7.3 0.7 copy.26
  8.2 0.5 copy-done.12
  8.9 0.6 slice.172
  10.1 0.7 compare_convert_fusion
  10.9 0.3 reduce_window_sum.30
  11.7 0.8 copy-done.10
  12.6 0.5 abs_reduce_fusion.6
  13.2 0.5 abs_reduce_fusion.7
  14.3 3.5 %collective-permute-start = (s16[1033,128]{1,0:T(8,128)(2,1)S(1)}, s16[1033,128]{1,0:T(8,128)(2,1)S(1)}, u32[]{:S(2)}, u32[]{:S(2)}) collective-permute-start(s16[1033,128]{1,0:T(8,128)(2,1)S(1)} %get-tuple-element.19), channel_id=1, source_target_pairs={{0,8},{8,16},{16,24},{24,32},{32,40},{40,48},{48,56},{56,64},{64,7... | collective-permute-start | bytes 793352 | tf_op jit(solution)/shard_map/ppermute | solution.py:12
  17.8 1.9 %collective-permute-start.1 = (s16[1033,128]{1,0:T(8,128)(2,1)S(1)}, s16[1033,128]{1,0:T(8,128)(2,1)S(1)}, u32[]{:S(2)}, u32[]{:S(2)}) collective-permute-start(s16[1033,128]{1,0:T(8,128)(2,1)S(1)} %get-tuple-element.20), channel_id=1, source_target_pairs={{8,0},{16,8},{24,16},{32,24},{40,32},{48,40},{56,48},{64,56},{72,6... | collective-permute-start | bytes 793352 | tf_op jit(solution)/shard_map/ppermute | solution.py:12
  19.7 4.0 %collective-permute-done = s16[1033,128]{1,0:T(8,128)(2,1)S(1)} collective-permute-done((s16[1033,128]{1,0:T(8,128)(2,1)S(1)}, s16[1033,128]{1,0:T(8,128)(2,1)S(1)}, u32[]{:S(2)}, u32[]{:S(2)}) %collective-permute-start) | collective-permute-done | bytes 264480 | tf_op jit(solution)/shard_map/ppermute | solution.py:12
  23.9 4.9 %collective-permute-done.1 = s16[1033,128]{1,0:T(8,128)(2,1)S(1)} collective-permute-done((s16[1033,128]{1,0:T(8,128)(2,1)S(1)}, s16[1033,128]{1,0:T(8,128)(2,1)S(1)}, u32[]{:S(2)}, u32[]{:S(2)}) %collective-permute-start.1) | collective-permute-done | bytes 264480 | tf_op jit(solution)/shard_map/ppermute | solution.py:12
  28.9 0.7 abs_reduce_fusion.4
  29.8 0.6 fusion.225
  30.4 0.5 copy-done.15
  31.0 0.7 clamp_convert_fusion.4
  31.8 4.8 %collective-permute-start.2 = (s16[1033,128]{1,0:T(8,128)(2,1)S(1)}, s16[1033,128]{1,0:T(8,128)(2,1)S(1)}, u32[]{:S(2)}, u32[]{:S(2)}) collective-permute-start(s16[1033,128]{1,0:T(8,128)(2,1)S(1)} %get-tuple-element.21), channel_id=1, source_target_pairs={{0,16},{8,24},{16,32},{24,40},{32,48},{40,56},{48,64},{56,72},{64,... | collective-permute-start | bytes 793352 | tf_op jit(solution)/shard_map/ppermute | solution.py:12
  36.6 2.4 %collective-permute-start.3 = (s16[1033,128]{1,0:T(8,128)(2,1)S(1)}, s16[1033,128]{1,0:T(8,128)(2,1)S(1)}, u32[]{:S(2)}, u32[]{:S(2)}) collective-permute-start(s16[1033,128]{1,0:T(8,128)(2,1)S(1)} %get-tuple-element.22), channel_id=1, source_target_pairs={{16,0},{24,8},{32,16},{40,24},{48,32},{56,40},{64,48},{72,56},{80,... | collective-permute-start | bytes 793352 | tf_op jit(solution)/shard_map/ppermute | solution.py:12
  39.0 3.9 %collective-permute-done.2 = s16[1033,128]{1,0:T(8,128)(2,1)S(1)} collective-permute-done((s16[1033,128]{1,0:T(8,128)(2,1)S(1)}, s16[1033,128]{1,0:T(8,128)(2,1)S(1)}, u32[]{:S(2)}, u32[]{:S(2)}) %collective-permute-start.2) | collective-permute-done | bytes 264480 | tf_op jit(solution)/shard_map/ppermute | solution.py:12
  43.0 5.2 %collective-permute-done.3 = s16[1033,128]{1,0:T(8,128)(2,1)S(1)} collective-permute-done((s16[1033,128]{1,0:T(8,128)(2,1)S(1)}, s16[1033,128]{1,0:T(8,128)(2,1)S(1)}, u32[]{:S(2)}, u32[]{:S(2)}) %collective-permute-start.3) | collective-permute-done | bytes 264480 | tf_op jit(solution)/shard_map/ppermute | solution.py:12
  48.3 0.6 copy-done.7
  48.9 0.9 copy-done.3
  49.8 0.8 fusion.15
  51.2 0.7 slice_convert_fusion.9
  52.0 0.7 slice_convert_fusion.8
  53.3 0.9 fusion.59
  54.2 7.5 %collective-permute-start.4 = (s16[1033,128]{1,0:T(8,128)(2,1)}, s16[1033,128]{1,0:T(8,128)(2,1)S(1)}, u32[]{:S(2)}, u32[]{:S(2)}) collective-permute-start(s16[1033,128]{1,0:T(8,128)(2,1)} %get-tuple-element.32), channel_id=1, source_target_pairs={{0,32},{8,40},{16,48},{24,56},{32,64},{40,72},{48,80},{56,88},{64,... | collective-permute-start | bytes 793352 | tf_op jit(solution)/shard_map/ppermute | solution.py:12
  61.8 2.6 %collective-permute-start.5 = (s16[1033,128]{1,0:T(8,128)(2,1)}, s16[1033,128]{1,0:T(8,128)(2,1)S(1)}, u32[]{:S(2)}, u32[]{:S(2)}) collective-permute-start(s16[1033,128]{1,0:T(8,128)(2,1)} %get-tuple-element.29), channel_id=1, source_target_pairs={{32,0},{40,8},{48,16},{56,24},{64,32},{72,40},{80,48},{88,56},{96,... | collective-permute-start | bytes 793352 | tf_op jit(solution)/shard_map/ppermute | solution.py:12
  64.5 5.0 %collective-permute-done.4 = s16[1033,128]{1,0:T(8,128)(2,1)S(1)} collective-permute-done((s16[1033,128]{1,0:T(8,128)(2,1)}, s16[1033,128]{1,0:T(8,128)(2,1)S(1)}, u32[]{:S(2)}, u32[]{:S(2)}) %collective-permute-start.4) | collective-permute-done | bytes 264480 | tf_op jit(solution)/shard_map/ppermute | solution.py:12
  69.6 0.4 abs_reduce_fusion.1
  70.1 5.6 %collective-permute-done.5 = s16[1033,128]{1,0:T(8,128)(2,1)S(1)} collective-permute-done((s16[1033,128]{1,0:T(8,128)(2,1)}, s16[1033,128]{1,0:T(8,128)(2,1)S(1)}, u32[]{:S(2)}, u32[]{:S(2)}) %collective-permute-start.5) | collective-permute-done | bytes 264480 | tf_op jit(solution)/shard_map/ppermute | solution.py:12
  75.8 0.4 abs_reduce_fusion
  76.6 0.4 clamp_convert_fusion.1
  76.9 0.4 clamp_convert_fusion
  77.3 0.9 fusion.61
  78.2 14.4 %collective-permute-start.6 = (s16[1033,128]{1,0:T(8,128)(2,1)}, s16[1033,128]{1,0:T(8,128)(2,1)S(1)}, u32[]{:S(2)}, u32[]{:S(2)}) collective-permute-start(s16[1033,128]{1,0:T(8,128)(2,1)} %get-tuple-element.29), channel_id=1, source_target_pairs={{8,0},{16,8},{24,16},{32,24},{40,32},{48,40},{56,48},{64,56},{72,6... | collective-permute-start | bytes 793352 | tf_op jit(solution)/shard_map/ppermute | solution.py:12
  92.6 2.4 %fusion.8 = (f32[16,128]{1,0:T(8,128)S(1)}, f32[16,128]{1,0:T(8,128)S(1)}, f32[128,128]{1,0:T(8,128)S(1)}) fusion(f32[128,128]{1,0:T(8,128)S(1)} %fusion.231, f32[16,128]{1,0:T(8,128)S(1)} %reduce_window_sum.30, pred[128,128]{1,0:T(8,128)(4,1)S(1)} %fusion.72, f32[16,128,64]{1,2,0:T(8,128)S(1)} %bitcast.198, f32[16,128,64]{1,2,0:T(8,128)S(1)} %copy-done.1), kind=kOutput, calls=%fused_computation.21 | convolution fusion | flops 203403264 | bytes 1220608 | tf_op jit(solution)/shard_map/hip,hjp->hij/dot_general | solution.py:158
  95.0 0.3 reduce_window_sum.31
  95.3 0.3 reduce_window_sum.32
  95.5 1.3 fusion.6
  96.8 9.1 %collective-permute-start.7 = (s16[1033,128]{1,0:T(8,128)(2,1)}, s16[1033,128]{1,0:T(8,128)(2,1)S(1)}, u32[]{:S(2)}, u32[]{:S(2)}) collective-permute-start(s16[1033,128]{1,0:T(8,128)(2,1)} %get-tuple-element.30), channel_id=1, source_target_pairs={{40,0},{48,8},{56,16},{64,24},{72,32},{80,40},{88,48},{96,56},{104... | collective-permute-start | bytes 793352 | tf_op jit(solution)/shard_map/ppermute | solution.py:12
  106.0 1.9 %collective-permute-start.8 = (s16[1033,128]{1,0:T(8,128)(2,1)}, s16[1033,128]{1,0:T(8,128)(2,1)S(1)}, u32[]{:S(2)}, u32[]{:S(2)}) collective-permute-start(s16[1033,128]{1,0:T(8,128)(2,1)} %get-tuple-element.32), channel_id=1, source_target_pairs={{0,8},{8,16},{16,24},{24,32},{32,40},{40,48},{48,56},{56,64},{64,7... | collective-permute-start | bytes 793352 | tf_op jit(solution)/shard_map/ppermute | solution.py:12
  107.9 8.7 %collective-permute-start.9 = (s16[1033,128]{1,0:T(8,128)(2,1)}, s16[1033,128]{1,0:T(8,128)(2,1)S(1)}, u32[]{:S(2)}, u32[]{:S(2)}) collective-permute-start(s16[1033,128]{1,0:T(8,128)(2,1)} %get-tuple-element.33), channel_id=1, source_target_pairs={{0,40},{8,48},{16,56},{24,64},{32,72},{40,80},{48,88},{56,96},{64,... | collective-permute-start | bytes 793352 | tf_op jit(solution)/shard_map/ppermute | solution.py:12
  116.7 2.8 %collective-permute-done.7 = s16[1033,128]{1,0:T(8,128)(2,1)S(1)} collective-permute-done((s16[1033,128]{1,0:T(8,128)(2,1)}, s16[1033,128]{1,0:T(8,128)(2,1)S(1)}, u32[]{:S(2)}, u32[]{:S(2)}) %collective-permute-start.7) | collective-permute-done | bytes 264480 | tf_op jit(solution)/shard_map/ppermute | solution.py:12
  120.1 28.5 %collective-permute-done.9 = s16[1033,128]{1,0:T(8,128)(2,1)S(1)} collective-permute-done((s16[1033,128]{1,0:T(8,128)(2,1)}, s16[1033,128]{1,0:T(8,128)(2,1)S(1)}, u32[]{:S(2)}, u32[]{:S(2)}) %collective-permute-start.9) | collective-permute-done | bytes 264480 | tf_op jit(solution)/shard_map/ppermute | solution.py:12
  148.8 1.8 %multiply_reduce_fusion.1 = (f32[1024]{0:T(1024)S(1)}, f32[1024,128]{1,0:T(8,128)S(1)}, f32[1024,128]{1,0:T(8,128)}) fusion(f32[1024]{0:T(1024)S(1)} %get-tuple-element.83, s16[1033,128]{1,0:T(8,128)(2,1)S(1)} %collective-permute-done.9, f32[1024]{0:T(1024)S(1)} %mul.481, f32[1024]{0:T(1024)S(1)} %get-tuple-element.81, ...), kind=kLoop, calls=%fused_computation.59 | loop fusion | flops 1833984 | bytes 2125824 | tf_op jit(solution)/shard_map/reduce_sum | solution.py:178
  150.6 0.4 fusion.1
  151.0 1.2 fusion.3
  152.5 1.3 convolution_bitcast_fusion.1
  154.1 0.9 copy-done.6
  155.1 1.3 convolution_bitcast_fusion.2
  156.4 0.3 convolution_add_fusion.1
  156.7 0.6 maximum_bitcast_fusion
  157.3 6.6 %all-to-all-start.1 = ((f32[8,2,16,128]{3,2,1,0:T(8,128)}), f32[8,2,16,128]{3,2,1,0:T(8,128)S(1)}, u32[]{:S(2)}, u32[]{:S(2)}) async-start(f32[8,2,16,128]{3,2,1,0:T(8,128)} %maximum_bitcast_fusion), calls=%async_computation.1 | async-start | bytes 262144 | tf_op jit(solution)/shard_map/all_to_all | solution.py:67
  163.9 0.7 copy-done.21
  164.6 0.4 fusion.28
  165.2 1.0 copy.31
  166.2 1.9 %fusion.2 = f32[16,1,128]{2,1,0:T(1,128)S(1)} fusion(f32[16,128,1]{1,2,0:T(1,128)S(1)} %bitcast.237, f32[16,128]{1,0:T(8,128)S(1)} %reduce_window_sum.30, pred[128,128]{1,0:T(8,128)(4,1)S(1)} %fusion.72), kind=kOutput, calls=%fused_computation.9 | convolution fusion | flops 3670016 | bytes 40960 | tf_op jit(solution)/shard_map/hij,hj->hi/dot_general | solution.py:175
  168.1 0.7 copy-done.20
  168.8 0.7 multiply_subtract_fusion
  169.5 0.6 slice_bitcast_fusion
  (145 shorter events, 6.3 us)
Async XLA Ops:
  0.6 10.7 %copy-start.9 = (bf16[128,1024]{1,0:T(8,128)(2,1)S(1)}, bf16[128,1024]{1,0:T(8,128)(2,1)}, u32[]{:S(2)}) copy-start(bf16[128,1024]{1,0:T(8,128)(2,1)} %param.8) | copy-start | bytes 786436
  2.0 10.6 %all-to-all-start = ((bf16[8,2,16,128]{3,2,1,0:T(8,128)(2,1)}), bf16[8,2,16,128]{3,2,1,0:T(8,128)(2,1)S(1)}, u32[]{:S(2)}, u32[]{:S(2)}) async-start(bf16[8,2,16,128]{3,2,1,0:T(8,128)(2,1)} %broadcast_in_dim.28), calls=%async_computation | async-start | bytes 131072 | tf_op jit(solution)/shard_map/all_to_all | solution.py:92
  8.1 0.7 copy-start.12
  8.7 2.0 %copy-start.11 = (f32[16,128]{1,0:T(8,128)S(1)}, f32[16,128]{1,0:T(8,128)}, u32[]{:S(2)}) copy-start(f32[16,128]{1,0:T(8,128)} %param.10) | copy-start | bytes 24580
  10.1 0.7 copy-start.19
  11.5 1.0 copy-start.10
  11.5 1.6 copy-start
  14.3 9.5 %collective-permute-start = (s16[1033,128]{1,0:T(8,128)(2,1)S(1)}, s16[1033,128]{1,0:T(8,128)(2,1)S(1)}, u32[]{:S(2)}, u32[]{:S(2)}) collective-permute-start(s16[1033,128]{1,0:T(8,128)(2,1)S(1)} %get-tuple-element.19), channel_id=1, source_target_pairs={{0,8},{8,16},{16,24},{24,32},{32,40},{40,48},{48,56},{56,64},{64,7... | collective-permute-start | bytes 793352 | tf_op jit(solution)/shard_map/ppermute | solution.py:12
  17.8 10.9 %collective-permute-start.1 = (s16[1033,128]{1,0:T(8,128)(2,1)S(1)}, s16[1033,128]{1,0:T(8,128)(2,1)S(1)}, u32[]{:S(2)}, u32[]{:S(2)}) collective-permute-start(s16[1033,128]{1,0:T(8,128)(2,1)S(1)} %get-tuple-element.20), channel_id=1, source_target_pairs={{8,0},{16,8},{24,16},{32,24},{40,32},{48,40},{56,48},{64,56},{72,6... | collective-permute-start | bytes 793352 | tf_op jit(solution)/shard_map/ppermute | solution.py:12
  28.7 2.3 %copy-start.2 = (s16[1033,128]{1,0:T(8,128)(2,1)}, s16[1033,128]{1,0:T(8,128)(2,1)S(1)}, u32[]{:S(2)}) copy-start(s16[1033,128]{1,0:T(8,128)(2,1)S(1)} %collective-permute-done.1) | copy-start | bytes 793348
  30.4 0.5 copy-start.15
  30.4 0.6 copy-start.17
  31.8 11.1 %collective-permute-start.2 = (s16[1033,128]{1,0:T(8,128)(2,1)S(1)}, s16[1033,128]{1,0:T(8,128)(2,1)S(1)}, u32[]{:S(2)}, u32[]{:S(2)}) collective-permute-start(s16[1033,128]{1,0:T(8,128)(2,1)S(1)} %get-tuple-element.21), channel_id=1, source_target_pairs={{0,16},{8,24},{16,32},{24,40},{32,48},{40,56},{48,64},{56,72},{64,... | collective-permute-start | bytes 793352 | tf_op jit(solution)/shard_map/ppermute | solution.py:12
  36.6 11.6 %collective-permute-start.3 = (s16[1033,128]{1,0:T(8,128)(2,1)S(1)}, s16[1033,128]{1,0:T(8,128)(2,1)S(1)}, u32[]{:S(2)}, u32[]{:S(2)}) collective-permute-start(s16[1033,128]{1,0:T(8,128)(2,1)S(1)} %get-tuple-element.22), channel_id=1, source_target_pairs={{16,0},{24,8},{32,16},{40,24},{48,32},{56,40},{64,48},{72,56},{80,... | collective-permute-start | bytes 793352 | tf_op jit(solution)/shard_map/ppermute | solution.py:12
  42.9 5.4 %copy-start.8 = (s16[1033,128]{1,0:T(8,128)(2,1)}, s16[1033,128]{1,0:T(8,128)(2,1)S(1)}, u32[]{:S(2)}) copy-start(s16[1033,128]{1,0:T(8,128)(2,1)S(1)} %collective-permute-done.2) | copy-start | bytes 793348
  48.2 0.7 copy-start.7
  48.9 1.0 copy-start.3
  48.9 0.9 copy-start.13
  48.9 0.9 copy-start.14
  51.2 0.7 copy-start.18
  52.0 0.7 copy-start.16
  54.2 15.3 %collective-permute-start.4 = (s16[1033,128]{1,0:T(8,128)(2,1)}, s16[1033,128]{1,0:T(8,128)(2,1)S(1)}, u32[]{:S(2)}, u32[]{:S(2)}) collective-permute-start(s16[1033,128]{1,0:T(8,128)(2,1)} %get-tuple-element.32), channel_id=1, source_target_pairs={{0,32},{8,40},{16,48},{24,56},{32,64},{40,72},{48,80},{56,88},{64,... | collective-permute-start | bytes 793352 | tf_op jit(solution)/shard_map/ppermute | solution.py:12
  61.8 13.9 %collective-permute-start.5 = (s16[1033,128]{1,0:T(8,128)(2,1)}, s16[1033,128]{1,0:T(8,128)(2,1)S(1)}, u32[]{:S(2)}, u32[]{:S(2)}) collective-permute-start(s16[1033,128]{1,0:T(8,128)(2,1)} %get-tuple-element.29), channel_id=1, source_target_pairs={{32,0},{40,8},{48,16},{56,24},{64,32},{72,40},{80,48},{88,56},{96,... | collective-permute-start | bytes 793352 | tf_op jit(solution)/shard_map/ppermute | solution.py:12
  77.3 15.3 %copy-start.1 = (f32[16,128,64]{1,2,0:T(8,128)S(1)}, f32[16,128,64]{1,2,0:T(8,128)}, u32[]{:S(2)}) copy-start(f32[16,128,64]{1,2,0:T(8,128)} %copy-done) | copy-start | bytes 1572868
  78.2 38.4 %collective-permute-start.6 = (s16[1033,128]{1,0:T(8,128)(2,1)}, s16[1033,128]{1,0:T(8,128)(2,1)S(1)}, u32[]{:S(2)}, u32[]{:S(2)}) collective-permute-start(s16[1033,128]{1,0:T(8,128)(2,1)} %get-tuple-element.29), channel_id=1, source_target_pairs={{8,0},{16,8},{24,16},{32,24},{40,32},{48,40},{56,48},{64,56},{72,6... | collective-permute-start | bytes 793352 | tf_op jit(solution)/shard_map/ppermute | solution.py:12
  96.8 22.7 %collective-permute-start.7 = (s16[1033,128]{1,0:T(8,128)(2,1)}, s16[1033,128]{1,0:T(8,128)(2,1)S(1)}, u32[]{:S(2)}, u32[]{:S(2)}) collective-permute-start(s16[1033,128]{1,0:T(8,128)(2,1)} %get-tuple-element.30), channel_id=1, source_target_pairs={{40,0},{48,8},{56,16},{64,24},{72,32},{80,40},{88,48},{96,56},{104... | collective-permute-start | bytes 793352 | tf_op jit(solution)/shard_map/ppermute | solution.py:12
  106.0 13.6 %collective-permute-start.8 = (s16[1033,128]{1,0:T(8,128)(2,1)}, s16[1033,128]{1,0:T(8,128)(2,1)S(1)}, u32[]{:S(2)}, u32[]{:S(2)}) collective-permute-start(s16[1033,128]{1,0:T(8,128)(2,1)} %get-tuple-element.32), channel_id=1, source_target_pairs={{0,8},{8,16},{16,24},{24,32},{32,40},{40,48},{48,56},{56,64},{64,7... | collective-permute-start | bytes 793352 | tf_op jit(solution)/shard_map/ppermute | solution.py:12
  107.9 40.8 %collective-permute-start.9 = (s16[1033,128]{1,0:T(8,128)(2,1)}, s16[1033,128]{1,0:T(8,128)(2,1)S(1)}, u32[]{:S(2)}, u32[]{:S(2)}) collective-permute-start(s16[1033,128]{1,0:T(8,128)(2,1)} %get-tuple-element.33), channel_id=1, source_target_pairs={{0,40},{8,48},{16,56},{24,64},{32,72},{40,80},{48,88},{56,96},{64,... | collective-permute-start | bytes 793352 | tf_op jit(solution)/shard_map/ppermute | solution.py:12
  119.5 31.0 %copy-start.5 = (s16[1033,128]{1,0:T(8,128)(2,1)}, s16[1033,128]{1,0:T(8,128)(2,1)S(1)}, u32[]{:S(2)}) copy-start(s16[1033,128]{1,0:T(8,128)(2,1)S(1)} %collective-permute-done.7) | copy-start | bytes 793348
  154.0 1.0 copy-start.6
  156.4 7.6 %copy-start.4 = (f32[1024,128]{1,0:T(8,128)S(1)}, f32[1024,128]{1,0:T(8,128)}, u32[]{:S(2)}) copy-start(f32[1024,128]{1,0:T(8,128)} %get-tuple-element.59) | copy-start | bytes 1572868
  157.3 12.1 %all-to-all-start.1 = ((f32[8,2,16,128]{3,2,1,0:T(8,128)}), f32[8,2,16,128]{3,2,1,0:T(8,128)S(1)}, u32[]{:S(2)}, u32[]{:S(2)}) async-start(f32[8,2,16,128]{3,2,1,0:T(8,128)} %maximum_bitcast_fusion), calls=%async_computation.1 | async-start | bytes 262144 | tf_op jit(solution)/shard_map/all_to_all | solution.py:67
  163.9 0.7 copy-start.21
  168.1 0.7 copy-start.20

commit v12 on v11

--- a/solution.py
+++ b/solution.py
@@ -164,8 +164,17 @@
     gb_loc = jnp.dot(weighted.T, cmat, precision=HIGH)
     gc_loc = jnp.dot(weighted, bmat, precision=HIGH)
 
-    b_adj = jnp.einsum("ln,hpn->hlp", bmat, g_in, precision=HIGH)
-    c_state = jnp.einsum("ln,hpn->hlp", cmat, s_in, precision=HIGH)
+    gb = gb_loc + jnp.einsum("hlp,hpn->ln", left_u, g_in, precision=HIGH)
+    gc = gc_loc + jnp.einsum("hlp,hpn->ln", enter_dy, s_in, precision=HIGH)
+    sums = jnp.stack([gb, gc])
+    grad_bc = scatter_sum(sums, "tensor")
+    _, b_adj, c_state = lax.optimization_barrier(
+        (
+            sums,
+            jnp.einsum("ln,hpn->hlp", bmat, g_in, precision=HIGH),
+            jnp.einsum("ln,hpn->hlp", cmat, s_in, precision=HIGH),
+        )
+    )
     core = core_loc + leave[:, :, None] * b_adj
     gx = step_size[:, :, None] * core + skip_gain[:, None, None] * dys
     along = jnp.sum(xs * core, axis=2)
@@ -177,11 +186,8 @@
     )
     both = leave * enter * jnp.sum(g_in * s_in, axis=(1, 2))[:, None]
     grad_step = along * (1.0 + rate * step_size) - rate * (inner + from_state + from_adj + both)
-    gb = gb_loc + jnp.einsum("hlp,hpn->ln", left_u, g_in, precision=HIGH)
-    gc = gc_loc + jnp.einsum("hlp,hpn->ln", enter_dy, s_in, precision=HIGH)
 
     grad_x = gx.transpose(1, 0, 2).reshape(length, heads * width)
-    grad_bc = scatter_sum(jnp.stack([gb, gc]), "tensor")
     return (grad_x, grad_step, grad_bc[0], grad_bc[1])
 
 

time: 171 us -> 172 us (level)
    unnamed x45 -> x53, local copies, waits for them, and re-layouts: 6.63 us -> 7.59 us
where the time goes in v12:
time: 172 us; the launch traced here: 171 us
  starting transfers between devices  67.2 us (39%)
  waiting for transfers between devices  61.4 us (36%)
  other arithmetic  16.2 us (9%)
  local copies, waits for them, and re-layouts  12.4 us (7%)
  matrix products  11.6 us (7%)
  between operations  2.01 us (1%)
    ppermute x10, waiting for transfers between devices, from_behind(): return lax.ppermute(x, axis, pairs)  61.4 us
    ppermute x10, starting transfers between devices, from_behind(): return lax.ppermute(x, axis, pairs)  55.3 us
    unnamed x53, local copies, waits for them, and re-layouts  7.59 us
    all_to_all x1, starting transfers between devices, scatter_sum(): got = lax.all_to_all(parts, axis, 0, 0, tiled=True)  6.65 us
    all_to_all x1, starting transfers between devices, local(): lax.all_to_all(jnp.broadcast_to(piece, (count,) + piece.shape), 'tensor',...  5.23 us
  transfers between devices with their start and end apart: 12, of which 8 were waited for; matrix products, arithmetic and copies ran while one was open for 8% of the time, Pallas kernels for 0%

profile of v12, /device:TPU:75, one launch (start us, length us, event | category | flops | bytes accessed | tf_op | source)
XLA Modules:
  0.0 170.7 jit_solution(1048169319975984205)
XLA Ops:
  0.6 0.7 pad_maximum_fusion
  1.4 0.6 broadcast_in_dim.28
  2.0 5.2 %all-to-all-start = ((bf16[8,2,16,128]{3,2,1,0:T(8,128)(2,1)}), bf16[8,2,16,128]{3,2,1,0:T(8,128)(2,1)S(1)}, u32[]{:S(2)}, u32[]{:S(2)}) async-start(bf16[8,2,16,128]{3,2,1,0:T(8,128)(2,1)} %broadcast_in_dim.28), calls=%async_computation | async-start | bytes 131072 | tf_op jit(solution)/shard_map/all_to_all | solution.py:92
  7.2 0.7 copy.26
  8.2 0.5 copy-done.16
  8.9 0.6 slice.172
  10.1 0.7 compare_convert_fusion
  10.9 0.3 reduce_window_sum.30
  11.7 0.8 copy-done.12
  12.6 0.5 abs_reduce_fusion.6
  13.2 0.5 abs_reduce_fusion.7
  14.3 3.5 %collective-permute-start = (s16[1033,128]{1,0:T(8,128)(2,1)S(1)}, s16[1033,128]{1,0:T(8,128)(2,1)S(1)}, u32[]{:S(2)}, u32[]{:S(2)}) collective-permute-start(s16[1033,128]{1,0:T(8,128)(2,1)S(1)} %get-tuple-element.21), channel_id=1, source_target_pairs={{0,8},{8,16},{16,24},{24,32},{32,40},{40,48},{48,56},{56,64},{64,7... | collective-permute-start | bytes 793352 | tf_op jit(solution)/shard_map/ppermute | solution.py:12
  17.8 1.9 %collective-permute-start.1 = (s16[1033,128]{1,0:T(8,128)(2,1)S(1)}, s16[1033,128]{1,0:T(8,128)(2,1)S(1)}, u32[]{:S(2)}, u32[]{:S(2)}) collective-permute-start(s16[1033,128]{1,0:T(8,128)(2,1)S(1)} %get-tuple-element.22), channel_id=1, source_target_pairs={{8,0},{16,8},{24,16},{32,24},{40,32},{48,40},{56,48},{64,56},{72,6... | collective-permute-start | bytes 793352 | tf_op jit(solution)/shard_map/ppermute | solution.py:12
  19.7 4.0 %collective-permute-done = s16[1033,128]{1,0:T(8,128)(2,1)S(1)} collective-permute-done((s16[1033,128]{1,0:T(8,128)(2,1)S(1)}, s16[1033,128]{1,0:T(8,128)(2,1)S(1)}, u32[]{:S(2)}, u32[]{:S(2)}) %collective-permute-start) | collective-permute-done | bytes 264480 | tf_op jit(solution)/shard_map/ppermute | solution.py:12
  23.9 4.9 %collective-permute-done.1 = s16[1033,128]{1,0:T(8,128)(2,1)S(1)} collective-permute-done((s16[1033,128]{1,0:T(8,128)(2,1)S(1)}, s16[1033,128]{1,0:T(8,128)(2,1)S(1)}, u32[]{:S(2)}, u32[]{:S(2)}) %collective-permute-start.1) | collective-permute-done | bytes 264480 | tf_op jit(solution)/shard_map/ppermute | solution.py:12
  28.9 0.7 abs_reduce_fusion.4
  29.8 0.6 fusion.215
  30.4 0.5 copy-done.19
  31.0 0.7 clamp_convert_fusion.4
  31.8 4.8 %collective-permute-start.2 = (s16[1033,128]{1,0:T(8,128)(2,1)S(1)}, s16[1033,128]{1,0:T(8,128)(2,1)S(1)}, u32[]{:S(2)}, u32[]{:S(2)}) collective-permute-start(s16[1033,128]{1,0:T(8,128)(2,1)S(1)} %get-tuple-element.23), channel_id=1, source_target_pairs={{0,16},{8,24},{16,32},{24,40},{32,48},{40,56},{48,64},{56,72},{64,... | collective-permute-start | bytes 793352 | tf_op jit(solution)/shard_map/ppermute | solution.py:12
  36.6 2.4 %collective-permute-start.3 = (s16[1033,128]{1,0:T(8,128)(2,1)S(1)}, s16[1033,128]{1,0:T(8,128)(2,1)S(1)}, u32[]{:S(2)}, u32[]{:S(2)}) collective-permute-start(s16[1033,128]{1,0:T(8,128)(2,1)S(1)} %get-tuple-element.24), channel_id=1, source_target_pairs={{16,0},{24,8},{32,16},{40,24},{48,32},{56,40},{64,48},{72,56},{80,... | collective-permute-start | bytes 793352 | tf_op jit(solution)/shard_map/ppermute | solution.py:12
  39.0 3.9 %collective-permute-done.2 = s16[1033,128]{1,0:T(8,128)(2,1)S(1)} collective-permute-done((s16[1033,128]{1,0:T(8,128)(2,1)S(1)}, s16[1033,128]{1,0:T(8,128)(2,1)S(1)}, u32[]{:S(2)}, u32[]{:S(2)}) %collective-permute-start.2) | collective-permute-done | bytes 264480 | tf_op jit(solution)/shard_map/ppermute | solution.py:12
  43.0 5.2 %collective-permute-done.3 = s16[1033,128]{1,0:T(8,128)(2,1)S(1)} collective-permute-done((s16[1033,128]{1,0:T(8,128)(2,1)S(1)}, s16[1033,128]{1,0:T(8,128)(2,1)S(1)}, u32[]{:S(2)}, u32[]{:S(2)}) %collective-permute-start.3) | collective-permute-done | bytes 264480 | tf_op jit(solution)/shard_map/ppermute | solution.py:12
  48.3 0.6 copy-done.9
  48.9 0.9 copy-done.3
  49.8 0.8 fusion.12
  51.2 0.7 slice_convert_fusion.9
  52.0 0.7 slice_convert_fusion.8
  53.2 0.8 fusion.49
  54.0 7.5 %collective-permute-start.4 = (s16[1033,128]{1,0:T(8,128)(2,1)S(1)}, s16[1033,128]{1,0:T(8,128)(2,1)S(1)}, u32[]{:S(2)}, u32[]{:S(2)}) collective-permute-start(s16[1033,128]{1,0:T(8,128)(2,1)S(1)} %get-tuple-element.33), channel_id=1, source_target_pairs={{0,32},{8,40},{16,48},{24,56},{32,64},{40,72},{48,80},{56,88},{64,... | collective-permute-start | bytes 793352 | tf_op jit(solution)/shard_map/ppermute | solution.py:12
  61.6 2.6 %collective-permute-start.5 = (s16[1033,128]{1,0:T(8,128)(2,1)}, s16[1033,128]{1,0:T(8,128)(2,1)S(1)}, u32[]{:S(2)}, u32[]{:S(2)}) collective-permute-start(s16[1033,128]{1,0:T(8,128)(2,1)} %get-tuple-element.31), channel_id=1, source_target_pairs={{32,0},{40,8},{48,16},{56,24},{64,32},{72,40},{80,48},{88,56},{96,... | collective-permute-start | bytes 793352 | tf_op jit(solution)/shard_map/ppermute | solution.py:12
  64.2 4.9 %collective-permute-done.4 = s16[1033,128]{1,0:T(8,128)(2,1)S(1)} collective-permute-done((s16[1033,128]{1,0:T(8,128)(2,1)S(1)}, s16[1033,128]{1,0:T(8,128)(2,1)S(1)}, u32[]{:S(2)}, u32[]{:S(2)}) %collective-permute-start.4) | collective-permute-done | bytes 264480 | tf_op jit(solution)/shard_map/ppermute | solution.py:12
  69.2 0.4 abs_reduce_fusion.1
  69.8 5.8 %collective-permute-done.5 = s16[1033,128]{1,0:T(8,128)(2,1)S(1)} collective-permute-done((s16[1033,128]{1,0:T(8,128)(2,1)}, s16[1033,128]{1,0:T(8,128)(2,1)S(1)}, u32[]{:S(2)}, u32[]{:S(2)}) %collective-permute-start.5) | collective-permute-done | bytes 264480 | tf_op jit(solution)/shard_map/ppermute | solution.py:12
  75.7 0.4 abs_reduce_fusion
  76.4 0.4 clamp_convert_fusion.1
  76.8 0.4 clamp_convert_fusion
  77.2 0.8 fusion.51
  78.0 14.4 %collective-permute-start.6 = (s16[1033,128]{1,0:T(8,128)(2,1)}, s16[1033,128]{1,0:T(8,128)(2,1)S(1)}, u32[]{:S(2)}, u32[]{:S(2)}) collective-permute-start(s16[1033,128]{1,0:T(8,128)(2,1)} %get-tuple-element.31), channel_id=1, source_target_pairs={{8,0},{16,8},{24,16},{32,24},{40,32},{48,40},{56,48},{64,56},{72,6... | collective-permute-start | bytes 793352 | tf_op jit(solution)/shard_map/ppermute | solution.py:12
  92.6 2.4 %fusion.5 = (f32[16,128]{1,0:T(8,128)S(1)}, f32[16,128]{1,0:T(8,128)S(1)}, f32[128,128]{1,0:T(8,128)S(1)}) fusion(f32[128,128]{1,0:T(8,128)S(1)} %fusion.221, f32[16,128]{1,0:T(8,128)S(1)} %reduce_window_sum.30, pred[128,128]{1,0:T(8,128)(4,1)S(1)} %fusion.62, f32[16,128,64]{1,2,0:T(8,128)S(1)} %bitcast.176, f32[16,128,64]{1,2,0:T(8,128)S(1)} %copy-done.1), kind=kOutput, calls=%fused_computation.20 | convolution fusion | flops 203403264 | bytes 1220608 | tf_op jit(solution)/shard_map/hip,hjp->hij/dot_general | solution.py:158
  94.9 0.3 reduce_window_sum.31
  95.2 0.3 reduce_window_sum.32
  95.5 9.1 %collective-permute-start.7 = (s16[1033,128]{1,0:T(8,128)(2,1)}, s16[1033,128]{1,0:T(8,128)(2,1)S(1)}, u32[]{:S(2)}, u32[]{:S(2)}) collective-permute-start(s16[1033,128]{1,0:T(8,128)(2,1)} %get-tuple-element.32), channel_id=1, source_target_pairs={{40,0},{48,8},{56,16},{64,24},{72,32},{80,40},{88,48},{96,56},{104... | collective-permute-start | bytes 793352 | tf_op jit(solution)/shard_map/ppermute | solution.py:12
  104.6 1.9 %collective-permute-start.8 = (s16[1033,128]{1,0:T(8,128)(2,1)S(1)}, s16[1033,128]{1,0:T(8,128)(2,1)S(1)}, u32[]{:S(2)}, u32[]{:S(2)}) collective-permute-start(s16[1033,128]{1,0:T(8,128)(2,1)S(1)} %get-tuple-element.33), channel_id=1, source_target_pairs={{0,8},{8,16},{16,24},{24,32},{32,40},{40,48},{48,56},{56,64},{64,7... | collective-permute-start | bytes 793352 | tf_op jit(solution)/shard_map/ppermute | solution.py:12
  106.5 7.2 %collective-permute-start.9 = (s16[1033,128]{1,0:T(8,128)(2,1)S(1)}, s16[1033,128]{1,0:T(8,128)(2,1)S(1)}, u32[]{:S(2)}, u32[]{:S(2)}) collective-permute-start(s16[1033,128]{1,0:T(8,128)(2,1)S(1)} %get-tuple-element.34), channel_id=1, source_target_pairs={{0,40},{8,48},{16,56},{24,64},{32,72},{40,80},{48,88},{56,96},{64,... | collective-permute-start | bytes 793352 | tf_op jit(solution)/shard_map/ppermute | solution.py:12
  113.8 10.8 %collective-permute-done.7 = s16[1033,128]{1,0:T(8,128)(2,1)S(1)} collective-permute-done((s16[1033,128]{1,0:T(8,128)(2,1)}, s16[1033,128]{1,0:T(8,128)(2,1)S(1)}, u32[]{:S(2)}, u32[]{:S(2)}) %collective-permute-start.7) | collective-permute-done | bytes 264480 | tf_op jit(solution)/shard_map/ppermute | solution.py:12
  125.2 21.9 %collective-permute-done.9 = s16[1033,128]{1,0:T(8,128)(2,1)S(1)} collective-permute-done((s16[1033,128]{1,0:T(8,128)(2,1)S(1)}, s16[1033,128]{1,0:T(8,128)(2,1)S(1)}, u32[]{:S(2)}, u32[]{:S(2)}) %collective-permute-start.9) | collective-permute-done | bytes 264480 | tf_op jit(solution)/shard_map/ppermute | solution.py:12
  147.2 1.8 %multiply_reduce_fusion.1 = (f32[1024]{0:T(1024)S(1)}, f32[1024,128]{1,0:T(8,128)S(1)}, f32[1024,128]{1,0:T(8,128)}) fusion(f32[1024]{0:T(1024)S(1)} %get-tuple-element.87, s16[1033,128]{1,0:T(8,128)(2,1)S(1)} %collective-permute-done.9, f32[1024]{0:T(1024)S(1)} %mul.453, f32[1024]{0:T(1024)S(1)} %get-tuple-element.85, ...), kind=kLoop, calls=%fused_computation.48 | loop fusion | flops 1833984 | bytes 2125824 | tf_op jit(solution)/shard_map/reduce_sum | solution.py:187
  149.0 0.4 convolution_bitcast_fusion
  149.6 0.9 copy-done.8
  150.6 1.3 convolution_bitcast_fusion.2
  152.2 0.9 copy-done.6
  153.1 1.3 convolution_bitcast_fusion.3
  154.7 0.6 maximum_bitcast_fusion
  155.4 6.7 %all-to-all-start.1 = ((f32[8,2,16,128]{3,2,1,0:T(8,128)}), f32[8,2,16,128]{3,2,1,0:T(8,128)S(1)}, u32[]{:S(2)}, u32[]{:S(2)}) async-start(f32[8,2,16,128]{3,2,1,0:T(8,128)} %maximum_bitcast_fusion), calls=%async_computation.1 | async-start | bytes 262144 | tf_op jit(solution)/shard_map/all_to_all | solution.py:67
  162.0 0.4 convolution_bitcast_fusion.1
  162.5 1.2 fusion.1
  163.8 0.7 copy-done.15
  164.5 1.3 multiply_reduce_fusion.4
  165.9 1.0 copy.31
  166.9 1.9 %fusion = f32[16,1,128]{2,1,0:T(1,128)S(1)} fusion(f32[16,128,1]{1,2,0:T(1,128)S(1)} %bitcast.211, f32[16,128]{1,0:T(8,128)S(1)} %reduce_window_sum.30, pred[128,128]{1,0:T(8,128)(4,1)S(1)} %fusion.62), kind=kOutput, calls=%fused_computation.9 | convolution fusion | flops 3670016 | bytes 40960 | tf_op jit(solution)/shard_map/hij,hj->hi/dot_general | solution.py:184
  168.8 0.7 copy-done.24
  169.4 0.7 multiply_subtract_fusion
  170.1 0.6 slice_bitcast_fusion
  (154 shorter events, 6.5 us)
Async XLA Ops:
  0.6 10.7 %copy-start.11 = (bf16[128,1024]{1,0:T(8,128)(2,1)S(1)}, bf16[128,1024]{1,0:T(8,128)(2,1)}, u32[]{:S(2)}) copy-start(bf16[128,1024]{1,0:T(8,128)(2,1)} %param.8) | copy-start | bytes 786436
  2.0 10.6 %all-to-all-start = ((bf16[8,2,16,128]{3,2,1,0:T(8,128)(2,1)}), bf16[8,2,16,128]{3,2,1,0:T(8,128)(2,1)S(1)}, u32[]{:S(2)}, u32[]{:S(2)}) async-start(bf16[8,2,16,128]{3,2,1,0:T(8,128)(2,1)} %broadcast_in_dim.28), calls=%async_computation | async-start | bytes 131072 | tf_op jit(solution)/shard_map/all_to_all | solution.py:92
  8.1 0.7 copy-start.16
  8.7 2.0 %copy-start.13 = (f32[16,128]{1,0:T(8,128)S(1)}, f32[16,128]{1,0:T(8,128)}, u32[]{:S(2)}) copy-start(f32[16,128]{1,0:T(8,128)} %param.10) | copy-start | bytes 24580
  10.1 0.7 copy-start.23
  11.5 1.0 copy-start.12
  11.5 1.6 copy-start
  14.3 9.5 %collective-permute-start = (s16[1033,128]{1,0:T(8,128)(2,1)S(1)}, s16[1033,128]{1,0:T(8,128)(2,1)S(1)}, u32[]{:S(2)}, u32[]{:S(2)}) collective-permute-start(s16[1033,128]{1,0:T(8,128)(2,1)S(1)} %get-tuple-element.21), channel_id=1, source_target_pairs={{0,8},{8,16},{16,24},{24,32},{32,40},{40,48},{48,56},{56,64},{64,7... | collective-permute-start | bytes 793352 | tf_op jit(solution)/shard_map/ppermute | solution.py:12
  17.8 10.9 %collective-permute-start.1 = (s16[1033,128]{1,0:T(8,128)(2,1)S(1)}, s16[1033,128]{1,0:T(8,128)(2,1)S(1)}, u32[]{:S(2)}, u32[]{:S(2)}) collective-permute-start(s16[1033,128]{1,0:T(8,128)(2,1)S(1)} %get-tuple-element.22), channel_id=1, source_target_pairs={{8,0},{16,8},{24,16},{32,24},{40,32},{48,40},{56,48},{64,56},{72,6... | collective-permute-start | bytes 793352 | tf_op jit(solution)/shard_map/ppermute | solution.py:12
  28.7 2.2 %copy-start.2 = (s16[1033,128]{1,0:T(8,128)(2,1)}, s16[1033,128]{1,0:T(8,128)(2,1)S(1)}, u32[]{:S(2)}) copy-start(s16[1033,128]{1,0:T(8,128)(2,1)S(1)} %collective-permute-done.1) | copy-start | bytes 793348
  30.4 0.5 copy-start.19
  30.4 0.6 copy-start.21
  31.8 11.1 %collective-permute-start.2 = (s16[1033,128]{1,0:T(8,128)(2,1)S(1)}, s16[1033,128]{1,0:T(8,128)(2,1)S(1)}, u32[]{:S(2)}, u32[]{:S(2)}) collective-permute-start(s16[1033,128]{1,0:T(8,128)(2,1)S(1)} %get-tuple-element.23), channel_id=1, source_target_pairs={{0,16},{8,24},{16,32},{24,40},{32,48},{40,56},{48,64},{56,72},{64,... | collective-permute-start | bytes 793352 | tf_op jit(solution)/shard_map/ppermute | solution.py:12
  36.6 11.6 %collective-permute-start.3 = (s16[1033,128]{1,0:T(8,128)(2,1)S(1)}, s16[1033,128]{1,0:T(8,128)(2,1)S(1)}, u32[]{:S(2)}, u32[]{:S(2)}) collective-permute-start(s16[1033,128]{1,0:T(8,128)(2,1)S(1)} %get-tuple-element.24), channel_id=1, source_target_pairs={{16,0},{24,8},{32,16},{40,24},{48,32},{56,40},{64,48},{72,56},{80,... | collective-permute-start | bytes 793352 | tf_op jit(solution)/shard_map/ppermute | solution.py:12
  42.9 5.4 %copy-start.10 = (s16[1033,128]{1,0:T(8,128)(2,1)}, s16[1033,128]{1,0:T(8,128)(2,1)S(1)}, u32[]{:S(2)}) copy-start(s16[1033,128]{1,0:T(8,128)(2,1)S(1)} %collective-permute-done.2) | copy-start | bytes 793348
  48.2 0.7 copy-start.9
  48.8 1.0 copy-start.3
  48.9 0.9 copy-start.17
  48.9 0.9 copy-start.18
  51.2 0.7 copy-start.22
  52.0 0.7 copy-start.20
  54.0 15.1 %collective-permute-start.4 = (s16[1033,128]{1,0:T(8,128)(2,1)S(1)}, s16[1033,128]{1,0:T(8,128)(2,1)S(1)}, u32[]{:S(2)}, u32[]{:S(2)}) collective-permute-start(s16[1033,128]{1,0:T(8,128)(2,1)S(1)} %get-tuple-element.33), channel_id=1, source_target_pairs={{0,32},{8,40},{16,48},{24,56},{32,64},{40,72},{48,80},{56,88},{64,... | collective-permute-start | bytes 793352 | tf_op jit(solution)/shard_map/ppermute | solution.py:12
  61.6 13.9 %collective-permute-start.5 = (s16[1033,128]{1,0:T(8,128)(2,1)}, s16[1033,128]{1,0:T(8,128)(2,1)S(1)}, u32[]{:S(2)}, u32[]{:S(2)}) collective-permute-start(s16[1033,128]{1,0:T(8,128)(2,1)} %get-tuple-element.31), channel_id=1, source_target_pairs={{32,0},{40,8},{48,16},{56,24},{64,32},{72,40},{80,48},{88,56},{96,... | collective-permute-start | bytes 793352 | tf_op jit(solution)/shard_map/ppermute | solution.py:12
  77.2 15.4 %copy-start.1 = (f32[16,128,64]{1,2,0:T(8,128)S(1)}, f32[16,128,64]{1,2,0:T(8,128)}, u32[]{:S(2)}) copy-start(f32[16,128,64]{1,2,0:T(8,128)} %copy-done) | copy-start | bytes 1572868
  78.0 35.7 %collective-permute-start.6 = (s16[1033,128]{1,0:T(8,128)(2,1)}, s16[1033,128]{1,0:T(8,128)(2,1)S(1)}, u32[]{:S(2)}, u32[]{:S(2)}) collective-permute-start(s16[1033,128]{1,0:T(8,128)(2,1)} %get-tuple-element.31), channel_id=1, source_target_pairs={{8,0},{16,8},{24,16},{32,24},{40,32},{48,40},{56,48},{64,56},{72,6... | collective-permute-start | bytes 793352 | tf_op jit(solution)/shard_map/ppermute | solution.py:12
  92.5 2.4 %copy-start.14 = (f32[128,128]{1,0:T(8,128)}, f32[128,128]{1,0:T(8,128)S(1)}, u32[]{:S(2)}) copy-start(f32[128,128]{1,0:T(8,128)S(1)} %fusion.221) | copy-start | bytes 196612
  95.5 29.1 %collective-permute-start.7 = (s16[1033,128]{1,0:T(8,128)(2,1)}, s16[1033,128]{1,0:T(8,128)(2,1)S(1)}, u32[]{:S(2)}, u32[]{:S(2)}) collective-permute-start(s16[1033,128]{1,0:T(8,128)(2,1)} %get-tuple-element.32), channel_id=1, source_target_pairs={{40,0},{48,8},{56,16},{64,24},{72,32},{80,40},{88,48},{96,56},{104... | collective-permute-start | bytes 793352 | tf_op jit(solution)/shard_map/ppermute | solution.py:12
  104.6 20.0 %collective-permute-start.8 = (s16[1033,128]{1,0:T(8,128)(2,1)S(1)}, s16[1033,128]{1,0:T(8,128)(2,1)S(1)}, u32[]{:S(2)}, u32[]{:S(2)}) collective-permute-start(s16[1033,128]{1,0:T(8,128)(2,1)S(1)} %get-tuple-element.33), channel_id=1, source_target_pairs={{0,8},{8,16},{16,24},{24,32},{32,40},{40,48},{48,56},{56,64},{64,7... | collective-permute-start | bytes 793352 | tf_op jit(solution)/shard_map/ppermute | solution.py:12
  106.5 40.6 %collective-permute-start.9 = (s16[1033,128]{1,0:T(8,128)(2,1)S(1)}, s16[1033,128]{1,0:T(8,128)(2,1)S(1)}, u32[]{:S(2)}, u32[]{:S(2)}) collective-permute-start(s16[1033,128]{1,0:T(8,128)(2,1)S(1)} %get-tuple-element.34), channel_id=1, source_target_pairs={{0,40},{8,48},{16,56},{24,64},{32,72},{40,80},{48,88},{56,96},{64,... | collective-permute-start | bytes 793352 | tf_op jit(solution)/shard_map/ppermute | solution.py:12
  124.6 24.4 %copy-start.5 = (s16[1033,128]{1,0:T(8,128)(2,1)}, s16[1033,128]{1,0:T(8,128)(2,1)S(1)}, u32[]{:S(2)}) copy-start(s16[1033,128]{1,0:T(8,128)(2,1)S(1)} %collective-permute-done.7) | copy-start | bytes 793348
  124.6 24.4 %copy-start.7 = (s16[1033,128]{1,0:T(8,128)(2,1)}, s16[1033,128]{1,0:T(8,128)(2,1)S(1)}, u32[]{:S(2)}) copy-start(s16[1033,128]{1,0:T(8,128)(2,1)S(1)} %collective-permute-done.8) | copy-start | bytes 793348
  149.5 1.0 copy-start.8
  152.1 1.0 copy-start.6
  154.5 7.6 %copy-start.4 = (f32[1024,128]{1,0:T(8,128)S(1)}, f32[1024,128]{1,0:T(8,128)}, u32[]{:S(2)}) copy-start(f32[1024,128]{1,0:T(8,128)} %get-tuple-element.61) | copy-start | bytes 1572868
  155.4 14.7 %all-to-all-start.1 = ((f32[8,2,16,128]{3,2,1,0:T(8,128)}), f32[8,2,16,128]{3,2,1,0:T(8,128)S(1)}, u32[]{:S(2)}, u32[]{:S(2)}) async-start(f32[8,2,16,128]{3,2,1,0:T(8,128)} %maximum_bitcast_fusion), calls=%async_computation.1 | async-start | bytes 262144 | tf_op jit(solution)/shard_map/all_to_all | solution.py:67
  163.7 0.8 copy-start.15
  163.7 0.8 copy-start.25
  168.7 0.7 copy-start.24

commit v13 on v11

--- a/solution.py
+++ b/solution.py
@@ -127,10 +127,7 @@
     held = (logc, dys, moved, b_bf, c_bf)
     while span < high:
         kept[span] = (fwd, bwd)
-        if 2 * span < high:
-            got_f, got_b, _ = shift_pair(fwd, bwd, span)
-        else:
-            got_f, got_b, held = shift_pair(fwd, bwd, span, held)
+        got_f, got_b, _ = shift_pair(fwd, bwd, span)
         fwd = combine(fwd, got_f)
         bwd = combine(bwd, got_b)
         span *= 2
@@ -142,7 +139,8 @@
         from_behind(sends[2], "context", -1),
         from_behind(sends[3], "context", -low - 1),
     )
-    got = [unpack(g, shape) for g in got]
+    first, held = lax.optimization_barrier((got[0], held))
+    got = [unpack(g, shape) for g in (first,) + got[1:]]
     s_in = combine(got[0], got[1])[0]
     g_in = combine(got[2], got[3])[0]
 

time: 171 us -> 176 us (1.029)
  the two profiles are of different devices: /device:TPU:75 before, /device:TPU:105 now
where the time goes in v13:
time: 176 us; the launch traced here: 175 us
  waiting for transfers between devices  62.3 us (35%)
  starting transfers between devices  61.7 us (35%)
  other arithmetic  21.8 us (12%)
  local copies, waits for them, and re-layouts  14.2 us (8%)
  matrix products  13.1 us (7%)
  between operations  2.01 us (1%)
    ppermute x10, waiting for transfers between devices, from_behind(): return lax.ppermute(x, axis, pairs)  62.3 us
    ppermute x10, starting transfers between devices, from_behind(): return lax.ppermute(x, axis, pairs)  41.3 us
    all_to_all x1, starting transfers between devices, scatter_sum(): got = lax.all_to_all(parts, axis, 0, 0, tiled=True)  15.2 us
    unnamed x65, local copies, waits for them, and re-layouts  8.72 us
    all_to_all x1, starting transfers between devices, local(): lax.all_to_all(jnp.broadcast_to(piece, (count,) + piece.shape), 'tensor',...  5.23 us
  transfers between devices with their start and end apart: 12, of which 7 were waited for; matrix products, arithmetic and copies ran while one was open for 12% of the time, Pallas kernels for 0%

profile of v13, /device:TPU:105, one launch (start us, length us, event | category | flops | bytes accessed | tf_op | source)
XLA Modules:
  0.0 175.1 jit_solution(1405364090179229066)
XLA Ops:
  0.6 0.7 pad_maximum_fusion
  1.4 0.6 broadcast_in_dim.28
  2.0 5.2 %all-to-all-start = ((bf16[8,2,16,128]{3,2,1,0:T(8,128)(2,1)}), bf16[8,2,16,128]{3,2,1,0:T(8,128)(2,1)S(1)}, u32[]{:S(2)}, u32[]{:S(2)}) async-start(bf16[8,2,16,128]{3,2,1,0:T(8,128)(2,1)} %broadcast_in_dim.28), calls=%async_computation | async-start | bytes 131072 | tf_op jit(solution)/shard_map/all_to_all | solution.py:92
  7.3 0.7 copy.26
  8.2 0.6 copy-done.18
  9.0 0.6 slice.172
  9.6 0.6 compare_convert_fusion
  11.8 0.8 copy-done.7
  12.7 0.5 abs_reduce_fusion.7
  13.3 0.5 abs_reduce_fusion.6
  14.4 4.7 %collective-permute-start = (s16[1033,128]{1,0:T(8,128)(2,1)S(1)}, s16[1033,128]{1,0:T(8,128)(2,1)S(1)}, u32[]{:S(2)}, u32[]{:S(2)}) collective-permute-start(s16[1033,128]{1,0:T(8,128)(2,1)S(1)} %get-tuple-element.20), channel_id=1, source_target_pairs={{0,8},{8,16},{16,24},{24,32},{32,40},{40,48},{48,56},{56,64},{64,7... | collective-permute-start | bytes 793352 | tf_op jit(solution)/shard_map/ppermute | solution.py:12
  19.2 1.9 %collective-permute-start.1 = (s16[1033,128]{1,0:T(8,128)(2,1)S(1)}, s16[1033,128]{1,0:T(8,128)(2,1)S(1)}, u32[]{:S(2)}, u32[]{:S(2)}) collective-permute-start(s16[1033,128]{1,0:T(8,128)(2,1)S(1)} %get-tuple-element.21), channel_id=1, source_target_pairs={{8,0},{16,8},{24,16},{32,24},{40,32},{48,40},{56,48},{64,56},{72,6... | collective-permute-start | bytes 793352 | tf_op jit(solution)/shard_map/ppermute | solution.py:12
  21.1 3.5 %collective-permute-done = s16[1033,128]{1,0:T(8,128)(2,1)S(1)} collective-permute-done((s16[1033,128]{1,0:T(8,128)(2,1)S(1)}, s16[1033,128]{1,0:T(8,128)(2,1)S(1)}, u32[]{:S(2)}, u32[]{:S(2)}) %collective-permute-start) | collective-permute-done | bytes 264480 | tf_op jit(solution)/shard_map/ppermute | solution.py:12
  24.6 4.9 %collective-permute-done.1 = s16[1033,128]{1,0:T(8,128)(2,1)S(1)} collective-permute-done((s16[1033,128]{1,0:T(8,128)(2,1)S(1)}, s16[1033,128]{1,0:T(8,128)(2,1)S(1)}, u32[]{:S(2)}, u32[]{:S(2)}) %collective-permute-start.1) | collective-permute-done | bytes 264480 | tf_op jit(solution)/shard_map/ppermute | solution.py:12
  29.7 0.7 abs_reduce_fusion.4
  30.6 0.6 fusion.225
  31.2 0.5 copy-done.25
  31.8 0.7 clamp_convert_fusion.4
  32.7 4.1 %collective-permute-start.2 = (s16[1033,128]{1,0:T(8,128)(2,1)S(1)}, s16[1033,128]{1,0:T(8,128)(2,1)S(1)}, u32[]{:S(2)}, u32[]{:S(2)}) collective-permute-start(s16[1033,128]{1,0:T(8,128)(2,1)S(1)} %get-tuple-element.22), channel_id=1, source_target_pairs={{0,16},{8,24},{16,32},{24,40},{32,48},{40,56},{48,64},{56,72},{64,... | collective-permute-start | bytes 793352 | tf_op jit(solution)/shard_map/ppermute | solution.py:12
  36.7 2.1 %collective-permute-start.3 = (s16[1033,128]{1,0:T(8,128)(2,1)S(1)}, s16[1033,128]{1,0:T(8,128)(2,1)S(1)}, u32[]{:S(2)}, u32[]{:S(2)}) collective-permute-start(s16[1033,128]{1,0:T(8,128)(2,1)S(1)} %get-tuple-element.23), channel_id=1, source_target_pairs={{16,0},{24,8},{32,16},{40,24},{48,32},{56,40},{64,48},{72,56},{80,... | collective-permute-start | bytes 793352 | tf_op jit(solution)/shard_map/ppermute | solution.py:12
  38.9 9.5 %collective-permute-done.2 = s16[1033,128]{1,0:T(8,128)(2,1)S(1)} collective-permute-done((s16[1033,128]{1,0:T(8,128)(2,1)S(1)}, s16[1033,128]{1,0:T(8,128)(2,1)S(1)}, u32[]{:S(2)}, u32[]{:S(2)}) %collective-permute-start.2) | collective-permute-done | bytes 264480 | tf_op jit(solution)/shard_map/ppermute | solution.py:12
  48.4 7.6 %collective-permute-done.3 = s16[1033,128]{1,0:T(8,128)(2,1)S(1)} collective-permute-done((s16[1033,128]{1,0:T(8,128)(2,1)S(1)}, s16[1033,128]{1,0:T(8,128)(2,1)S(1)}, u32[]{:S(2)}, u32[]{:S(2)}) %collective-permute-start.3) | collective-permute-done | bytes 264480 | tf_op jit(solution)/shard_map/ppermute | solution.py:12
  56.2 0.6 copy-done.4
  56.8 0.9 copy-done.3
  57.7 0.8 fusion.15
  59.3 0.7 slice_convert_fusion.8
  60.4 0.7 slice_convert_fusion.7
  61.1 0.9 fusion.59
  62.0 2.0 %collective-permute-start.4 = (s16[1033,128]{1,0:T(8,128)(2,1)}, s16[1033,128]{1,0:T(8,128)(2,1)S(1)}, u32[]{:S(2)}, u32[]{:S(2)}) collective-permute-start(s16[1033,128]{1,0:T(8,128)(2,1)} %get-tuple-element.26), channel_id=1, source_target_pairs={{0,32},{8,40},{16,48},{24,56},{32,64},{40,72},{48,80},{56,88},{64,... | collective-permute-start | bytes 793352 | tf_op jit(solution)/shard_map/ppermute | solution.py:12
  64.0 1.3 collective-permute-start.5
  65.3 20.4 %collective-permute-done.4 = s16[1033,128]{1,0:T(8,128)(2,1)S(1)} collective-permute-done((s16[1033,128]{1,0:T(8,128)(2,1)}, s16[1033,128]{1,0:T(8,128)(2,1)S(1)}, u32[]{:S(2)}, u32[]{:S(2)}) %collective-permute-start.4) | collective-permute-done | bytes 264480 | tf_op jit(solution)/shard_map/ppermute | solution.py:12
  85.9 0.4 abs_reduce_fusion.1
  88.0 0.8 fusion.61
  88.8 11.2 %collective-permute-start.6 = (s16[1033,128]{1,0:T(8,128)(2,1)}, s16[1033,128]{1,0:T(8,128)(2,1)S(1)}, u32[]{:S(2)}, u32[]{:S(2)}) collective-permute-start(s16[1033,128]{1,0:T(8,128)(2,1)} %get-tuple-element.26), channel_id=1, source_target_pairs={{0,8},{8,16},{16,24},{24,32},{32,40},{40,48},{48,56},{56,64},{64,7... | collective-permute-start | bytes 793352 | tf_op jit(solution)/shard_map/ppermute | solution.py:12
  100.1 1.9 %collective-permute-start.7 = (s16[1033,128]{1,0:T(8,128)(2,1)}, s16[1033,128]{1,0:T(8,128)(2,1)S(1)}, u32[]{:S(2)}, u32[]{:S(2)}) collective-permute-start(s16[1033,128]{1,0:T(8,128)(2,1)} %get-tuple-element.31), channel_id=1, source_target_pairs={{8,0},{16,8},{24,16},{32,24},{40,32},{48,40},{56,48},{64,56},{72,6... | collective-permute-start | bytes 793352 | tf_op jit(solution)/shard_map/ppermute | solution.py:12
  102.0 1.3 collective-permute-start.8
  103.3 10.7 %collective-permute-start.9 = (s16[1033,128]{1,0:T(8,128)(2,1)}, s16[1033,128]{1,0:T(8,128)(2,1)}, u32[]{:S(2)}, u32[]{:S(2)}) collective-permute-start(s16[1033,128]{1,0:T(8,128)(2,1)} %get-tuple-element.35), channel_id=1, source_target_pairs={{0,40},{8,48},{16,56},{24,64},{32,72},{40,80},{48,88},{56,96},{64,... | collective-permute-start | bytes 793352 | tf_op jit(solution)/shard_map/ppermute | solution.py:12
  114.1 0.6 slice_convert_fusion.11
  114.8 7.6 %collective-permute-done.7 = s16[1033,128]{1,0:T(8,128)(2,1)S(1)} collective-permute-done((s16[1033,128]{1,0:T(8,128)(2,1)}, s16[1033,128]{1,0:T(8,128)(2,1)S(1)}, u32[]{:S(2)}, u32[]{:S(2)}) %collective-permute-start.7) | collective-permute-done | bytes 264480 | tf_op jit(solution)/shard_map/ppermute | solution.py:12
  122.4 0.6 multiply_exponential_fusion.3
  123.0 0.6 exponential_bitcast_fusion.1
  123.6 8.7 %collective-permute-done.8 = s16[1033,128]{1,0:T(8,128)(2,1)S(1)} collective-permute-done((s16[1033,128]{1,0:T(8,128)(2,1)S(1)}, s16[1033,128]{1,0:T(8,128)(2,1)S(1)}, u32[]{:S(2)}, u32[]{:S(2)}) %collective-permute-start.8) | collective-permute-done | bytes 264480 | tf_op jit(solution)/shard_map/ppermute | solution.py:12
  132.3 0.6 multiply_exponential_fusion.2
  133.0 3.0 %fusion.8 = (f32[16,128]{1,0:T(8,128)}, f32[16,128]{1,0:T(8,128)}, f32[128,128]{1,0:T(8,128)}) fusion(f32[128,128]{1,0:T(8,128)S(1)} %fusion.231, f32[16,128]{1,0:T(8,128)S(1)} %reduce_window_sum.30, pred[128,128]{1,0:T(8,128)(4,1)S(1)} %fusion.72, f32[16,128,64]{1,2,0:T(8,128)S(1)} %bitcast.198, f32[16,128,64]{1,2,0:T(8,128)S(1)} %copy-done.1), kind=kOutput, calls=%fused_computation.21 | convolution fusion | flops 203403264 | bytes 1220608 | tf_op jit(solution)/shard_map/hip,hjp->hij/dot_general | solution.py:156
  136.2 2.1 %fusion.6 = f32[16,128,64]{1,2,0:T(8,128)S(1)} fusion(f32[16,128,64]{1,2,0:T(8,128)S(1)} %bitcast.199, f32[128,128]{1,0:T(8,128)} %copy-done.10, f32[16,128]{1,0:T(8,128)S(1)} %reduce_window_sum.30, pred[128,128]{1,0:T(8,128)(4,1)} %copy-done.15), kind=kOutput, calls=%fused_computation.13 | convolution fusion | flops 202113024 | bytes 1138688 | tf_op jit(solution)/shard_map/hij,hip->hjp/dot_general | solution.py:155
  138.3 1.3 multiply_exponential_fusion
  139.6 0.8 exp2.405
  140.3 0.8 exponential_bitcast_fusion
  141.3 0.6 copy-done.19
  141.9 1.3 convolution_bitcast_fusion.2
  143.5 1.0 slice_convert_fusion
  144.5 1.3 convolution_bitcast_fusion.1
  146.0 0.7 maximum_bitcast_fusion
  146.7 15.2 %all-to-all-start.1 = ((f32[8,2,16,128]{3,2,1,0:T(8,128)}), f32[8,2,16,128]{3,2,1,0:T(8,128)S(1)}, u32[]{:S(2)}, u32[]{:S(2)}) async-start(f32[8,2,16,128]{3,2,1,0:T(8,128)} %maximum_bitcast_fusion), calls=%async_computation.1 | async-start | bytes 262144 | tf_op jit(solution)/shard_map/all_to_all | solution.py:67
  163.4 0.5 copy-done.20
  164.0 0.6 copy-done.13
  164.7 2.1 %multiply_reduce_fusion.1 = (f32[1024]{0:T(1024)S(1)}, f32[1024,128]{1,0:T(8,128)S(1)}, f32[1024,128]{1,0:T(8,128)S(1)}) fusion(f32[1024]{0:T(1024)S(1)} %copy-done.14, s16[1033,128]{1,0:T(8,128)(2,1)} %collective-permute-done.9, f32[1024]{0:T(1024)S(1)} %mul.481, f32[1024]{0:T(1024)S(1)} %get-tuple-element.83, ...), kind=kLoop, calls=%fused_computation.59 | loop fusion | flops 1833984 | bytes 2125824 | tf_op jit(solution)/shard_map/reduce_sum | solution.py:176
  167.5 1.2 fusion.3
  168.7 0.7 copy-done.31
  170.0 1.9 %fusion.2 = f32[16,1,128]{2,1,0:T(1,128)S(1)} fusion(f32[16,128,1]{1,2,0:T(1,128)S(1)} %bitcast.237, f32[16,128]{1,0:T(8,128)S(1)} %reduce_window_sum.30, pred[128,128]{1,0:T(8,128)(4,1)S(1)} %copy-done.16), kind=kOutput, calls=%fused_computation.9 | convolution fusion | flops 3670016 | bytes 40960 | tf_op jit(solution)/shard_map/hij,hj->hi/dot_general | solution.py:173
  172.1 1.0 copy.31
  173.1 0.7 copy-done.30
  173.8 0.7 multiply_subtract_fusion
  174.5 0.6 slice_bitcast_fusion
  (165 shorter events, 10.1 us)
Async XLA Ops:
  0.6 10.8 %copy-start.6 = (bf16[128,1024]{1,0:T(8,128)(2,1)S(1)}, bf16[128,1024]{1,0:T(8,128)(2,1)}, u32[]{:S(2)}) copy-start(bf16[128,1024]{1,0:T(8,128)(2,1)} %param.8) | copy-start | bytes 786436
  2.0 10.7 %all-to-all-start = ((bf16[8,2,16,128]{3,2,1,0:T(8,128)(2,1)}), bf16[8,2,16,128]{3,2,1,0:T(8,128)(2,1)S(1)}, u32[]{:S(2)}, u32[]{:S(2)}) async-start(bf16[8,2,16,128]{3,2,1,0:T(8,128)(2,1)} %broadcast_in_dim.28), calls=%async_computation | async-start | bytes 131072 | tf_op jit(solution)/shard_map/all_to_all | solution.py:92
  8.2 0.7 copy-start.18
  8.9 2.0 %copy-start.9 = (f32[16,128]{1,0:T(8,128)S(1)}, f32[16,128]{1,0:T(8,128)}, u32[]{:S(2)}) copy-start(f32[16,128]{1,0:T(8,128)} %param.10) | copy-start | bytes 24580
  10.2 0.7 copy-start.29
  11.6 1.0 copy-start.7
  11.7 1.5 copy-start
  14.4 10.1 %collective-permute-start = (s16[1033,128]{1,0:T(8,128)(2,1)S(1)}, s16[1033,128]{1,0:T(8,128)(2,1)S(1)}, u32[]{:S(2)}, u32[]{:S(2)}) collective-permute-start(s16[1033,128]{1,0:T(8,128)(2,1)S(1)} %get-tuple-element.20), channel_id=1, source_target_pairs={{0,8},{8,16},{16,24},{24,32},{32,40},{40,48},{48,56},{56,64},{64,7... | collective-permute-start | bytes 793352 | tf_op jit(solution)/shard_map/ppermute | solution.py:12
  19.2 10.4 %collective-permute-start.1 = (s16[1033,128]{1,0:T(8,128)(2,1)S(1)}, s16[1033,128]{1,0:T(8,128)(2,1)S(1)}, u32[]{:S(2)}, u32[]{:S(2)}) collective-permute-start(s16[1033,128]{1,0:T(8,128)(2,1)S(1)} %get-tuple-element.21), channel_id=1, source_target_pairs={{8,0},{16,8},{24,16},{32,24},{40,32},{48,40},{56,48},{64,56},{72,6... | collective-permute-start | bytes 793352 | tf_op jit(solution)/shard_map/ppermute | solution.py:12
  29.6 2.3 %copy-start.2 = (s16[1033,128]{1,0:T(8,128)(2,1)}, s16[1033,128]{1,0:T(8,128)(2,1)S(1)}, u32[]{:S(2)}) copy-start(s16[1033,128]{1,0:T(8,128)(2,1)S(1)} %collective-permute-done.1) | copy-start | bytes 793348
  31.2 0.5 copy-start.25
  31.2 0.6 copy-start.27
  32.7 15.7 %collective-permute-start.2 = (s16[1033,128]{1,0:T(8,128)(2,1)S(1)}, s16[1033,128]{1,0:T(8,128)(2,1)S(1)}, u32[]{:S(2)}, u32[]{:S(2)}) collective-permute-start(s16[1033,128]{1,0:T(8,128)(2,1)S(1)} %get-tuple-element.22), channel_id=1, source_target_pairs={{0,16},{8,24},{16,32},{24,40},{32,48},{40,56},{48,64},{56,72},{64,... | collective-permute-start | bytes 793352 | tf_op jit(solution)/shard_map/ppermute | solution.py:12
  36.7 19.3 %collective-permute-start.3 = (s16[1033,128]{1,0:T(8,128)(2,1)S(1)}, s16[1033,128]{1,0:T(8,128)(2,1)S(1)}, u32[]{:S(2)}, u32[]{:S(2)}) collective-permute-start(s16[1033,128]{1,0:T(8,128)(2,1)S(1)} %get-tuple-element.23), channel_id=1, source_target_pairs={{16,0},{24,8},{32,16},{40,24},{48,32},{56,40},{64,48},{72,56},{80,... | collective-permute-start | bytes 793352 | tf_op jit(solution)/shard_map/ppermute | solution.py:12
  48.3 7.8 %copy-start.5 = (s16[1033,128]{1,0:T(8,128)(2,1)}, s16[1033,128]{1,0:T(8,128)(2,1)S(1)}, u32[]{:S(2)}) copy-start(s16[1033,128]{1,0:T(8,128)(2,1)S(1)} %collective-permute-done.2) | copy-start | bytes 793348
  56.1 0.7 copy-start.4
  56.8 1.0 copy-start.3
  56.8 0.9 copy-start.21
  56.8 0.9 copy-start.22
  59.3 0.7 copy-start.28
  60.4 0.7 copy-start.26
  62.0 23.7 %collective-permute-start.4 = (s16[1033,128]{1,0:T(8,128)(2,1)}, s16[1033,128]{1,0:T(8,128)(2,1)S(1)}, u32[]{:S(2)}, u32[]{:S(2)}) collective-permute-start(s16[1033,128]{1,0:T(8,128)(2,1)} %get-tuple-element.26), channel_id=1, source_target_pairs={{0,32},{8,40},{16,48},{24,56},{32,64},{40,72},{48,80},{56,88},{64,... | collective-permute-start | bytes 793352 | tf_op jit(solution)/shard_map/ppermute | solution.py:12
  64.0 22.4 %collective-permute-start.5 = (s16[1033,128]{1,0:T(8,128)(2,1)}, s16[1033,128]{1,0:T(8,128)(2,1)S(1)}, u32[]{:S(2)}, u32[]{:S(2)}) collective-permute-start(s16[1033,128]{1,0:T(8,128)(2,1)} %get-tuple-element.31), channel_id=1, source_target_pairs={{32,0},{40,8},{48,16},{56,24},{64,32},{72,40},{80,48},{88,56},{96,... | collective-permute-start | bytes 793352 | tf_op jit(solution)/shard_map/ppermute | solution.py:12
  88.8 44.2 %copy-start.1 = (f32[16,128,64]{1,2,0:T(8,128)S(1)}, f32[16,128,64]{1,2,0:T(8,128)}, u32[]{:S(2)}) copy-start(f32[16,128,64]{1,2,0:T(8,128)} %copy-done) | copy-start | bytes 1572868
  88.8 25.3 %collective-permute-start.6 = (s16[1033,128]{1,0:T(8,128)(2,1)}, s16[1033,128]{1,0:T(8,128)(2,1)S(1)}, u32[]{:S(2)}, u32[]{:S(2)}) collective-permute-start(s16[1033,128]{1,0:T(8,128)(2,1)} %get-tuple-element.26), channel_id=1, source_target_pairs={{0,8},{8,16},{16,24},{24,32},{32,40},{40,48},{48,56},{56,64},{64,7... | collective-permute-start | bytes 793352 | tf_op jit(solution)/shard_map/ppermute | solution.py:12
  100.1 32.9 %copy-start.15 = (pred[128,128]{1,0:T(8,128)(4,1)}, pred[128,128]{1,0:T(8,128)(4,1)S(1)}, u32[]{:S(2)}) copy-start(pred[128,128]{1,0:T(8,128)(4,1)S(1)} %fusion.72) | copy-start | bytes 49156
  100.1 22.3 %collective-permute-start.7 = (s16[1033,128]{1,0:T(8,128)(2,1)}, s16[1033,128]{1,0:T(8,128)(2,1)S(1)}, u32[]{:S(2)}, u32[]{:S(2)}) collective-permute-start(s16[1033,128]{1,0:T(8,128)(2,1)} %get-tuple-element.31), channel_id=1, source_target_pairs={{8,0},{16,8},{24,16},{32,24},{40,32},{48,40},{56,48},{64,56},{72,6... | collective-permute-start | bytes 793352 | tf_op jit(solution)/shard_map/ppermute | solution.py:12
  102.0 30.3 %collective-permute-start.8 = (s16[1033,128]{1,0:T(8,128)(2,1)S(1)}, s16[1033,128]{1,0:T(8,128)(2,1)S(1)}, u32[]{:S(2)}, u32[]{:S(2)}) collective-permute-start(s16[1033,128]{1,0:T(8,128)(2,1)S(1)} %get-tuple-element.32), channel_id=1, source_target_pairs={{40,0},{48,8},{56,16},{64,24},{72,32},{80,40},{88,48},{96,56},{104... | collective-permute-start | bytes 793352 | tf_op jit(solution)/shard_map/ppermute | solution.py:12
  103.3 35.0 %collective-permute-start.9 = (s16[1033,128]{1,0:T(8,128)(2,1)}, s16[1033,128]{1,0:T(8,128)(2,1)}, u32[]{:S(2)}, u32[]{:S(2)}) collective-permute-start(s16[1033,128]{1,0:T(8,128)(2,1)} %get-tuple-element.35), channel_id=1, source_target_pairs={{0,40},{8,48},{16,56},{24,64},{32,72},{40,80},{48,88},{56,96},{64,... | collective-permute-start | bytes 793352 | tf_op jit(solution)/shard_map/ppermute | solution.py:12
  114.8 18.2 %copy-start.10 = (f32[128,128]{1,0:T(8,128)}, f32[128,128]{1,0:T(8,128)S(1)}, u32[]{:S(2)}) copy-start(f32[128,128]{1,0:T(8,128)S(1)} %fusion.231) | copy-start | bytes 196612
  141.1 3.4 %copy-start.23 = (f32[16]{0:T(128)}, f32[16]{0:T(128)S(1)}, u32[]{:S(2)}) copy-start(f32[16]{0:T(128)S(1)} %exponential_bitcast_fusion) | copy-start | bytes 196
  141.3 0.6 copy-start.19
  141.9 1.3 copy-start.8
  146.7 15.2 %copy-start.17 = (f32[16,128]{1,0:T(8,128)S(1)}, f32[16,128]{1,0:T(8,128)}, u32[]{:S(2)}) copy-start(f32[16,128]{1,0:T(8,128)} %get-tuple-element.53) | copy-start | bytes 24580
  146.7 27.7 %all-to-all-start.1 = ((f32[8,2,16,128]{3,2,1,0:T(8,128)}), f32[8,2,16,128]{3,2,1,0:T(8,128)S(1)}, u32[]{:S(2)}, u32[]{:S(2)}) async-start(f32[8,2,16,128]{3,2,1,0:T(8,128)} %maximum_bitcast_fusion), calls=%async_computation.1 | async-start | bytes 262144 | tf_op jit(solution)/shard_map/all_to_all | solution.py:67
  161.9 0.7 copy-start.11
  162.6 0.7 copy-start.24
  163.3 0.6 copy-start.20
  163.9 0.7 copy-start.13
  163.9 0.7 copy-start.14
  164.0 0.7 copy-start.12
  166.8 0.7 copy-start.16
  168.7 0.7 copy-start.31
  173.1 0.7 copy-start.30

commit v14 on v11

--- a/solution.py
+++ b/solution.py
@@ -18,7 +18,7 @@
 def pack(value, decay):
     top = jnp.max(jnp.abs(value), axis=-1, keepdims=True)
     expo = jnp.maximum(jnp.ceil(jnp.log2(jnp.where(top > 0, top, 1.0))), -100.0)
-    code = jnp.clip(jnp.round(value / jnp.exp2(expo - 15.0)), -32767.0, 32767.0).astype(jnp.int16)
+    code = jnp.clip(jnp.round(value * jnp.exp2(15.0 - expo)), -32767.0, 32767.0).astype(jnp.int16)
     scaled = decay * 64.0
     high = jnp.floor(scaled)
     low = jnp.round((scaled - high) * 16384.0)

time: 171 us -> 171 us (level)
  no operation moved by 1% of the time
where the time goes in v14:
time: 171 us; the launch traced here: 170 us
  starting transfers between devices  68.7 us (40%)
  waiting for transfers between devices  59.9 us (35%)
  other arithmetic  16.4 us (10%)
  matrix products  11.6 us (7%)
  local copies, waits for them, and re-layouts  11.4 us (7%)
  between operations  1.98 us (1%)
    ppermute x10, waiting for transfers between devices, from_behind(): return lax.ppermute(x, axis, pairs)  59.9 us
    ppermute x10, starting transfers between devices, from_behind(): return lax.ppermute(x, axis, pairs)  56.8 us
    all_to_all x1, starting transfers between devices, scatter_sum(): got = lax.all_to_all(parts, axis, 0, 0, tiled=True)  6.63 us
    unnamed x45, local copies, waits for them, and re-layouts  6.63 us
    all_to_all x1, starting transfers between devices, local(): lax.all_to_all(jnp.broadcast_to(piece, (count,) + piece.shape), 'tensor',...  5.23 us
  transfers between devices with their start and end apart: 12, of which 8 were waited for; matrix products, arithmetic and copies ran while one was open for 8% of the time, Pallas kernels for 0%

profile of v14, /device:TPU:75, one launch (start us, length us, event | category | flops | bytes accessed | tf_op | source)
XLA Modules:
  0.0 170.0 jit_solution(9573954620651043204)
XLA Ops:
  0.6 0.7 pad_maximum_fusion
  1.4 0.6 broadcast_in_dim.28
  2.0 5.2 %all-to-all-start = ((bf16[8,2,16,128]{3,2,1,0:T(8,128)(2,1)}), bf16[8,2,16,128]{3,2,1,0:T(8,128)(2,1)S(1)}, u32[]{:S(2)}, u32[]{:S(2)}) async-start(bf16[8,2,16,128]{3,2,1,0:T(8,128)(2,1)} %broadcast_in_dim.28), calls=%async_computation | async-start | bytes 131072 | tf_op jit(solution)/shard_map/all_to_all | solution.py:92
  7.3 0.7 copy.26
  8.2 0.5 copy-done.12
  8.9 0.6 slice.172
  10.1 0.7 compare_convert_fusion
  10.9 0.3 reduce_window_sum.30
  11.7 0.8 copy-done.10
  12.6 0.5 abs_reduce_fusion.6
  13.2 0.5 abs_reduce_fusion.7
  14.3 3.5 %collective-permute-start = (s16[1033,128]{1,0:T(8,128)(2,1)S(1)}, s16[1033,128]{1,0:T(8,128)(2,1)S(1)}, u32[]{:S(2)}, u32[]{:S(2)}) collective-permute-start(s16[1033,128]{1,0:T(8,128)(2,1)S(1)} %get-tuple-element.19), channel_id=1, source_target_pairs={{0,8},{8,16},{16,24},{24,32},{32,40},{40,48},{48,56},{56,64},{64,7... | collective-permute-start | bytes 793352 | tf_op jit(solution)/shard_map/ppermute | solution.py:12
  17.8 1.9 %collective-permute-start.1 = (s16[1033,128]{1,0:T(8,128)(2,1)S(1)}, s16[1033,128]{1,0:T(8,128)(2,1)S(1)}, u32[]{:S(2)}, u32[]{:S(2)}) collective-permute-start(s16[1033,128]{1,0:T(8,128)(2,1)S(1)} %get-tuple-element.20), channel_id=1, source_target_pairs={{8,0},{16,8},{24,16},{32,24},{40,32},{48,40},{56,48},{64,56},{72,6... | collective-permute-start | bytes 793352 | tf_op jit(solution)/shard_map/ppermute | solution.py:12
  19.7 4.0 %collective-permute-done = s16[1033,128]{1,0:T(8,128)(2,1)S(1)} collective-permute-done((s16[1033,128]{1,0:T(8,128)(2,1)S(1)}, s16[1033,128]{1,0:T(8,128)(2,1)S(1)}, u32[]{:S(2)}, u32[]{:S(2)}) %collective-permute-start) | collective-permute-done | bytes 264480 | tf_op jit(solution)/shard_map/ppermute | solution.py:12
  23.8 4.9 %collective-permute-done.1 = s16[1033,128]{1,0:T(8,128)(2,1)S(1)} collective-permute-done((s16[1033,128]{1,0:T(8,128)(2,1)S(1)}, s16[1033,128]{1,0:T(8,128)(2,1)S(1)}, u32[]{:S(2)}, u32[]{:S(2)}) %collective-permute-start.1) | collective-permute-done | bytes 264480 | tf_op jit(solution)/shard_map/ppermute | solution.py:12
  28.8 0.7 abs_reduce_fusion.4
  29.7 0.6 fusion.225
  30.4 0.5 copy-done.15
  31.0 0.7 clamp_convert_fusion.4
  31.8 4.8 %collective-permute-start.2 = (s16[1033,128]{1,0:T(8,128)(2,1)S(1)}, s16[1033,128]{1,0:T(8,128)(2,1)S(1)}, u32[]{:S(2)}, u32[]{:S(2)}) collective-permute-start(s16[1033,128]{1,0:T(8,128)(2,1)S(1)} %get-tuple-element.21), channel_id=1, source_target_pairs={{0,16},{8,24},{16,32},{24,40},{32,48},{40,56},{48,64},{56,72},{64,... | collective-permute-start | bytes 793352 | tf_op jit(solution)/shard_map/ppermute | solution.py:12
  36.6 2.4 %collective-permute-start.3 = (s16[1033,128]{1,0:T(8,128)(2,1)S(1)}, s16[1033,128]{1,0:T(8,128)(2,1)S(1)}, u32[]{:S(2)}, u32[]{:S(2)}) collective-permute-start(s16[1033,128]{1,0:T(8,128)(2,1)S(1)} %get-tuple-element.22), channel_id=1, source_target_pairs={{16,0},{24,8},{32,16},{40,24},{48,32},{56,40},{64,48},{72,56},{80,... | collective-permute-start | bytes 793352 | tf_op jit(solution)/shard_map/ppermute | solution.py:12
  39.0 3.9 %collective-permute-done.2 = s16[1033,128]{1,0:T(8,128)(2,1)S(1)} collective-permute-done((s16[1033,128]{1,0:T(8,128)(2,1)S(1)}, s16[1033,128]{1,0:T(8,128)(2,1)S(1)}, u32[]{:S(2)}, u32[]{:S(2)}) %collective-permute-start.2) | collective-permute-done | bytes 264480 | tf_op jit(solution)/shard_map/ppermute | solution.py:12
  43.0 5.2 %collective-permute-done.3 = s16[1033,128]{1,0:T(8,128)(2,1)S(1)} collective-permute-done((s16[1033,128]{1,0:T(8,128)(2,1)S(1)}, s16[1033,128]{1,0:T(8,128)(2,1)S(1)}, u32[]{:S(2)}, u32[]{:S(2)}) %collective-permute-start.3) | collective-permute-done | bytes 264480 | tf_op jit(solution)/shard_map/ppermute | solution.py:12
  48.3 0.6 copy-done.7
  48.9 0.9 copy-done.3
  49.8 0.8 fusion.15
  51.2 0.7 slice_convert_fusion.9
  52.0 0.7 slice_convert_fusion.8
  53.3 0.9 fusion.59
  54.1 7.5 %collective-permute-start.4 = (s16[1033,128]{1,0:T(8,128)(2,1)}, s16[1033,128]{1,0:T(8,128)(2,1)S(1)}, u32[]{:S(2)}, u32[]{:S(2)}) collective-permute-start(s16[1033,128]{1,0:T(8,128)(2,1)} %get-tuple-element.32), channel_id=1, source_target_pairs={{0,32},{8,40},{16,48},{24,56},{32,64},{40,72},{48,80},{56,88},{64,... | collective-permute-start | bytes 793352 | tf_op jit(solution)/shard_map/ppermute | solution.py:12
  61.7 2.6 %collective-permute-start.5 = (s16[1033,128]{1,0:T(8,128)(2,1)}, s16[1033,128]{1,0:T(8,128)(2,1)S(1)}, u32[]{:S(2)}, u32[]{:S(2)}) collective-permute-start(s16[1033,128]{1,0:T(8,128)(2,1)} %get-tuple-element.29), channel_id=1, source_target_pairs={{32,0},{40,8},{48,16},{56,24},{64,32},{72,40},{80,48},{88,56},{96,... | collective-permute-start | bytes 793352 | tf_op jit(solution)/shard_map/ppermute | solution.py:12
  64.4 5.0 %collective-permute-done.4 = s16[1033,128]{1,0:T(8,128)(2,1)S(1)} collective-permute-done((s16[1033,128]{1,0:T(8,128)(2,1)}, s16[1033,128]{1,0:T(8,128)(2,1)S(1)}, u32[]{:S(2)}, u32[]{:S(2)}) %collective-permute-start.4) | collective-permute-done | bytes 264480 | tf_op jit(solution)/shard_map/ppermute | solution.py:12
  69.6 0.4 abs_reduce_fusion.1
  70.1 5.6 %collective-permute-done.5 = s16[1033,128]{1,0:T(8,128)(2,1)S(1)} collective-permute-done((s16[1033,128]{1,0:T(8,128)(2,1)}, s16[1033,128]{1,0:T(8,128)(2,1)S(1)}, u32[]{:S(2)}, u32[]{:S(2)}) %collective-permute-start.5) | collective-permute-done | bytes 264480 | tf_op jit(solution)/shard_map/ppermute | solution.py:12
  75.8 0.4 abs_reduce_fusion
  76.5 0.4 clamp_convert_fusion.1
  76.9 0.4 clamp_convert_fusion
  77.3 0.9 fusion.61
  78.2 14.4 %collective-permute-start.6 = (s16[1033,128]{1,0:T(8,128)(2,1)}, s16[1033,128]{1,0:T(8,128)(2,1)S(1)}, u32[]{:S(2)}, u32[]{:S(2)}) collective-permute-start(s16[1033,128]{1,0:T(8,128)(2,1)} %get-tuple-element.29), channel_id=1, source_target_pairs={{8,0},{16,8},{24,16},{32,24},{40,32},{48,40},{56,48},{64,56},{72,6... | collective-permute-start | bytes 793352 | tf_op jit(solution)/shard_map/ppermute | solution.py:12
  92.6 2.4 %fusion.8 = (f32[16,128]{1,0:T(8,128)S(1)}, f32[16,128]{1,0:T(8,128)S(1)}, f32[128,128]{1,0:T(8,128)S(1)}) fusion(f32[128,128]{1,0:T(8,128)S(1)} %fusion.231, f32[16,128]{1,0:T(8,128)S(1)} %reduce_window_sum.30, pred[128,128]{1,0:T(8,128)(4,1)S(1)} %fusion.72, f32[16,128,64]{1,2,0:T(8,128)S(1)} %bitcast.198, f32[16,128,64]{1,2,0:T(8,128)S(1)} %copy-done.1), kind=kOutput, calls=%fused_computation.21 | convolution fusion | flops 203403264 | bytes 1220608 | tf_op jit(solution)/shard_map/hip,hjp->hij/dot_general | solution.py:158
  94.9 0.3 reduce_window_sum.31
  95.2 0.3 reduce_window_sum.32
  95.5 1.3 fusion.6
  96.8 9.1 %collective-permute-start.7 = (s16[1033,128]{1,0:T(8,128)(2,1)}, s16[1033,128]{1,0:T(8,128)(2,1)S(1)}, u32[]{:S(2)}, u32[]{:S(2)}) collective-permute-start(s16[1033,128]{1,0:T(8,128)(2,1)} %get-tuple-element.30), channel_id=1, source_target_pairs={{40,0},{48,8},{56,16},{64,24},{72,32},{80,40},{88,48},{96,56},{104... | collective-permute-start | bytes 793352 | tf_op jit(solution)/shard_map/ppermute | solution.py:12
  105.9 1.9 %collective-permute-start.8 = (s16[1033,128]{1,0:T(8,128)(2,1)}, s16[1033,128]{1,0:T(8,128)(2,1)S(1)}, u32[]{:S(2)}, u32[]{:S(2)}) collective-permute-start(s16[1033,128]{1,0:T(8,128)(2,1)} %get-tuple-element.32), channel_id=1, source_target_pairs={{0,8},{8,16},{16,24},{24,32},{32,40},{40,48},{48,56},{56,64},{64,7... | collective-permute-start | bytes 793352 | tf_op jit(solution)/shard_map/ppermute | solution.py:12
  107.9 8.7 %collective-permute-start.9 = (s16[1033,128]{1,0:T(8,128)(2,1)}, s16[1033,128]{1,0:T(8,128)(2,1)S(1)}, u32[]{:S(2)}, u32[]{:S(2)}) collective-permute-start(s16[1033,128]{1,0:T(8,128)(2,1)} %get-tuple-element.33), channel_id=1, source_target_pairs={{0,40},{8,48},{16,56},{24,64},{32,72},{40,80},{48,88},{56,96},{64,... | collective-permute-start | bytes 793352 | tf_op jit(solution)/shard_map/ppermute | solution.py:12
  116.7 0.9 collective-permute-done.7
  118.2 30.5 %collective-permute-done.9 = s16[1033,128]{1,0:T(8,128)(2,1)S(1)} collective-permute-done((s16[1033,128]{1,0:T(8,128)(2,1)}, s16[1033,128]{1,0:T(8,128)(2,1)S(1)}, u32[]{:S(2)}, u32[]{:S(2)}) %collective-permute-start.9) | collective-permute-done | bytes 264480 | tf_op jit(solution)/shard_map/ppermute | solution.py:12
  148.7 1.8 %multiply_reduce_fusion.1 = (f32[1024]{0:T(1024)S(1)}, f32[1024,128]{1,0:T(8,128)S(1)}, f32[1024,128]{1,0:T(8,128)}) fusion(f32[1024]{0:T(1024)S(1)} %get-tuple-element.83, s16[1033,128]{1,0:T(8,128)(2,1)S(1)} %collective-permute-done.9, f32[1024]{0:T(1024)S(1)} %mul.569, f32[1024]{0:T(1024)S(1)} %get-tuple-element.81, ...), kind=kLoop, calls=%fused_computation.59 | loop fusion | flops 1833984 | bytes 2125824 | tf_op jit(solution)/shard_map/reduce_sum | solution.py:178
  150.5 0.4 fusion.1
  150.9 1.2 fusion.3
  152.5 1.3 convolution_bitcast_fusion.1
  154.1 0.9 copy-done.6
  155.0 1.3 convolution_bitcast_fusion.2
  156.4 0.3 convolution_add_fusion.1
  156.6 0.6 maximum_bitcast_fusion
  157.3 6.6 %all-to-all-start.1 = ((f32[8,2,16,128]{3,2,1,0:T(8,128)}), f32[8,2,16,128]{3,2,1,0:T(8,128)S(1)}, u32[]{:S(2)}, u32[]{:S(2)}) async-start(f32[8,2,16,128]{3,2,1,0:T(8,128)} %maximum_bitcast_fusion), calls=%async_computation.1 | async-start | bytes 262144 | tf_op jit(solution)/shard_map/all_to_all | solution.py:67
  163.9 0.7 copy-done.21
  164.6 0.4 fusion.28
  165.2 1.0 copy.31
  166.2 1.9 %fusion.2 = f32[16,1,128]{2,1,0:T(1,128)S(1)} fusion(f32[16,128,1]{1,2,0:T(1,128)S(1)} %bitcast.237, f32[16,128]{1,0:T(8,128)S(1)} %reduce_window_sum.30, pred[128,128]{1,0:T(8,128)(4,1)S(1)} %fusion.72), kind=kOutput, calls=%fused_computation.9 | convolution fusion | flops 3670016 | bytes 40960 | tf_op jit(solution)/shard_map/hij,hj->hi/dot_general | solution.py:175
  168.1 0.7 copy-done.20
  168.7 0.7 multiply_subtract_fusion
  169.4 0.6 slice_bitcast_fusion
  (145 shorter events, 6.2 us)
Async XLA Ops:
  0.6 10.7 %copy-start.9 = (bf16[128,1024]{1,0:T(8,128)(2,1)S(1)}, bf16[128,1024]{1,0:T(8,128)(2,1)}, u32[]{:S(2)}) copy-start(bf16[128,1024]{1,0:T(8,128)(2,1)} %param.8) | copy-start | bytes 786436
  2.0 10.6 %all-to-all-start = ((bf16[8,2,16,128]{3,2,1,0:T(8,128)(2,1)}), bf16[8,2,16,128]{3,2,1,0:T(8,128)(2,1)S(1)}, u32[]{:S(2)}, u32[]{:S(2)}) async-start(bf16[8,2,16,128]{3,2,1,0:T(8,128)(2,1)} %broadcast_in_dim.28), calls=%async_computation | async-start | bytes 131072 | tf_op jit(solution)/shard_map/all_to_all | solution.py:92
  8.1 0.7 copy-start.12
  8.7 2.0 %copy-start.11 = (f32[16,128]{1,0:T(8,128)S(1)}, f32[16,128]{1,0:T(8,128)}, u32[]{:S(2)}) copy-start(f32[16,128]{1,0:T(8,128)} %param.10) | copy-start | bytes 24580
  10.1 0.7 copy-start.19
  11.5 1.0 copy-start.10
  11.5 1.6 copy-start
  14.3 9.5 %collective-permute-start = (s16[1033,128]{1,0:T(8,128)(2,1)S(1)}, s16[1033,128]{1,0:T(8,128)(2,1)S(1)}, u32[]{:S(2)}, u32[]{:S(2)}) collective-permute-start(s16[1033,128]{1,0:T(8,128)(2,1)S(1)} %get-tuple-element.19), channel_id=1, source_target_pairs={{0,8},{8,16},{16,24},{24,32},{32,40},{40,48},{48,56},{56,64},{64,7... | collective-permute-start | bytes 793352 | tf_op jit(solution)/shard_map/ppermute | solution.py:12
  17.8 10.9 %collective-permute-start.1 = (s16[1033,128]{1,0:T(8,128)(2,1)S(1)}, s16[1033,128]{1,0:T(8,128)(2,1)S(1)}, u32[]{:S(2)}, u32[]{:S(2)}) collective-permute-start(s16[1033,128]{1,0:T(8,128)(2,1)S(1)} %get-tuple-element.20), channel_id=1, source_target_pairs={{8,0},{16,8},{24,16},{32,24},{40,32},{48,40},{56,48},{64,56},{72,6... | collective-permute-start | bytes 793352 | tf_op jit(solution)/shard_map/ppermute | solution.py:12
  28.7 2.3 %copy-start.2 = (s16[1033,128]{1,0:T(8,128)(2,1)}, s16[1033,128]{1,0:T(8,128)(2,1)S(1)}, u32[]{:S(2)}) copy-start(s16[1033,128]{1,0:T(8,128)(2,1)S(1)} %collective-permute-done.1) | copy-start | bytes 793348
  30.3 0.5 copy-start.15
  30.3 0.6 copy-start.17
  31.8 11.1 %collective-permute-start.2 = (s16[1033,128]{1,0:T(8,128)(2,1)S(1)}, s16[1033,128]{1,0:T(8,128)(2,1)S(1)}, u32[]{:S(2)}, u32[]{:S(2)}) collective-permute-start(s16[1033,128]{1,0:T(8,128)(2,1)S(1)} %get-tuple-element.21), channel_id=1, source_target_pairs={{0,16},{8,24},{16,32},{24,40},{32,48},{40,56},{48,64},{56,72},{64,... | collective-permute-start | bytes 793352 | tf_op jit(solution)/shard_map/ppermute | solution.py:12
  36.6 11.6 %collective-permute-start.3 = (s16[1033,128]{1,0:T(8,128)(2,1)S(1)}, s16[1033,128]{1,0:T(8,128)(2,1)S(1)}, u32[]{:S(2)}, u32[]{:S(2)}) collective-permute-start(s16[1033,128]{1,0:T(8,128)(2,1)S(1)} %get-tuple-element.22), channel_id=1, source_target_pairs={{16,0},{24,8},{32,16},{40,24},{48,32},{56,40},{64,48},{72,56},{80,... | collective-permute-start | bytes 793352 | tf_op jit(solution)/shard_map/ppermute | solution.py:12
  42.9 5.4 %copy-start.8 = (s16[1033,128]{1,0:T(8,128)(2,1)}, s16[1033,128]{1,0:T(8,128)(2,1)S(1)}, u32[]{:S(2)}) copy-start(s16[1033,128]{1,0:T(8,128)(2,1)S(1)} %collective-permute-done.2) | copy-start | bytes 793348
  48.2 0.7 copy-start.7
  48.9 1.0 copy-start.3
  48.9 0.9 copy-start.13
  48.9 0.9 copy-start.14
  51.2 0.7 copy-start.18
  52.0 0.7 copy-start.16
  54.1 15.3 %collective-permute-start.4 = (s16[1033,128]{1,0:T(8,128)(2,1)}, s16[1033,128]{1,0:T(8,128)(2,1)S(1)}, u32[]{:S(2)}, u32[]{:S(2)}) collective-permute-start(s16[1033,128]{1,0:T(8,128)(2,1)} %get-tuple-element.32), channel_id=1, source_target_pairs={{0,32},{8,40},{16,48},{24,56},{32,64},{40,72},{48,80},{56,88},{64,... | collective-permute-start | bytes 793352 | tf_op jit(solution)/shard_map/ppermute | solution.py:12
  61.7 13.9 %collective-permute-start.5 = (s16[1033,128]{1,0:T(8,128)(2,1)}, s16[1033,128]{1,0:T(8,128)(2,1)S(1)}, u32[]{:S(2)}, u32[]{:S(2)}) collective-permute-start(s16[1033,128]{1,0:T(8,128)(2,1)} %get-tuple-element.29), channel_id=1, source_target_pairs={{32,0},{40,8},{48,16},{56,24},{64,32},{72,40},{80,48},{88,56},{96,... | collective-permute-start | bytes 793352 | tf_op jit(solution)/shard_map/ppermute | solution.py:12
  77.3 15.3 %copy-start.1 = (f32[16,128,64]{1,2,0:T(8,128)S(1)}, f32[16,128,64]{1,2,0:T(8,128)}, u32[]{:S(2)}) copy-start(f32[16,128,64]{1,2,0:T(8,128)} %copy-done) | copy-start | bytes 1572868
  78.2 38.4 %collective-permute-start.6 = (s16[1033,128]{1,0:T(8,128)(2,1)}, s16[1033,128]{1,0:T(8,128)(2,1)S(1)}, u32[]{:S(2)}, u32[]{:S(2)}) collective-permute-start(s16[1033,128]{1,0:T(8,128)(2,1)} %get-tuple-element.29), channel_id=1, source_target_pairs={{8,0},{16,8},{24,16},{32,24},{40,32},{48,40},{56,48},{64,56},{72,6... | collective-permute-start | bytes 793352 | tf_op jit(solution)/shard_map/ppermute | solution.py:12
  96.8 20.8 %collective-permute-start.7 = (s16[1033,128]{1,0:T(8,128)(2,1)}, s16[1033,128]{1,0:T(8,128)(2,1)S(1)}, u32[]{:S(2)}, u32[]{:S(2)}) collective-permute-start(s16[1033,128]{1,0:T(8,128)(2,1)} %get-tuple-element.30), channel_id=1, source_target_pairs={{40,0},{48,8},{56,16},{64,24},{72,32},{80,40},{88,48},{96,56},{104... | collective-permute-start | bytes 793352 | tf_op jit(solution)/shard_map/ppermute | solution.py:12
  105.9 11.6 %collective-permute-start.8 = (s16[1033,128]{1,0:T(8,128)(2,1)}, s16[1033,128]{1,0:T(8,128)(2,1)S(1)}, u32[]{:S(2)}, u32[]{:S(2)}) collective-permute-start(s16[1033,128]{1,0:T(8,128)(2,1)} %get-tuple-element.32), channel_id=1, source_target_pairs={{0,8},{8,16},{16,24},{24,32},{32,40},{40,48},{48,56},{56,64},{64,7... | collective-permute-start | bytes 793352 | tf_op jit(solution)/shard_map/ppermute | solution.py:12
  107.9 40.8 %collective-permute-start.9 = (s16[1033,128]{1,0:T(8,128)(2,1)}, s16[1033,128]{1,0:T(8,128)(2,1)S(1)}, u32[]{:S(2)}, u32[]{:S(2)}) collective-permute-start(s16[1033,128]{1,0:T(8,128)(2,1)} %get-tuple-element.33), channel_id=1, source_target_pairs={{0,40},{8,48},{16,56},{24,64},{32,72},{40,80},{48,88},{56,96},{64,... | collective-permute-start | bytes 793352 | tf_op jit(solution)/shard_map/ppermute | solution.py:12
  117.6 33.0 %copy-start.5 = (s16[1033,128]{1,0:T(8,128)(2,1)}, s16[1033,128]{1,0:T(8,128)(2,1)S(1)}, u32[]{:S(2)}) copy-start(s16[1033,128]{1,0:T(8,128)(2,1)S(1)} %collective-permute-done.7) | copy-start | bytes 793348
  154.0 1.0 copy-start.6
  156.4 7.6 %copy-start.4 = (f32[1024,128]{1,0:T(8,128)S(1)}, f32[1024,128]{1,0:T(8,128)}, u32[]{:S(2)}) copy-start(f32[1024,128]{1,0:T(8,128)} %get-tuple-element.59) | copy-start | bytes 1572868
  157.3 12.1 %all-to-all-start.1 = ((f32[8,2,16,128]{3,2,1,0:T(8,128)}), f32[8,2,16,128]{3,2,1,0:T(8,128)S(1)}, u32[]{:S(2)}, u32[]{:S(2)}) async-start(f32[8,2,16,128]{3,2,1,0:T(8,128)} %maximum_bitcast_fusion), calls=%async_computation.1 | async-start | bytes 262144 | tf_op jit(solution)/shard_map/all_to_all | solution.py:67
  163.9 0.7 copy-start.21
  168.1 0.7 copy-start.20

commit v15 on v11

--- a/solution.py
+++ b/solution.py
@@ -166,9 +166,12 @@
 
     b_adj = jnp.einsum("ln,hpn->hlp", bmat, g_in, precision=HIGH)
     c_state = jnp.einsum("ln,hpn->hlp", cmat, s_in, precision=HIGH)
-    core = core_loc + leave[:, :, None] * b_adj
-    gx = step_size[:, :, None] * core + skip_gain[:, None, None] * dys
-    along = jnp.sum(xs * core, axis=2)
+    b_adj_t = jnp.einsum("ln,hpn->lhp", bmat, g_in, precision=HIGH)
+    core_t = core_loc.transpose(1, 0, 2) + leave.T[:, :, None] * b_adj_t
+    dys_t = grads.astype(jnp.float32).reshape(length, heads, width)
+    xs_t = inputs.astype(jnp.float32).reshape(length, heads, width)
+    gx_t = step_size.T[:, :, None] * core_t + skip_gain[None, :, None] * dys_t
+    along = jnp.sum(xs_t * core_t, axis=2).T
     from_state = enter * jnp.einsum(
         "hij,hi->hj", weights, jnp.sum(dys * c_state, axis=2), precision=HIGH
     )
@@ -180,7 +183,7 @@
     gb = gb_loc + jnp.einsum("hlp,hpn->ln", left_u, g_in, precision=HIGH)
     gc = gc_loc + jnp.einsum("hlp,hpn->ln", enter_dy, s_in, precision=HIGH)
 
-    grad_x = gx.transpose(1, 0, 2).reshape(length, heads * width)
+    grad_x = gx_t.reshape(length, heads * width)
     grad_bc = scatter_sum(jnp.stack([gb, gc]), "tensor")
     return (grad_x, grad_step, grad_bc[0], grad_bc[1])
 

time: 171 us -> 174 us (1.018)
  the two profiles are of different devices: /device:TPU:75 before, /device:TPU:66 now
where the time goes in v15:
time: 174 us
  waiting for transfers between devices  71.7 us (41%)
  starting transfers between devices  60.9 us (35%)
  other arithmetic  15.4 us (9%)
  matrix products  12.1 us (7%)
  local copies, waits for them, and re-layouts  11.6 us (7%)
  between operations  1.96 us (1%)
    ppermute x10, waiting for transfers between devices, from_behind(): return lax.ppermute(x, axis, pairs)  66.8 us
    ppermute x10, starting transfers between devices, from_behind(): return lax.ppermute(x, axis, pairs)  52.8 us
    unnamed x43, local copies, waits for them, and re-layouts  6.85 us
    all_to_all x1, waiting for transfers between devices, scatter_sum(): got = lax.all_to_all(parts, axis, 0, 0, tiled=True)  4.81 us
    all_to_all x1, starting transfers between devices, local(): lax.all_to_all(jnp.broadcast_to(piece, (count,) + piece.shape), 'tensor',...  4.47 us
    all_to_all x1, starting transfers between devices, scatter_sum(): got = lax.all_to_all(parts, axis, 0, 0, tiled=True)  3.65 us
  transfers between devices with their start and end apart: 12, of which 10 were waited for; matrix products, arithmetic and copies ran while one was open for 5% of the time, Pallas kernels for 0%

profile of v15, /device:TPU:66, one launch (start us, length us, event | category | flops | bytes accessed | tf_op | source)
XLA Modules:
  0.0 173.7 jit_solution(4370922824881151974)
XLA Ops:
  0.6 0.7 pad_maximum_fusion
  1.4 0.6 broadcast_in_dim.28
  2.0 4.5 %all-to-all-start = ((bf16[8,2,16,128]{3,2,1,0:T(8,128)(2,1)}), bf16[8,2,16,128]{3,2,1,0:T(8,128)(2,1)S(1)}, u32[]{:S(2)}, u32[]{:S(2)}) async-start(bf16[8,2,16,128]{3,2,1,0:T(8,128)(2,1)} %broadcast_in_dim.28), calls=%async_computation | async-start | bytes 131072 | tf_op jit(solution)/shard_map/all_to_all | solution.py:92
  6.5 0.7 copy.26
  7.4 0.5 copy-done.11
  8.1 0.6 slice.172
  9.4 0.7 compare_convert_fusion
  10.1 0.3 reduce_window_sum.30
  10.8 0.7 copy-done
  12.1 0.5 abs_reduce_fusion.6
  12.7 0.5 abs_reduce_fusion.7
  13.8 3.8 %collective-permute-start = (s16[1033,128]{1,0:T(8,128)(2,1)S(1)}, s16[1033,128]{1,0:T(8,128)(2,1)S(1)}, u32[]{:S(2)}, u32[]{:S(2)}) collective-permute-start(s16[1033,128]{1,0:T(8,128)(2,1)S(1)} %get-tuple-element.19), channel_id=1, source_target_pairs={{0,8},{8,16},{16,24},{24,32},{32,40},{40,48},{48,56},{56,64},{64,7... | collective-permute-start | bytes 793352 | tf_op jit(solution)/shard_map/ppermute | solution.py:12
  17.6 2.0 %collective-permute-start.1 = (s16[1033,128]{1,0:T(8,128)(2,1)S(1)}, s16[1033,128]{1,0:T(8,128)(2,1)S(1)}, u32[]{:S(2)}, u32[]{:S(2)}) collective-permute-start(s16[1033,128]{1,0:T(8,128)(2,1)S(1)} %get-tuple-element.20), channel_id=1, source_target_pairs={{8,0},{16,8},{24,16},{32,24},{40,32},{48,40},{56,48},{64,56},{72,6... | collective-permute-start | bytes 793352 | tf_op jit(solution)/shard_map/ppermute | solution.py:12
  19.6 4.8 %collective-permute-done = s16[1033,128]{1,0:T(8,128)(2,1)S(1)} collective-permute-done((s16[1033,128]{1,0:T(8,128)(2,1)S(1)}, s16[1033,128]{1,0:T(8,128)(2,1)S(1)}, u32[]{:S(2)}, u32[]{:S(2)}) %collective-permute-start) | collective-permute-done | bytes 264480 | tf_op jit(solution)/shard_map/ppermute | solution.py:12
  24.5 4.9 %collective-permute-done.1 = s16[1033,128]{1,0:T(8,128)(2,1)S(1)} collective-permute-done((s16[1033,128]{1,0:T(8,128)(2,1)S(1)}, s16[1033,128]{1,0:T(8,128)(2,1)S(1)}, u32[]{:S(2)}, u32[]{:S(2)}) %collective-permute-start.1) | collective-permute-done | bytes 264480 | tf_op jit(solution)/shard_map/ppermute | solution.py:12
  29.5 0.7 abs_reduce_fusion.4
  30.4 0.6 fusion.221
  31.0 0.5 copy-done.14
  31.6 0.7 clamp_convert_fusion.4
  32.5 5.2 %collective-permute-start.2 = (s16[1033,128]{1,0:T(8,128)(2,1)S(1)}, s16[1033,128]{1,0:T(8,128)(2,1)S(1)}, u32[]{:S(2)}, u32[]{:S(2)}) collective-permute-start(s16[1033,128]{1,0:T(8,128)(2,1)S(1)} %get-tuple-element.21), channel_id=1, source_target_pairs={{0,16},{8,24},{16,32},{24,40},{32,48},{40,56},{48,64},{56,72},{64,... | collective-permute-start | bytes 793352 | tf_op jit(solution)/shard_map/ppermute | solution.py:12
  37.6 2.3 %collective-permute-start.3 = (s16[1033,128]{1,0:T(8,128)(2,1)S(1)}, s16[1033,128]{1,0:T(8,128)(2,1)S(1)}, u32[]{:S(2)}, u32[]{:S(2)}) collective-permute-start(s16[1033,128]{1,0:T(8,128)(2,1)S(1)} %get-tuple-element.22), channel_id=1, source_target_pairs={{16,0},{24,8},{32,16},{40,24},{48,32},{56,40},{64,48},{72,56},{80,... | collective-permute-start | bytes 793352 | tf_op jit(solution)/shard_map/ppermute | solution.py:12
  39.9 4.6 %collective-permute-done.2 = s16[1033,128]{1,0:T(8,128)(2,1)S(1)} collective-permute-done((s16[1033,128]{1,0:T(8,128)(2,1)S(1)}, s16[1033,128]{1,0:T(8,128)(2,1)S(1)}, u32[]{:S(2)}, u32[]{:S(2)}) %collective-permute-start.2) | collective-permute-done | bytes 264480 | tf_op jit(solution)/shard_map/ppermute | solution.py:12
  44.6 6.2 %collective-permute-done.3 = s16[1033,128]{1,0:T(8,128)(2,1)S(1)} collective-permute-done((s16[1033,128]{1,0:T(8,128)(2,1)S(1)}, s16[1033,128]{1,0:T(8,128)(2,1)S(1)}, u32[]{:S(2)}, u32[]{:S(2)}) %collective-permute-start.3) | collective-permute-done | bytes 264480 | tf_op jit(solution)/shard_map/ppermute | solution.py:12
  50.9 0.6 copy-done.6
  51.5 0.9 copy-done.3
  52.4 0.8 fusion.17
  53.8 0.7 slice_convert_fusion.9
  54.6 0.7 slice_convert_fusion.8
  55.9 0.8 fusion.54
  56.7 11.9 %collective-permute-start.4 = (s16[1033,128]{1,0:T(8,128)(2,1)S(1)}, s16[1033,128]{1,0:T(8,128)(2,1)S(1)}, u32[]{:S(2)}, u32[]{:S(2)}) collective-permute-start(s16[1033,128]{1,0:T(8,128)(2,1)S(1)} %get-tuple-element.32), channel_id=1, source_target_pairs={{0,32},{8,40},{16,48},{24,56},{32,64},{40,72},{48,80},{56,88},{64,... | collective-permute-start | bytes 793352 | tf_op jit(solution)/shard_map/ppermute | solution.py:12
  68.7 1.9 %collective-permute-start.5 = (s16[1033,128]{1,0:T(8,128)(2,1)}, s16[1033,128]{1,0:T(8,128)(2,1)S(1)}, u32[]{:S(2)}, u32[]{:S(2)}) collective-permute-start(s16[1033,128]{1,0:T(8,128)(2,1)} %get-tuple-element.29), channel_id=1, source_target_pairs={{32,0},{40,8},{48,16},{56,24},{64,32},{72,40},{80,48},{88,56},{96,... | collective-permute-start | bytes 793352 | tf_op jit(solution)/shard_map/ppermute | solution.py:12
  70.6 12.1 %collective-permute-done.4 = s16[1033,128]{1,0:T(8,128)(2,1)S(1)} collective-permute-done((s16[1033,128]{1,0:T(8,128)(2,1)S(1)}, s16[1033,128]{1,0:T(8,128)(2,1)S(1)}, u32[]{:S(2)}, u32[]{:S(2)}) %collective-permute-start.4) | collective-permute-done | bytes 264480 | tf_op jit(solution)/shard_map/ppermute | solution.py:12
  82.9 0.4 abs_reduce_fusion.1
  83.4 2.2 %collective-permute-done.5 = s16[1033,128]{1,0:T(8,128)(2,1)S(1)} collective-permute-done((s16[1033,128]{1,0:T(8,128)(2,1)}, s16[1033,128]{1,0:T(8,128)(2,1)S(1)}, u32[]{:S(2)}, u32[]{:S(2)}) %collective-permute-start.5) | collective-permute-done | bytes 264480 | tf_op jit(solution)/shard_map/ppermute | solution.py:12
  85.7 0.4 abs_reduce_fusion
  86.4 0.4 clamp_convert_fusion.1
  86.8 0.4 clamp_convert_fusion
  87.2 0.8 fusion.56
  87.9 6.4 %collective-permute-start.6 = (s16[1033,128]{1,0:T(8,128)(2,1)}, s16[1033,128]{1,0:T(8,128)(2,1)S(1)}, u32[]{:S(2)}, u32[]{:S(2)}) collective-permute-start(s16[1033,128]{1,0:T(8,128)(2,1)} %get-tuple-element.29), channel_id=1, source_target_pairs={{8,0},{16,8},{24,16},{32,24},{40,32},{48,40},{56,48},{64,56},{72,6... | collective-permute-start | bytes 793352 | tf_op jit(solution)/shard_map/ppermute | solution.py:12
  94.5 2.4 %fusion.10 = (f32[16,128]{1,0:T(8,128)S(1)}, f32[16,128]{1,0:T(8,128)S(1)}, f32[128,128]{1,0:T(8,128)S(1)}) fusion(f32[128,128]{1,0:T(8,128)S(1)} %fusion.227, f32[16,128]{1,0:T(8,128)S(1)} %reduce_window_sum.30, pred[128,128]{1,0:T(8,128)(4,1)S(1)} %fusion.67, f32[16,128,64]{1,2,0:T(8,128)S(1)} %bitcast.192, f32[16,128,64]{1,2,0:T(8,128)S(1)} %broadcast_multiply_fusion), kind=kOutput, calls=%fused_computation.26 | convolution fusion | flops 203403264 | bytes 1220608 | tf_op jit(solution)/shard_map/hip,hjp->hij/dot_general | solution.py:158
  96.9 0.3 reduce_window_sum.31
  97.4 8.5 %collective-permute-start.7 = (s16[1033,128]{1,0:T(8,128)(2,1)}, s16[1033,128]{1,0:T(8,128)(2,1)S(1)}, u32[]{:S(2)}, u32[]{:S(2)}) collective-permute-start(s16[1033,128]{1,0:T(8,128)(2,1)} %get-tuple-element.30), channel_id=1, source_target_pairs={{40,0},{48,8},{56,16},{64,24},{72,32},{80,40},{88,48},{96,56},{104... | collective-permute-start | bytes 793352 | tf_op jit(solution)/shard_map/ppermute | solution.py:12
  106.0 1.9 %collective-permute-start.8 = (s16[1033,128]{1,0:T(8,128)(2,1)S(1)}, s16[1033,128]{1,0:T(8,128)(2,1)S(1)}, u32[]{:S(2)}, u32[]{:S(2)}) collective-permute-start(s16[1033,128]{1,0:T(8,128)(2,1)S(1)} %get-tuple-element.32), channel_id=1, source_target_pairs={{0,8},{8,16},{16,24},{24,32},{32,40},{40,48},{48,56},{56,64},{64,7... | collective-permute-start | bytes 793352 | tf_op jit(solution)/shard_map/ppermute | solution.py:12
  107.9 8.8 %collective-permute-start.9 = (s16[1033,128]{1,0:T(8,128)(2,1)S(1)}, s16[1033,128]{1,0:T(8,128)(2,1)S(1)}, u32[]{:S(2)}, u32[]{:S(2)}) collective-permute-start(s16[1033,128]{1,0:T(8,128)(2,1)S(1)} %get-tuple-element.33), channel_id=1, source_target_pairs={{0,40},{8,48},{16,56},{24,64},{32,72},{40,80},{48,88},{56,96},{64,... | collective-permute-start | bytes 793352 | tf_op jit(solution)/shard_map/ppermute | solution.py:12
  116.8 3.4 %collective-permute-done.7 = s16[1033,128]{1,0:T(8,128)(2,1)S(1)} collective-permute-done((s16[1033,128]{1,0:T(8,128)(2,1)}, s16[1033,128]{1,0:T(8,128)(2,1)S(1)}, u32[]{:S(2)}, u32[]{:S(2)}) %collective-permute-start.7) | collective-permute-done | bytes 264480 | tf_op jit(solution)/shard_map/ppermute | solution.py:12
  120.8 28.7 %collective-permute-done.9 = s16[1033,128]{1,0:T(8,128)(2,1)S(1)} collective-permute-done((s16[1033,128]{1,0:T(8,128)(2,1)S(1)}, s16[1033,128]{1,0:T(8,128)(2,1)S(1)}, u32[]{:S(2)}, u32[]{:S(2)}) %collective-permute-start.9) | collective-permute-done | bytes 264480 | tf_op jit(solution)/shard_map/ppermute | solution.py:12
  149.6 1.2 multiply_reduce_fusion.1
  150.8 0.4 fusion.4
  151.2 1.2 fusion.6
  152.6 0.4 fusion.3
  153.0 0.4 convolution_multiply_fusion
  153.4 0.6 copy-done.1
  154.1 1.3 multiply_reduce_fusion.2
  155.4 1.0 copy.31
  156.4 1.9 %fusion.5 = f32[16,1,128]{2,1,0:T(1,128)S(1)} fusion(f32[16,128,1]{1,2,0:T(1,128)S(1)} %bitcast.233, f32[16,128]{1,0:T(8,128)S(1)} %reduce_window_sum.30, pred[128,128]{1,0:T(8,128)(4,1)S(1)} %fusion.67), kind=kOutput, calls=%fused_computation.15 | convolution fusion | flops 3670016 | bytes 40960 | tf_op jit(solution)/shard_map/hij,hj->hi/dot_general | solution.py:178
  158.4 0.9 copy-done.5
  159.3 1.3 convolution_bitcast_fusion.3
  161.0 1.3 convolution_bitcast_fusion.4
  162.6 0.6 maximum_bitcast_fusion
  163.2 3.7 %all-to-all-start.1 = ((f32[8,2,16,128]{3,2,1,0:T(8,128)}), f32[8,2,16,128]{3,2,1,0:T(8,128)S(1)}, u32[]{:S(2)}, u32[]{:S(2)}) async-start(f32[8,2,16,128]{3,2,1,0:T(8,128)} %maximum_bitcast_fusion), calls=%async_computation.1 | async-start | bytes 262144 | tf_op jit(solution)/shard_map/all_to_all | solution.py:67
  166.9 0.7 copy-done.19
  167.6 0.7 fusion.124
  168.2 4.8 %all-to-all-done.1 = f32[8,2,16,128]{3,2,1,0:T(8,128)S(1)} async-done(((f32[8,2,16,128]{3,2,1,0:T(8,128)}), f32[8,2,16,128]{3,2,1,0:T(8,128)S(1)}, u32[]{:S(2)}, u32[]{:S(2)}) %all-to-all-start.1) | async-done | bytes 131104 | tf_op jit(solution)/shard_map/all_to_all | solution.py:67
  173.1 0.6 slice_bitcast_fusion
  (143 shorter events, 6.9 us)
Async XLA Ops:
  0.6 10.0 %copy-start.8 = (bf16[128,1024]{1,0:T(8,128)(2,1)S(1)}, bf16[128,1024]{1,0:T(8,128)(2,1)}, u32[]{:S(2)}) copy-start(bf16[128,1024]{1,0:T(8,128)(2,1)} %param.8) | copy-start | bytes 786436
  2.0 10.1 %all-to-all-start = ((bf16[8,2,16,128]{3,2,1,0:T(8,128)(2,1)}), bf16[8,2,16,128]{3,2,1,0:T(8,128)(2,1)S(1)}, u32[]{:S(2)}, u32[]{:S(2)}) async-start(bf16[8,2,16,128]{3,2,1,0:T(8,128)(2,1)} %broadcast_in_dim.28), calls=%async_computation | async-start | bytes 131072 | tf_op jit(solution)/shard_map/all_to_all | solution.py:92
  7.3 0.7 copy-start.11
  8.0 2.0 %copy-start.10 = (f32[16,128]{1,0:T(8,128)S(1)}, f32[16,128]{1,0:T(8,128)}, u32[]{:S(2)}) copy-start(f32[16,128]{1,0:T(8,128)} %param.10) | copy-start | bytes 24580
  9.3 0.7 copy-start.18
  10.7 0.8 copy-start
  10.7 1.1 copy-start.9
  13.8 10.6 %collective-permute-start = (s16[1033,128]{1,0:T(8,128)(2,1)S(1)}, s16[1033,128]{1,0:T(8,128)(2,1)S(1)}, u32[]{:S(2)}, u32[]{:S(2)}) collective-permute-start(s16[1033,128]{1,0:T(8,128)(2,1)S(1)} %get-tuple-element.19), channel_id=1, source_target_pairs={{0,8},{8,16},{16,24},{24,32},{32,40},{40,48},{48,56},{56,64},{64,7... | collective-permute-start | bytes 793352 | tf_op jit(solution)/shard_map/ppermute | solution.py:12
  17.6 11.8 %collective-permute-start.1 = (s16[1033,128]{1,0:T(8,128)(2,1)S(1)}, s16[1033,128]{1,0:T(8,128)(2,1)S(1)}, u32[]{:S(2)}, u32[]{:S(2)}) collective-permute-start(s16[1033,128]{1,0:T(8,128)(2,1)S(1)} %get-tuple-element.20), channel_id=1, source_target_pairs={{8,0},{16,8},{24,16},{32,24},{40,32},{48,40},{56,48},{64,56},{72,6... | collective-permute-start | bytes 793352 | tf_op jit(solution)/shard_map/ppermute | solution.py:12
  29.4 2.3 %copy-start.2 = (s16[1033,128]{1,0:T(8,128)(2,1)}, s16[1033,128]{1,0:T(8,128)(2,1)S(1)}, u32[]{:S(2)}) copy-start(s16[1033,128]{1,0:T(8,128)(2,1)S(1)} %collective-permute-done.1) | copy-start | bytes 793348
  31.0 0.5 copy-start.14
  31.0 0.6 copy-start.16
  32.5 12.0 %collective-permute-start.2 = (s16[1033,128]{1,0:T(8,128)(2,1)S(1)}, s16[1033,128]{1,0:T(8,128)(2,1)S(1)}, u32[]{:S(2)}, u32[]{:S(2)}) collective-permute-start(s16[1033,128]{1,0:T(8,128)(2,1)S(1)} %get-tuple-element.21), channel_id=1, source_target_pairs={{0,16},{8,24},{16,32},{24,40},{32,48},{40,56},{48,64},{56,72},{64,... | collective-permute-start | bytes 793352 | tf_op jit(solution)/shard_map/ppermute | solution.py:12
  37.6 13.1 %collective-permute-start.3 = (s16[1033,128]{1,0:T(8,128)(2,1)S(1)}, s16[1033,128]{1,0:T(8,128)(2,1)S(1)}, u32[]{:S(2)}, u32[]{:S(2)}) collective-permute-start(s16[1033,128]{1,0:T(8,128)(2,1)S(1)} %get-tuple-element.22), channel_id=1, source_target_pairs={{16,0},{24,8},{32,16},{40,24},{48,32},{56,40},{64,48},{72,56},{80,... | collective-permute-start | bytes 793352 | tf_op jit(solution)/shard_map/ppermute | solution.py:12
  44.5 6.4 %copy-start.7 = (s16[1033,128]{1,0:T(8,128)(2,1)}, s16[1033,128]{1,0:T(8,128)(2,1)S(1)}, u32[]{:S(2)}) copy-start(s16[1033,128]{1,0:T(8,128)(2,1)S(1)} %collective-permute-done.2) | copy-start | bytes 793348
  50.8 0.7 copy-start.6
  51.5 1.0 copy-start.3
  51.5 0.9 copy-start.12
  51.5 0.9 copy-start.13
  53.8 0.7 copy-start.17
  54.6 0.7 copy-start.15
  56.7 26.1 %collective-permute-start.4 = (s16[1033,128]{1,0:T(8,128)(2,1)S(1)}, s16[1033,128]{1,0:T(8,128)(2,1)S(1)}, u32[]{:S(2)}, u32[]{:S(2)}) collective-permute-start(s16[1033,128]{1,0:T(8,128)(2,1)S(1)} %get-tuple-element.32), channel_id=1, source_target_pairs={{0,32},{8,40},{16,48},{24,56},{32,64},{40,72},{48,80},{56,88},{64,... | collective-permute-start | bytes 793352 | tf_op jit(solution)/shard_map/ppermute | solution.py:12
  68.7 16.9 %collective-permute-start.5 = (s16[1033,128]{1,0:T(8,128)(2,1)}, s16[1033,128]{1,0:T(8,128)(2,1)S(1)}, u32[]{:S(2)}, u32[]{:S(2)}) collective-permute-start(s16[1033,128]{1,0:T(8,128)(2,1)} %get-tuple-element.29), channel_id=1, source_target_pairs={{32,0},{40,8},{48,16},{56,24},{64,32},{72,40},{80,48},{88,56},{96,... | collective-permute-start | bytes 793352 | tf_op jit(solution)/shard_map/ppermute | solution.py:12
  87.9 28.8 %collective-permute-start.6 = (s16[1033,128]{1,0:T(8,128)(2,1)}, s16[1033,128]{1,0:T(8,128)(2,1)S(1)}, u32[]{:S(2)}, u32[]{:S(2)}) collective-permute-start(s16[1033,128]{1,0:T(8,128)(2,1)} %get-tuple-element.29), channel_id=1, source_target_pairs={{8,0},{16,8},{24,16},{32,24},{40,32},{48,40},{56,48},{64,56},{72,6... | collective-permute-start | bytes 793352 | tf_op jit(solution)/shard_map/ppermute | solution.py:12
  97.4 22.7 %collective-permute-start.7 = (s16[1033,128]{1,0:T(8,128)(2,1)}, s16[1033,128]{1,0:T(8,128)(2,1)S(1)}, u32[]{:S(2)}, u32[]{:S(2)}) collective-permute-start(s16[1033,128]{1,0:T(8,128)(2,1)} %get-tuple-element.30), channel_id=1, source_target_pairs={{40,0},{48,8},{56,16},{64,24},{72,32},{80,40},{88,48},{96,56},{104... | collective-permute-start | bytes 793352 | tf_op jit(solution)/shard_map/ppermute | solution.py:12
  106.0 14.2 %collective-permute-start.8 = (s16[1033,128]{1,0:T(8,128)(2,1)S(1)}, s16[1033,128]{1,0:T(8,128)(2,1)S(1)}, u32[]{:S(2)}, u32[]{:S(2)}) collective-permute-start(s16[1033,128]{1,0:T(8,128)(2,1)S(1)} %get-tuple-element.32), channel_id=1, source_target_pairs={{0,8},{8,16},{16,24},{24,32},{32,40},{40,48},{48,56},{56,64},{64,7... | collective-permute-start | bytes 793352 | tf_op jit(solution)/shard_map/ppermute | solution.py:12
  107.9 41.6 %collective-permute-start.9 = (s16[1033,128]{1,0:T(8,128)(2,1)S(1)}, s16[1033,128]{1,0:T(8,128)(2,1)S(1)}, u32[]{:S(2)}, u32[]{:S(2)}) collective-permute-start(s16[1033,128]{1,0:T(8,128)(2,1)S(1)} %get-tuple-element.33), channel_id=1, source_target_pairs={{0,40},{8,48},{16,56},{24,64},{32,72},{40,80},{48,88},{56,96},{64,... | collective-permute-start | bytes 793352 | tf_op jit(solution)/shard_map/ppermute | solution.py:12
  120.2 30.6 %copy-start.4 = (s16[1033,128]{1,0:T(8,128)(2,1)}, s16[1033,128]{1,0:T(8,128)(2,1)S(1)}, u32[]{:S(2)}) copy-start(s16[1033,128]{1,0:T(8,128)(2,1)S(1)} %collective-permute-done.8) | copy-start | bytes 793348
  153.0 1.0 copy-start.1
  153.4 0.7 copy-start.20
  158.3 1.0 copy-start.5
  163.2 9.8 %all-to-all-start.1 = ((f32[8,2,16,128]{3,2,1,0:T(8,128)}), f32[8,2,16,128]{3,2,1,0:T(8,128)S(1)}, u32[]{:S(2)}, u32[]{:S(2)}) async-start(f32[8,2,16,128]{3,2,1,0:T(8,128)} %maximum_bitcast_fusion), calls=%async_computation.1 | async-start | bytes 262144 | tf_op jit(solution)/shard_map/all_to_all | solution.py:67
  166.9 0.7 copy-start.19

commit v16 on v11

--- a/solution.py
+++ b/solution.py
@@ -111,8 +111,8 @@
     moved = step_size[:, :, None] * xs
     left_u = leave[:, :, None] * moved
     enter_dy = enter[:, :, None] * dys
-    local_state = jnp.einsum("hlp,ln->hpn", left_u, bmat, precision=HIGH)
-    local_adj = jnp.einsum("hlp,ln->hpn", enter_dy, cmat, precision=HIGH)
+    local_state = jnp.einsum("hlp,ln->hpn", left_u, bmat, precision=lax.Precision.HIGH)
+    local_adj = jnp.einsum("hlp,ln->hpn", enter_dy, cmat, precision=lax.Precision.HIGH)
 
     reach = 3 * lax.axis_size("context") // 16
     low = reach & -reach

time: 171 us -> 171 us (level)
  no operation moved by 1% of the time
where the time goes in v16:
time: 171 us; the launch traced here: 170 us
  starting transfers between devices  68.7 us (40%)
  waiting for transfers between devices  59.9 us (35%)
  other arithmetic  16.4 us (10%)
  local copies, waits for them, and re-layouts  11.4 us (7%)
  matrix products  11.4 us (7%)
  between operations  1.98 us (1%)
    ppermute x10, waiting for transfers between devices, from_behind(): return lax.ppermute(x, axis, pairs)  59.9 us
    ppermute x10, starting transfers between devices, from_behind(): return lax.ppermute(x, axis, pairs)  56.8 us
    unnamed x45, local copies, waits for them, and re-layouts  6.63 us
    all_to_all x1, starting transfers between devices, scatter_sum(): got = lax.all_to_all(parts, axis, 0, 0, tiled=True)  6.6 us
    all_to_all x1, starting transfers between devices, local(): lax.all_to_all(jnp.broadcast_to(piece, (count,) + piece.shape), 'tensor',...  5.23 us
  transfers between devices with their start and end apart: 12, of which 8 were waited for; matrix products, arithmetic and copies ran while one was open for 8% of the time, Pallas kernels for 0%

profile of v16, /device:TPU:75, one launch (start us, length us, event | category | flops | bytes accessed | tf_op | source)
XLA Modules:
  0.0 169.9 jit_solution(745314726743830576)
XLA Ops:
  0.6 0.7 pad_maximum_fusion
  1.4 0.6 broadcast_in_dim.28
  2.0 5.2 %all-to-all-start = ((bf16[8,2,16,128]{3,2,1,0:T(8,128)(2,1)}), bf16[8,2,16,128]{3,2,1,0:T(8,128)(2,1)S(1)}, u32[]{:S(2)}, u32[]{:S(2)}) async-start(bf16[8,2,16,128]{3,2,1,0:T(8,128)(2,1)} %broadcast_in_dim.28), calls=%async_computation | async-start | bytes 131072 | tf_op jit(solution)/shard_map/all_to_all | solution.py:92
  7.3 0.7 copy.26
  8.2 0.5 copy-done.12
  8.9 0.6 slice.172
  10.1 0.7 compare_convert_fusion
  10.9 0.3 reduce_window_sum.30
  11.7 0.8 copy-done.10
  12.6 0.4 abs_reduce_fusion.6
  13.1 0.4 abs_reduce_fusion.7
  14.1 3.5 %collective-permute-start = (s16[1033,128]{1,0:T(8,128)(2,1)S(1)}, s16[1033,128]{1,0:T(8,128)(2,1)S(1)}, u32[]{:S(2)}, u32[]{:S(2)}) collective-permute-start(s16[1033,128]{1,0:T(8,128)(2,1)S(1)} %get-tuple-element.19), channel_id=1, source_target_pairs={{0,8},{8,16},{16,24},{24,32},{32,40},{40,48},{48,56},{56,64},{64,7... | collective-permute-start | bytes 793352 | tf_op jit(solution)/shard_map/ppermute | solution.py:12
  17.6 1.9 %collective-permute-start.1 = (s16[1033,128]{1,0:T(8,128)(2,1)S(1)}, s16[1033,128]{1,0:T(8,128)(2,1)S(1)}, u32[]{:S(2)}, u32[]{:S(2)}) collective-permute-start(s16[1033,128]{1,0:T(8,128)(2,1)S(1)} %get-tuple-element.20), channel_id=1, source_target_pairs={{8,0},{16,8},{24,16},{32,24},{40,32},{48,40},{56,48},{64,56},{72,6... | collective-permute-start | bytes 793352 | tf_op jit(solution)/shard_map/ppermute | solution.py:12
  19.6 4.0 %collective-permute-done = s16[1033,128]{1,0:T(8,128)(2,1)S(1)} collective-permute-done((s16[1033,128]{1,0:T(8,128)(2,1)S(1)}, s16[1033,128]{1,0:T(8,128)(2,1)S(1)}, u32[]{:S(2)}, u32[]{:S(2)}) %collective-permute-start) | collective-permute-done | bytes 264480 | tf_op jit(solution)/shard_map/ppermute | solution.py:12
  23.7 4.9 %collective-permute-done.1 = s16[1033,128]{1,0:T(8,128)(2,1)S(1)} collective-permute-done((s16[1033,128]{1,0:T(8,128)(2,1)S(1)}, s16[1033,128]{1,0:T(8,128)(2,1)S(1)}, u32[]{:S(2)}, u32[]{:S(2)}) %collective-permute-start.1) | collective-permute-done | bytes 264480 | tf_op jit(solution)/shard_map/ppermute | solution.py:12
  28.7 0.7 abs_reduce_fusion.4
  29.6 0.6 fusion.225
  30.2 0.5 copy-done.15
  30.8 0.7 clamp_convert_fusion.4
  31.7 4.8 %collective-permute-start.2 = (s16[1033,128]{1,0:T(8,128)(2,1)S(1)}, s16[1033,128]{1,0:T(8,128)(2,1)S(1)}, u32[]{:S(2)}, u32[]{:S(2)}) collective-permute-start(s16[1033,128]{1,0:T(8,128)(2,1)S(1)} %get-tuple-element.21), channel_id=1, source_target_pairs={{0,16},{8,24},{16,32},{24,40},{32,48},{40,56},{48,64},{56,72},{64,... | collective-permute-start | bytes 793352 | tf_op jit(solution)/shard_map/ppermute | solution.py:12
  36.4 2.4 %collective-permute-start.3 = (s16[1033,128]{1,0:T(8,128)(2,1)S(1)}, s16[1033,128]{1,0:T(8,128)(2,1)S(1)}, u32[]{:S(2)}, u32[]{:S(2)}) collective-permute-start(s16[1033,128]{1,0:T(8,128)(2,1)S(1)} %get-tuple-element.22), channel_id=1, source_target_pairs={{16,0},{24,8},{32,16},{40,24},{48,32},{56,40},{64,48},{72,56},{80,... | collective-permute-start | bytes 793352 | tf_op jit(solution)/shard_map/ppermute | solution.py:12
  38.8 3.9 %collective-permute-done.2 = s16[1033,128]{1,0:T(8,128)(2,1)S(1)} collective-permute-done((s16[1033,128]{1,0:T(8,128)(2,1)S(1)}, s16[1033,128]{1,0:T(8,128)(2,1)S(1)}, u32[]{:S(2)}, u32[]{:S(2)}) %collective-permute-start.2) | collective-permute-done | bytes 264480 | tf_op jit(solution)/shard_map/ppermute | solution.py:12
  42.8 5.2 %collective-permute-done.3 = s16[1033,128]{1,0:T(8,128)(2,1)S(1)} collective-permute-done((s16[1033,128]{1,0:T(8,128)(2,1)S(1)}, s16[1033,128]{1,0:T(8,128)(2,1)S(1)}, u32[]{:S(2)}, u32[]{:S(2)}) %collective-permute-start.3) | collective-permute-done | bytes 264480 | tf_op jit(solution)/shard_map/ppermute | solution.py:12
  48.1 0.6 copy-done.7
  48.7 0.9 copy-done.3
  49.7 0.8 fusion.15
  51.1 0.7 slice_convert_fusion.9
  51.8 0.7 slice_convert_fusion.8
  53.1 0.9 fusion.59
  54.0 7.5 %collective-permute-start.4 = (s16[1033,128]{1,0:T(8,128)(2,1)}, s16[1033,128]{1,0:T(8,128)(2,1)S(1)}, u32[]{:S(2)}, u32[]{:S(2)}) collective-permute-start(s16[1033,128]{1,0:T(8,128)(2,1)} %get-tuple-element.32), channel_id=1, source_target_pairs={{0,32},{8,40},{16,48},{24,56},{32,64},{40,72},{48,80},{56,88},{64,... | collective-permute-start | bytes 793352 | tf_op jit(solution)/shard_map/ppermute | solution.py:12
  61.6 2.6 %collective-permute-start.5 = (s16[1033,128]{1,0:T(8,128)(2,1)}, s16[1033,128]{1,0:T(8,128)(2,1)S(1)}, u32[]{:S(2)}, u32[]{:S(2)}) collective-permute-start(s16[1033,128]{1,0:T(8,128)(2,1)} %get-tuple-element.29), channel_id=1, source_target_pairs={{32,0},{40,8},{48,16},{56,24},{64,32},{72,40},{80,48},{88,56},{96,... | collective-permute-start | bytes 793352 | tf_op jit(solution)/shard_map/ppermute | solution.py:12
  64.3 5.0 %collective-permute-done.4 = s16[1033,128]{1,0:T(8,128)(2,1)S(1)} collective-permute-done((s16[1033,128]{1,0:T(8,128)(2,1)}, s16[1033,128]{1,0:T(8,128)(2,1)S(1)}, u32[]{:S(2)}, u32[]{:S(2)}) %collective-permute-start.4) | collective-permute-done | bytes 264480 | tf_op jit(solution)/shard_map/ppermute | solution.py:12
  69.4 0.4 abs_reduce_fusion.1
  69.9 5.6 %collective-permute-done.5 = s16[1033,128]{1,0:T(8,128)(2,1)S(1)} collective-permute-done((s16[1033,128]{1,0:T(8,128)(2,1)}, s16[1033,128]{1,0:T(8,128)(2,1)S(1)}, u32[]{:S(2)}, u32[]{:S(2)}) %collective-permute-start.5) | collective-permute-done | bytes 264480 | tf_op jit(solution)/shard_map/ppermute | solution.py:12
  75.6 0.4 abs_reduce_fusion
  76.4 0.4 clamp_convert_fusion.1
  76.8 0.4 clamp_convert_fusion
  77.2 0.9 fusion.61
  78.0 14.4 %collective-permute-start.6 = (s16[1033,128]{1,0:T(8,128)(2,1)}, s16[1033,128]{1,0:T(8,128)(2,1)S(1)}, u32[]{:S(2)}, u32[]{:S(2)}) collective-permute-start(s16[1033,128]{1,0:T(8,128)(2,1)} %get-tuple-element.29), channel_id=1, source_target_pairs={{8,0},{16,8},{24,16},{32,24},{40,32},{48,40},{56,48},{64,56},{72,6... | collective-permute-start | bytes 793352 | tf_op jit(solution)/shard_map/ppermute | solution.py:12
  92.5 2.4 %fusion.8 = (f32[16,128]{1,0:T(8,128)S(1)}, f32[16,128]{1,0:T(8,128)S(1)}, f32[128,128]{1,0:T(8,128)S(1)}) fusion(f32[128,128]{1,0:T(8,128)S(1)} %fusion.231, f32[16,128]{1,0:T(8,128)S(1)} %reduce_window_sum.30, pred[128,128]{1,0:T(8,128)(4,1)S(1)} %fusion.72, f32[16,128,64]{1,2,0:T(8,128)S(1)} %bitcast.198, f32[16,128,64]{1,2,0:T(8,128)S(1)} %copy-done.1), kind=kOutput, calls=%fused_computation.21 | convolution fusion | flops 203403264 | bytes 1220608 | tf_op jit(solution)/shard_map/hip,hjp->hij/dot_general | solution.py:158
  94.8 0.3 reduce_window_sum.31
  95.1 0.3 reduce_window_sum.32
  95.4 1.3 fusion.6
  96.7 9.1 %collective-permute-start.7 = (s16[1033,128]{1,0:T(8,128)(2,1)}, s16[1033,128]{1,0:T(8,128)(2,1)S(1)}, u32[]{:S(2)}, u32[]{:S(2)}) collective-permute-start(s16[1033,128]{1,0:T(8,128)(2,1)} %get-tuple-element.30), channel_id=1, source_target_pairs={{40,0},{48,8},{56,16},{64,24},{72,32},{80,40},{88,48},{96,56},{104... | collective-permute-start | bytes 793352 | tf_op jit(solution)/shard_map/ppermute | solution.py:12
  105.8 1.9 %collective-permute-start.8 = (s16[1033,128]{1,0:T(8,128)(2,1)}, s16[1033,128]{1,0:T(8,128)(2,1)S(1)}, u32[]{:S(2)}, u32[]{:S(2)}) collective-permute-start(s16[1033,128]{1,0:T(8,128)(2,1)} %get-tuple-element.32), channel_id=1, source_target_pairs={{0,8},{8,16},{16,24},{24,32},{32,40},{40,48},{48,56},{56,64},{64,7... | collective-permute-start | bytes 793352 | tf_op jit(solution)/shard_map/ppermute | solution.py:12
  107.7 8.7 %collective-permute-start.9 = (s16[1033,128]{1,0:T(8,128)(2,1)}, s16[1033,128]{1,0:T(8,128)(2,1)S(1)}, u32[]{:S(2)}, u32[]{:S(2)}) collective-permute-start(s16[1033,128]{1,0:T(8,128)(2,1)} %get-tuple-element.33), channel_id=1, source_target_pairs={{0,40},{8,48},{16,56},{24,64},{32,72},{40,80},{48,88},{56,96},{64,... | collective-permute-start | bytes 793352 | tf_op jit(solution)/shard_map/ppermute | solution.py:12
  116.6 3.3 %collective-permute-done.7 = s16[1033,128]{1,0:T(8,128)(2,1)S(1)} collective-permute-done((s16[1033,128]{1,0:T(8,128)(2,1)}, s16[1033,128]{1,0:T(8,128)(2,1)S(1)}, u32[]{:S(2)}, u32[]{:S(2)}) %collective-permute-start.7) | collective-permute-done | bytes 264480 | tf_op jit(solution)/shard_map/ppermute | solution.py:12
  120.5 28.0 %collective-permute-done.9 = s16[1033,128]{1,0:T(8,128)(2,1)S(1)} collective-permute-done((s16[1033,128]{1,0:T(8,128)(2,1)}, s16[1033,128]{1,0:T(8,128)(2,1)S(1)}, u32[]{:S(2)}, u32[]{:S(2)}) %collective-permute-start.9) | collective-permute-done | bytes 264480 | tf_op jit(solution)/shard_map/ppermute | solution.py:12
  148.6 1.8 %multiply_reduce_fusion.1 = (f32[1024]{0:T(1024)S(1)}, f32[1024,128]{1,0:T(8,128)S(1)}, f32[1024,128]{1,0:T(8,128)}) fusion(f32[1024]{0:T(1024)S(1)} %get-tuple-element.83, s16[1033,128]{1,0:T(8,128)(2,1)S(1)} %collective-permute-done.9, f32[1024]{0:T(1024)S(1)} %mul.481, f32[1024]{0:T(1024)S(1)} %get-tuple-element.81, ...), kind=kLoop, calls=%fused_computation.59 | loop fusion | flops 1833984 | bytes 2125824 | tf_op jit(solution)/shard_map/reduce_sum | solution.py:178
  150.4 0.4 fusion.1
  150.8 1.2 fusion.3
  152.4 1.3 convolution_bitcast_fusion.1
  154.0 0.9 copy-done.6
  154.9 1.3 convolution_bitcast_fusion.2
  156.3 0.3 convolution_add_fusion.1
  156.5 0.6 maximum_bitcast_fusion
  157.2 6.6 %all-to-all-start.1 = ((f32[8,2,16,128]{3,2,1,0:T(8,128)}), f32[8,2,16,128]{3,2,1,0:T(8,128)S(1)}, u32[]{:S(2)}, u32[]{:S(2)}) async-start(f32[8,2,16,128]{3,2,1,0:T(8,128)} %maximum_bitcast_fusion), calls=%async_computation.1 | async-start | bytes 262144 | tf_op jit(solution)/shard_map/all_to_all | solution.py:67
  163.8 0.7 copy-done.21
  164.4 0.4 fusion.28
  165.1 1.0 copy.31
  166.1 1.9 %fusion.2 = f32[16,1,128]{2,1,0:T(1,128)S(1)} fusion(f32[16,128,1]{1,2,0:T(1,128)S(1)} %bitcast.237, f32[16,128]{1,0:T(8,128)S(1)} %reduce_window_sum.30, pred[128,128]{1,0:T(8,128)(4,1)S(1)} %fusion.72), kind=kOutput, calls=%fused_computation.9 | convolution fusion | flops 3670016 | bytes 40960 | tf_op jit(solution)/shard_map/hij,hj->hi/dot_general | solution.py:175
  167.9 0.7 copy-done.20
  168.6 0.7 multiply_subtract_fusion
  169.3 0.6 slice_bitcast_fusion
  (145 shorter events, 6.3 us)
Async XLA Ops:
  0.6 10.7 %copy-start.9 = (bf16[128,1024]{1,0:T(8,128)(2,1)S(1)}, bf16[128,1024]{1,0:T(8,128)(2,1)}, u32[]{:S(2)}) copy-start(bf16[128,1024]{1,0:T(8,128)(2,1)} %param.8) | copy-start | bytes 786436
  2.0 10.6 %all-to-all-start = ((bf16[8,2,16,128]{3,2,1,0:T(8,128)(2,1)}), bf16[8,2,16,128]{3,2,1,0:T(8,128)(2,1)S(1)}, u32[]{:S(2)}, u32[]{:S(2)}) async-start(bf16[8,2,16,128]{3,2,1,0:T(8,128)(2,1)} %broadcast_in_dim.28), calls=%async_computation | async-start | bytes 131072 | tf_op jit(solution)/shard_map/all_to_all | solution.py:92
  8.1 0.7 copy-start.12
  8.7 2.0 %copy-start.11 = (f32[16,128]{1,0:T(8,128)S(1)}, f32[16,128]{1,0:T(8,128)}, u32[]{:S(2)}) copy-start(f32[16,128]{1,0:T(8,128)} %param.10) | copy-start | bytes 24580
  10.1 0.7 copy-start.19
  11.5 1.0 copy-start.10
  11.5 1.5 copy-start
  14.1 9.5 %collective-permute-start = (s16[1033,128]{1,0:T(8,128)(2,1)S(1)}, s16[1033,128]{1,0:T(8,128)(2,1)S(1)}, u32[]{:S(2)}, u32[]{:S(2)}) collective-permute-start(s16[1033,128]{1,0:T(8,128)(2,1)S(1)} %get-tuple-element.19), channel_id=1, source_target_pairs={{0,8},{8,16},{16,24},{24,32},{32,40},{40,48},{48,56},{56,64},{64,7... | collective-permute-start | bytes 793352 | tf_op jit(solution)/shard_map/ppermute | solution.py:12
  17.6 10.9 %collective-permute-start.1 = (s16[1033,128]{1,0:T(8,128)(2,1)S(1)}, s16[1033,128]{1,0:T(8,128)(2,1)S(1)}, u32[]{:S(2)}, u32[]{:S(2)}) collective-permute-start(s16[1033,128]{1,0:T(8,128)(2,1)S(1)} %get-tuple-element.20), channel_id=1, source_target_pairs={{8,0},{16,8},{24,16},{32,24},{40,32},{48,40},{56,48},{64,56},{72,6... | collective-permute-start | bytes 793352 | tf_op jit(solution)/shard_map/ppermute | solution.py:12
  28.6 2.3 %copy-start.2 = (s16[1033,128]{1,0:T(8,128)(2,1)}, s16[1033,128]{1,0:T(8,128)(2,1)S(1)}, u32[]{:S(2)}) copy-start(s16[1033,128]{1,0:T(8,128)(2,1)S(1)} %collective-permute-done.1) | copy-start | bytes 793348
  30.2 0.5 copy-start.15
  30.2 0.6 copy-start.17
  31.7 11.1 %collective-permute-start.2 = (s16[1033,128]{1,0:T(8,128)(2,1)S(1)}, s16[1033,128]{1,0:T(8,128)(2,1)S(1)}, u32[]{:S(2)}, u32[]{:S(2)}) collective-permute-start(s16[1033,128]{1,0:T(8,128)(2,1)S(1)} %get-tuple-element.21), channel_id=1, source_target_pairs={{0,16},{8,24},{16,32},{24,40},{32,48},{40,56},{48,64},{56,72},{64,... | collective-permute-start | bytes 793352 | tf_op jit(solution)/shard_map/ppermute | solution.py:12
  36.4 11.5 %collective-permute-start.3 = (s16[1033,128]{1,0:T(8,128)(2,1)S(1)}, s16[1033,128]{1,0:T(8,128)(2,1)S(1)}, u32[]{:S(2)}, u32[]{:S(2)}) collective-permute-start(s16[1033,128]{1,0:T(8,128)(2,1)S(1)} %get-tuple-element.22), channel_id=1, source_target_pairs={{16,0},{24,8},{32,16},{40,24},{48,32},{56,40},{64,48},{72,56},{80,... | collective-permute-start | bytes 793352 | tf_op jit(solution)/shard_map/ppermute | solution.py:12
  42.7 5.4 %copy-start.8 = (s16[1033,128]{1,0:T(8,128)(2,1)}, s16[1033,128]{1,0:T(8,128)(2,1)S(1)}, u32[]{:S(2)}) copy-start(s16[1033,128]{1,0:T(8,128)(2,1)S(1)} %collective-permute-done.2) | copy-start | bytes 793348
  48.0 0.7 copy-start.7
  48.7 1.0 copy-start.3
  48.7 0.9 copy-start.13
  48.7 0.9 copy-start.14
  51.0 0.7 copy-start.18
  51.8 0.7 copy-start.16
  54.0 15.3 %collective-permute-start.4 = (s16[1033,128]{1,0:T(8,128)(2,1)}, s16[1033,128]{1,0:T(8,128)(2,1)S(1)}, u32[]{:S(2)}, u32[]{:S(2)}) collective-permute-start(s16[1033,128]{1,0:T(8,128)(2,1)} %get-tuple-element.32), channel_id=1, source_target_pairs={{0,32},{8,40},{16,48},{24,56},{32,64},{40,72},{48,80},{56,88},{64,... | collective-permute-start | bytes 793352 | tf_op jit(solution)/shard_map/ppermute | solution.py:12
  61.6 14.0 %collective-permute-start.5 = (s16[1033,128]{1,0:T(8,128)(2,1)}, s16[1033,128]{1,0:T(8,128)(2,1)S(1)}, u32[]{:S(2)}, u32[]{:S(2)}) collective-permute-start(s16[1033,128]{1,0:T(8,128)(2,1)} %get-tuple-element.29), channel_id=1, source_target_pairs={{32,0},{40,8},{48,16},{56,24},{64,32},{72,40},{80,48},{88,56},{96,... | collective-permute-start | bytes 793352 | tf_op jit(solution)/shard_map/ppermute | solution.py:12
  77.2 15.3 %copy-start.1 = (f32[16,128,64]{1,2,0:T(8,128)S(1)}, f32[16,128,64]{1,2,0:T(8,128)}, u32[]{:S(2)}) copy-start(f32[16,128,64]{1,2,0:T(8,128)} %copy-done) | copy-start | bytes 1572868
  78.0 38.4 %collective-permute-start.6 = (s16[1033,128]{1,0:T(8,128)(2,1)}, s16[1033,128]{1,0:T(8,128)(2,1)S(1)}, u32[]{:S(2)}, u32[]{:S(2)}) collective-permute-start(s16[1033,128]{1,0:T(8,128)(2,1)} %get-tuple-element.29), channel_id=1, source_target_pairs={{8,0},{16,8},{24,16},{32,24},{40,32},{48,40},{56,48},{64,56},{72,6... | collective-permute-start | bytes 793352 | tf_op jit(solution)/shard_map/ppermute | solution.py:12
  96.7 23.2 %collective-permute-start.7 = (s16[1033,128]{1,0:T(8,128)(2,1)}, s16[1033,128]{1,0:T(8,128)(2,1)S(1)}, u32[]{:S(2)}, u32[]{:S(2)}) collective-permute-start(s16[1033,128]{1,0:T(8,128)(2,1)} %get-tuple-element.30), channel_id=1, source_target_pairs={{40,0},{48,8},{56,16},{64,24},{72,32},{80,40},{88,48},{96,56},{104... | collective-permute-start | bytes 793352 | tf_op jit(solution)/shard_map/ppermute | solution.py:12
  105.8 14.1 %collective-permute-start.8 = (s16[1033,128]{1,0:T(8,128)(2,1)}, s16[1033,128]{1,0:T(8,128)(2,1)S(1)}, u32[]{:S(2)}, u32[]{:S(2)}) collective-permute-start(s16[1033,128]{1,0:T(8,128)(2,1)} %get-tuple-element.32), channel_id=1, source_target_pairs={{0,8},{8,16},{16,24},{24,32},{32,40},{40,48},{48,56},{56,64},{64,7... | collective-permute-start | bytes 793352 | tf_op jit(solution)/shard_map/ppermute | solution.py:12
  107.7 40.8 %collective-permute-start.9 = (s16[1033,128]{1,0:T(8,128)(2,1)}, s16[1033,128]{1,0:T(8,128)(2,1)S(1)}, u32[]{:S(2)}, u32[]{:S(2)}) collective-permute-start(s16[1033,128]{1,0:T(8,128)(2,1)} %get-tuple-element.33), channel_id=1, source_target_pairs={{0,40},{8,48},{16,56},{24,64},{32,72},{40,80},{48,88},{56,96},{64,... | collective-permute-start | bytes 793352 | tf_op jit(solution)/shard_map/ppermute | solution.py:12
  119.9 30.5 %copy-start.5 = (s16[1033,128]{1,0:T(8,128)(2,1)}, s16[1033,128]{1,0:T(8,128)(2,1)S(1)}, u32[]{:S(2)}) copy-start(s16[1033,128]{1,0:T(8,128)(2,1)S(1)} %collective-permute-done.7) | copy-start | bytes 793348
  153.9 1.0 copy-start.6
  156.2 7.5 %copy-start.4 = (f32[1024,128]{1,0:T(8,128)S(1)}, f32[1024,128]{1,0:T(8,128)}, u32[]{:S(2)}) copy-start(f32[1024,128]{1,0:T(8,128)} %get-tuple-element.59) | copy-start | bytes 1572868
  157.2 12.1 %all-to-all-start.1 = ((f32[8,2,16,128]{3,2,1,0:T(8,128)}), f32[8,2,16,128]{3,2,1,0:T(8,128)S(1)}, u32[]{:S(2)}, u32[]{:S(2)}) async-start(f32[8,2,16,128]{3,2,1,0:T(8,128)} %maximum_bitcast_fusion), calls=%async_computation.1 | async-start | bytes 262144 | tf_op jit(solution)/shard_map/all_to_all | solution.py:67
  163.8 0.7 copy-start.21
  167.9 0.7 copy-start.20

commit v17 on v16

--- a/solution.py
+++ b/solution.py
@@ -164,8 +164,8 @@
     gb_loc = jnp.dot(weighted.T, cmat, precision=HIGH)
     gc_loc = jnp.dot(weighted, bmat, precision=HIGH)
 
-    b_adj = jnp.einsum("ln,hpn->hlp", bmat, g_in, precision=HIGH)
-    c_state = jnp.einsum("ln,hpn->hlp", cmat, s_in, precision=HIGH)
+    b_adj = jnp.einsum("ln,hpn->hlp", bmat, g_in, precision=lax.Precision.HIGH)
+    c_state = jnp.einsum("ln,hpn->hlp", cmat, s_in, precision=lax.Precision.HIGH)
     core = core_loc + leave[:, :, None] * b_adj
     gx = step_size[:, :, None] * core + skip_gain[:, None, None] * dys
     along = jnp.sum(xs * core, axis=2)

time: 171 us -> 170 us (level)
  no operation moved by 1% of the time
where the time goes in v17:
time: 170 us
  starting transfers between devices  68.7 us (40%)
  waiting for transfers between devices  59.9 us (35%)
  other arithmetic  16.4 us (10%)
  local copies, waits for them, and re-layouts  11.4 us (7%)
  matrix products  11.3 us (7%)
  between operations  1.98 us (1%)
    ppermute x10, waiting for transfers between devices, from_behind(): return lax.ppermute(x, axis, pairs)  59.9 us
    ppermute x10, starting transfers between devices, from_behind(): return lax.ppermute(x, axis, pairs)  56.8 us
    unnamed x45, local copies, waits for them, and re-layouts  6.63 us
    all_to_all x1, starting transfers between devices, scatter_sum(): got = lax.all_to_all(parts, axis, 0, 0, tiled=True)  6.59 us
    all_to_all x1, starting transfers between devices, local(): lax.all_to_all(jnp.broadcast_to(piece, (count,) + piece.shape), 'tensor',...  5.23 us
  transfers between devices with their start and end apart: 12, of which 8 were waited for; matrix products, arithmetic and copies ran while one was open for 8% of the time, Pallas kernels for 0%

profile of v17, /device:TPU:75, one launch (start us, length us, event | category | flops | bytes accessed | tf_op | source)
XLA Modules:
  0.0 169.7 jit_solution(10390780549004608584)
XLA Ops:
  0.6 0.7 pad_maximum_fusion
  1.4 0.6 broadcast_in_dim.28
  2.0 5.2 %all-to-all-start = ((bf16[8,2,16,128]{3,2,1,0:T(8,128)(2,1)}), bf16[8,2,16,128]{3,2,1,0:T(8,128)(2,1)S(1)}, u32[]{:S(2)}, u32[]{:S(2)}) async-start(bf16[8,2,16,128]{3,2,1,0:T(8,128)(2,1)} %broadcast_in_dim.28), calls=%async_computation | async-start | bytes 131072 | tf_op jit(solution)/shard_map/all_to_all | solution.py:92
  7.3 0.7 copy.26
  8.2 0.5 copy-done.12
  8.9 0.6 slice.172
  10.1 0.7 compare_convert_fusion
  10.9 0.3 reduce_window_sum.30
  11.7 0.8 copy-done.10
  12.6 0.4 abs_reduce_fusion.6
  13.1 0.4 abs_reduce_fusion.7
  14.1 3.5 %collective-permute-start = (s16[1033,128]{1,0:T(8,128)(2,1)S(1)}, s16[1033,128]{1,0:T(8,128)(2,1)S(1)}, u32[]{:S(2)}, u32[]{:S(2)}) collective-permute-start(s16[1033,128]{1,0:T(8,128)(2,1)S(1)} %get-tuple-element.19), channel_id=1, source_target_pairs={{0,8},{8,16},{16,24},{24,32},{32,40},{40,48},{48,56},{56,64},{64,7... | collective-permute-start | bytes 793352 | tf_op jit(solution)/shard_map/ppermute | solution.py:12
  17.6 1.9 %collective-permute-start.1 = (s16[1033,128]{1,0:T(8,128)(2,1)S(1)}, s16[1033,128]{1,0:T(8,128)(2,1)S(1)}, u32[]{:S(2)}, u32[]{:S(2)}) collective-permute-start(s16[1033,128]{1,0:T(8,128)(2,1)S(1)} %get-tuple-element.20), channel_id=1, source_target_pairs={{8,0},{16,8},{24,16},{32,24},{40,32},{48,40},{56,48},{64,56},{72,6... | collective-permute-start | bytes 793352 | tf_op jit(solution)/shard_map/ppermute | solution.py:12
  19.6 4.0 %collective-permute-done = s16[1033,128]{1,0:T(8,128)(2,1)S(1)} collective-permute-done((s16[1033,128]{1,0:T(8,128)(2,1)S(1)}, s16[1033,128]{1,0:T(8,128)(2,1)S(1)}, u32[]{:S(2)}, u32[]{:S(2)}) %collective-permute-start) | collective-permute-done | bytes 264480 | tf_op jit(solution)/shard_map/ppermute | solution.py:12
  23.7 4.9 %collective-permute-done.1 = s16[1033,128]{1,0:T(8,128)(2,1)S(1)} collective-permute-done((s16[1033,128]{1,0:T(8,128)(2,1)S(1)}, s16[1033,128]{1,0:T(8,128)(2,1)S(1)}, u32[]{:S(2)}, u32[]{:S(2)}) %collective-permute-start.1) | collective-permute-done | bytes 264480 | tf_op jit(solution)/shard_map/ppermute | solution.py:12
  28.7 0.7 abs_reduce_fusion.4
  29.6 0.6 fusion.225
  30.2 0.5 copy-done.15
  30.8 0.7 clamp_convert_fusion.4
  31.7 4.8 %collective-permute-start.2 = (s16[1033,128]{1,0:T(8,128)(2,1)S(1)}, s16[1033,128]{1,0:T(8,128)(2,1)S(1)}, u32[]{:S(2)}, u32[]{:S(2)}) collective-permute-start(s16[1033,128]{1,0:T(8,128)(2,1)S(1)} %get-tuple-element.21), channel_id=1, source_target_pairs={{0,16},{8,24},{16,32},{24,40},{32,48},{40,56},{48,64},{56,72},{64,... | collective-permute-start | bytes 793352 | tf_op jit(solution)/shard_map/ppermute | solution.py:12
  36.4 2.4 %collective-permute-start.3 = (s16[1033,128]{1,0:T(8,128)(2,1)S(1)}, s16[1033,128]{1,0:T(8,128)(2,1)S(1)}, u32[]{:S(2)}, u32[]{:S(2)}) collective-permute-start(s16[1033,128]{1,0:T(8,128)(2,1)S(1)} %get-tuple-element.22), channel_id=1, source_target_pairs={{16,0},{24,8},{32,16},{40,24},{48,32},{56,40},{64,48},{72,56},{80,... | collective-permute-start | bytes 793352 | tf_op jit(solution)/shard_map/ppermute | solution.py:12
  38.8 3.9 %collective-permute-done.2 = s16[1033,128]{1,0:T(8,128)(2,1)S(1)} collective-permute-done((s16[1033,128]{1,0:T(8,128)(2,1)S(1)}, s16[1033,128]{1,0:T(8,128)(2,1)S(1)}, u32[]{:S(2)}, u32[]{:S(2)}) %collective-permute-start.2) | collective-permute-done | bytes 264480 | tf_op jit(solution)/shard_map/ppermute | solution.py:12
  42.8 5.2 %collective-permute-done.3 = s16[1033,128]{1,0:T(8,128)(2,1)S(1)} collective-permute-done((s16[1033,128]{1,0:T(8,128)(2,1)S(1)}, s16[1033,128]{1,0:T(8,128)(2,1)S(1)}, u32[]{:S(2)}, u32[]{:S(2)}) %collective-permute-start.3) | collective-permute-done | bytes 264480 | tf_op jit(solution)/shard_map/ppermute | solution.py:12
  48.1 0.6 copy-done.7
  48.7 0.9 copy-done.3
  49.7 0.8 fusion.15
  51.1 0.7 slice_convert_fusion.9
  51.8 0.7 slice_convert_fusion.8
  53.1 0.9 fusion.59
  54.0 7.5 %collective-permute-start.4 = (s16[1033,128]{1,0:T(8,128)(2,1)}, s16[1033,128]{1,0:T(8,128)(2,1)S(1)}, u32[]{:S(2)}, u32[]{:S(2)}) collective-permute-start(s16[1033,128]{1,0:T(8,128)(2,1)} %get-tuple-element.32), channel_id=1, source_target_pairs={{0,32},{8,40},{16,48},{24,56},{32,64},{40,72},{48,80},{56,88},{64,... | collective-permute-start | bytes 793352 | tf_op jit(solution)/shard_map/ppermute | solution.py:12
  61.6 2.6 %collective-permute-start.5 = (s16[1033,128]{1,0:T(8,128)(2,1)}, s16[1033,128]{1,0:T(8,128)(2,1)S(1)}, u32[]{:S(2)}, u32[]{:S(2)}) collective-permute-start(s16[1033,128]{1,0:T(8,128)(2,1)} %get-tuple-element.29), channel_id=1, source_target_pairs={{32,0},{40,8},{48,16},{56,24},{64,32},{72,40},{80,48},{88,56},{96,... | collective-permute-start | bytes 793352 | tf_op jit(solution)/shard_map/ppermute | solution.py:12
  64.3 5.0 %collective-permute-done.4 = s16[1033,128]{1,0:T(8,128)(2,1)S(1)} collective-permute-done((s16[1033,128]{1,0:T(8,128)(2,1)}, s16[1033,128]{1,0:T(8,128)(2,1)S(1)}, u32[]{:S(2)}, u32[]{:S(2)}) %collective-permute-start.4) | collective-permute-done | bytes 264480 | tf_op jit(solution)/shard_map/ppermute | solution.py:12
  69.4 0.4 abs_reduce_fusion.1
  69.9 5.6 %collective-permute-done.5 = s16[1033,128]{1,0:T(8,128)(2,1)S(1)} collective-permute-done((s16[1033,128]{1,0:T(8,128)(2,1)}, s16[1033,128]{1,0:T(8,128)(2,1)S(1)}, u32[]{:S(2)}, u32[]{:S(2)}) %collective-permute-start.5) | collective-permute-done | bytes 264480 | tf_op jit(solution)/shard_map/ppermute | solution.py:12
  75.6 0.4 abs_reduce_fusion
  76.4 0.4 clamp_convert_fusion.1
  76.8 0.4 clamp_convert_fusion
  77.2 0.9 fusion.61
  78.0 14.4 %collective-permute-start.6 = (s16[1033,128]{1,0:T(8,128)(2,1)}, s16[1033,128]{1,0:T(8,128)(2,1)S(1)}, u32[]{:S(2)}, u32[]{:S(2)}) collective-permute-start(s16[1033,128]{1,0:T(8,128)(2,1)} %get-tuple-element.29), channel_id=1, source_target_pairs={{8,0},{16,8},{24,16},{32,24},{40,32},{48,40},{56,48},{64,56},{72,6... | collective-permute-start | bytes 793352 | tf_op jit(solution)/shard_map/ppermute | solution.py:12
  92.5 2.4 %fusion.8 = (f32[16,128]{1,0:T(8,128)S(1)}, f32[16,128]{1,0:T(8,128)S(1)}, f32[128,128]{1,0:T(8,128)S(1)}) fusion(f32[128,128]{1,0:T(8,128)S(1)} %fusion.231, f32[16,128]{1,0:T(8,128)S(1)} %reduce_window_sum.30, pred[128,128]{1,0:T(8,128)(4,1)S(1)} %fusion.72, f32[16,128,64]{1,2,0:T(8,128)S(1)} %bitcast.198, f32[16,128,64]{1,2,0:T(8,128)S(1)} %copy-done.1), kind=kOutput, calls=%fused_computation.21 | convolution fusion | flops 203403264 | bytes 1220608 | tf_op jit(solution)/shard_map/hip,hjp->hij/dot_general | solution.py:158
  94.8 0.3 reduce_window_sum.31
  95.1 0.3 reduce_window_sum.32
  95.4 1.3 fusion.6
  96.7 9.1 %collective-permute-start.7 = (s16[1033,128]{1,0:T(8,128)(2,1)}, s16[1033,128]{1,0:T(8,128)(2,1)S(1)}, u32[]{:S(2)}, u32[]{:S(2)}) collective-permute-start(s16[1033,128]{1,0:T(8,128)(2,1)} %get-tuple-element.30), channel_id=1, source_target_pairs={{40,0},{48,8},{56,16},{64,24},{72,32},{80,40},{88,48},{96,56},{104... | collective-permute-start | bytes 793352 | tf_op jit(solution)/shard_map/ppermute | solution.py:12
  105.8 1.9 %collective-permute-start.8 = (s16[1033,128]{1,0:T(8,128)(2,1)}, s16[1033,128]{1,0:T(8,128)(2,1)S(1)}, u32[]{:S(2)}, u32[]{:S(2)}) collective-permute-start(s16[1033,128]{1,0:T(8,128)(2,1)} %get-tuple-element.32), channel_id=1, source_target_pairs={{0,8},{8,16},{16,24},{24,32},{32,40},{40,48},{48,56},{56,64},{64,7... | collective-permute-start | bytes 793352 | tf_op jit(solution)/shard_map/ppermute | solution.py:12
  107.7 8.7 %collective-permute-start.9 = (s16[1033,128]{1,0:T(8,128)(2,1)}, s16[1033,128]{1,0:T(8,128)(2,1)S(1)}, u32[]{:S(2)}, u32[]{:S(2)}) collective-permute-start(s16[1033,128]{1,0:T(8,128)(2,1)} %get-tuple-element.33), channel_id=1, source_target_pairs={{0,40},{8,48},{16,56},{24,64},{32,72},{40,80},{48,88},{56,96},{64,... | collective-permute-start | bytes 793352 | tf_op jit(solution)/shard_map/ppermute | solution.py:12
  116.6 3.3 %collective-permute-done.7 = s16[1033,128]{1,0:T(8,128)(2,1)S(1)} collective-permute-done((s16[1033,128]{1,0:T(8,128)(2,1)}, s16[1033,128]{1,0:T(8,128)(2,1)S(1)}, u32[]{:S(2)}, u32[]{:S(2)}) %collective-permute-start.7) | collective-permute-done | bytes 264480 | tf_op jit(solution)/shard_map/ppermute | solution.py:12
  120.5 28.0 %collective-permute-done.9 = s16[1033,128]{1,0:T(8,128)(2,1)S(1)} collective-permute-done((s16[1033,128]{1,0:T(8,128)(2,1)}, s16[1033,128]{1,0:T(8,128)(2,1)S(1)}, u32[]{:S(2)}, u32[]{:S(2)}) %collective-permute-start.9) | collective-permute-done | bytes 264480 | tf_op jit(solution)/shard_map/ppermute | solution.py:12
  148.6 1.8 %multiply_reduce_fusion.1 = (f32[1024]{0:T(1024)S(1)}, f32[1024,128]{1,0:T(8,128)S(1)}, f32[1024,128]{1,0:T(8,128)}) fusion(f32[1024]{0:T(1024)S(1)} %get-tuple-element.83, s16[1033,128]{1,0:T(8,128)(2,1)S(1)} %collective-permute-done.9, f32[1024]{0:T(1024)S(1)} %mul.481, f32[1024]{0:T(1024)S(1)} %get-tuple-element.81, ...), kind=kLoop, calls=%fused_computation.59 | loop fusion | flops 1833984 | bytes 2125824 | tf_op jit(solution)/shard_map/reduce_sum | solution.py:178
  150.4 0.3 fusion.1
  150.7 1.2 fusion.3
  152.3 1.3 convolution_bitcast_fusion.1
  153.9 0.9 copy-done.6
  154.8 1.3 convolution_bitcast_fusion.2
  156.2 0.3 convolution_add_fusion.1
  156.4 0.6 maximum_bitcast_fusion
  157.1 6.6 %all-to-all-start.1 = ((f32[8,2,16,128]{3,2,1,0:T(8,128)}), f32[8,2,16,128]{3,2,1,0:T(8,128)S(1)}, u32[]{:S(2)}, u32[]{:S(2)}) async-start(f32[8,2,16,128]{3,2,1,0:T(8,128)} %maximum_bitcast_fusion), calls=%async_computation.1 | async-start | bytes 262144 | tf_op jit(solution)/shard_map/all_to_all | solution.py:67
  163.7 0.7 copy-done.21
  164.3 0.3 fusion.28
  164.9 1.0 copy.31
  165.9 1.9 %fusion.2 = f32[16,1,128]{2,1,0:T(1,128)S(1)} fusion(f32[16,128,1]{1,2,0:T(1,128)S(1)} %bitcast.237, f32[16,128]{1,0:T(8,128)S(1)} %reduce_window_sum.30, pred[128,128]{1,0:T(8,128)(4,1)S(1)} %fusion.72), kind=kOutput, calls=%fused_computation.9 | convolution fusion | flops 3670016 | bytes 40960 | tf_op jit(solution)/shard_map/hij,hj->hi/dot_general | solution.py:175
  167.8 0.7 copy-done.20
  168.4 0.7 multiply_subtract_fusion
  169.1 0.6 slice_bitcast_fusion
  (145 shorter events, 6.3 us)
Async XLA Ops:
  0.6 10.7 %copy-start.9 = (bf16[128,1024]{1,0:T(8,128)(2,1)S(1)}, bf16[128,1024]{1,0:T(8,128)(2,1)}, u32[]{:S(2)}) copy-start(bf16[128,1024]{1,0:T(8,128)(2,1)} %param.8) | copy-start | bytes 786436
  2.0 10.6 %all-to-all-start = ((bf16[8,2,16,128]{3,2,1,0:T(8,128)(2,1)}), bf16[8,2,16,128]{3,2,1,0:T(8,128)(2,1)S(1)}, u32[]{:S(2)}, u32[]{:S(2)}) async-start(bf16[8,2,16,128]{3,2,1,0:T(8,128)(2,1)} %broadcast_in_dim.28), calls=%async_computation | async-start | bytes 131072 | tf_op jit(solution)/shard_map/all_to_all | solution.py:92
  8.1 0.7 copy-start.12
  8.7 2.0 %copy-start.11 = (f32[16,128]{1,0:T(8,128)S(1)}, f32[16,128]{1,0:T(8,128)}, u32[]{:S(2)}) copy-start(f32[16,128]{1,0:T(8,128)} %param.10) | copy-start | bytes 24580
  10.1 0.7 copy-start.19
  11.5 1.0 copy-start.10
  11.5 1.5 copy-start
  14.1 9.5 %collective-permute-start = (s16[1033,128]{1,0:T(8,128)(2,1)S(1)}, s16[1033,128]{1,0:T(8,128)(2,1)S(1)}, u32[]{:S(2)}, u32[]{:S(2)}) collective-permute-start(s16[1033,128]{1,0:T(8,128)(2,1)S(1)} %get-tuple-element.19), channel_id=1, source_target_pairs={{0,8},{8,16},{16,24},{24,32},{32,40},{40,48},{48,56},{56,64},{64,7... | collective-permute-start | bytes 793352 | tf_op jit(solution)/shard_map/ppermute | solution.py:12
  17.6 10.9 %collective-permute-start.1 = (s16[1033,128]{1,0:T(8,128)(2,1)S(1)}, s16[1033,128]{1,0:T(8,128)(2,1)S(1)}, u32[]{:S(2)}, u32[]{:S(2)}) collective-permute-start(s16[1033,128]{1,0:T(8,128)(2,1)S(1)} %get-tuple-element.20), channel_id=1, source_target_pairs={{8,0},{16,8},{24,16},{32,24},{40,32},{48,40},{56,48},{64,56},{72,6... | collective-permute-start | bytes 793352 | tf_op jit(solution)/shard_map/ppermute | solution.py:12
  28.6 2.3 %copy-start.2 = (s16[1033,128]{1,0:T(8,128)(2,1)}, s16[1033,128]{1,0:T(8,128)(2,1)S(1)}, u32[]{:S(2)}) copy-start(s16[1033,128]{1,0:T(8,128)(2,1)S(1)} %collective-permute-done.1) | copy-start | bytes 793348
  30.2 0.5 copy-start.15
  30.2 0.6 copy-start.17
  31.7 11.1 %collective-permute-start.2 = (s16[1033,128]{1,0:T(8,128)(2,1)S(1)}, s16[1033,128]{1,0:T(8,128)(2,1)S(1)}, u32[]{:S(2)}, u32[]{:S(2)}) collective-permute-start(s16[1033,128]{1,0:T(8,128)(2,1)S(1)} %get-tuple-element.21), channel_id=1, source_target_pairs={{0,16},{8,24},{16,32},{24,40},{32,48},{40,56},{48,64},{56,72},{64,... | collective-permute-start | bytes 793352 | tf_op jit(solution)/shard_map/ppermute | solution.py:12
  36.4 11.5 %collective-permute-start.3 = (s16[1033,128]{1,0:T(8,128)(2,1)S(1)}, s16[1033,128]{1,0:T(8,128)(2,1)S(1)}, u32[]{:S(2)}, u32[]{:S(2)}) collective-permute-start(s16[1033,128]{1,0:T(8,128)(2,1)S(1)} %get-tuple-element.22), channel_id=1, source_target_pairs={{16,0},{24,8},{32,16},{40,24},{48,32},{56,40},{64,48},{72,56},{80,... | collective-permute-start | bytes 793352 | tf_op jit(solution)/shard_map/ppermute | solution.py:12
  42.7 5.4 %copy-start.8 = (s16[1033,128]{1,0:T(8,128)(2,1)}, s16[1033,128]{1,0:T(8,128)(2,1)S(1)}, u32[]{:S(2)}) copy-start(s16[1033,128]{1,0:T(8,128)(2,1)S(1)} %collective-permute-done.2) | copy-start | bytes 793348
  48.0 0.7 copy-start.7
  48.7 1.0 copy-start.3
  48.7 0.9 copy-start.13
  48.7 0.9 copy-start.14
  51.0 0.7 copy-start.18
  51.8 0.7 copy-start.16
  54.0 15.3 %collective-permute-start.4 = (s16[1033,128]{1,0:T(8,128)(2,1)}, s16[1033,128]{1,0:T(8,128)(2,1)S(1)}, u32[]{:S(2)}, u32[]{:S(2)}) collective-permute-start(s16[1033,128]{1,0:T(8,128)(2,1)} %get-tuple-element.32), channel_id=1, source_target_pairs={{0,32},{8,40},{16,48},{24,56},{32,64},{40,72},{48,80},{56,88},{64,... | collective-permute-start | bytes 793352 | tf_op jit(solution)/shard_map/ppermute | solution.py:12
  61.6 14.0 %collective-permute-start.5 = (s16[1033,128]{1,0:T(8,128)(2,1)}, s16[1033,128]{1,0:T(8,128)(2,1)S(1)}, u32[]{:S(2)}, u32[]{:S(2)}) collective-permute-start(s16[1033,128]{1,0:T(8,128)(2,1)} %get-tuple-element.29), channel_id=1, source_target_pairs={{32,0},{40,8},{48,16},{56,24},{64,32},{72,40},{80,48},{88,56},{96,... | collective-permute-start | bytes 793352 | tf_op jit(solution)/shard_map/ppermute | solution.py:12
  77.2 15.3 %copy-start.1 = (f32[16,128,64]{1,2,0:T(8,128)S(1)}, f32[16,128,64]{1,2,0:T(8,128)}, u32[]{:S(2)}) copy-start(f32[16,128,64]{1,2,0:T(8,128)} %copy-done) | copy-start | bytes 1572868
  78.0 38.4 %collective-permute-start.6 = (s16[1033,128]{1,0:T(8,128)(2,1)}, s16[1033,128]{1,0:T(8,128)(2,1)S(1)}, u32[]{:S(2)}, u32[]{:S(2)}) collective-permute-start(s16[1033,128]{1,0:T(8,128)(2,1)} %get-tuple-element.29), channel_id=1, source_target_pairs={{8,0},{16,8},{24,16},{32,24},{40,32},{48,40},{56,48},{64,56},{72,6... | collective-permute-start | bytes 793352 | tf_op jit(solution)/shard_map/ppermute | solution.py:12
  96.7 23.2 %collective-permute-start.7 = (s16[1033,128]{1,0:T(8,128)(2,1)}, s16[1033,128]{1,0:T(8,128)(2,1)S(1)}, u32[]{:S(2)}, u32[]{:S(2)}) collective-permute-start(s16[1033,128]{1,0:T(8,128)(2,1)} %get-tuple-element.30), channel_id=1, source_target_pairs={{40,0},{48,8},{56,16},{64,24},{72,32},{80,40},{88,48},{96,56},{104... | collective-permute-start | bytes 793352 | tf_op jit(solution)/shard_map/ppermute | solution.py:12
  105.8 14.1 %collective-permute-start.8 = (s16[1033,128]{1,0:T(8,128)(2,1)}, s16[1033,128]{1,0:T(8,128)(2,1)S(1)}, u32[]{:S(2)}, u32[]{:S(2)}) collective-permute-start(s16[1033,128]{1,0:T(8,128)(2,1)} %get-tuple-element.32), channel_id=1, source_target_pairs={{0,8},{8,16},{16,24},{24,32},{32,40},{40,48},{48,56},{56,64},{64,7... | collective-permute-start | bytes 793352 | tf_op jit(solution)/shard_map/ppermute | solution.py:12
  107.7 40.8 %collective-permute-start.9 = (s16[1033,128]{1,0:T(8,128)(2,1)}, s16[1033,128]{1,0:T(8,128)(2,1)S(1)}, u32[]{:S(2)}, u32[]{:S(2)}) collective-permute-start(s16[1033,128]{1,0:T(8,128)(2,1)} %get-tuple-element.33), channel_id=1, source_target_pairs={{0,40},{8,48},{16,56},{24,64},{32,72},{40,80},{48,88},{56,96},{64,... | collective-permute-start | bytes 793352 | tf_op jit(solution)/shard_map/ppermute | solution.py:12
  119.9 30.5 %copy-start.5 = (s16[1033,128]{1,0:T(8,128)(2,1)}, s16[1033,128]{1,0:T(8,128)(2,1)S(1)}, u32[]{:S(2)}) copy-start(s16[1033,128]{1,0:T(8,128)(2,1)S(1)} %collective-permute-done.7) | copy-start | bytes 793348
  153.8 1.0 copy-start.6
  156.2 7.5 %copy-start.4 = (f32[1024,128]{1,0:T(8,128)S(1)}, f32[1024,128]{1,0:T(8,128)}, u32[]{:S(2)}) copy-start(f32[1024,128]{1,0:T(8,128)} %get-tuple-element.59) | copy-start | bytes 1572868
  157.1 12.0 %all-to-all-start.1 = ((f32[8,2,16,128]{3,2,1,0:T(8,128)}), f32[8,2,16,128]{3,2,1,0:T(8,128)S(1)}, u32[]{:S(2)}, u32[]{:S(2)}) async-start(f32[8,2,16,128]{3,2,1,0:T(8,128)} %maximum_bitcast_fusion), calls=%async_computation.1 | async-start | bytes 262144 | tf_op jit(solution)/shard_map/all_to_all | solution.py:67
  163.7 0.7 copy-start.21
  167.8 0.7 copy-start.20
